TPU v7x, 512 devices: a whole 4x8x8 slice. The times are simulated.
512 devices in a mesh: dom: 128 (over z, y, core), feat: 4 (over x).
Axes of the slice: x: 4, y: 8, z: 8, core: 2. Of those that a mesh axis runs over, the one named last changes fastest.
Arguments:
- node_feats: bfloat16 [256, 262144], P('feat', 'dom'), may hold values from -6 to 6
- weight: bfloat16 [256, 256], P(None, 'feat'), may hold values from -0.375 to 0.375
- bias_vec: bfloat16 [256], P('feat'), may hold values from -3 to 3
- adj_tiles: bfloat16 [12288, 128, 128], P('dom'), may hold values from -0.25 to 0.25
- tile_row: int32 [12288], P('dom'), may hold values from 0 to 15, as said below
- tile_col: int32 [12288], P('dom'), may hold values from 0 to 143, as said below
- tile_count: int32 [128], P('dom'), may hold values from 58 to 96
- send_block: int32 [16384], P('dom'), may hold values from 0 to 15, as said below
- cotangent: bfloat16 [256, 262144], P('feat', 'dom'), may hold values from -6 to 6
Outputs:
- activations: bfloat16 [256, 262144], P('feat', 'dom')
- grad_input: bfloat16 [256, 262144], P('feat', 'dom')
- grad_weight: float32 [256, 256], P(None, 'feat')
- grad_bias: float32 [256], P('feat')
Inputs may be any that keep to these rules, and one draw needn't show every extreme that they name: `tile_row`: entries past a partition's tile_count are padding, of the same range. `tile_col`: among a partition's valid entries, each peer's halo slot 16 + q is named at most once, and a partition's own slot never. `send_block`: entry q * 128 + p is the local block that partition q sends to partition p; it is defined for every pair.
All inputs are finite; a program needn't handle non-finite values.
Results may differ from a plain program's by a relative error of at most 0.0064.
Values may be sent and summed in bfloat16 or wider, within the bound.
No kernel may reach another device: no remote copies, remote signals or barrier semaphores. Data moves between devices by JAX's collectives and lax.ppermute only.
A program may use at most 64 MiB of HBM per device.

v0:
```python
import math

import jax
import jax.numpy as jnp
from jax import lax
from jax.sharding import PartitionSpec as P


def smooth_gate(values):
    return jax.nn.gelu(values, approximate=True)


def per_device(
    node_feats, weight, bias_vec, adj_tiles, tile_row, tile_col, tile_count, send_block, cotangent
):
    feat_rows, node_rows = node_feats.shape
    tile_slots = adj_tiles.shape[0]
    tile_size = adj_tiles.shape[1]
    blocks = node_rows // tile_size
    domains = lax.axis_size("dom")
    whole = lax.all_gather(node_feats, "feat", axis=0, tiled=True)
    hidden = lax.dot_general(
        weight, whole, (((0,), (0,)), ((), ())), preferred_element_type=jnp.float32
    ).astype(jnp.bfloat16)
    hid_blocks = hidden.reshape(feat_rows, blocks, tile_size)
    outgoing = jnp.take(hid_blocks, send_block, axis=1)
    incoming = lax.all_to_all(outgoing, "dom", split_axis=1, concat_axis=1, tiled=True)
    sources = jnp.concatenate([hid_blocks, incoming], axis=1)
    live_tiles = jnp.arange(tile_slots) < tile_count[0]
    live_float = live_tiles.astype(jnp.float32)
    row_place = (tile_row[:, None] == jnp.arange(blocks)[None, :]).astype(jnp.float32) * live_float[
        :, None
    ]
    picked = jnp.take(sources, tile_col, axis=1)
    products = jnp.einsum("otb,tab->ota", picked, adj_tiles, preferred_element_type=jnp.float32)
    summed = jnp.einsum(
        "ota,tr->ora", products, row_place, precision=lax.Precision.HIGHEST
    ).reshape(feat_rows, node_rows)
    preact = summed + bias_vec.astype(jnp.float32)[:, None]
    activated, pullback = jax.vjp(smooth_gate, preact)
    grad_pre = pullback(cotangent.astype(jnp.float32))[0]
    grad_low = grad_pre.astype(jnp.bfloat16)
    grad_blocks = grad_low.reshape(feat_rows, blocks, tile_size)
    rows_picked = jnp.take(grad_blocks, tile_row, axis=1)
    backward = jnp.einsum(
        "ota,tab->otb", rows_picked, adj_tiles, preferred_element_type=jnp.float32
    )
    src_place = (tile_col[:, None] == jnp.arange(blocks + domains)[None, :]).astype(
        jnp.float32
    ) * live_float[:, None]
    recv_place = (send_block[:, None] == jnp.arange(blocks)[None, :]).astype(jnp.float32)
    own_sum = jnp.einsum(
        "otb,tr->orb", backward, src_place[:, :blocks], precision=lax.Precision.HIGHEST
    )
    slot_hit = jnp.logical_and(
        tile_col[:, None] == blocks + jnp.arange(domains)[None, :], live_tiles[:, None]
    )
    slot_rows = jnp.sum(jnp.where(slot_hit, tile_row[:, None], 0), axis=0)
    out_tiles = jnp.einsum(
        "tq,tab->qab", slot_hit.astype(jnp.bfloat16), adj_tiles, preferred_element_type=jnp.float32
    ).astype(jnp.bfloat16)
    out_rows = jnp.take(grad_blocks, slot_rows, axis=1)
    in_tiles = lax.all_to_all(out_tiles, "dom", split_axis=0, concat_axis=0, tiled=True)
    in_rows = lax.all_to_all(out_rows, "dom", split_axis=1, concat_axis=1, tiled=True)
    remote_sum = jnp.einsum("oqa,qab->oqb", in_rows, in_tiles, preferred_element_type=jnp.float32)
    grad_sum = own_sum + jnp.einsum(
        "oqb,qr->orb", remote_sum, recv_place, precision=lax.Precision.HIGHEST
    )
    grad_hidden = grad_sum.reshape(feat_rows, node_rows).astype(jnp.bfloat16)
    norm_scale = 1.0 / math.sqrt(domains * node_rows)
    weight_part = lax.dot_general(
        whole, grad_hidden, (((1,), (1,)), ((), ())), preferred_element_type=jnp.float32
    )
    bias_part = jnp.sum(grad_pre, axis=1)
    weight_sum, bias_sum = lax.psum((weight_part, bias_part), "dom")
    grad_weight = weight_sum * norm_scale
    grad_bias = bias_sum * norm_scale
    full_weight, all_grad = (
        lax.all_gather(weight, "feat", axis=1, tiled=True),
        lax.all_gather(grad_hidden, "feat", axis=0, tiled=True),
    )
    my_rows = lax.dynamic_slice_in_dim(
        full_weight, lax.axis_index("feat") * feat_rows, feat_rows, 0
    )
    grad_input = jnp.dot(my_rows, all_grad, preferred_element_type=jnp.float32).astype(jnp.bfloat16)
    return (activated.astype(jnp.bfloat16), grad_input, grad_weight, grad_bias)


def solution(mesh):
    placed = (
        P("feat", "dom"),
        P(None, "feat"),
        P("feat"),
        P("dom", None, None),
        P("dom"),
        P("dom"),
        P("dom"),
        P("dom"),
        P("feat", "dom"),
    )
    return jax.shard_map(
        per_device,
        mesh=mesh,
        in_specs=placed,
        out_specs=(P("feat", "dom"), P("feat", "dom"), P(None, "feat"), P("feat")),
        check_vma=False,
    )
```

profile of v0, /device:TPU:1, one launch (start us, length us, event | category | flops | bytes accessed | tf_op | source)
XLA Modules:
  0.0 581.7 jit_solution(17211733674106753430)
XLA Ops:
  9.4 34.6 %all-gather.3.cloned.1.call-done = bf16[256,2048]{1,0:T(8,128)(2,1)} async-done(((bf16[64,2048]{1,0:T(8,128)(2,1)}), bf16[256,2048]{1,0:T(8,128)(2,1)}) %all-gather.3.cloned.1.call-update) | async-done | bytes 1048592 | tf_op jit(solution)/shard_map/all_gather | solution.py:21
  45.6 2.2 gather_fusion.2
  47.8 3.2 select_bitcast_fusion.1
  51.0 15.8 %all-to-all-start = ((bf16[64,128,128]{2,0,1:T(8,128)(2,1)}), bf16[64,128,128]{2,0,1:T(8,128)(2,1)}, u32[]{:S(2)}, u32[]{:S(2)}) async-start(bf16[64,128,128]{2,0,1:T(8,128)(2,1)} %select_bitcast_fusion.1), calls=%async_computation | async-start | bytes 4194304 | tf_op jit(solution)/shard_map/all_to_all | solution.py:27
  67.5 2.9 fusion.8
  70.4 4.7 copy.30
  75.1 42.6 %all-to-all-done = bf16[64,128,128]{2,0,1:T(8,128)(2,1)} async-done(((bf16[64,128,128]{2,0,1:T(8,128)(2,1)}), bf16[64,128,128]{2,0,1:T(8,128)(2,1)}, u32[]{:S(2)}, u32[]{:S(2)}) %all-to-all-start) | async-done | bytes 2097184 | tf_op jit(solution)/shard_map/all_to_all | solution.py:27
  117.7 9.3 %all-to-all-start.1 = ((bf16[128,128,128]{2,1,0:T(8,128)(2,1)}), bf16[128,128,128]{2,1,0:T(8,128)(2,1)}, u32[]{:S(2)}, u32[]{:S(2)}) async-start(bf16[128,128,128]{2,1,0:T(8,128)(2,1)} %copy.30), calls=%async_computation.1 | async-start | bytes 8388608 | tf_op jit(solution)/shard_map/all_to_all | solution.py:63
  127.3 3.3 pad_maximum_fusion
  130.6 3.6 gather_fusion
  134.2 3.6 convolution_bitcast_fusion.2
  137.8 3.3 fusion.6
  142.6 2.1 gather_fusion.3
  144.7 3.2 select_bitcast_fusion
  147.9 75.7 %all-to-all-done.1 = bf16[128,128,128]{2,1,0:T(8,128)(2,1)} async-done(((bf16[128,128,128]{2,1,0:T(8,128)(2,1)}), bf16[128,128,128]{2,1,0:T(8,128)(2,1)}, u32[]{:S(2)}, u32[]{:S(2)}) %all-to-all-start.1) | async-done | bytes 4194336 | tf_op jit(solution)/shard_map/all_to_all | solution.py:63
  223.6 22.7 %all-to-all-start.2 = ((bf16[64,128,128]{2,0,1:T(8,128)(2,1)}), bf16[64,128,128]{2,0,1:T(8,128)(2,1)}, u32[]{:S(2)}, u32[]{:S(2)}) async-start(bf16[64,128,128]{2,0,1:T(8,128)(2,1)} %select_bitcast_fusion), calls=%async_computation.2 | async-start | bytes 4194304 | tf_op jit(solution)/shard_map/all_to_all | solution.py:64
  248.6 4.1 convolution_bitcast_fusion.1
  252.7 44.5 %all-to-all-done.2 = bf16[64,128,128]{2,0,1:T(8,128)(2,1)} async-done(((bf16[64,128,128]{2,0,1:T(8,128)(2,1)}), bf16[64,128,128]{2,0,1:T(8,128)(2,1)}, u32[]{:S(2)}, u32[]{:S(2)}) %all-to-all-start.2) | async-done | bytes 2097184 | tf_op jit(solution)/shard_map/all_to_all | solution.py:64
  297.2 4.0 convolution_bitcast_fusion
  301.3 3.8 fusion
  305.2 3.3 fusion.20
  310.4 9.1 %all_gather.10 = bf16[256,256]{0,1:T(8,128)(2,1)S(1)} all-gather(bf16[256,64]{0,1:T(8,128)(2,1)S(1)} %copy-done.4), channel_id=1, replica_groups=mesh['dom'=128,'feat'=4] {'feat'}, dimensions={1}, use_global_device_ids=true | all-gather | bytes 163840 | tf_op jit(solution)/shard_map/all_gather | solution.py:79
  319.5 251.3 %psum.15 = f32[64]{0:T(128)S(1)} all-reduce(f32[64]{0:T(128)S(1)} %get-tuple-element.5), channel_id=1, replica_groups=mesh['dom'=128,'feat'=4] {'dom'}, use_global_device_ids=true, to_apply=%region_3.5 | all-reduce | flops 64 | bytes 512 | tf_op jit(solution)/shard_map/psum | solution.py:75
  572.8 2.3 convolution_convert_fusion
  (52 shorter events, 11.7 us)
Async XLA Ops:
  7.2 60.3 %copy-start = (bf16[96,128,128]{2,1,0:T(8,128)(2,1)S(1)}, bf16[96,128,128]{2,1,0:T(8,128)(2,1)}, u32[]{:S(2)}) copy-start(bf16[96,128,128]{2,1,0:T(8,128)(2,1)} %param.14) | copy-start | bytes 9437188
  7.2 36.8 %all-gather.3.cloned.1.call-start = ((), (), s32[]{:S(2)}) async-start(), calls=%async_computation.3 | async-start | bytes 1310720 | tf_op jit(solution)/shard_map/all_gather | solution.py:21
  51.0 16.5 %copy-start.5 = (s32[96]{0:T(128)S(1)}, s32[96]{0:T(128)}, u32[]{:S(2)}) copy-start(s32[96]{0:T(128)} %param.16) | copy-start | bytes 1156
  51.0 66.7 %all-to-all-start = ((bf16[64,128,128]{2,0,1:T(8,128)(2,1)}), bf16[64,128,128]{2,0,1:T(8,128)(2,1)}, u32[]{:S(2)}, u32[]{:S(2)}) async-start(bf16[64,128,128]{2,0,1:T(8,128)(2,1)} %select_bitcast_fusion.1), calls=%async_computation | async-start | bytes 4194304 | tf_op jit(solution)/shard_map/all_to_all | solution.py:27
  75.1 52.0 %copy-start.8 = (bf16[64]{0:T(256)(128)(2,1)S(1)}, bf16[64]{0:T(256)(128)(2,1)}, u32[]{:S(2)}) copy-start(bf16[64]{0:T(256)(128)(2,1)} %param.13) | copy-start | bytes 388
  75.1 52.0 %copy-start.6 = (s32[96]{0:T(128)S(1)}, s32[96]{0:T(128)}, u32[]{:S(2)}) copy-start(s32[96]{0:T(128)} %param.15) | copy-start | bytes 1156
  117.7 105.8 %all-to-all-start.1 = ((bf16[128,128,128]{2,1,0:T(8,128)(2,1)}), bf16[128,128,128]{2,1,0:T(8,128)(2,1)}, u32[]{:S(2)}, u32[]{:S(2)}) async-start(bf16[128,128,128]{2,1,0:T(8,128)(2,1)} %copy.30), calls=%async_computation.1 | async-start | bytes 8388608 | tf_op jit(solution)/shard_map/all_to_all | solution.py:63
  137.8 3.3 copy-start.3
  223.6 73.6 %all-to-all-start.2 = ((bf16[64,128,128]{2,0,1:T(8,128)(2,1)}), bf16[64,128,128]{2,0,1:T(8,128)(2,1)}, u32[]{:S(2)}, u32[]{:S(2)}) async-start(bf16[64,128,128]{2,0,1:T(8,128)(2,1)} %select_bitcast_fusion), calls=%async_computation.2 | async-start | bytes 4194304 | tf_op jit(solution)/shard_map/all_to_all | solution.py:64
  246.3 325.0 %all-reduce.2.cloned.1.call-start = ((), (), s32[]{:S(2)}) async-start(), calls=%async_computation.5 | async-start | bytes 131072 | tf_op jit(solution)/shard_map/psum | solution.py:75
  252.7 48.5 %copy-start.7 = (s32[128]{0:T(128)S(1)}, s32[128]{0:T(128)}, u32[]{:S(2)}) copy-start(s32[128]{0:T(128)} %param.18) | copy-start | bytes 1540
  301.3 3.9 copy-start.1
  305.1 3.3 copy-start.2
  305.1 5.3 copy-start.4
  309.6 263.2 %all-gather.5.cloned.1.call-start = ((), (), s32[]{:S(2)}) async-start(), calls=%async_computation.4 | async-start | bytes 1310720 | tf_op jit(solution)/shard_map/all_gather | solution.py:80
Sparse Core Ops, SparseCore 0:
  10.1 33.8 all-gather.2
  309.7 175.5 all-reduce.1
  488.0 21.2 all-gather.4
where the time goes:
time: 582 us
  blocking collectives  260 us (45%)
  waiting for transfers between devices  198 us (34%)
  starting transfers between devices  48.1 us (8%)
  matrix products  30.1 us (5%)
  local copies, waits for them, and re-layouts  15.6 us (3%)
  other arithmetic  14.7 us (3%)
  between operations  14.7 us (3%)
    psum x1, blocking collectives, per_device(): weight_sum, bias_sum = lax.psum((weight_part, bias_part), 'dom')  251 us
    all_to_all x1, waiting for transfers between devices, per_device(): lax.all_to_all(out_tiles, 'dom', split_axis=0, concat_axis=0, tiled=True)  75.7 us
    all_to_all x1, waiting for transfers between devices, per_device(): lax.all_to_all(out_rows, 'dom', split_axis=1, concat_axis=1, tiled=True)  44.5 us
    all_to_all x1, waiting for transfers between devices, per_device(): lax.all_to_all(outgoing, 'dom', split_axis=1, concat_axis=1, tiled=True)  42.6 us
    all_gather x1, waiting for transfers between devices, per_device(): whole = lax.all_gather(node_feats, 'feat', axis=0, tiled=True)  34.6 us
    all_to_all x1, starting transfers between devices, per_device(): lax.all_to_all(out_rows, 'dom', split_axis=1, concat_axis=1, tiled=True)  22.7 us
    all_to_all x1, starting transfers between devices, per_device(): lax.all_to_all(outgoing, 'dom', split_axis=1, concat_axis=1, tiled=True)  15.8 us
  transfers between devices with their start and end apart: 6, of which 4 were waited for; matrix products, arithmetic and copies ran while one was open for 7% of the time, Pallas kernels for 0%

commit v1 on v0

--- a/solution.py
+++ b/solution.py
@@ -8,6 +8,15 @@
 
 def smooth_gate(values):
     return jax.nn.gelu(values, approximate=True)
+
+
+def butterfly_sum(values, axis, size):
+    step = 1
+    while step < size:
+        pairs = [(i, i ^ step) for i in range(size)]
+        values = values + lax.ppermute(values, axis, pairs)
+        step *= 2
+    return values
 
 
 def per_device(
@@ -45,26 +54,24 @@
     backward = jnp.einsum(
         "ota,tab->otb", rows_picked, adj_tiles, preferred_element_type=jnp.float32
     )
-    src_place = (tile_col[:, None] == jnp.arange(blocks + domains)[None, :]).astype(
+    src_place = (tile_col[:, None] == jnp.arange(blocks)[None, :]).astype(
         jnp.float32
     ) * live_float[:, None]
     recv_place = (send_block[:, None] == jnp.arange(blocks)[None, :]).astype(jnp.float32)
     own_sum = jnp.einsum(
-        "otb,tr->orb", backward, src_place[:, :blocks], precision=lax.Precision.HIGHEST
+        "otb,tr->orb", backward, src_place, precision=lax.Precision.HIGHEST
     )
     slot_hit = jnp.logical_and(
         tile_col[:, None] == blocks + jnp.arange(domains)[None, :], live_tiles[:, None]
     )
-    slot_rows = jnp.sum(jnp.where(slot_hit, tile_row[:, None], 0), axis=0)
-    out_tiles = jnp.einsum(
-        "tq,tab->qab", slot_hit.astype(jnp.bfloat16), adj_tiles, preferred_element_type=jnp.float32
-    ).astype(jnp.bfloat16)
-    out_rows = jnp.take(grad_blocks, slot_rows, axis=1)
-    in_tiles = lax.all_to_all(out_tiles, "dom", split_axis=0, concat_axis=0, tiled=True)
-    in_rows = lax.all_to_all(out_rows, "dom", split_axis=1, concat_axis=1, tiled=True)
-    remote_sum = jnp.einsum("oqa,qab->oqb", in_rows, in_tiles, preferred_element_type=jnp.float32)
+    hit_tile = jnp.sum(jnp.where(slot_hit, jnp.arange(tile_slots)[:, None], 0), axis=0)
+    has_hit = jnp.any(slot_hit, axis=0)
+    out_parts = jnp.where(
+        has_hit[None, :, None], jnp.take(backward, hit_tile, axis=1), 0.0
+    )
+    in_parts = lax.all_to_all(out_parts, "dom", split_axis=1, concat_axis=1, tiled=True)
     grad_sum = own_sum + jnp.einsum(
-        "oqb,qr->orb", remote_sum, recv_place, precision=lax.Precision.HIGHEST
+        "oqb,qr->orb", in_parts, recv_place, precision=lax.Precision.HIGHEST
     )
     grad_hidden = grad_sum.reshape(feat_rows, node_rows).astype(jnp.bfloat16)
     norm_scale = 1.0 / math.sqrt(domains * node_rows)
@@ -72,9 +79,10 @@
         whole, grad_hidden, (((1,), (1,)), ((), ())), preferred_element_type=jnp.float32
     )
     bias_part = jnp.sum(grad_pre, axis=1)
-    weight_sum, bias_sum = lax.psum((weight_part, bias_part), "dom")
-    grad_weight = weight_sum * norm_scale
-    grad_bias = bias_sum * norm_scale
+    packed = jnp.concatenate([weight_part, bias_part[None, :]], axis=0)
+    packed = butterfly_sum(packed, "dom", domains)
+    grad_weight = packed[:-1] * norm_scale
+    grad_bias = packed[-1] * norm_scale
     full_weight, all_grad = (
         lax.all_gather(weight, "feat", axis=1, tiled=True),
         lax.all_gather(grad_hidden, "feat", axis=0, tiled=True),

time: 582 us -> 340 us (0.58)
  blocking collectives: 260 us -> 115 us
  waiting for transfers between devices: 198 us -> 103 us
  matrix products: 30.1 us -> 23.7 us
    psum x1 -> x0, blocking collectives: 251 us -> none  [per_device(): weight_sum, bias_sum = lax.psum((weight_part, bias_part), 'dom')]
    all_to_all x2 -> x0, waiting for transfers between devices: 120 us -> none  [the longest x1 75.7 us: per_device(): lax.all_to_all(out_tiles, 'dom', split_axis=0, concat_axis=0, tiled=True)]
    all_to_all x0 -> x1, blocking collectives: none -> 106 us  [per_device(): lax.all_to_all(out_parts, 'dom', split_axis=1, concat_axis=1, tiled=True)]
    ppermute x0 -> x7, starting transfers between devices: none -> 33.3 us  [butterfly_sum(): values = values + lax.ppermute(values, axis, pairs)]
    all_to_all x2 -> x0, starting transfers between devices: 32 us -> none  [the longest x1 22.7 us: per_device(): lax.all_to_all(out_rows, 'dom', split_axis=1, concat_axis=1, tiled=True)]
    ppermute x0 -> x7, waiting for transfers between devices: none -> 18.3 us  [butterfly_sum(): values = values + lax.ppermute(values, axis, pairs)]
    all_to_all x1, waiting for transfers between devices: 42.6 us -> 49.8 us  [per_device(): lax.all_to_all(outgoing, 'dom', split_axis=1, concat_axis=1, tiled=True)]
    dot_general x4 -> x2, matrix products: 14.1 us -> 7.13 us  [the longest x1 3.84 us: per_device(): jnp.einsum('oqb,qr->orb', in_parts, recv_place, precision=lax.Precision.H...]
  transfers between devices with their start and end apart: 6 -> 10, of which waited for: 4 -> 8; matrix products, arithmetic and copies ran while one was open for 7% -> 2% of each run, Pallas kernels for 0% -> 0%
where the time goes in v1:
time: 340 us; the launch traced here: 334 us
  blocking collectives  115 us (34%)
  waiting for transfers between devices  103 us (30%)
  starting transfers between devices  49.2 us (14%)
  matrix products  23.7 us (7%)
  between operations  15 us (4%)
  other arithmetic  14.6 us (4%)
  local copies, waits for them, and re-layouts  13.4 us (4%)
    all_to_all x1, blocking collectives, per_device(): lax.all_to_all(out_parts, 'dom', split_axis=1, concat_axis=1, tiled=True)  106 us
    all_to_all x1, waiting for transfers between devices, per_device(): lax.all_to_all(outgoing, 'dom', split_axis=1, concat_axis=1, tiled=True)  49.8 us
    all_gather x1, waiting for transfers between devices, per_device(): whole = lax.all_gather(node_feats, 'feat', axis=0, tiled=True)  34.6 us
    ppermute x7, starting transfers between devices, butterfly_sum(): values = values + lax.ppermute(values, axis, pairs)  33.3 us
    ppermute x7, waiting for transfers between devices, butterfly_sum(): values = values + lax.ppermute(values, axis, pairs)  18.3 us
    all_to_all x1, starting transfers between devices, per_device(): lax.all_to_all(outgoing, 'dom', split_axis=1, concat_axis=1, tiled=True)  15.8 us
    all_gather x1, blocking collectives, per_device(): lax.all_gather(weight, 'feat', axis=1, tiled=True)  9.51 us
  transfers between devices with their start and end apart: 10, of which 8 were waited for; matrix products, arithmetic and copies ran while one was open for 2% of the time, Pallas kernels for 0%

profile of v1, /device:TPU:1, one launch (start us, length us, event | category | flops | bytes accessed | tf_op | source)
XLA Modules:
  0.0 334.4 jit_solution(7539842585771590036)
XLA Ops:
  9.4 34.6 %all-gather.3.cloned.1.call-done = bf16[256,2048]{1,0:T(8,128)(2,1)} async-done(((bf16[64,2048]{1,0:T(8,128)(2,1)}), bf16[256,2048]{1,0:T(8,128)(2,1)}) %all-gather.3.cloned.1.call-update) | async-done | bytes 1048592 | tf_op jit(solution)/shard_map/all_gather | solution.py:30
  47.8 3.2 select_bitcast_fusion.1
  51.0 15.8 %all-to-all-start = ((bf16[64,128,128]{2,0,1:T(8,128)(2,1)}), bf16[64,128,128]{2,0,1:T(8,128)(2,1)}, u32[]{:S(2)}, u32[]{:S(2)}) async-start(bf16[64,128,128]{2,0,1:T(8,128)(2,1)} %select_bitcast_fusion.1), calls=%async_computation | async-start | bytes 4194304 | tf_op jit(solution)/shard_map/all_to_all | solution.py:36
  67.9 49.8 %all-to-all-done = bf16[64,128,128]{2,0,1:T(8,128)(2,1)} async-done(((bf16[64,128,128]{2,0,1:T(8,128)(2,1)}), bf16[64,128,128]{2,0,1:T(8,128)(2,1)}, u32[]{:S(2)}, u32[]{:S(2)}) %all-to-all-start) | async-done | bytes 2097184 | tf_op jit(solution)/shard_map/all_to_all | solution.py:36
  117.7 3.2 pad_maximum_fusion
  120.9 3.6 %gather_fusion.1 = bf16[96,64,128]{2,1,0:T(8,128)(2,1)} fusion(bf16[64,144,128]{2,0,1:T(8,128)(2,1)} %pad_maximum_fusion, s32[1024]{0:T(1024)S(1)} %pad_clamp_fusion.2), kind=kCustom, calls=%fused_computation.1 | custom fusion | bytes 3146112 | tf_op jit(solution)/shard_map/jit(_take)/gather | solution.py:43
  124.5 3.6 %convolution_bitcast_fusion.1 = f32[64,96,128]{2,0,1:T(8,128)S(1)} fusion(bf16[96,128,128]{2,1,0:T(8,128)(2,1)S(1)} %copy-done, bf16[96,64,128]{2,1,0:T(8,128)(2,1)} %gather_fusion.1, pred[96]{0:T(512)(128)(4,1)S(1)} %compare_and_fusion.4), kind=kOutput, calls=%fused_computation.16 | convolution fusion | flops 202113024 | bytes 7864416 | tf_op jit(solution)/shard_map/otb,tab->ota/dot_general | solution.py:44
  128.1 3.3 fusion.4
  134.8 4.1 %convolution_bitcast_fusion = f32[64,96,128]{2,0,1:T(8,128)} fusion(bf16[96,128,128]{2,1,0:T(8,128)(2,1)S(1)} %copy-done, bf16[96,64,128]{2,1,0:T(8,128)(2,1)} %gather_fusion.2, pred[96]{0:T(512)(128)(4,1)S(1)} %compare_and_fusion.2), kind=kOutput, calls=%fused_computation.15 | convolution fusion | flops 202113024 | bytes 7864416 | tf_op jit(solution)/shard_map/ota,tab->otb/dot_general | solution.py:54
  138.9 4.6 %gather_fusion.3 = f32[128,64,128]{2,1,0:T(8,128)} fusion(f32[64,96,128]{2,0,1:T(8,128)} %convolution_bitcast_fusion, s32[1024]{0:T(1024)S(1)} %pad_clamp_fusion), kind=kCustom, calls=%fused_computation.3 | custom fusion | bytes 8389120 | tf_op jit(solution)/shard_map/jit(_take)/gather | solution.py:70
  143.6 2.8 select_bitcast_fusion
  146.4 105.6 %all_to_all.10 = f32[64,128,128]{2,0,1:T(8,128)S(1)} all-to-all(f32[64,128,128]{2,0,1:T(8,128)S(1)} %select_bitcast_fusion), channel_id=1, replica_groups=mesh['dom'=128,'feat'=4] {'dom'}, dimensions={1} | all-to-all | bytes 8388608 | tf_op jit(solution)/shard_map/all_to_all | solution.py:72
  251.9 3.8 %fusion = f32[16,64,128]{2,0,1:T(8,128)S(1)} fusion(f32[64,128,128]{2,0,1:T(8,128)S(1)} %all_to_all.10, s32[128]{0:T(128)S(1)} %copy-done.6), kind=kOutput, calls=%fused_computation.4 | convolution fusion | flops 201328640 | bytes 4719104 | tf_op jit(solution)/shard_map/oqb,qr->orb/dot_general | solution.py:73
  255.8 3.3 fusion.15
  261.7 2.9 collective-permute-start
  265.5 4.4 %collective-permute-start.1 = (f32[257,64]{0,1:T(8,128)S(1)}, f32[257,64]{0,1:T(8,128)S(1)}, u32[]{:S(2)}, u32[]{:S(2)}) collective-permute-start(f32[257,64]{0,1:T(8,128)S(1)} %fusion.53), channel_id=1, source_target_pairs={{0,8},{4,12},{8,0},{12,4},{16,24},{20,28},{24,16},{28,20},{32,40},... | collective-permute-start | bytes 197384 | tf_op jit(solution)/shard_map/ppermute | solution.py:17
  269.9 2.9 collective-permute-done.1
  272.8 5.8 %collective-permute-start.2 = (f32[257,64]{0,1:T(8,128)S(1)}, f32[257,64]{0,1:T(8,128)S(1)}, u32[]{:S(2)}, u32[]{:S(2)}) collective-permute-start(f32[257,64]{0,1:T(8,128)S(1)} %add.115), channel_id=1, source_target_pairs={{0,16},{4,20},{8,24},{12,28},{16,0},{20,4},{24,8},{28,12},{32,48},... | collective-permute-start | bytes 197384 | tf_op jit(solution)/shard_map/ppermute | solution.py:17
  278.6 3.5 %collective-permute-done.2 = f32[257,64]{0,1:T(8,128)S(1)} collective-permute-done((f32[257,64]{0,1:T(8,128)S(1)}, f32[257,64]{0,1:T(8,128)S(1)}, u32[]{:S(2)}, u32[]{:S(2)}) %collective-permute-start.2) | collective-permute-done | bytes 65824 | tf_op jit(solution)/shard_map/ppermute | solution.py:17
  282.2 11.3 %collective-permute-start.3 = (f32[257,64]{0,1:T(8,128)S(1)}, f32[257,64]{0,1:T(8,128)S(1)}, u32[]{:S(2)}, u32[]{:S(2)}) collective-permute-start(f32[257,64]{0,1:T(8,128)S(1)} %add.116), channel_id=1, source_target_pairs={{0,32},{4,36},{8,40},{12,44},{16,48},{20,52},{24,56},{28,60},{32,0... | collective-permute-start | bytes 197384 | tf_op jit(solution)/shard_map/ppermute | solution.py:17
  298.0 3.4 %collective-permute-done.4 = f32[257,64]{0,1:T(8,128)S(1)} collective-permute-done((f32[257,64]{0,1:T(8,128)S(1)}, f32[257,64]{0,1:T(8,128)S(1)}, u32[]{:S(2)}, u32[]{:S(2)}) %collective-permute-start.4) | collective-permute-done | bytes 65824 | tf_op jit(solution)/shard_map/ppermute | solution.py:17
  303.3 5.1 %collective-permute-done.5 = f32[257,64]{0,1:T(8,128)S(1)} collective-permute-done((f32[257,64]{0,1:T(8,128)S(1)}, f32[257,64]{0,1:T(8,128)S(1)}, u32[]{:S(2)}, u32[]{:S(2)}) %collective-permute-start.5) | collective-permute-done | bytes 65824 | tf_op jit(solution)/shard_map/ppermute | solution.py:17
  308.5 5.0 %collective-permute-start.6 = (f32[257,64]{0,1:T(8,128)S(1)}, f32[257,64]{0,1:T(8,128)}, u32[]{:S(2)}, u32[]{:S(2)}) collective-permute-start(f32[257,64]{0,1:T(8,128)S(1)} %add.119), channel_id=1, source_target_pairs={{0,256},{4,260},{8,264},{12,268},{16,272},{20,276},{24,280},{28,28... | collective-permute-start | bytes 197384 | tf_op jit(solution)/shard_map/ppermute | solution.py:17
  313.5 9.5 %all_gather.10 = bf16[256,256]{0,1:T(8,128)(2,1)S(1)} all-gather(bf16[256,64]{0,1:T(8,128)(2,1)S(1)} %copy-done.3), channel_id=1, replica_groups=mesh['dom'=128,'feat'=4] {'feat'}, dimensions={1}, use_global_device_ids=true | all-gather | bytes 163840 | tf_op jit(solution)/shard_map/all_gather | solution.py:87
  (63 shorter events, 24.1 us)
Async XLA Ops:
  7.2 117.3 %copy-start = (bf16[96,128,128]{2,1,0:T(8,128)(2,1)S(1)}, bf16[96,128,128]{2,1,0:T(8,128)(2,1)}, u32[]{:S(2)}) copy-start(bf16[96,128,128]{2,1,0:T(8,128)(2,1)} %param.12) | copy-start | bytes 9437188
  7.2 36.8 %all-gather.3.cloned.1.call-start = ((), (), s32[]{:S(2)}) async-start(), calls=%async_computation.2 | async-start | bytes 1310720 | tf_op jit(solution)/shard_map/all_gather | solution.py:30
  51.0 16.5 %copy-start.7 = (bf16[64]{0:T(256)(128)(2,1)S(1)}, bf16[64]{0:T(256)(128)(2,1)}, u32[]{:S(2)}) copy-start(bf16[64]{0:T(256)(128)(2,1)} %param.11) | copy-start | bytes 388
  51.0 16.5 %copy-start.4 = (s32[96]{0:T(128)S(1)}, s32[96]{0:T(128)}, u32[]{:S(2)}) copy-start(s32[96]{0:T(128)} %param.14) | copy-start | bytes 1156
  51.0 16.6 %copy-start.5 = (s32[96]{0:T(128)S(1)}, s32[96]{0:T(128)}, u32[]{:S(2)}) copy-start(s32[96]{0:T(128)} %param.13) | copy-start | bytes 1156
  51.0 66.7 %all-to-all-start = ((bf16[64,128,128]{2,0,1:T(8,128)(2,1)}), bf16[64,128,128]{2,0,1:T(8,128)(2,1)}, u32[]{:S(2)}, u32[]{:S(2)}) async-start(bf16[64,128,128]{2,0,1:T(8,128)(2,1)} %select_bitcast_fusion.1), calls=%async_computation | async-start | bytes 4194304 | tf_op jit(solution)/shard_map/all_to_all | solution.py:36
  66.8 258.4 %all-gather.5.cloned.1.call-start = ((), (), s32[]{:S(2)}) async-start(), calls=%async_computation.3 | async-start | bytes 1310720 | tf_op jit(solution)/shard_map/all_gather | solution.py:88
  128.1 3.3 copy-start.2
  146.4 105.6 %copy-start.6 = (s32[128]{0:T(128)S(1)}, s32[128]{0:T(128)}, u32[]{:S(2)}) copy-start(s32[128]{0:T(128)} %param.16) | copy-start | bytes 1540
  251.9 3.8 %copy-start.1 = (f32[64,96,128]{2,0,1:T(8,128)S(1)}, f32[64,96,128]{2,0,1:T(8,128)}, u32[]{:S(2)}) copy-start(f32[64,96,128]{2,0,1:T(8,128)} %convolution_bitcast_fusion) | copy-start | bytes 9437188
  255.8 57.7 %copy-start.3 = (bf16[256,64]{0,1:T(8,128)(2,1)S(1)}, bf16[256,64]{0,1:T(8,128)(2,1)}, u32[]{:S(2)}) copy-start(bf16[256,64]{0,1:T(8,128)(2,1)} %param.10) | copy-start | bytes 98308
  261.7 3.8 %collective-permute-start = (f32[257,64]{0,1:T(8,128)S(1)}, f32[257,64]{0,1:T(8,128)S(1)}, u32[]{:S(2)}, u32[]{:S(2)}) collective-permute-start(f32[257,64]{0,1:T(8,128)S(1)} %pad_maximum_fusion.1), channel_id=1, source_target_pairs={{0,4},{4,0},{8,12},{12,8},{16,20},{20,16},{24,28},{28,24},{32,36},... | collective-permute-start | bytes 197384 | tf_op jit(solution)/shard_map/ppermute | solution.py:17
  265.5 7.3 %collective-permute-start.1 = (f32[257,64]{0,1:T(8,128)S(1)}, f32[257,64]{0,1:T(8,128)S(1)}, u32[]{:S(2)}, u32[]{:S(2)}) collective-permute-start(f32[257,64]{0,1:T(8,128)S(1)} %fusion.53), channel_id=1, source_target_pairs={{0,8},{4,12},{8,0},{12,4},{16,24},{20,28},{24,16},{28,20},{32,40},... | collective-permute-start | bytes 197384 | tf_op jit(solution)/shard_map/ppermute | solution.py:17
  272.8 9.4 %collective-permute-start.2 = (f32[257,64]{0,1:T(8,128)S(1)}, f32[257,64]{0,1:T(8,128)S(1)}, u32[]{:S(2)}, u32[]{:S(2)}) collective-permute-start(f32[257,64]{0,1:T(8,128)S(1)} %add.115), channel_id=1, source_target_pairs={{0,16},{4,20},{8,24},{12,28},{16,0},{20,4},{24,8},{28,12},{32,48},... | collective-permute-start | bytes 197384 | tf_op jit(solution)/shard_map/ppermute | solution.py:17
  282.2 13.8 %collective-permute-start.3 = (f32[257,64]{0,1:T(8,128)S(1)}, f32[257,64]{0,1:T(8,128)S(1)}, u32[]{:S(2)}, u32[]{:S(2)}) collective-permute-start(f32[257,64]{0,1:T(8,128)S(1)} %add.116), channel_id=1, source_target_pairs={{0,32},{4,36},{8,40},{12,44},{16,48},{20,52},{24,56},{28,60},{32,0... | collective-permute-start | bytes 197384 | tf_op jit(solution)/shard_map/ppermute | solution.py:17
  296.0 5.4 %collective-permute-start.4 = (f32[257,64]{0,1:T(8,128)S(1)}, f32[257,64]{0,1:T(8,128)S(1)}, u32[]{:S(2)}, u32[]{:S(2)}) collective-permute-start(f32[257,64]{0,1:T(8,128)S(1)} %add.117), channel_id=1, source_target_pairs={{0,64},{4,68},{8,72},{12,76},{16,80},{20,84},{24,88},{28,92},{32,9... | collective-permute-start | bytes 197384 | tf_op jit(solution)/shard_map/ppermute | solution.py:17
  301.4 7.0 %collective-permute-start.5 = (f32[257,64]{0,1:T(8,128)S(1)}, f32[257,64]{0,1:T(8,128)S(1)}, u32[]{:S(2)}, u32[]{:S(2)}) collective-permute-start(f32[257,64]{0,1:T(8,128)S(1)} %add.118), channel_id=1, source_target_pairs={{0,128},{4,132},{8,136},{12,140},{16,144},{20,148},{24,152},{28,15... | collective-permute-start | bytes 197384 | tf_op jit(solution)/shard_map/ppermute | solution.py:17
  308.5 14.6 %collective-permute-start.6 = (f32[257,64]{0,1:T(8,128)S(1)}, f32[257,64]{0,1:T(8,128)}, u32[]{:S(2)}, u32[]{:S(2)}) collective-permute-start(f32[257,64]{0,1:T(8,128)S(1)} %add.119), channel_id=1, source_target_pairs={{0,256},{4,260},{8,264},{12,268},{16,272},{20,276},{24,280},{28,28... | collective-permute-start | bytes 197384 | tf_op jit(solution)/shard_map/ppermute | solution.py:17
Sparse Core Ops, SparseCore 0:
  10.1 33.8 all-gather.2
  260.0 30.7 all-gather.4

commit v2 on v1

--- a/solution.py
+++ b/solution.py
@@ -10,13 +10,18 @@
     return jax.nn.gelu(values, approximate=True)
 
 
-def butterfly_sum(values, axis, size):
-    step = 1
-    while step < size:
-        pairs = [(i, i ^ step) for i in range(size)]
-        values = values + lax.ppermute(values, axis, pairs)
-        step *= 2
-    return values
+def group_stack(values, axis, size, stride, count):
+    received = [values]
+    for offset in range(1, count):
+        pairs = [(i, i ^ (offset * stride)) for i in range(size)]
+        received.append(lax.ppermute(values, axis, pairs))
+    stacked = jnp.stack(received)
+    mine = (lax.axis_index(axis) // stride) % count
+    return jnp.take(stacked, mine ^ jnp.arange(count), axis=0)
+
+
+def group_sum(values, axis, size, stride, count):
+    return jnp.sum(group_stack(values, axis, size, stride, count), axis=0)
 
 
 def per_device(
@@ -27,7 +32,8 @@
     tile_size = adj_tiles.shape[1]
     blocks = node_rows // tile_size
     domains = lax.axis_size("dom")
-    whole = lax.all_gather(node_feats, "feat", axis=0, tiled=True)
+    parts = lax.axis_size("feat")
+    whole = group_stack(node_feats, "feat", parts, 1, parts).reshape(parts * feat_rows, node_rows)
     hidden = lax.dot_general(
         weight, whole, (((0,), (0,)), ((), ())), preferred_element_type=jnp.float32
     ).astype(jnp.bfloat16)
@@ -80,13 +86,13 @@
     )
     bias_part = jnp.sum(grad_pre, axis=1)
     packed = jnp.concatenate([weight_part, bias_part[None, :]], axis=0)
-    packed = butterfly_sum(packed, "dom", domains)
+    low = 16 if domains % 16 == 0 else 1
+    packed = group_sum(packed, "dom", domains, 1, low)
+    packed = group_sum(packed, "dom", domains, low, domains // low)
     grad_weight = packed[:-1] * norm_scale
     grad_bias = packed[-1] * norm_scale
-    full_weight, all_grad = (
-        lax.all_gather(weight, "feat", axis=1, tiled=True),
-        lax.all_gather(grad_hidden, "feat", axis=0, tiled=True),
-    )
+    full_weight = jnp.concatenate(list(group_stack(weight, "feat", parts, 1, parts)), axis=1)
+    all_grad = group_stack(grad_hidden, "feat", parts, 1, parts).reshape(parts * feat_rows, node_rows)
     my_rows = lax.dynamic_slice_in_dim(
         full_weight, lax.axis_index("feat") * feat_rows, feat_rows, 0
     )

time: 340 us -> 404 us (1.19)
  blocking collectives: 115 us -> 0 us
  starting transfers between devices: 49.2 us -> 145 us
  waiting for transfers between devices: 103 us -> 153 us
  local copies, waits for them, and re-layouts: 13.4 us -> 47.3 us
  other arithmetic: 14.6 us -> 28 us
  between operations: 15 us -> 1.97 us
    all_to_all x1 -> x0, blocking collectives: 106 us -> none  [per_device(): lax.all_to_all(out_parts, 'dom', split_axis=1, concat_axis=1, tiled=True)]
    all_to_all x0 -> x1, waiting for transfers between devices: none -> 83.7 us  [per_device(): lax.all_to_all(out_parts, 'dom', split_axis=1, concat_axis=1, tiled=True)]
    ppermute x7 -> x31, starting transfers between devices: 33.3 us -> 117 us  [group_stack(): received.append(lax.ppermute(values, axis, pairs))]
    all_gather x2 -> x0, waiting for transfers between devices: 34.6 us -> none  [the longest x1 34.6 us: per_device(): whole = lax.all_gather(node_feats, 'feat', axis=0, tiled=True)]
    unnamed x17 -> x54, local copies, waits for them, and re-layouts: 0.82 us -> 19.8 us
    gather x0 -> x5, local copies, waits for them, and re-layouts: none -> 12.1 us  [group_stack(): return jnp.take(stacked, mine ^ jnp.arange(count), axis=0)]
    all_to_all x0 -> x1, starting transfers between devices: none -> 9.62 us  [per_device(): lax.all_to_all(out_parts, 'dom', split_axis=1, concat_axis=1, tiled=True)]
    all_gather x1 -> x0, blocking collectives: 9.51 us -> none  [per_device(): lax.all_gather(weight, 'feat', axis=1, tiled=True)]
  transfers between devices with their start and end apart: 10 -> 33, of which waited for: 8 -> 7; matrix products, arithmetic and copies ran while one was open for 2% -> 9% of each run, Pallas kernels for 0% -> 0%
where the time goes in v2:
time: 404 us; the launch traced here: 396 us
  waiting for transfers between devices  153 us (38%)
  starting transfers between devices  145 us (36%)
  local copies, waits for them, and re-layouts  47.3 us (12%)
  other arithmetic  28 us (7%)
  matrix products  22.1 us (5%)
    ppermute x31, starting transfers between devices, group_stack(): received.append(lax.ppermute(values, axis, pairs))  117 us
    all_to_all x1, waiting for transfers between devices, per_device(): lax.all_to_all(out_parts, 'dom', split_axis=1, concat_axis=1, tiled=True)  83.7 us
    all_to_all x1, waiting for transfers between devices, per_device(): lax.all_to_all(outgoing, 'dom', split_axis=1, concat_axis=1, tiled=True)  50.7 us
    unnamed x54, local copies, waits for them, and re-layouts  19.8 us
    ppermute x31, waiting for transfers between devices, group_stack(): received.append(lax.ppermute(values, axis, pairs))  18.2 us
    all_to_all x1, starting transfers between devices, per_device(): lax.all_to_all(outgoing, 'dom', split_axis=1, concat_axis=1, tiled=True)  18.1 us
    gather x5, local copies, waits for them, and re-layouts, group_stack(): return jnp.take(stacked, mine ^ jnp.arange(count), axis=0)  12.1 us
    all_to_all x1, starting transfers between devices, per_device(): lax.all_to_all(out_parts, 'dom', split_axis=1, concat_axis=1, tiled=True)  9.62 us
  transfers between devices with their start and end apart: 33, of which 7 were waited for; matrix products, arithmetic and copies ran while one was open for 9% of the time, Pallas kernels for 0%

profile of v2, /device:TPU:1, one launch (start us, length us, event | category | flops | bytes accessed | tf_op | source)
XLA Modules:
  0.0 396.4 jit_solution(4336570680088711719)
XLA Ops:
  0.6 4.2 %collective-permute-start = (bf16[64,2048]{1,0:T(8,128)(2,1)}, bf16[64,2048]{1,0:T(8,128)(2,1)S(1)}, u32[]{:S(2)}, u32[]{:S(2)}) collective-permute-start(bf16[64,2048]{1,0:T(8,128)(2,1)} %param.11), channel_id=1, source_target_pairs={{0,1},{1,0},{2,3},{3,2},{4,5},{5,4},{6,7},{7,6},{8,9},{9,8},{10,11... | collective-permute-start | bytes 786440 | tf_op jit(solution)/shard_map/ppermute | solution.py:17
  4.9 4.4 %collective-permute-start.1 = (bf16[64,2048]{1,0:T(8,128)(2,1)}, bf16[64,2048]{1,0:T(8,128)(2,1)}, u32[]{:S(2)}, u32[]{:S(2)}) collective-permute-start(bf16[64,2048]{1,0:T(8,128)(2,1)} %param.11), channel_id=1, source_target_pairs={{0,2},{1,3},{2,0},{3,1},{4,6},{5,7},{6,4},{7,5},{8,10},{9,11},{10,... | collective-permute-start | bytes 786440 | tf_op jit(solution)/shard_map/ppermute | solution.py:17
  18.0 7.4 %collective-permute-done.2 = bf16[64,2048]{1,0:T(8,128)(2,1)} collective-permute-done((bf16[64,2048]{1,0:T(8,128)(2,1)}, bf16[64,2048]{1,0:T(8,128)(2,1)}, u32[]{:S(2)}, u32[]{:S(2)}) %collective-permute-start.2) | collective-permute-done | bytes 262176 | tf_op jit(solution)/shard_map/ppermute | solution.py:17
  38.5 18.1 %all-to-all-start = ((bf16[64,128,128]{2,0,1:T(8,128)(2,1)}), bf16[64,128,128]{2,0,1:T(8,128)(2,1)}, u32[]{:S(2)}, u32[]{:S(2)}) async-start(bf16[64,128,128]{2,0,1:T(8,128)(2,1)} %select_bitcast_fusion.1), calls=%async_computation | async-start | bytes 4194304 | tf_op jit(solution)/shard_map/all_to_all | solution.py:42
  56.9 50.7 %all-to-all-done = bf16[64,128,128]{2,0,1:T(8,128)(2,1)} async-done(((bf16[64,128,128]{2,0,1:T(8,128)(2,1)}), bf16[64,128,128]{2,0,1:T(8,128)(2,1)}, u32[]{:S(2)}, u32[]{:S(2)}) %all-to-all-start) | async-done | bytes 2097184 | tf_op jit(solution)/shard_map/all_to_all | solution.py:42
  124.8 4.1 %convolution_bitcast_fusion = f32[64,96,128]{2,0,1:T(8,128)} fusion(bf16[96,128,128]{2,1,0:T(8,128)(2,1)S(1)} %copy-done, bf16[96,64,128]{2,1,0:T(8,128)(2,1)} %gather_fusion.3, pred[96]{0:T(512)(128)(4,1)S(1)} %compare_and_fusion.5), kind=kOutput, calls=%fused_computation.20 | convolution fusion | flops 202113024 | bytes 7864416 | tf_op jit(solution)/shard_map/ota,tab->otb/dot_general | solution.py:60
  128.8 4.7 %gather_fusion.4 = f32[128,64,128]{2,1,0:T(8,128)} fusion(f32[64,96,128]{2,0,1:T(8,128)} %convolution_bitcast_fusion, s32[1024]{0:T(1024)S(1)} %get-tuple-element.14), kind=kCustom, calls=%fused_computation.6 | custom fusion | bytes 8389120 | tf_op jit(solution)/shard_map/jit(_take)/gather | solution.py:76
  133.6 4.1 %select_bitcast_fusion = f32[64,128,128]{2,0,1:T(8,128)} fusion(f32[128,64,128]{2,1,0:T(8,128)} %gather_fusion.4, pred[128]{0:T(512)(128)(4,1)S(1)} %fusion.34, pred[128]{0:T(512)(128)(4,1)S(1)} %get-tuple-element.12), kind=kLoop, calls=%fused_computation.11 | loop fusion | flops 2097152 | bytes 8388864 | tf_op jit(solution)/shard_map/jit(_where)/select_n | solution.py:75
  137.7 9.6 %all-to-all-start.1 = ((f32[64,128,128]{2,0,1:T(8,128)}), f32[64,128,128]{2,0,1:T(8,128)}, u32[]{:S(2)}, u32[]{:S(2)}) async-start(f32[64,128,128]{2,0,1:T(8,128)} %select_bitcast_fusion), calls=%async_computation.1 | async-start | bytes 8388608 | tf_op jit(solution)/shard_map/all_to_all | solution.py:78
  152.5 4.4 %collective-permute-start.5 = (bf16[256,64]{0,1:T(8,128)(2,1)S(1)}, bf16[256,64]{0,1:T(8,128)(2,1)S(1)}, u32[]{:S(2)}, u32[]{:S(2)}) collective-permute-start(bf16[256,64]{0,1:T(8,128)(2,1)S(1)} %copy-done.6), channel_id=1, source_target_pairs={{0,3},{1,2},{2,1},{3,0},{4,7},{5,6},{6,5},{7,4},{8,11},{9,10},{10,... | collective-permute-start | bytes 98312 | tf_op jit(solution)/shard_map/ppermute | solution.py:17
  160.2 83.7 %all-to-all-done.1 = f32[64,128,128]{2,0,1:T(8,128)} async-done(((f32[64,128,128]{2,0,1:T(8,128)}), f32[64,128,128]{2,0,1:T(8,128)}, u32[]{:S(2)}, u32[]{:S(2)}) %all-to-all-start.1) | async-done | bytes 4194336 | tf_op jit(solution)/shard_map/all_to_all | solution.py:78
  243.9 5.9 %fusion = f32[16,64,128]{2,0,1:T(8,128)S(1)} fusion(f32[64,128,128]{2,0,1:T(8,128)} %all-to-all-done.1, s32[128]{0:T(128)S(1)} %copy-done.11), kind=kOutput, calls=%fused_computation.9 | convolution fusion | flops 201328640 | bytes 4719104 | tf_op jit(solution)/shard_map/oqb,qr->orb/dot_general | solution.py:79
  257.1 4.8 %collective-permute-start.10 = (f32[257,64]{0,1:T(8,128)}, f32[257,64]{0,1:T(8,128)}, u32[]{:S(2)}, u32[]{:S(2)}) collective-permute-start(f32[257,64]{0,1:T(8,128)} %pad_maximum_fusion.4), channel_id=1, source_target_pairs={{0,8},{4,12},{8,0},{12,4},{16,24},{20,28},{24,16},{28,20},{32,40},... | collective-permute-start | bytes 197384 | tf_op jit(solution)/shard_map/ppermute | solution.py:17
  263.9 5.3 %collective-permute-start.12 = (f32[257,64]{0,1:T(8,128)}, f32[257,64]{0,1:T(8,128)}, u32[]{:S(2)}, u32[]{:S(2)}) collective-permute-start(f32[257,64]{0,1:T(8,128)} %pad_maximum_fusion.4), channel_id=1, source_target_pairs={{0,16},{4,20},{8,24},{12,28},{16,0},{20,4},{24,8},{28,12},{32,48},... | collective-permute-start | bytes 197384 | tf_op jit(solution)/shard_map/ppermute | solution.py:17
  273.6 5.7 %collective-permute-start.14 = (f32[257,64]{0,1:T(8,128)}, f32[257,64]{0,1:T(8,128)S(1)}, u32[]{:S(2)}, u32[]{:S(2)}) collective-permute-start(f32[257,64]{0,1:T(8,128)} %pad_maximum_fusion.4), channel_id=1, source_target_pairs={{0,24},{4,28},{8,16},{12,20},{16,8},{20,12},{24,0},{28,4},{32,56},... | collective-permute-start | bytes 197384 | tf_op jit(solution)/shard_map/ppermute | solution.py:17
  284.3 9.9 %collective-permute-start.16 = (f32[257,64]{0,1:T(8,128)}, f32[257,64]{0,1:T(8,128)S(1)}, u32[]{:S(2)}, u32[]{:S(2)}) collective-permute-start(f32[257,64]{0,1:T(8,128)} %pad_maximum_fusion.4), channel_id=1, source_target_pairs={{0,32},{4,36},{8,40},{12,44},{16,48},{20,52},{24,56},{28,60},{32,0... | collective-permute-start | bytes 197384 | tf_op jit(solution)/shard_map/ppermute | solution.py:17
  299.4 4.6 %collective-permute-start.18 = (f32[257,64]{0,1:T(8,128)}, f32[257,64]{0,1:T(8,128)S(1)}, u32[]{:S(2)}, u32[]{:S(2)}) collective-permute-start(f32[257,64]{0,1:T(8,128)} %pad_maximum_fusion.4), channel_id=1, source_target_pairs={{0,40},{4,44},{8,32},{12,36},{16,56},{20,60},{24,48},{28,52},{32,8... | collective-permute-start | bytes 197384 | tf_op jit(solution)/shard_map/ppermute | solution.py:17
  305.5 4.2 %collective-permute-start.19 = (f32[257,64]{0,1:T(8,128)}, f32[257,64]{0,1:T(8,128)S(1)}, u32[]{:S(2)}, u32[]{:S(2)}) collective-permute-start(f32[257,64]{0,1:T(8,128)} %pad_maximum_fusion.4), channel_id=1, source_target_pairs={{0,44},{4,40},{8,36},{12,32},{16,60},{20,56},{24,52},{28,48},{32,1... | collective-permute-start | bytes 197384 | tf_op jit(solution)/shard_map/ppermute | solution.py:17
  319.1 4.6 %collective-permute-start.22 = (f32[257,64]{0,1:T(8,128)}, f32[257,64]{0,1:T(8,128)S(1)}, u32[]{:S(2)}, u32[]{:S(2)}) collective-permute-start(f32[257,64]{0,1:T(8,128)} %pad_maximum_fusion.4), channel_id=1, source_target_pairs={{0,56},{4,60},{8,48},{12,52},{16,40},{20,44},{24,32},{28,36},{32,2... | collective-permute-start | bytes 197384 | tf_op jit(solution)/shard_map/ppermute | solution.py:17
  333.9 4.4 %collective-permute-start.8 = (bf16[64,2048]{1,0:T(8,128)(2,1)}, bf16[64,2048]{1,0:T(8,128)(2,1)}, u32[]{:S(2)}, u32[]{:S(2)}) collective-permute-start(bf16[64,2048]{1,0:T(8,128)(2,1)} %bitcast.142), channel_id=1, source_target_pairs={{0,3},{1,2},{2,1},{3,0},{4,7},{5,6},{6,5},{7,4},{8,11},{9,10},{10,... | collective-permute-start | bytes 786440 | tf_op jit(solution)/shard_map/ppermute | solution.py:17
  350.5 4.6 %collective-permute-start.26 = (f32[257,64]{0,1:T(8,128)S(1)}, f32[257,64]{0,1:T(8,128)S(1)}, u32[]{:S(2)}, u32[]{:S(2)}) collective-permute-start(f32[257,64]{0,1:T(8,128)S(1)} %select_reduce_fusion), channel_id=1, source_target_pairs={{0,192},{4,196},{8,200},{12,204},{16,208},{20,212},{24,216},{28,22... | collective-permute-start | bytes 197384 | tf_op jit(solution)/shard_map/ppermute | solution.py:17
  355.7 5.4 %collective-permute-start.27 = (f32[257,64]{0,1:T(8,128)S(1)}, f32[257,64]{0,1:T(8,128)S(1)}, u32[]{:S(2)}, u32[]{:S(2)}) collective-permute-start(f32[257,64]{0,1:T(8,128)S(1)} %select_reduce_fusion), channel_id=1, source_target_pairs={{0,256},{4,260},{8,264},{12,268},{16,272},{20,276},{24,280},{28,28... | collective-permute-start | bytes 197384 | tf_op jit(solution)/shard_map/ppermute | solution.py:17
  366.1 7.8 %collective-permute-start.29 = (f32[257,64]{0,1:T(8,128)S(1)}, f32[257,64]{0,1:T(8,128)S(1)}, u32[]{:S(2)}, u32[]{:S(2)}) collective-permute-start(f32[257,64]{0,1:T(8,128)S(1)} %select_reduce_fusion), channel_id=1, source_target_pairs={{0,384},{4,388},{8,392},{12,396},{16,400},{20,404},{24,408},{28,41... | collective-permute-start | bytes 197384 | tf_op jit(solution)/shard_map/ppermute | solution.py:17
  377.8 5.2 %collective-permute-done.30 = f32[257,64]{0,1:T(8,128)S(1)} collective-permute-done((f32[257,64]{0,1:T(8,128)S(1)}, f32[257,64]{0,1:T(8,128)S(1)}, u32[]{:S(2)}, u32[]{:S(2)}) %collective-permute-start.30) | collective-permute-done | bytes 65824 | tf_op jit(solution)/shard_map/ppermute | solution.py:17
  (163 shorter events, 126.7 us)
Async XLA Ops:
  0.6 13.4 %collective-permute-start = (bf16[64,2048]{1,0:T(8,128)(2,1)}, bf16[64,2048]{1,0:T(8,128)(2,1)S(1)}, u32[]{:S(2)}, u32[]{:S(2)}) collective-permute-start(bf16[64,2048]{1,0:T(8,128)(2,1)} %param.11), channel_id=1, source_target_pairs={{0,1},{1,0},{2,3},{3,2},{4,5},{5,4},{6,7},{7,6},{8,9},{9,8},{10,11... | collective-permute-start | bytes 786440 | tf_op jit(solution)/shard_map/ppermute | solution.py:17
  4.9 13.1 %collective-permute-start.1 = (bf16[64,2048]{1,0:T(8,128)(2,1)}, bf16[64,2048]{1,0:T(8,128)(2,1)}, u32[]{:S(2)}, u32[]{:S(2)}) collective-permute-start(bf16[64,2048]{1,0:T(8,128)(2,1)} %param.11), channel_id=1, source_target_pairs={{0,2},{1,3},{2,0},{3,1},{4,6},{5,7},{6,4},{7,5},{8,10},{9,11},{10,... | collective-permute-start | bytes 786440 | tf_op jit(solution)/shard_map/ppermute | solution.py:17
  9.2 16.1 %collective-permute-start.2 = (bf16[64,2048]{1,0:T(8,128)(2,1)}, bf16[64,2048]{1,0:T(8,128)(2,1)}, u32[]{:S(2)}, u32[]{:S(2)}) collective-permute-start(bf16[64,2048]{1,0:T(8,128)(2,1)} %param.11), channel_id=1, source_target_pairs={{0,3},{1,2},{2,1},{3,0},{4,7},{5,6},{6,5},{7,4},{8,11},{9,10},{10,... | collective-permute-start | bytes 786440 | tf_op jit(solution)/shard_map/ppermute | solution.py:17
  38.5 69.0 %all-to-all-start = ((bf16[64,128,128]{2,0,1:T(8,128)(2,1)}), bf16[64,128,128]{2,0,1:T(8,128)(2,1)}, u32[]{:S(2)}, u32[]{:S(2)}) async-start(bf16[64,128,128]{2,0,1:T(8,128)(2,1)} %select_bitcast_fusion.1), calls=%async_computation | async-start | bytes 4194304 | tf_op jit(solution)/shard_map/all_to_all | solution.py:42
  137.7 106.2 %all-to-all-start.1 = ((f32[64,128,128]{2,0,1:T(8,128)}), f32[64,128,128]{2,0,1:T(8,128)}, u32[]{:S(2)}, u32[]{:S(2)}) async-start(f32[64,128,128]{2,0,1:T(8,128)} %select_bitcast_fusion), calls=%async_computation.1 | async-start | bytes 8388608 | tf_op jit(solution)/shard_map/all_to_all | solution.py:78
  254.3 19.4 %collective-permute-start.9 = (f32[257,64]{0,1:T(8,128)}, f32[257,64]{0,1:T(8,128)}, u32[]{:S(2)}, u32[]{:S(2)}) collective-permute-start(f32[257,64]{0,1:T(8,128)} %pad_maximum_fusion.4), channel_id=1, source_target_pairs={{0,4},{4,0},{8,12},{12,8},{16,20},{20,16},{24,28},{28,24},{32,36},... | collective-permute-start | bytes 197384 | tf_op jit(solution)/shard_map/ppermute | solution.py:17
  257.1 23.7 %collective-permute-start.10 = (f32[257,64]{0,1:T(8,128)}, f32[257,64]{0,1:T(8,128)}, u32[]{:S(2)}, u32[]{:S(2)}) collective-permute-start(f32[257,64]{0,1:T(8,128)} %pad_maximum_fusion.4), channel_id=1, source_target_pairs={{0,8},{4,12},{8,0},{12,4},{16,24},{20,28},{24,16},{28,20},{32,40},... | collective-permute-start | bytes 197384 | tf_op jit(solution)/shard_map/ppermute | solution.py:17
  262.0 22.3 %collective-permute-start.11 = (f32[257,64]{0,1:T(8,128)}, f32[257,64]{0,1:T(8,128)}, u32[]{:S(2)}, u32[]{:S(2)}) collective-permute-start(f32[257,64]{0,1:T(8,128)} %pad_maximum_fusion.4), channel_id=1, source_target_pairs={{0,12},{4,8},{8,4},{12,0},{16,28},{20,24},{24,20},{28,16},{32,44},... | collective-permute-start | bytes 197384 | tf_op jit(solution)/shard_map/ppermute | solution.py:17
  263.9 31.9 %collective-permute-start.12 = (f32[257,64]{0,1:T(8,128)}, f32[257,64]{0,1:T(8,128)}, u32[]{:S(2)}, u32[]{:S(2)}) collective-permute-start(f32[257,64]{0,1:T(8,128)} %pad_maximum_fusion.4), channel_id=1, source_target_pairs={{0,16},{4,20},{8,24},{12,28},{16,0},{20,4},{24,8},{28,12},{32,48},... | collective-permute-start | bytes 197384 | tf_op jit(solution)/shard_map/ppermute | solution.py:17
  269.2 30.2 %collective-permute-start.13 = (f32[257,64]{0,1:T(8,128)}, f32[257,64]{0,1:T(8,128)}, u32[]{:S(2)}, u32[]{:S(2)}) collective-permute-start(f32[257,64]{0,1:T(8,128)} %pad_maximum_fusion.4), channel_id=1, source_target_pairs={{0,20},{4,16},{8,28},{12,24},{16,4},{20,0},{24,12},{28,8},{32,52},... | collective-permute-start | bytes 197384 | tf_op jit(solution)/shard_map/ppermute | solution.py:17
  273.6 31.9 %collective-permute-start.14 = (f32[257,64]{0,1:T(8,128)}, f32[257,64]{0,1:T(8,128)S(1)}, u32[]{:S(2)}, u32[]{:S(2)}) collective-permute-start(f32[257,64]{0,1:T(8,128)} %pad_maximum_fusion.4), channel_id=1, source_target_pairs={{0,24},{4,28},{8,16},{12,20},{16,8},{20,12},{24,0},{28,4},{32,56},... | collective-permute-start | bytes 197384 | tf_op jit(solution)/shard_map/ppermute | solution.py:17
  280.8 29.6 %collective-permute-start.15 = (f32[257,64]{0,1:T(8,128)}, f32[257,64]{0,1:T(8,128)S(1)}, u32[]{:S(2)}, u32[]{:S(2)}) collective-permute-start(f32[257,64]{0,1:T(8,128)} %pad_maximum_fusion.4), channel_id=1, source_target_pairs={{0,28},{4,24},{8,20},{12,16},{16,12},{20,8},{24,4},{28,0},{32,60},... | collective-permute-start | bytes 197384 | tf_op jit(solution)/shard_map/ppermute | solution.py:17
  284.3 30.1 %collective-permute-start.16 = (f32[257,64]{0,1:T(8,128)}, f32[257,64]{0,1:T(8,128)S(1)}, u32[]{:S(2)}, u32[]{:S(2)}) collective-permute-start(f32[257,64]{0,1:T(8,128)} %pad_maximum_fusion.4), channel_id=1, source_target_pairs={{0,32},{4,36},{8,40},{12,44},{16,48},{20,52},{24,56},{28,60},{32,0... | collective-permute-start | bytes 197384 | tf_op jit(solution)/shard_map/ppermute | solution.py:17
  295.8 23.3 %collective-permute-start.17 = (f32[257,64]{0,1:T(8,128)}, f32[257,64]{0,1:T(8,128)S(1)}, u32[]{:S(2)}, u32[]{:S(2)}) collective-permute-start(f32[257,64]{0,1:T(8,128)} %pad_maximum_fusion.4), channel_id=1, source_target_pairs={{0,36},{4,32},{8,44},{12,40},{16,52},{20,48},{24,60},{28,56},{32,4... | collective-permute-start | bytes 197384 | tf_op jit(solution)/shard_map/ppermute | solution.py:17
  299.4 24.9 %collective-permute-start.18 = (f32[257,64]{0,1:T(8,128)}, f32[257,64]{0,1:T(8,128)S(1)}, u32[]{:S(2)}, u32[]{:S(2)}) collective-permute-start(f32[257,64]{0,1:T(8,128)} %pad_maximum_fusion.4), channel_id=1, source_target_pairs={{0,40},{4,44},{8,32},{12,36},{16,56},{20,60},{24,48},{28,52},{32,8... | collective-permute-start | bytes 197384 | tf_op jit(solution)/shard_map/ppermute | solution.py:17
  305.5 21.9 %collective-permute-start.19 = (f32[257,64]{0,1:T(8,128)}, f32[257,64]{0,1:T(8,128)S(1)}, u32[]{:S(2)}, u32[]{:S(2)}) collective-permute-start(f32[257,64]{0,1:T(8,128)} %pad_maximum_fusion.4), channel_id=1, source_target_pairs={{0,44},{4,40},{8,36},{12,32},{16,60},{20,56},{24,52},{28,48},{32,1... | collective-permute-start | bytes 197384 | tf_op jit(solution)/shard_map/ppermute | solution.py:17
  310.4 19.6 %collective-permute-start.20 = (f32[257,64]{0,1:T(8,128)}, f32[257,64]{0,1:T(8,128)S(1)}, u32[]{:S(2)}, u32[]{:S(2)}) collective-permute-start(f32[257,64]{0,1:T(8,128)} %pad_maximum_fusion.4), channel_id=1, source_target_pairs={{0,48},{4,52},{8,56},{12,60},{16,32},{20,36},{24,40},{28,44},{32,1... | collective-permute-start | bytes 197384 | tf_op jit(solution)/shard_map/ppermute | solution.py:17
  314.4 19.5 %collective-permute-start.21 = (f32[257,64]{0,1:T(8,128)}, f32[257,64]{0,1:T(8,128)S(1)}, u32[]{:S(2)}, u32[]{:S(2)}) collective-permute-start(f32[257,64]{0,1:T(8,128)} %pad_maximum_fusion.4), channel_id=1, source_target_pairs={{0,52},{4,48},{8,60},{12,56},{16,36},{20,32},{24,44},{28,40},{32,2... | collective-permute-start | bytes 197384 | tf_op jit(solution)/shard_map/ppermute | solution.py:17
  319.1 19.9 %collective-permute-start.22 = (f32[257,64]{0,1:T(8,128)}, f32[257,64]{0,1:T(8,128)S(1)}, u32[]{:S(2)}, u32[]{:S(2)}) collective-permute-start(f32[257,64]{0,1:T(8,128)} %pad_maximum_fusion.4), channel_id=1, source_target_pairs={{0,56},{4,60},{8,48},{12,52},{16,40},{20,44},{24,32},{28,36},{32,2... | collective-permute-start | bytes 197384 | tf_op jit(solution)/shard_map/ppermute | solution.py:17
  324.3 15.3 %collective-permute-start.23 = (f32[257,64]{0,1:T(8,128)}, f32[257,64]{0,1:T(8,128)S(1)}, u32[]{:S(2)}, u32[]{:S(2)}) collective-permute-start(f32[257,64]{0,1:T(8,128)} %pad_maximum_fusion.4), channel_id=1, source_target_pairs={{0,60},{4,56},{8,52},{12,48},{16,44},{20,40},{24,36},{28,32},{32,2... | collective-permute-start | bytes 197384 | tf_op jit(solution)/shard_map/ppermute | solution.py:17
  327.4 61.4 %collective-permute-start.6 = (bf16[64,2048]{1,0:T(8,128)(2,1)}, bf16[64,2048]{1,0:T(8,128)(2,1)}, u32[]{:S(2)}, u32[]{:S(2)}) collective-permute-start(bf16[64,2048]{1,0:T(8,128)(2,1)} %bitcast.142), channel_id=1, source_target_pairs={{0,1},{1,0},{2,3},{3,2},{4,5},{5,4},{6,7},{7,6},{8,9},{9,8},{10,11... | collective-permute-start | bytes 786440 | tf_op jit(solution)/shard_map/ppermute | solution.py:17
  330.0 58.8 %collective-permute-start.7 = (bf16[64,2048]{1,0:T(8,128)(2,1)}, bf16[64,2048]{1,0:T(8,128)(2,1)}, u32[]{:S(2)}, u32[]{:S(2)}) collective-permute-start(bf16[64,2048]{1,0:T(8,128)(2,1)} %bitcast.142), channel_id=1, source_target_pairs={{0,2},{1,3},{2,0},{3,1},{4,6},{5,7},{6,4},{7,5},{8,10},{9,11},{10,... | collective-permute-start | bytes 786440 | tf_op jit(solution)/shard_map/ppermute | solution.py:17
  333.9 54.9 %collective-permute-start.8 = (bf16[64,2048]{1,0:T(8,128)(2,1)}, bf16[64,2048]{1,0:T(8,128)(2,1)}, u32[]{:S(2)}, u32[]{:S(2)}) collective-permute-start(bf16[64,2048]{1,0:T(8,128)(2,1)} %bitcast.142), channel_id=1, source_target_pairs={{0,3},{1,2},{2,1},{3,0},{4,7},{5,6},{6,5},{7,4},{8,11},{9,10},{10,... | collective-permute-start | bytes 786440 | tf_op jit(solution)/shard_map/ppermute | solution.py:17
  361.7 12.9 %collective-permute-start.28 = (f32[257,64]{0,1:T(8,128)S(1)}, f32[257,64]{0,1:T(8,128)S(1)}, u32[]{:S(2)}, u32[]{:S(2)}) collective-permute-start(f32[257,64]{0,1:T(8,128)S(1)} %select_reduce_fusion), channel_id=1, source_target_pairs={{0,320},{4,324},{8,328},{12,332},{16,336},{20,340},{24,344},{28,34... | collective-permute-start | bytes 197384 | tf_op jit(solution)/shard_map/ppermute | solution.py:17
  (25 other events, 408.1 us)

commit v3 on v2

--- a/solution.py
+++ b/solution.py
@@ -20,8 +20,15 @@
     return jnp.take(stacked, mine ^ jnp.arange(count), axis=0)
 
 
-def group_sum(values, axis, size, stride, count):
-    return jnp.sum(group_stack(values, axis, size, stride, count), axis=0)
+def scatter_gather_sum(values, axis, size):
+    rows, cols = values.shape
+    chunk = -(-rows // size)
+    padded = jnp.pad(values, ((0, chunk * size - rows), (0, 0))).reshape(size, chunk, cols)
+    gathered = lax.all_to_all(padded, axis, 0, 0, tiled=True)
+    reduced = jnp.sum(gathered, axis=0)
+    spread = jnp.broadcast_to(reduced[None], (size, chunk, cols))
+    total = lax.all_to_all(spread, axis, 0, 0, tiled=True)
+    return total.reshape(size * chunk, cols)[:rows]
 
 
 def per_device(
@@ -86,9 +93,7 @@
     )
     bias_part = jnp.sum(grad_pre, axis=1)
     packed = jnp.concatenate([weight_part, bias_part[None, :]], axis=0)
-    low = 16 if domains % 16 == 0 else 1
-    packed = group_sum(packed, "dom", domains, 1, low)
-    packed = group_sum(packed, "dom", domains, low, domains // low)
+    packed = scatter_gather_sum(packed, "dom", domains)
     grad_weight = packed[:-1] * norm_scale
     grad_bias = packed[-1] * norm_scale
     full_weight = jnp.concatenate(list(group_stack(weight, "feat", parts, 1, parts)), axis=1)

time: 404 us -> 328 us (0.81); the launches traced: 396 us -> 327 us
  starting transfers between devices: 145 us -> 79.9 us
  local copies, waits for them, and re-layouts: 47.3 us -> 32 us
  waiting for transfers between devices: 153 us -> 163 us
    ppermute x31 -> x9, starting transfers between devices: 117 us -> 29.7 us  [group_stack(): received.append(lax.ppermute(values, axis, pairs))]
    all_to_all x0 -> x2, starting transfers between devices: none -> 22.5 us  [the longest x1 17 us: scatter_gather_sum(): gathered = lax.all_to_all(padded, axis, 0, 0, tiled=True)]
    all_to_all x0 -> x2, waiting for transfers between devices: none -> 15.5 us  [the longest x1 10.5 us: scatter_gather_sum(): gathered = lax.all_to_all(padded, axis, 0, 0, tiled=True)]
    unnamed x54 -> x37, local copies, waits for them, and re-layouts: 19.8 us -> 7.18 us
    gather x5 -> x3, local copies, waits for them, and re-layouts: 12.1 us -> 6.23 us  [group_stack(): return jnp.take(stacked, mine ^ jnp.arange(count), axis=0)]
    ppermute x31 -> x9, waiting for transfers between devices: 18.2 us -> 13.2 us  [group_stack(): received.append(lax.ppermute(values, axis, pairs))]
  transfers between devices with their start and end apart: 33 -> 13, of which waited for: 7 -> 7; matrix products, arithmetic and copies ran while one was open for 9% -> 7% of each run, Pallas kernels for 0% -> 0%
where the time goes in v3:
time: 328 us; the launch traced here: 327 us
  waiting for transfers between devices  163 us (50%)
  starting transfers between devices  79.9 us (24%)
  local copies, waits for them, and re-layouts  32 us (10%)
  other arithmetic  28 us (9%)
  matrix products  22.2 us (7%)
    all_to_all x1, waiting for transfers between devices, per_device(): lax.all_to_all(out_parts, 'dom', split_axis=1, concat_axis=1, tiled=True)  83.6 us
    all_to_all x1, waiting for transfers between devices, per_device(): lax.all_to_all(outgoing, 'dom', split_axis=1, concat_axis=1, tiled=True)  50.7 us
    ppermute x9, starting transfers between devices, group_stack(): received.append(lax.ppermute(values, axis, pairs))  29.7 us
    all_to_all x1, starting transfers between devices, per_device(): lax.all_to_all(outgoing, 'dom', split_axis=1, concat_axis=1, tiled=True)  18.1 us
    all_to_all x1, starting transfers between devices, scatter_gather_sum(): gathered = lax.all_to_all(padded, axis, 0, 0, tiled=True)  17 us
    ppermute x9, waiting for transfers between devices, group_stack(): received.append(lax.ppermute(values, axis, pairs))  13.2 us
    all_to_all x1, waiting for transfers between devices, scatter_gather_sum(): gathered = lax.all_to_all(padded, axis, 0, 0, tiled=True)  10.5 us
    all_to_all x1, starting transfers between devices, per_device(): lax.all_to_all(out_parts, 'dom', split_axis=1, concat_axis=1, tiled=True)  9.62 us
  transfers between devices with their start and end apart: 13, of which 7 were waited for; matrix products, arithmetic and copies ran while one was open for 7% of the time, Pallas kernels for 0%

profile of v3, /device:TPU:1, one launch (start us, length us, event | category | flops | bytes accessed | tf_op | source)
XLA Modules:
  0.0 327.0 jit_solution(7399230271208300399)
XLA Ops:
  0.6 4.2 %collective-permute-start = (bf16[64,2048]{1,0:T(8,128)(2,1)}, bf16[64,2048]{1,0:T(8,128)(2,1)S(1)}, u32[]{:S(2)}, u32[]{:S(2)}) collective-permute-start(bf16[64,2048]{1,0:T(8,128)(2,1)} %param.11), channel_id=1, source_target_pairs={{0,1},{1,0},{2,3},{3,2},{4,5},{5,4},{6,7},{7,6},{8,9},{9,8},{10,11... | collective-permute-start | bytes 786440 | tf_op jit(solution)/shard_map/ppermute | solution.py:17
  4.9 4.4 %collective-permute-start.1 = (bf16[64,2048]{1,0:T(8,128)(2,1)}, bf16[64,2048]{1,0:T(8,128)(2,1)}, u32[]{:S(2)}, u32[]{:S(2)}) collective-permute-start(bf16[64,2048]{1,0:T(8,128)(2,1)} %param.11), channel_id=1, source_target_pairs={{0,2},{1,3},{2,0},{3,1},{4,6},{5,7},{6,4},{7,5},{8,10},{9,11},{10,... | collective-permute-start | bytes 786440 | tf_op jit(solution)/shard_map/ppermute | solution.py:17
  14.0 3.9 %collective-permute-done.1 = bf16[64,2048]{1,0:T(8,128)(2,1)} collective-permute-done((bf16[64,2048]{1,0:T(8,128)(2,1)}, bf16[64,2048]{1,0:T(8,128)(2,1)}, u32[]{:S(2)}, u32[]{:S(2)}) %collective-permute-start.1) | collective-permute-done | bytes 262176 | tf_op jit(solution)/shard_map/ppermute | solution.py:17
  18.0 7.4 %collective-permute-done.2 = bf16[64,2048]{1,0:T(8,128)(2,1)} collective-permute-done((bf16[64,2048]{1,0:T(8,128)(2,1)}, bf16[64,2048]{1,0:T(8,128)(2,1)}, u32[]{:S(2)}, u32[]{:S(2)}) %collective-permute-start.2) | collective-permute-done | bytes 262176 | tf_op jit(solution)/shard_map/ppermute | solution.py:17
  38.6 18.1 %all-to-all-start = ((bf16[64,128,128]{2,0,1:T(8,128)(2,1)}), bf16[64,128,128]{2,0,1:T(8,128)(2,1)}, u32[]{:S(2)}, u32[]{:S(2)}) async-start(bf16[64,128,128]{2,0,1:T(8,128)(2,1)} %select_bitcast_fusion.1), calls=%async_computation | async-start | bytes 4194304 | tf_op jit(solution)/shard_map/all_to_all | solution.py:49
  57.0 50.7 %all-to-all-done = bf16[64,128,128]{2,0,1:T(8,128)(2,1)} async-done(((bf16[64,128,128]{2,0,1:T(8,128)(2,1)}), bf16[64,128,128]{2,0,1:T(8,128)(2,1)}, u32[]{:S(2)}, u32[]{:S(2)}) %all-to-all-start) | async-done | bytes 2097184 | tf_op jit(solution)/shard_map/all_to_all | solution.py:49
  110.8 3.6 %gather_fusion.1 = bf16[96,64,128]{2,1,0:T(8,128)(2,1)} fusion(bf16[64,144,128]{2,0,1:T(8,128)(2,1)} %pad_maximum_fusion, s32[1024]{0:T(1024)S(1)} %pad_clamp_fusion.3), kind=kCustom, calls=%fused_computation.3 | custom fusion | bytes 3146112 | tf_op jit(solution)/shard_map/jit(_take)/gather | solution.py:56
  114.4 3.6 %convolution_bitcast_fusion.1 = f32[64,96,128]{2,0,1:T(8,128)S(1)} fusion(bf16[96,128,128]{2,1,0:T(8,128)(2,1)S(1)} %copy-done, bf16[96,64,128]{2,1,0:T(8,128)(2,1)} %gather_fusion.1, pred[96]{0:T(512)(128)(4,1)S(1)} %compare_and_fusion.5), kind=kOutput, calls=%fused_computation.19 | convolution fusion | flops 202113024 | bytes 7864416 | tf_op jit(solution)/shard_map/otb,tab->ota/dot_general | solution.py:57
  118.1 3.3 %fusion.4 = f32[16,64,128]{2,0,1:T(8,128)S(1)} fusion(f32[64,96,128]{2,0,1:T(8,128)S(1)} %convolution_bitcast_fusion.1, f32[96]{0:T(128)S(1)} %fusion.57, s32[96]{0:T(128)S(1)} %copy-done.13), kind=kOutput, calls=%fused_computation.12 | convolution fusion | flops 150998016 | bytes 3670784 | tf_op jit(solution)/shard_map/ota,tr->ora/dot_general | solution.py:58
  124.8 4.1 %convolution_bitcast_fusion = f32[64,96,128]{2,0,1:T(8,128)} fusion(bf16[96,128,128]{2,1,0:T(8,128)(2,1)S(1)} %copy-done, bf16[96,64,128]{2,1,0:T(8,128)(2,1)} %gather_fusion.3, pred[96]{0:T(512)(128)(4,1)S(1)} %compare_and_fusion.3), kind=kOutput, calls=%fused_computation.18 | convolution fusion | flops 202113024 | bytes 7864416 | tf_op jit(solution)/shard_map/ota,tab->otb/dot_general | solution.py:67
  128.9 4.7 %gather_fusion.4 = f32[128,64,128]{2,1,0:T(8,128)} fusion(f32[64,96,128]{2,0,1:T(8,128)} %convolution_bitcast_fusion, s32[1024]{0:T(1024)S(1)} %pad_clamp_fusion), kind=kCustom, calls=%fused_computation.6 | custom fusion | bytes 8389120 | tf_op jit(solution)/shard_map/jit(_take)/gather | solution.py:83
  133.6 4.1 %select_bitcast_fusion = f32[64,128,128]{2,0,1:T(8,128)} fusion(f32[128,64,128]{2,1,0:T(8,128)} %gather_fusion.4, pred[128]{0:T(512)(128)(4,1)S(1)} %fusion.34, pred[128]{0:T(512)(128)(4,1)S(1)} %get-tuple-element.24), kind=kLoop, calls=%fused_computation.9 | loop fusion | flops 2097152 | bytes 8388864 | tf_op jit(solution)/shard_map/jit(_where)/select_n | solution.py:82
  137.7 9.6 %all-to-all-start.1 = ((f32[64,128,128]{2,0,1:T(8,128)}), f32[64,128,128]{2,0,1:T(8,128)}, u32[]{:S(2)}, u32[]{:S(2)}) async-start(f32[64,128,128]{2,0,1:T(8,128)} %select_bitcast_fusion), calls=%async_computation.1 | async-start | bytes 8388608 | tf_op jit(solution)/shard_map/all_to_all | solution.py:85
  149.3 3.3 %collective-permute-start.4 = (bf16[256,64]{0,1:T(8,128)(2,1)S(1)}, bf16[256,64]{0,1:T(8,128)(2,1)S(1)}, u32[]{:S(2)}, u32[]{:S(2)}) collective-permute-start(bf16[256,64]{0,1:T(8,128)(2,1)S(1)} %copy-done.6), channel_id=1, source_target_pairs={{0,2},{1,3},{2,0},{3,1},{4,6},{5,7},{6,4},{7,5},{8,10},{9,11},{10,... | collective-permute-start | bytes 98312 | tf_op jit(solution)/shard_map/ppermute | solution.py:17
  152.5 4.4 %collective-permute-start.5 = (bf16[256,64]{0,1:T(8,128)(2,1)S(1)}, bf16[256,64]{0,1:T(8,128)(2,1)S(1)}, u32[]{:S(2)}, u32[]{:S(2)}) collective-permute-start(bf16[256,64]{0,1:T(8,128)(2,1)S(1)} %copy-done.6), channel_id=1, source_target_pairs={{0,3},{1,2},{2,1},{3,0},{4,7},{5,6},{6,5},{7,4},{8,11},{9,10},{10,... | collective-permute-start | bytes 98312 | tf_op jit(solution)/shard_map/ppermute | solution.py:17
  160.2 83.6 %all-to-all-done.1 = f32[64,128,128]{2,0,1:T(8,128)} async-done(((f32[64,128,128]{2,0,1:T(8,128)}), f32[64,128,128]{2,0,1:T(8,128)}, u32[]{:S(2)}, u32[]{:S(2)}) %all-to-all-start.1) | async-done | bytes 4194336 | tf_op jit(solution)/shard_map/all_to_all | solution.py:85
  243.9 5.9 %fusion = f32[16,64,128]{2,0,1:T(8,128)S(1)} fusion(f32[64,128,128]{2,0,1:T(8,128)} %all-to-all-done.1, s32[128]{0:T(128)S(1)} %copy-done.12), kind=kOutput, calls=%fused_computation.7 | convolution fusion | flops 201328640 | bytes 4719104 | tf_op jit(solution)/shard_map/oqb,qr->orb/dot_general | solution.py:86
  249.8 3.3 %fusion.15 = bf16[16,64,128]{2,0,1:T(8,128)(2,1)S(1)} fusion(f32[16,64,128]{2,0,1:T(8,128)S(1)} %fusion, f32[64,96,128]{2,0,1:T(8,128)S(1)} %copy-done.1, s32[96]{0:T(128)S(1)} %copy-done.11, f32[96]{0:T(128)S(1)} %fusion.57), kind=kOutput, calls=%fused_computation.27 | convolution fusion | flops 151260160 | bytes 3932928 | tf_op jit(solution)/shard_map/otb,tr->orb/dot_general | solution.py:74
  256.3 3.3 %collective-permute-start.7 = (bf16[64,2048]{1,0:T(8,128)(2,1)}, bf16[64,2048]{1,0:T(8,128)(2,1)}, u32[]{:S(2)}, u32[]{:S(2)}) collective-permute-start(bf16[64,2048]{1,0:T(8,128)(2,1)} %bitcast.92), channel_id=1, source_target_pairs={{0,2},{1,3},{2,0},{3,1},{4,6},{5,7},{6,4},{7,5},{8,10},{9,11},{10,... | collective-permute-start | bytes 786440 | tf_op jit(solution)/shard_map/ppermute | solution.py:17
  259.6 4.4 %collective-permute-start.8 = (bf16[64,2048]{1,0:T(8,128)(2,1)}, bf16[64,2048]{1,0:T(8,128)(2,1)}, u32[]{:S(2)}, u32[]{:S(2)}) collective-permute-start(bf16[64,2048]{1,0:T(8,128)(2,1)} %bitcast.92), channel_id=1, source_target_pairs={{0,3},{1,2},{2,1},{3,0},{4,7},{5,6},{6,5},{7,4},{8,11},{9,10},{10,... | collective-permute-start | bytes 786440 | tf_op jit(solution)/shard_map/ppermute | solution.py:17
  269.9 17.0 %all-to-all-start.2 = ((f32[128,1,192]{2,1,0:T(1,128)}), f32[128,1,192]{2,1,0:T(1,128)S(1)}, u32[]{:S(2)}, u32[]{:S(2)}) async-start(f32[128,1,192]{2,1,0:T(1,128)} %reshape.197), calls=%async_computation.2 | async-start | bytes 262144 | tf_op jit(solution)/shard_map/all_to_all | solution.py:27
  289.1 10.5 %all-to-all-done.2 = f32[128,1,192]{2,1,0:T(1,128)S(1)} async-done(((f32[128,1,192]{2,1,0:T(1,128)}), f32[128,1,192]{2,1,0:T(1,128)S(1)}, u32[]{:S(2)}, u32[]{:S(2)}) %all-to-all-start.2) | async-done | bytes 98336 | tf_op jit(solution)/shard_map/all_to_all | solution.py:27
  303.8 5.6 %all-to-all-start.3 = ((f32[128,1,192]{2,1,0:T(1,128)}), f32[128,1,192]{2,1,0:T(1,128)S(1)}, u32[]{:S(2)}, u32[]{:S(2)}) async-start(f32[128,1,192]{2,1,0:T(1,128)} %reshape.199), calls=%async_computation.3 | async-start | bytes 262144 | tf_op jit(solution)/shard_map/all_to_all | solution.py:30
  317.2 5.1 %all-to-all-done.3 = f32[128,1,192]{2,1,0:T(1,128)S(1)} async-done(((f32[128,1,192]{2,1,0:T(1,128)}), f32[128,1,192]{2,1,0:T(1,128)S(1)}, u32[]{:S(2)}, u32[]{:S(2)}) %all-to-all-start.3) | async-done | bytes 98336 | tf_op jit(solution)/shard_map/all_to_all | solution.py:30
  (102 shorter events, 57.1 us)
Async XLA Ops:
  0.6 113.8 %copy-start = (bf16[96,128,128]{2,1,0:T(8,128)(2,1)S(1)}, bf16[96,128,128]{2,1,0:T(8,128)(2,1)}, u32[]{:S(2)}) copy-start(bf16[96,128,128]{2,1,0:T(8,128)(2,1)} %param.14) | copy-start | bytes 9437188
  0.6 13.4 %collective-permute-start = (bf16[64,2048]{1,0:T(8,128)(2,1)}, bf16[64,2048]{1,0:T(8,128)(2,1)S(1)}, u32[]{:S(2)}, u32[]{:S(2)}) collective-permute-start(bf16[64,2048]{1,0:T(8,128)(2,1)} %param.11), channel_id=1, source_target_pairs={{0,1},{1,0},{2,3},{3,2},{4,5},{5,4},{6,7},{7,6},{8,9},{9,8},{10,11... | collective-permute-start | bytes 786440 | tf_op jit(solution)/shard_map/ppermute | solution.py:17
  4.9 13.1 %collective-permute-start.1 = (bf16[64,2048]{1,0:T(8,128)(2,1)}, bf16[64,2048]{1,0:T(8,128)(2,1)}, u32[]{:S(2)}, u32[]{:S(2)}) collective-permute-start(bf16[64,2048]{1,0:T(8,128)(2,1)} %param.11), channel_id=1, source_target_pairs={{0,2},{1,3},{2,0},{3,1},{4,6},{5,7},{6,4},{7,5},{8,10},{9,11},{10,... | collective-permute-start | bytes 786440 | tf_op jit(solution)/shard_map/ppermute | solution.py:17
  9.2 16.1 %collective-permute-start.2 = (bf16[64,2048]{1,0:T(8,128)(2,1)}, bf16[64,2048]{1,0:T(8,128)(2,1)}, u32[]{:S(2)}, u32[]{:S(2)}) collective-permute-start(bf16[64,2048]{1,0:T(8,128)(2,1)} %param.11), channel_id=1, source_target_pairs={{0,3},{1,2},{2,1},{3,0},{4,7},{5,6},{6,5},{7,4},{8,11},{9,10},{10,... | collective-permute-start | bytes 786440 | tf_op jit(solution)/shard_map/ppermute | solution.py:17
  25.4 7.5 %copy-start.6 = (bf16[256,64]{0,1:T(8,128)(2,1)S(1)}, bf16[256,64]{0,1:T(8,128)(2,1)}, u32[]{:S(2)}) copy-start(bf16[256,64]{0,1:T(8,128)(2,1)} %param.12) | copy-start | bytes 98308
  38.6 18.1 %copy-start.14 = (bf16[64]{0:T(256)(128)(2,1)S(1)}, bf16[64]{0:T(256)(128)(2,1)}, u32[]{:S(2)}) copy-start(bf16[64]{0:T(256)(128)(2,1)} %param.13) | copy-start | bytes 388
  38.6 18.2 %copy-start.11 = (s32[96]{0:T(128)S(1)}, s32[96]{0:T(128)}, u32[]{:S(2)}) copy-start(s32[96]{0:T(128)} %param.16) | copy-start | bytes 1156
  38.6 18.2 %copy-start.13 = (s32[96]{0:T(128)S(1)}, s32[96]{0:T(128)}, u32[]{:S(2)}) copy-start(s32[96]{0:T(128)} %param.15) | copy-start | bytes 1156
  38.6 69.0 %all-to-all-start = ((bf16[64,128,128]{2,0,1:T(8,128)(2,1)}), bf16[64,128,128]{2,0,1:T(8,128)(2,1)}, u32[]{:S(2)}, u32[]{:S(2)}) async-start(bf16[64,128,128]{2,0,1:T(8,128)(2,1)} %select_bitcast_fusion.1), calls=%async_computation | async-start | bytes 4194304 | tf_op jit(solution)/shard_map/all_to_all | solution.py:49
  137.7 106.2 %copy-start.12 = (s32[128]{0:T(128)S(1)}, s32[128]{0:T(128)}, u32[]{:S(2)}) copy-start(s32[128]{0:T(128)} %param.18) | copy-start | bytes 1540
  137.7 106.2 %all-to-all-start.1 = ((f32[64,128,128]{2,0,1:T(8,128)}), f32[64,128,128]{2,0,1:T(8,128)}, u32[]{:S(2)}, u32[]{:S(2)}) async-start(f32[64,128,128]{2,0,1:T(8,128)} %select_bitcast_fusion), calls=%async_computation.1 | async-start | bytes 8388608 | tf_op jit(solution)/shard_map/all_to_all | solution.py:85
  147.3 9.6 %collective-permute-start.3 = (bf16[256,64]{0,1:T(8,128)(2,1)S(1)}, bf16[256,64]{0,1:T(8,128)(2,1)S(1)}, u32[]{:S(2)}, u32[]{:S(2)}) collective-permute-start(bf16[256,64]{0,1:T(8,128)(2,1)S(1)} %copy-done.6), channel_id=1, source_target_pairs={{0,1},{1,0},{2,3},{3,2},{4,5},{5,4},{6,7},{7,6},{8,9},{9,8},{10,11... | collective-permute-start | bytes 98312 | tf_op jit(solution)/shard_map/ppermute | solution.py:17
  149.3 7.7 %collective-permute-start.4 = (bf16[256,64]{0,1:T(8,128)(2,1)S(1)}, bf16[256,64]{0,1:T(8,128)(2,1)S(1)}, u32[]{:S(2)}, u32[]{:S(2)}) collective-permute-start(bf16[256,64]{0,1:T(8,128)(2,1)S(1)} %copy-done.6), channel_id=1, source_target_pairs={{0,2},{1,3},{2,0},{3,1},{4,6},{5,7},{6,4},{7,5},{8,10},{9,11},{10,... | collective-permute-start | bytes 98312 | tf_op jit(solution)/shard_map/ppermute | solution.py:17
  152.5 6.3 %collective-permute-start.5 = (bf16[256,64]{0,1:T(8,128)(2,1)S(1)}, bf16[256,64]{0,1:T(8,128)(2,1)S(1)}, u32[]{:S(2)}, u32[]{:S(2)}) collective-permute-start(bf16[256,64]{0,1:T(8,128)(2,1)S(1)} %copy-done.6), channel_id=1, source_target_pairs={{0,3},{1,2},{2,1},{3,0},{4,7},{5,6},{6,5},{7,4},{8,11},{9,10},{10,... | collective-permute-start | bytes 98312 | tf_op jit(solution)/shard_map/ppermute | solution.py:17
  243.9 6.0 %copy-start.1 = (f32[64,96,128]{2,0,1:T(8,128)S(1)}, f32[64,96,128]{2,0,1:T(8,128)}, u32[]{:S(2)}) copy-start(f32[64,96,128]{2,0,1:T(8,128)} %convolution_bitcast_fusion) | copy-start | bytes 9437188
  254.4 55.0 %collective-permute-start.6 = (bf16[64,2048]{1,0:T(8,128)(2,1)}, bf16[64,2048]{1,0:T(8,128)(2,1)}, u32[]{:S(2)}, u32[]{:S(2)}) collective-permute-start(bf16[64,2048]{1,0:T(8,128)(2,1)} %bitcast.92), channel_id=1, source_target_pairs={{0,1},{1,0},{2,3},{3,2},{4,5},{5,4},{6,7},{7,6},{8,9},{9,8},{10,11... | collective-permute-start | bytes 786440 | tf_op jit(solution)/shard_map/ppermute | solution.py:17
  256.3 53.1 %collective-permute-start.7 = (bf16[64,2048]{1,0:T(8,128)(2,1)}, bf16[64,2048]{1,0:T(8,128)(2,1)}, u32[]{:S(2)}, u32[]{:S(2)}) collective-permute-start(bf16[64,2048]{1,0:T(8,128)(2,1)} %bitcast.92), channel_id=1, source_target_pairs={{0,2},{1,3},{2,0},{3,1},{4,6},{5,7},{6,4},{7,5},{8,10},{9,11},{10,... | collective-permute-start | bytes 786440 | tf_op jit(solution)/shard_map/ppermute | solution.py:17
  259.6 49.8 %collective-permute-start.8 = (bf16[64,2048]{1,0:T(8,128)(2,1)}, bf16[64,2048]{1,0:T(8,128)(2,1)}, u32[]{:S(2)}, u32[]{:S(2)}) collective-permute-start(bf16[64,2048]{1,0:T(8,128)(2,1)} %bitcast.92), channel_id=1, source_target_pairs={{0,3},{1,2},{2,1},{3,0},{4,7},{5,6},{6,5},{7,4},{8,11},{9,10},{10,... | collective-permute-start | bytes 786440 | tf_op jit(solution)/shard_map/ppermute | solution.py:17
  269.9 29.7 %all-to-all-start.2 = ((f32[128,1,192]{2,1,0:T(1,128)}), f32[128,1,192]{2,1,0:T(1,128)S(1)}, u32[]{:S(2)}, u32[]{:S(2)}) async-start(f32[128,1,192]{2,1,0:T(1,128)} %reshape.197), calls=%async_computation.2 | async-start | bytes 262144 | tf_op jit(solution)/shard_map/all_to_all | solution.py:27
  303.8 18.4 %all-to-all-start.3 = ((f32[128,1,192]{2,1,0:T(1,128)}), f32[128,1,192]{2,1,0:T(1,128)S(1)}, u32[]{:S(2)}, u32[]{:S(2)}) async-start(f32[128,1,192]{2,1,0:T(1,128)} %reshape.199), calls=%async_computation.3 | async-start | bytes 262144 | tf_op jit(solution)/shard_map/all_to_all | solution.py:30
  309.4 6.6 %copy-start.7 = (bf16[256,64]{0,1:T(8,128)(2,1)S(1)}, bf16[256,64]{0,1:T(8,128)(2,1)}, u32[]{:S(2)}) copy-start(bf16[256,64]{0,1:T(8,128)(2,1)} %get-tuple-element.20) | copy-start | bytes 98308
  309.5 6.6 %copy-start.8 = (bf16[256,64]{0,1:T(8,128)(2,1)S(1)}, bf16[256,64]{0,1:T(8,128)(2,1)}, u32[]{:S(2)}) copy-start(bf16[256,64]{0,1:T(8,128)(2,1)} %get-tuple-element.21) | copy-start | bytes 98308
  309.5 6.6 %copy-start.9 = (bf16[256,64]{0,1:T(8,128)(2,1)S(1)}, bf16[256,64]{0,1:T(8,128)(2,1)}, u32[]{:S(2)}) copy-start(bf16[256,64]{0,1:T(8,128)(2,1)} %get-tuple-element.22) | copy-start | bytes 98308
  309.5 6.6 %copy-start.10 = (bf16[256,64]{0,1:T(8,128)(2,1)S(1)}, bf16[256,64]{0,1:T(8,128)(2,1)}, u32[]{:S(2)}) copy-start(bf16[256,64]{0,1:T(8,128)(2,1)} %get-tuple-element.23) | copy-start | bytes 98308
  (4 other events, 8.3 us)

commit v4 on v3

--- a/solution.py
+++ b/solution.py
@@ -40,6 +40,29 @@
     blocks = node_rows // tile_size
     domains = lax.axis_size("dom")
     parts = lax.axis_size("feat")
+    live_tiles = jnp.arange(tile_slots) < tile_count[0]
+    slot_hit = jnp.logical_and(
+        tile_col[:, None] == blocks + jnp.arange(domains)[None, :], live_tiles[:, None]
+    )
+    hit_tile = jnp.sum(jnp.where(slot_hit, jnp.arange(tile_slots)[:, None], 0), axis=0)
+    has_hit = jnp.any(slot_hit, axis=0)
+    slot_rows = jnp.sum(jnp.where(slot_hit, tile_row[:, None], 0), axis=0)
+    quarter = tile_size // parts
+    my_quarter = lax.dynamic_slice_in_dim(
+        adj_tiles, lax.axis_index("feat") * quarter, quarter, 1
+    )
+    out_quarters = jnp.where(
+        has_hit[:, None, None], jnp.take(my_quarter, hit_tile, axis=0), jnp.zeros((), adj_tiles.dtype)
+    )
+    in_quarters = lax.all_to_all(out_quarters, "dom", split_axis=0, concat_axis=0, tiled=True)
+    in_tiles = jnp.moveaxis(group_stack(in_quarters, "feat", parts, 1, parts), 0, 1).reshape(
+        domains, tile_size, tile_size
+    )
+
+    def in_rows(grad_blocks):
+        out_rows = jnp.take(grad_blocks, slot_rows, axis=1)
+        return lax.all_to_all(out_rows, "dom", split_axis=1, concat_axis=1, tiled=True)
+
     whole = group_stack(node_feats, "feat", parts, 1, parts).reshape(parts * feat_rows, node_rows)
     hidden = lax.dot_general(
         weight, whole, (((0,), (0,)), ((), ())), preferred_element_type=jnp.float32
@@ -48,7 +71,6 @@
     outgoing = jnp.take(hid_blocks, send_block, axis=1)
     incoming = lax.all_to_all(outgoing, "dom", split_axis=1, concat_axis=1, tiled=True)
     sources = jnp.concatenate([hid_blocks, incoming], axis=1)
-    live_tiles = jnp.arange(tile_slots) < tile_count[0]
     live_float = live_tiles.astype(jnp.float32)
     row_place = (tile_row[:, None] == jnp.arange(blocks)[None, :]).astype(jnp.float32) * live_float[
         :, None
@@ -74,17 +96,9 @@
     own_sum = jnp.einsum(
         "otb,tr->orb", backward, src_place, precision=lax.Precision.HIGHEST
     )
-    slot_hit = jnp.logical_and(
-        tile_col[:, None] == blocks + jnp.arange(domains)[None, :], live_tiles[:, None]
-    )
-    hit_tile = jnp.sum(jnp.where(slot_hit, jnp.arange(tile_slots)[:, None], 0), axis=0)
-    has_hit = jnp.any(slot_hit, axis=0)
-    out_parts = jnp.where(
-        has_hit[None, :, None], jnp.take(backward, hit_tile, axis=1), 0.0
-    )
-    in_parts = lax.all_to_all(out_parts, "dom", split_axis=1, concat_axis=1, tiled=True)
+    remote_sum = jnp.einsum("opa,pab->opb", in_rows(grad_blocks), in_tiles, preferred_element_type=jnp.float32)
     grad_sum = own_sum + jnp.einsum(
-        "oqb,qr->orb", in_parts, recv_place, precision=lax.Precision.HIGHEST
+        "oqb,qr->orb", remote_sum, recv_place, precision=lax.Precision.HIGHEST
     )
     grad_hidden = grad_sum.reshape(feat_rows, node_rows).astype(jnp.bfloat16)
     norm_scale = 1.0 / math.sqrt(domains * node_rows)

time: 328 us -> 329 us (level)
  waiting for transfers between devices: 163 us -> 123 us
  starting transfers between devices: 79.9 us -> 96.5 us
  local copies, waits for them, and re-layouts: 32 us -> 43.1 us
  other arithmetic: 28 us -> 38.3 us
    all_to_all x1 -> x2, waiting for transfers between devices: 83.6 us -> 9.36 us  [the longest x1 9.36 us: per_device(): lax.all_to_all(out_quarters, 'dom', split_axis=0, concat_axis=0, tiled=True)]
    ppermute x9 -> x12, waiting for transfers between devices: 13.2 us -> 54.8 us  [group_stack(): received.append(lax.ppermute(values, axis, pairs))]
    ppermute x9 -> x12, starting transfers between devices: 29.7 us -> 39.5 us  [group_stack(): received.append(lax.ppermute(values, axis, pairs))]
    all_to_all x1, waiting for transfers between devices: 50.7 us -> 43.5 us  [per_device(): lax.all_to_all(outgoing, 'dom', split_axis=1, concat_axis=1, tiled=True)]
    all_to_all x1 -> x2, starting transfers between devices: 9.62 us -> 16.3 us  [the longest x1 9.32 us: per_device(): lax.all_to_all(out_quarters, 'dom', split_axis=0, concat_axis=0, tiled=True)]
    gather x3 -> x4, local copies, waits for them, and re-layouts: 6.23 us -> 12.1 us  [group_stack(): return jnp.take(stacked, mine ^ jnp.arange(count), axis=0)]
    another operation x3 -> x4, other arithmetic: 4.58 us -> 9.19 us  [group_stack(): stacked = jnp.stack(received)]
    select_n x5 -> x6, other arithmetic: 3.51 us -> 7.08 us  [group_stack(): return jnp.take(stacked, mine ^ jnp.arange(count), axis=0)]
  transfers between devices with their start and end apart: 13 -> 17, of which waited for: 7 -> 7; matrix products, arithmetic and copies ran while one was open for 7% -> 23% of each run, Pallas kernels for 0% -> 0%
where the time goes in v4:
time: 329 us; the launch traced here: 327 us
  waiting for transfers between devices  123 us (37%)
  starting transfers between devices  96.5 us (29%)
  local copies, waits for them, and re-layouts  43.1 us (13%)
  other arithmetic  38.3 us (12%)
  matrix products  24.1 us (7%)
    ppermute x12, waiting for transfers between devices, group_stack(): received.append(lax.ppermute(values, axis, pairs))  54.8 us
    all_to_all x1, waiting for transfers between devices, per_device(): lax.all_to_all(outgoing, 'dom', split_axis=1, concat_axis=1, tiled=True)  43.5 us
    ppermute x12, starting transfers between devices, group_stack(): received.append(lax.ppermute(values, axis, pairs))  39.5 us
    all_to_all x1, starting transfers between devices, per_device(): lax.all_to_all(outgoing, 'dom', split_axis=1, concat_axis=1, tiled=True)  18.1 us
    all_to_all x1, starting transfers between devices, scatter_gather_sum(): gathered = lax.all_to_all(padded, axis, 0, 0, tiled=True)  17.1 us
    gather x4, local copies, waits for them, and re-layouts, group_stack(): return jnp.take(stacked, mine ^ jnp.arange(count), axis=0)  12.1 us
    all_to_all x1, waiting for transfers between devices, scatter_gather_sum(): gathered = lax.all_to_all(padded, axis, 0, 0, tiled=True)  10.5 us
    all_to_all x1, waiting for transfers between devices, per_device(): lax.all_to_all(out_quarters, 'dom', split_axis=0, concat_axis=0, tiled=True)  9.36 us
  transfers between devices with their start and end apart: 17, of which 7 were waited for; matrix products, arithmetic and copies ran while one was open for 23% of the time, Pallas kernels for 0%

profile of v4, /device:TPU:1, one launch (start us, length us, event | category | flops | bytes accessed | tf_op | source)
XLA Modules:
  0.0 327.2 jit_solution(1412530734998043204)
XLA Ops:
  0.6 4.2 %collective-permute-start = (bf16[64,2048]{1,0:T(8,128)(2,1)}, bf16[64,2048]{1,0:T(8,128)(2,1)S(1)}, u32[]{:S(2)}, u32[]{:S(2)}) collective-permute-start(bf16[64,2048]{1,0:T(8,128)(2,1)} %param.13), channel_id=1, source_target_pairs={{0,1},{1,0},{2,3},{3,2},{4,5},{5,4},{6,7},{7,6},{8,9},{9,8},{10,11... | collective-permute-start | bytes 786440 | tf_op jit(solution)/shard_map/ppermute | solution.py:17
  4.9 4.4 %collective-permute-start.1 = (bf16[64,2048]{1,0:T(8,128)(2,1)}, bf16[64,2048]{1,0:T(8,128)(2,1)}, u32[]{:S(2)}, u32[]{:S(2)}) collective-permute-start(bf16[64,2048]{1,0:T(8,128)(2,1)} %param.13), channel_id=1, source_target_pairs={{0,2},{1,3},{2,0},{3,1},{4,6},{5,7},{6,4},{7,5},{8,10},{9,11},{10,... | collective-permute-start | bytes 786440 | tf_op jit(solution)/shard_map/ppermute | solution.py:17
  12.6 5.4 %collective-permute-done.1 = bf16[64,2048]{1,0:T(8,128)(2,1)} collective-permute-done((bf16[64,2048]{1,0:T(8,128)(2,1)}, bf16[64,2048]{1,0:T(8,128)(2,1)}, u32[]{:S(2)}, u32[]{:S(2)}) %collective-permute-start.1) | collective-permute-done | bytes 262176 | tf_op jit(solution)/shard_map/ppermute | solution.py:17
  18.0 7.4 %collective-permute-done.2 = bf16[64,2048]{1,0:T(8,128)(2,1)} collective-permute-done((bf16[64,2048]{1,0:T(8,128)(2,1)}, bf16[64,2048]{1,0:T(8,128)(2,1)}, u32[]{:S(2)}, u32[]{:S(2)}) %collective-permute-start.2) | collective-permute-done | bytes 262176 | tf_op jit(solution)/shard_map/ppermute | solution.py:17
  38.5 18.1 %all-to-all-start = ((bf16[64,128,128]{2,0,1:T(8,128)(2,1)}), bf16[64,128,128]{2,0,1:T(8,128)(2,1)}, u32[]{:S(2)}, u32[]{:S(2)}) async-start(bf16[64,128,128]{2,0,1:T(8,128)(2,1)} %select_bitcast_fusion.2), calls=%async_computation | async-start | bytes 4194304 | tf_op jit(solution)/shard_map/all_to_all | solution.py:72
  64.1 43.5 %all-to-all-done = bf16[64,128,128]{2,0,1:T(8,128)(2,1)} async-done(((bf16[64,128,128]{2,0,1:T(8,128)(2,1)}), bf16[64,128,128]{2,0,1:T(8,128)(2,1)}, u32[]{:S(2)}, u32[]{:S(2)}) %all-to-all-start) | async-done | bytes 2097184 | tf_op jit(solution)/shard_map/all_to_all | solution.py:72
  107.6 9.3 %all-to-all-start.1 = ((bf16[128,32,128]{2,1,0:T(8,128)(2,1)}), bf16[128,32,128]{2,1,0:T(8,128)(2,1)}, u32[]{:S(2)}, u32[]{:S(2)}) async-start(bf16[128,32,128]{2,1,0:T(8,128)(2,1)} %select_select_fusion), calls=%async_computation.1 | async-start | bytes 2097152 | tf_op jit(solution)/shard_map/all_to_all | solution.py:57
  120.2 3.6 %gather_fusion = bf16[96,64,128]{2,1,0:T(8,128)(2,1)} fusion(bf16[64,144,128]{2,0,1:T(8,128)(2,1)} %pad_maximum_fusion.1, s32[1024]{0:T(1024)S(1)} %pad_clamp_fusion.4), kind=kCustom, calls=%fused_computation.4 | custom fusion | bytes 3146112 | tf_op jit(solution)/shard_map/jit(_take)/gather | solution.py:78
  123.8 3.6 %convolution_bitcast_fusion.2 = f32[64,96,128]{2,0,1:T(8,128)S(1)} fusion(bf16[96,128,128]{2,1,0:T(8,128)(2,1)S(1)} %copy-done, bf16[96,64,128]{2,1,0:T(8,128)(2,1)} %gather_fusion, pred[96]{0:T(512)(128)(4,1)S(1)} %compare_and_fusion.6), kind=kOutput, calls=%fused_computation.24 | convolution fusion | flops 202113024 | bytes 7864416 | tf_op jit(solution)/shard_map/otb,tab->ota/dot_general | solution.py:79
  138.1 9.4 %all-to-all-done.1 = bf16[128,32,128]{2,1,0:T(8,128)(2,1)} async-done(((bf16[128,32,128]{2,1,0:T(8,128)(2,1)}), bf16[128,32,128]{2,1,0:T(8,128)(2,1)}, u32[]{:S(2)}, u32[]{:S(2)}) %all-to-all-start.1) | async-done | bytes 1048608 | tf_op jit(solution)/shard_map/all_to_all | solution.py:57
  147.4 6.9 %all-to-all-start.2 = ((bf16[64,128,128]{2,0,1:T(8,128)(2,1)}), bf16[64,128,128]{2,0,1:T(8,128)(2,1)}, u32[]{:S(2)}, u32[]{:S(2)}) async-start(bf16[64,128,128]{2,0,1:T(8,128)(2,1)} %select_bitcast_fusion.1), calls=%async_computation.2 | async-start | bytes 4194304 | tf_op jit(solution)/shard_map/all_to_all | solution.py:64
  161.6 5.5 %collective-permute-start.7 = (bf16[128,32,128]{2,1,0:T(8,128)(2,1)}, bf16[128,32,128]{2,1,0:T(8,128)(2,1)}, u32[]{:S(2)}, u32[]{:S(2)}) collective-permute-start(bf16[128,32,128]{2,1,0:T(8,128)(2,1)} %all-to-all-done.1), channel_id=1, source_target_pairs={{0,2},{1,3},{2,0},{3,1},{4,6},{5,7},{6,4},{7,5},{8,10},{9,11},{10,... | collective-permute-start | bytes 3145736 | tf_op jit(solution)/shard_map/ppermute | solution.py:17
  169.8 4.4 %collective-permute-start.5 = (bf16[256,64]{0,1:T(8,128)(2,1)S(1)}, bf16[256,64]{0,1:T(8,128)(2,1)S(1)}, u32[]{:S(2)}, u32[]{:S(2)}) collective-permute-start(bf16[256,64]{0,1:T(8,128)(2,1)S(1)} %copy-done.6), channel_id=1, source_target_pairs={{0,3},{1,2},{2,1},{3,0},{4,7},{5,6},{6,5},{7,4},{8,11},{9,10},{10,... | collective-permute-start | bytes 98312 | tf_op jit(solution)/shard_map/ppermute | solution.py:17
  174.3 42.0 %collective-permute-done.5 = bf16[256,64]{0,1:T(8,128)(2,1)S(1)} collective-permute-done((bf16[256,64]{0,1:T(8,128)(2,1)S(1)}, bf16[256,64]{0,1:T(8,128)(2,1)S(1)}, u32[]{:S(2)}, u32[]{:S(2)}) %collective-permute-start.5) | collective-permute-done | bytes 32800 | tf_op jit(solution)/shard_map/ppermute | solution.py:17
  220.5 3.8 %pad_maximum_fusion = bf16[4,128,32,128]{3,2,1,0:T(8,128)(2,1)} fusion(bf16[1,128,32,128]{3,2,1,0:T(8,128)(2,1)} %bitcast.30, bf16[1,128,32,128]{3,2,1,0:T(8,128)(2,1)} %bitcast.29, bf16[1,128,32,128]{3,2,1,0:T(8,128)(2,1)} %bitcast.28, bf16[1,128,32,128]{3,2,1,0:T(8,128)(2,1)} %bitcast.27), kind=kLoop, calls=%fused_computation.9 | loop fusion | flops 6291456 | bytes 8388608 | tf_op jit(solution)/shard_map/stack | solution.py:18
  224.3 5.3 %gather_fusion.4 = bf16[4,128,32,128]{3,2,1,0:T(8,128)(2,1)} fusion(bf16[4,128,32,128]{3,2,1,0:T(8,128)(2,1)} %pad_maximum_fusion, s32[1024]{0:T(1024)S(1)} %pad_clamp_fusion.3), kind=kCustom, calls=%fused_computation.8 | custom fusion | bytes 8388624 | tf_op jit(solution)/shard_map/jit(_take)/gather | solution.py:20
  237.6 4.1 %convolution_bitcast_fusion.1 = f32[64,96,128]{2,0,1:T(8,128)} fusion(bf16[96,128,128]{2,1,0:T(8,128)(2,1)S(1)} %copy-done, bf16[96,64,128]{2,1,0:T(8,128)(2,1)} %gather_fusion.2, pred[96]{0:T(512)(128)(4,1)S(1)} %copy-done.21), kind=kOutput, calls=%fused_computation.23 | convolution fusion | flops 202113024 | bytes 7864416 | tf_op jit(solution)/shard_map/ota,tab->otb/dot_general | solution.py:89
  241.7 4.1 %convolution_bitcast_fusion = f32[64,128,128]{2,0,1:T(8,128)S(1)} fusion(bf16[64,128,128]{2,0,1:T(8,128)(2,1)} %all-to-all-done.2, bf16[128,128,128]{2,1,0:T(8,128)(2,1)} %bitcast.108), kind=kOutput, calls=%fused_computation.20 | convolution fusion | flops 268435456 | bytes 10485760 | tf_op jit(solution)/shard_map/opa,pab->opb/dot_general | solution.py:99
  245.8 3.8 %fusion = f32[16,64,128]{2,0,1:T(8,128)S(1)} fusion(f32[64,128,128]{2,0,1:T(8,128)S(1)} %convolution_bitcast_fusion, s32[128]{0:T(128)S(1)} %copy-done.20), kind=kOutput, calls=%fused_computation.10 | convolution fusion | flops 201328640 | bytes 4719104 | tf_op jit(solution)/shard_map/oqb,qr->orb/dot_general | solution.py:100
  259.7 4.4 %collective-permute-start.11 = (bf16[64,2048]{1,0:T(8,128)(2,1)}, bf16[64,2048]{1,0:T(8,128)(2,1)}, u32[]{:S(2)}, u32[]{:S(2)}) collective-permute-start(bf16[64,2048]{1,0:T(8,128)(2,1)} %bitcast.103), channel_id=1, source_target_pairs={{0,3},{1,2},{2,1},{3,0},{4,7},{5,6},{6,5},{7,4},{8,11},{9,10},{10,... | collective-permute-start | bytes 786440 | tf_op jit(solution)/shard_map/ppermute | solution.py:17
  270.0 17.1 %all-to-all-start.3 = ((f32[128,1,192]{2,1,0:T(1,128)}), f32[128,1,192]{2,1,0:T(1,128)S(1)}, u32[]{:S(2)}, u32[]{:S(2)}) async-start(f32[128,1,192]{2,1,0:T(1,128)} %reshape.222), calls=%async_computation.3 | async-start | bytes 262144 | tf_op jit(solution)/shard_map/all_to_all | solution.py:27
  289.4 10.5 %all-to-all-done.3 = f32[128,1,192]{2,1,0:T(1,128)S(1)} async-done(((f32[128,1,192]{2,1,0:T(1,128)}), f32[128,1,192]{2,1,0:T(1,128)S(1)}, u32[]{:S(2)}, u32[]{:S(2)}) %all-to-all-start.3) | async-done | bytes 98336 | tf_op jit(solution)/shard_map/all_to_all | solution.py:27
  304.1 5.5 %all-to-all-start.4 = ((f32[128,1,192]{2,1,0:T(1,128)}), f32[128,1,192]{2,1,0:T(1,128)S(1)}, u32[]{:S(2)}, u32[]{:S(2)}) async-start(f32[128,1,192]{2,1,0:T(1,128)} %reshape.224), calls=%async_computation.4 | async-start | bytes 262144 | tf_op jit(solution)/shard_map/all_to_all | solution.py:30
  317.4 5.1 %all-to-all-done.4 = f32[128,1,192]{2,1,0:T(1,128)S(1)} async-done(((f32[128,1,192]{2,1,0:T(1,128)}), f32[128,1,192]{2,1,0:T(1,128)S(1)}, u32[]{:S(2)}, u32[]{:S(2)}) %all-to-all-start.4) | async-done | bytes 98336 | tf_op jit(solution)/shard_map/all_to_all | solution.py:30
  (137 shorter events, 93.9 us)
Async XLA Ops:
  0.6 56.9 %copy-start = (bf16[96,128,128]{2,1,0:T(8,128)(2,1)S(1)}, bf16[96,128,128]{2,1,0:T(8,128)(2,1)}, u32[]{:S(2)}) copy-start(bf16[96,128,128]{2,1,0:T(8,128)(2,1)} %param.16) | copy-start | bytes 9437188
  0.6 11.9 %collective-permute-start = (bf16[64,2048]{1,0:T(8,128)(2,1)}, bf16[64,2048]{1,0:T(8,128)(2,1)S(1)}, u32[]{:S(2)}, u32[]{:S(2)}) collective-permute-start(bf16[64,2048]{1,0:T(8,128)(2,1)} %param.13), channel_id=1, source_target_pairs={{0,1},{1,0},{2,3},{3,2},{4,5},{5,4},{6,7},{7,6},{8,9},{9,8},{10,11... | collective-permute-start | bytes 786440 | tf_op jit(solution)/shard_map/ppermute | solution.py:17
  4.9 13.1 %collective-permute-start.1 = (bf16[64,2048]{1,0:T(8,128)(2,1)}, bf16[64,2048]{1,0:T(8,128)(2,1)}, u32[]{:S(2)}, u32[]{:S(2)}) collective-permute-start(bf16[64,2048]{1,0:T(8,128)(2,1)} %param.13), channel_id=1, source_target_pairs={{0,2},{1,3},{2,0},{3,1},{4,6},{5,7},{6,4},{7,5},{8,10},{9,11},{10,... | collective-permute-start | bytes 786440 | tf_op jit(solution)/shard_map/ppermute | solution.py:17
  9.2 16.1 %collective-permute-start.2 = (bf16[64,2048]{1,0:T(8,128)(2,1)}, bf16[64,2048]{1,0:T(8,128)(2,1)}, u32[]{:S(2)}, u32[]{:S(2)}) collective-permute-start(bf16[64,2048]{1,0:T(8,128)(2,1)} %param.13), channel_id=1, source_target_pairs={{0,3},{1,2},{2,1},{3,0},{4,7},{5,6},{6,5},{7,4},{8,11},{9,10},{10,... | collective-permute-start | bytes 786440 | tf_op jit(solution)/shard_map/ppermute | solution.py:17
  38.5 18.8 %copy-start.14 = (s32[96]{0:T(128)S(1)}, s32[96]{0:T(128)}, u32[]{:S(2)}) copy-start(s32[96]{0:T(128)} %param.18) | copy-start | bytes 1156
  38.5 18.8 %copy-start.19 = (s32[96]{0:T(128)S(1)}, s32[96]{0:T(128)}, u32[]{:S(2)}) copy-start(s32[96]{0:T(128)} %param.17) | copy-start | bytes 1156
  38.5 69.0 %all-to-all-start = ((bf16[64,128,128]{2,0,1:T(8,128)(2,1)}), bf16[64,128,128]{2,0,1:T(8,128)(2,1)}, u32[]{:S(2)}, u32[]{:S(2)}) async-start(bf16[64,128,128]{2,0,1:T(8,128)(2,1)} %select_bitcast_fusion.2), calls=%async_computation | async-start | bytes 4194304 | tf_op jit(solution)/shard_map/all_to_all | solution.py:72
  57.3 70.1 %copy-start.16 = (f32[96]{0:T(128)}, f32[96]{0:T(128)S(1)}, u32[]{:S(2)}) copy-start(f32[96]{0:T(128)S(1)} %get-tuple-element.28) | copy-start | bytes 1156
  58.5 58.4 %copy-start.22 = (bf16[64]{0:T(256)(128)(2,1)S(1)}, bf16[64]{0:T(256)(128)(2,1)}, u32[]{:S(2)}) copy-start(bf16[64]{0:T(256)(128)(2,1)} %param.15) | copy-start | bytes 388
  107.6 39.9 %all-to-all-start.1 = ((bf16[128,32,128]{2,1,0:T(8,128)(2,1)}), bf16[128,32,128]{2,1,0:T(8,128)(2,1)}, u32[]{:S(2)}, u32[]{:S(2)}) async-start(bf16[128,32,128]{2,1,0:T(8,128)(2,1)} %select_select_fusion), calls=%async_computation.1 | async-start | bytes 2097152 | tf_op jit(solution)/shard_map/all_to_all | solution.py:57
  147.4 94.3 %all-to-all-start.2 = ((bf16[64,128,128]{2,0,1:T(8,128)(2,1)}), bf16[64,128,128]{2,0,1:T(8,128)(2,1)}, u32[]{:S(2)}, u32[]{:S(2)}) async-start(bf16[64,128,128]{2,0,1:T(8,128)(2,1)} %select_bitcast_fusion.1), calls=%async_computation.2 | async-start | bytes 4194304 | tf_op jit(solution)/shard_map/all_to_all | solution.py:64
  154.4 15.4 %collective-permute-start.3 = (bf16[256,64]{0,1:T(8,128)(2,1)S(1)}, bf16[256,64]{0,1:T(8,128)(2,1)S(1)}, u32[]{:S(2)}, u32[]{:S(2)}) collective-permute-start(bf16[256,64]{0,1:T(8,128)(2,1)S(1)} %copy-done.6), channel_id=1, source_target_pairs={{0,1},{1,0},{2,3},{3,2},{4,5},{5,4},{6,7},{7,6},{8,9},{9,8},{10,11... | collective-permute-start | bytes 98312 | tf_op jit(solution)/shard_map/ppermute | solution.py:17
  156.3 17.9 %collective-permute-start.4 = (bf16[256,64]{0,1:T(8,128)(2,1)S(1)}, bf16[256,64]{0,1:T(8,128)(2,1)S(1)}, u32[]{:S(2)}, u32[]{:S(2)}) collective-permute-start(bf16[256,64]{0,1:T(8,128)(2,1)S(1)} %copy-done.6), channel_id=1, source_target_pairs={{0,2},{1,3},{2,0},{3,1},{4,6},{5,7},{6,4},{7,5},{8,10},{9,11},{10,... | collective-permute-start | bytes 98312 | tf_op jit(solution)/shard_map/ppermute | solution.py:17
  159.6 60.9 %collective-permute-start.6 = (bf16[128,32,128]{2,1,0:T(8,128)(2,1)}, bf16[128,32,128]{2,1,0:T(8,128)(2,1)}, u32[]{:S(2)}, u32[]{:S(2)}) collective-permute-start(bf16[128,32,128]{2,1,0:T(8,128)(2,1)} %all-to-all-done.1), channel_id=1, source_target_pairs={{0,1},{1,0},{2,3},{3,2},{4,5},{5,4},{6,7},{7,6},{8,9},{9,8},{10,11... | collective-permute-start | bytes 3145736 | tf_op jit(solution)/shard_map/ppermute | solution.py:17
  161.6 58.9 %collective-permute-start.7 = (bf16[128,32,128]{2,1,0:T(8,128)(2,1)}, bf16[128,32,128]{2,1,0:T(8,128)(2,1)}, u32[]{:S(2)}, u32[]{:S(2)}) collective-permute-start(bf16[128,32,128]{2,1,0:T(8,128)(2,1)} %all-to-all-done.1), channel_id=1, source_target_pairs={{0,2},{1,3},{2,0},{3,1},{4,6},{5,7},{6,4},{7,5},{8,10},{9,11},{10,... | collective-permute-start | bytes 3145736 | tf_op jit(solution)/shard_map/ppermute | solution.py:17
  167.1 53.5 %collective-permute-start.8 = (bf16[128,32,128]{2,1,0:T(8,128)(2,1)}, bf16[128,32,128]{2,1,0:T(8,128)(2,1)}, u32[]{:S(2)}, u32[]{:S(2)}) collective-permute-start(bf16[128,32,128]{2,1,0:T(8,128)(2,1)} %all-to-all-done.1), channel_id=1, source_target_pairs={{0,3},{1,2},{2,1},{3,0},{4,7},{5,6},{6,5},{7,4},{8,11},{9,10},{10,... | collective-permute-start | bytes 3145736 | tf_op jit(solution)/shard_map/ppermute | solution.py:17
  169.8 46.4 %copy-start.11 = (bf16[256,64]{0,1:T(8,128)(2,1)}, bf16[256,64]{0,1:T(8,128)(2,1)S(1)}, u32[]{:S(2)}) copy-start(bf16[256,64]{0,1:T(8,128)(2,1)S(1)} %collective-permute-done.3) | copy-start | bytes 98308
  169.8 46.4 %collective-permute-start.5 = (bf16[256,64]{0,1:T(8,128)(2,1)S(1)}, bf16[256,64]{0,1:T(8,128)(2,1)S(1)}, u32[]{:S(2)}, u32[]{:S(2)}) collective-permute-start(bf16[256,64]{0,1:T(8,128)(2,1)S(1)} %copy-done.6), channel_id=1, source_target_pairs={{0,3},{1,2},{2,1},{3,0},{4,7},{5,6},{6,5},{7,4},{8,11},{9,10},{10,... | collective-permute-start | bytes 98312 | tf_op jit(solution)/shard_map/ppermute | solution.py:17
  174.2 42.0 %copy-start.12 = (bf16[256,64]{0,1:T(8,128)(2,1)}, bf16[256,64]{0,1:T(8,128)(2,1)S(1)}, u32[]{:S(2)}) copy-start(bf16[256,64]{0,1:T(8,128)(2,1)S(1)} %collective-permute-done.4) | copy-start | bytes 98308
  254.2 55.4 %collective-permute-start.9 = (bf16[64,2048]{1,0:T(8,128)(2,1)}, bf16[64,2048]{1,0:T(8,128)(2,1)}, u32[]{:S(2)}, u32[]{:S(2)}) collective-permute-start(bf16[64,2048]{1,0:T(8,128)(2,1)} %bitcast.103), channel_id=1, source_target_pairs={{0,1},{1,0},{2,3},{3,2},{4,5},{5,4},{6,7},{7,6},{8,9},{9,8},{10,11... | collective-permute-start | bytes 786440 | tf_op jit(solution)/shard_map/ppermute | solution.py:17
  256.4 53.3 %collective-permute-start.10 = (bf16[64,2048]{1,0:T(8,128)(2,1)}, bf16[64,2048]{1,0:T(8,128)(2,1)}, u32[]{:S(2)}, u32[]{:S(2)}) collective-permute-start(bf16[64,2048]{1,0:T(8,128)(2,1)} %bitcast.103), channel_id=1, source_target_pairs={{0,2},{1,3},{2,0},{3,1},{4,6},{5,7},{6,4},{7,5},{8,10},{9,11},{10,... | collective-permute-start | bytes 786440 | tf_op jit(solution)/shard_map/ppermute | solution.py:17
  259.7 50.0 %collective-permute-start.11 = (bf16[64,2048]{1,0:T(8,128)(2,1)}, bf16[64,2048]{1,0:T(8,128)(2,1)}, u32[]{:S(2)}, u32[]{:S(2)}) collective-permute-start(bf16[64,2048]{1,0:T(8,128)(2,1)} %bitcast.103), channel_id=1, source_target_pairs={{0,3},{1,2},{2,1},{3,0},{4,7},{5,6},{6,5},{7,4},{8,11},{9,10},{10,... | collective-permute-start | bytes 786440 | tf_op jit(solution)/shard_map/ppermute | solution.py:17
  270.0 29.8 %all-to-all-start.3 = ((f32[128,1,192]{2,1,0:T(1,128)}), f32[128,1,192]{2,1,0:T(1,128)S(1)}, u32[]{:S(2)}, u32[]{:S(2)}) async-start(f32[128,1,192]{2,1,0:T(1,128)} %reshape.222), calls=%async_computation.3 | async-start | bytes 262144 | tf_op jit(solution)/shard_map/all_to_all | solution.py:27
  304.1 18.4 %all-to-all-start.4 = ((f32[128,1,192]{2,1,0:T(1,128)}), f32[128,1,192]{2,1,0:T(1,128)S(1)}, u32[]{:S(2)}, u32[]{:S(2)}) async-start(f32[128,1,192]{2,1,0:T(1,128)} %reshape.224), calls=%async_computation.4 | async-start | bytes 262144 | tf_op jit(solution)/shard_map/all_to_all | solution.py:30
  (16 other events, 62.3 us)

commit v5 on v4

--- a/solution.py
+++ b/solution.py
@@ -55,9 +55,6 @@
         has_hit[:, None, None], jnp.take(my_quarter, hit_tile, axis=0), jnp.zeros((), adj_tiles.dtype)
     )
     in_quarters = lax.all_to_all(out_quarters, "dom", split_axis=0, concat_axis=0, tiled=True)
-    in_tiles = jnp.moveaxis(group_stack(in_quarters, "feat", parts, 1, parts), 0, 1).reshape(
-        domains, tile_size, tile_size
-    )
 
     def in_rows(grad_blocks):
         out_rows = jnp.take(grad_blocks, slot_rows, axis=1)
@@ -69,7 +66,12 @@
     ).astype(jnp.bfloat16)
     hid_blocks = hidden.reshape(feat_rows, blocks, tile_size)
     outgoing = jnp.take(hid_blocks, send_block, axis=1)
+    outgoing, in_quarters = lax.optimization_barrier((outgoing, in_quarters))
+    in_tiles = jnp.moveaxis(group_stack(in_quarters, "feat", parts, 1, parts), 0, 1).reshape(
+        domains, tile_size, tile_size
+    )
     incoming = lax.all_to_all(outgoing, "dom", split_axis=1, concat_axis=1, tiled=True)
+    incoming, in_tiles = lax.optimization_barrier((incoming, in_tiles))
     sources = jnp.concatenate([hid_blocks, incoming], axis=1)
     live_float = live_tiles.astype(jnp.float32)
     row_place = (tile_row[:, None] == jnp.arange(blocks)[None, :]).astype(jnp.float32) * live_float[

time: 329 us -> 315 us (0.957)
  waiting for transfers between devices: 123 us -> 109 us
    all_to_all x1, waiting for transfers between devices: 43.5 us -> 0.01 us  [per_device(): lax.all_to_all(outgoing, 'dom', split_axis=1, concat_axis=1, tiled=True)]
    all_to_all x1, waiting for transfers between devices: 0.01 us -> 28.3 us  [in_rows(): lax.all_to_all(out_rows, 'dom', split_axis=1, concat_axis=1, tiled=True)]
    all_to_all x1, starting transfers between devices: 18.1 us -> 6.94 us  [per_device(): lax.all_to_all(outgoing, 'dom', split_axis=1, concat_axis=1, tiled=True)]
    all_to_all x1, starting transfers between devices: 9.32 us -> 19.1 us  [per_device(): lax.all_to_all(out_quarters, 'dom', split_axis=0, concat_axis=0, tiled=True)]
    all_to_all x1, starting transfers between devices: 6.93 us -> 16.3 us  [in_rows(): lax.all_to_all(out_rows, 'dom', split_axis=1, concat_axis=1, tiled=True)]
    all_to_all x1, waiting for transfers between devices: 9.36 us -> 17.3 us  [per_device(): lax.all_to_all(out_quarters, 'dom', split_axis=0, concat_axis=0, tiled=True)]
    all_to_all x1, starting transfers between devices: 17.1 us -> 9.68 us  [scatter_gather_sum(): gathered = lax.all_to_all(padded, axis, 0, 0, tiled=True)]
    ppermute x12, waiting for transfers between devices: 54.8 us -> 47.5 us  [group_stack(): received.append(lax.ppermute(values, axis, pairs))]
  transfers between devices with their start and end apart: 17 -> 17, of which waited for: 7 -> 8; matrix products, arithmetic and copies ran while one was open for 23% -> 21% of each run, Pallas kernels for 0% -> 0%
where the time goes in v5:
time: 315 us; the launch traced here: 313 us
  waiting for transfers between devices  109 us (35%)
  starting transfers between devices  97.2 us (31%)
  local copies, waits for them, and re-layouts  43.8 us (14%)
  other arithmetic  37.7 us (12%)
  matrix products  24.1 us (8%)
    ppermute x12, waiting for transfers between devices, group_stack(): received.append(lax.ppermute(values, axis, pairs))  47.5 us
    ppermute x12, starting transfers between devices, group_stack(): received.append(lax.ppermute(values, axis, pairs))  39.6 us
    all_to_all x1, waiting for transfers between devices, in_rows(): lax.all_to_all(out_rows, 'dom', split_axis=1, concat_axis=1, tiled=True)  28.3 us
    all_to_all x1, starting transfers between devices, per_device(): lax.all_to_all(out_quarters, 'dom', split_axis=0, concat_axis=0, tiled=True)  19.1 us
    all_to_all x1, waiting for transfers between devices, per_device(): lax.all_to_all(out_quarters, 'dom', split_axis=0, concat_axis=0, tiled=True)  17.3 us
    all_to_all x1, starting transfers between devices, in_rows(): lax.all_to_all(out_rows, 'dom', split_axis=1, concat_axis=1, tiled=True)  16.3 us
    gather x4, local copies, waits for them, and re-layouts, group_stack(): return jnp.take(stacked, mine ^ jnp.arange(count), axis=0)  12.1 us
    all_to_all x1, waiting for transfers between devices, scatter_gather_sum(): gathered = lax.all_to_all(padded, axis, 0, 0, tiled=True)  10.5 us
  transfers between devices with their start and end apart: 17, of which 8 were waited for; matrix products, arithmetic and copies ran while one was open for 21% of the time, Pallas kernels for 0%

profile of v5, /device:TPU:1, one launch (start us, length us, event | category | flops | bytes accessed | tf_op | source)
XLA Modules:
  0.0 313.3 jit_solution(6253264958941580869)
XLA Ops:
  0.6 4.2 %collective-permute-start = (bf16[64,2048]{1,0:T(8,128)(2,1)}, bf16[64,2048]{1,0:T(8,128)(2,1)}, u32[]{:S(2)}, u32[]{:S(2)}) collective-permute-start(bf16[64,2048]{1,0:T(8,128)(2,1)} %param.13), channel_id=1, source_target_pairs={{0,1},{1,0},{2,3},{3,2},{4,5},{5,4},{6,7},{7,6},{8,9},{9,8},{10,11... | collective-permute-start | bytes 786440 | tf_op jit(solution)/shard_map/ppermute | solution.py:17
  4.9 4.4 %collective-permute-start.1 = (bf16[64,2048]{1,0:T(8,128)(2,1)}, bf16[64,2048]{1,0:T(8,128)(2,1)}, u32[]{:S(2)}, u32[]{:S(2)}) collective-permute-start(bf16[64,2048]{1,0:T(8,128)(2,1)} %param.13), channel_id=1, source_target_pairs={{0,2},{1,3},{2,0},{3,1},{4,6},{5,7},{6,4},{7,5},{8,10},{9,11},{10,... | collective-permute-start | bytes 786440 | tf_op jit(solution)/shard_map/ppermute | solution.py:17
  19.8 19.1 %all-to-all-start = ((bf16[128,32,128]{2,1,0:T(8,128)(2,1)}), bf16[128,32,128]{2,1,0:T(8,128)(2,1)}, u32[]{:S(2)}, u32[]{:S(2)}) async-start(bf16[128,32,128]{2,1,0:T(8,128)(2,1)} %select_select_fusion), calls=%async_computation | async-start | bytes 2097152 | tf_op jit(solution)/shard_map/all_to_all | solution.py:57
  52.2 17.3 %all-to-all-done = bf16[128,32,128]{2,1,0:T(8,128)(2,1)} async-done(((bf16[128,32,128]{2,1,0:T(8,128)(2,1)}), bf16[128,32,128]{2,1,0:T(8,128)(2,1)}, u32[]{:S(2)}, u32[]{:S(2)}) %all-to-all-start) | async-done | bytes 1048608 | tf_op jit(solution)/shard_map/all_to_all | solution.py:57
  69.4 6.9 %all-to-all-start.1 = ((bf16[64,128,128]{2,0,1:T(8,128)(2,1)}), bf16[64,128,128]{2,0,1:T(8,128)(2,1)}, u32[]{:S(2)}, u32[]{:S(2)}) async-start(bf16[64,128,128]{2,0,1:T(8,128)(2,1)} %select_bitcast_fusion.2), calls=%async_computation.1 | async-start | bytes 4194304 | tf_op jit(solution)/shard_map/all_to_all | solution.py:73
  78.3 5.6 %collective-permute-start.4 = (bf16[128,32,128]{2,1,0:T(8,128)(2,1)}, bf16[128,32,128]{2,1,0:T(8,128)(2,1)S(1)}, u32[]{:S(2)}, u32[]{:S(2)}) collective-permute-start(bf16[128,32,128]{2,1,0:T(8,128)(2,1)} %all-to-all-done), channel_id=1, source_target_pairs={{0,2},{1,3},{2,0},{3,1},{4,6},{5,7},{6,4},{7,5},{8,10},{9,11},{10,... | collective-permute-start | bytes 3145736 | tf_op jit(solution)/shard_map/ppermute | solution.py:17
  86.3 16.0 %collective-permute-done.3 = bf16[128,32,128]{2,1,0:T(8,128)(2,1)S(1)} collective-permute-done((bf16[128,32,128]{2,1,0:T(8,128)(2,1)}, bf16[128,32,128]{2,1,0:T(8,128)(2,1)S(1)}, u32[]{:S(2)}, u32[]{:S(2)}) %collective-permute-start.3) | collective-permute-done | bytes 1048608 | tf_op jit(solution)/shard_map/ppermute | solution.py:17
  102.3 24.7 %collective-permute-done.4 = bf16[128,32,128]{2,1,0:T(8,128)(2,1)S(1)} collective-permute-done((bf16[128,32,128]{2,1,0:T(8,128)(2,1)}, bf16[128,32,128]{2,1,0:T(8,128)(2,1)S(1)}, u32[]{:S(2)}, u32[]{:S(2)}) %collective-permute-start.4) | collective-permute-done | bytes 1048608 | tf_op jit(solution)/shard_map/ppermute | solution.py:17
  127.0 5.8 %collective-permute-done.5 = bf16[128,32,128]{2,1,0:T(8,128)(2,1)S(1)} collective-permute-done((bf16[128,32,128]{2,1,0:T(8,128)(2,1)}, bf16[128,32,128]{2,1,0:T(8,128)(2,1)S(1)}, u32[]{:S(2)}, u32[]{:S(2)}) %collective-permute-start.5) | collective-permute-done | bytes 1048608 | tf_op jit(solution)/shard_map/ppermute | solution.py:17
  136.1 5.3 %gather_fusion.1 = bf16[4,128,32,128]{3,2,1,0:T(8,128)(2,1)} fusion(bf16[4,128,32,128]{3,2,1,0:T(8,128)(2,1)} %pad_maximum_fusion, s32[1024]{0:T(1024)S(1)} %pad_clamp_fusion.3), kind=kCustom, calls=%fused_computation.5 | custom fusion | bytes 8388624 | tf_op jit(solution)/shard_map/jit(_take)/gather | solution.py:20
  150.6 3.6 %gather_fusion.2 = bf16[96,64,128]{2,1,0:T(8,128)(2,1)} fusion(bf16[64,144,128]{2,0,1:T(8,128)(2,1)} %pad_maximum_fusion.1, s32[1024]{0:T(1024)S(1)} %pad_clamp_fusion.2), kind=kCustom, calls=%fused_computation.6 | custom fusion | bytes 3146112 | tf_op jit(solution)/shard_map/jit(_take)/gather | solution.py:80
  154.2 3.7 %convolution_bitcast_fusion.2 = f32[64,96,128]{2,0,1:T(8,128)S(1)} fusion(bf16[96,128,128]{2,1,0:T(8,128)(2,1)S(1)} %copy-done, bf16[96,64,128]{2,1,0:T(8,128)(2,1)} %gather_fusion.2, pred[96]{0:T(512)(128)(4,1)S(1)} %compare_and_fusion.6), kind=kOutput, calls=%fused_computation.24 | convolution fusion | flops 202113024 | bytes 7864416 | tf_op jit(solution)/shard_map/otb,tab->ota/dot_general | solution.py:81
  168.4 16.3 %all-to-all-start.2 = ((bf16[64,128,128]{2,0,1:T(8,128)(2,1)}), bf16[64,128,128]{2,0,1:T(8,128)(2,1)}, u32[]{:S(2)}, u32[]{:S(2)}) async-start(bf16[64,128,128]{2,0,1:T(8,128)(2,1)} %select_bitcast_fusion.1), calls=%async_computation.2 | async-start | bytes 4194304 | tf_op jit(solution)/shard_map/all_to_all | solution.py:61
  189.9 4.6 %collective-permute-start.8 = (bf16[256,64]{0,1:T(8,128)(2,1)S(1)}, bf16[256,64]{0,1:T(8,128)(2,1)S(1)}, u32[]{:S(2)}, u32[]{:S(2)}) collective-permute-start(bf16[256,64]{0,1:T(8,128)(2,1)S(1)} %copy-done.7), channel_id=1, source_target_pairs={{0,3},{1,2},{2,1},{3,0},{4,7},{5,6},{6,5},{7,4},{8,11},{9,10},{10,... | collective-permute-start | bytes 98312 | tf_op jit(solution)/shard_map/ppermute | solution.py:17
  203.3 4.1 %convolution_bitcast_fusion.1 = f32[64,96,128]{2,0,1:T(8,128)} fusion(bf16[96,128,128]{2,1,0:T(8,128)(2,1)S(1)} %copy-done, bf16[96,64,128]{2,1,0:T(8,128)(2,1)} %gather_fusion.4, pred[96]{0:T(512)(128)(4,1)S(1)} %copy-done.22), kind=kOutput, calls=%fused_computation.23 | convolution fusion | flops 202113024 | bytes 7864416 | tf_op jit(solution)/shard_map/ota,tab->otb/dot_general | solution.py:91
  207.4 28.3 %all-to-all-done.2 = bf16[64,128,128]{2,0,1:T(8,128)(2,1)} async-done(((bf16[64,128,128]{2,0,1:T(8,128)(2,1)}), bf16[64,128,128]{2,0,1:T(8,128)(2,1)}, u32[]{:S(2)}, u32[]{:S(2)}) %all-to-all-start.2) | async-done | bytes 2097184 | tf_op jit(solution)/shard_map/all_to_all | solution.py:61
  235.6 4.0 %convolution_bitcast_fusion = f32[64,128,128]{2,0,1:T(8,128)S(1)} fusion(bf16[64,128,128]{2,0,1:T(8,128)(2,1)} %all-to-all-done.2, bf16[128,128,128]{2,1,0:T(8,128)(2,1)} %bitcast.109), kind=kOutput, calls=%fused_computation.20 | convolution fusion | flops 268435456 | bytes 10485760 | tf_op jit(solution)/shard_map/opa,pab->opb/dot_general | solution.py:101
  239.7 3.8 %fusion = f32[16,64,128]{2,0,1:T(8,128)S(1)} fusion(f32[64,128,128]{2,0,1:T(8,128)S(1)} %convolution_bitcast_fusion, s32[128]{0:T(128)S(1)} %copy-done.21), kind=kOutput, calls=%fused_computation.10 | convolution fusion | flops 201328640 | bytes 4719104 | tf_op jit(solution)/shard_map/oqb,qr->orb/dot_general | solution.py:102
  243.6 3.3 %fusion.15 = bf16[16,64,128]{2,0,1:T(8,128)(2,1)S(1)} fusion(f32[16,64,128]{2,0,1:T(8,128)S(1)} %fusion, f32[64,96,128]{2,0,1:T(8,128)S(1)} %copy-done.1, s32[96]{0:T(128)S(1)} %copy-done.16, f32[96]{0:T(128)S(1)} %copy-done.18), kind=kOutput, calls=%fused_computation.32 | convolution fusion | flops 151260160 | bytes 3932928 | tf_op jit(solution)/shard_map/otb,tr->orb/dot_general | solution.py:98
  253.3 4.4 %collective-permute-start.11 = (bf16[64,2048]{1,0:T(8,128)(2,1)}, bf16[64,2048]{1,0:T(8,128)(2,1)}, u32[]{:S(2)}, u32[]{:S(2)}) collective-permute-start(bf16[64,2048]{1,0:T(8,128)(2,1)} %bitcast.103), channel_id=1, source_target_pairs={{0,3},{1,2},{2,1},{3,0},{4,7},{5,6},{6,5},{7,4},{8,11},{9,10},{10,... | collective-permute-start | bytes 786440 | tf_op jit(solution)/shard_map/ppermute | solution.py:17
  263.6 9.7 %all-to-all-start.3 = ((f32[128,1,192]{2,1,0:T(1,128)}), f32[128,1,192]{2,1,0:T(1,128)S(1)}, u32[]{:S(2)}, u32[]{:S(2)}) async-start(f32[128,1,192]{2,1,0:T(1,128)} %reshape.222), calls=%async_computation.3 | async-start | bytes 262144 | tf_op jit(solution)/shard_map/all_to_all | solution.py:27
  275.5 10.5 %all-to-all-done.3 = f32[128,1,192]{2,1,0:T(1,128)S(1)} async-done(((f32[128,1,192]{2,1,0:T(1,128)}), f32[128,1,192]{2,1,0:T(1,128)S(1)}, u32[]{:S(2)}, u32[]{:S(2)}) %all-to-all-start.3) | async-done | bytes 98336 | tf_op jit(solution)/shard_map/all_to_all | solution.py:27
  290.2 5.5 %all-to-all-start.4 = ((f32[128,1,192]{2,1,0:T(1,128)}), f32[128,1,192]{2,1,0:T(1,128)S(1)}, u32[]{:S(2)}, u32[]{:S(2)}) async-start(f32[128,1,192]{2,1,0:T(1,128)} %reshape.224), calls=%async_computation.4 | async-start | bytes 262144 | tf_op jit(solution)/shard_map/all_to_all | solution.py:30
  303.5 5.1 %all-to-all-done.4 = f32[128,1,192]{2,1,0:T(1,128)S(1)} async-done(((f32[128,1,192]{2,1,0:T(1,128)}), f32[128,1,192]{2,1,0:T(1,128)S(1)}, u32[]{:S(2)}, u32[]{:S(2)}) %all-to-all-start.4) | async-done | bytes 98336 | tf_op jit(solution)/shard_map/all_to_all | solution.py:30
  (139 shorter events, 95.2 us)
Async XLA Ops:
  0.6 12.8 %copy-start = (bf16[96,128,128]{2,1,0:T(8,128)(2,1)S(1)}, bf16[96,128,128]{2,1,0:T(8,128)(2,1)}, u32[]{:S(2)}) copy-start(bf16[96,128,128]{2,1,0:T(8,128)(2,1)} %param.16) | copy-start | bytes 9437188
  0.6 38.4 %collective-permute-start = (bf16[64,2048]{1,0:T(8,128)(2,1)}, bf16[64,2048]{1,0:T(8,128)(2,1)}, u32[]{:S(2)}, u32[]{:S(2)}) collective-permute-start(bf16[64,2048]{1,0:T(8,128)(2,1)} %param.13), channel_id=1, source_target_pairs={{0,1},{1,0},{2,3},{3,2},{4,5},{5,4},{6,7},{7,6},{8,9},{9,8},{10,11... | collective-permute-start | bytes 786440 | tf_op jit(solution)/shard_map/ppermute | solution.py:17
  4.9 34.1 %collective-permute-start.1 = (bf16[64,2048]{1,0:T(8,128)(2,1)}, bf16[64,2048]{1,0:T(8,128)(2,1)}, u32[]{:S(2)}, u32[]{:S(2)}) collective-permute-start(bf16[64,2048]{1,0:T(8,128)(2,1)} %param.13), channel_id=1, source_target_pairs={{0,2},{1,3},{2,0},{3,1},{4,6},{5,7},{6,4},{7,5},{8,10},{9,11},{10,... | collective-permute-start | bytes 786440 | tf_op jit(solution)/shard_map/ppermute | solution.py:17
  9.2 29.8 %collective-permute-start.2 = (bf16[64,2048]{1,0:T(8,128)(2,1)}, bf16[64,2048]{1,0:T(8,128)(2,1)}, u32[]{:S(2)}, u32[]{:S(2)}) collective-permute-start(bf16[64,2048]{1,0:T(8,128)(2,1)} %param.13), channel_id=1, source_target_pairs={{0,3},{1,2},{2,1},{3,0},{4,7},{5,6},{6,5},{7,4},{8,11},{9,10},{10,... | collective-permute-start | bytes 786440 | tf_op jit(solution)/shard_map/ppermute | solution.py:17
  14.4 24.5 %copy-start.20 = (s32[128]{0:T(128)S(1)}, s32[128]{0:T(128)}, u32[]{:S(2)}) copy-start(s32[128]{0:T(128)} %param.20) | copy-start | bytes 1540
  14.4 24.6 %copy-start.6 = (bf16[64,2048]{1,0:T(8,128)(2,1)S(1)}, bf16[64,2048]{1,0:T(8,128)(2,1)}, u32[]{:S(2)}) copy-start(bf16[64,2048]{1,0:T(8,128)(2,1)} %param.13) | copy-start | bytes 786436
  19.8 49.6 %all-to-all-start = ((bf16[128,32,128]{2,1,0:T(8,128)(2,1)}), bf16[128,32,128]{2,1,0:T(8,128)(2,1)}, u32[]{:S(2)}, u32[]{:S(2)}) async-start(bf16[128,32,128]{2,1,0:T(8,128)(2,1)} %select_select_fusion), calls=%async_computation | async-start | bytes 2097152 | tf_op jit(solution)/shard_map/all_to_all | solution.py:57
  52.2 34.0 %copy-start.23 = (bf16[64]{0:T(256)(128)(2,1)S(1)}, bf16[64]{0:T(256)(128)(2,1)}, u32[]{:S(2)}) copy-start(bf16[64]{0:T(256)(128)(2,1)} %param.15) | copy-start | bytes 388
  52.2 34.1 %copy-start.15 = (s32[96]{0:T(128)S(1)}, s32[96]{0:T(128)}, u32[]{:S(2)}) copy-start(s32[96]{0:T(128)} %param.18) | copy-start | bytes 1156
  69.4 77.9 %all-to-all-start.1 = ((bf16[64,128,128]{2,0,1:T(8,128)(2,1)}), bf16[64,128,128]{2,0,1:T(8,128)(2,1)}, u32[]{:S(2)}, u32[]{:S(2)}) async-start(bf16[64,128,128]{2,0,1:T(8,128)(2,1)} %select_bitcast_fusion.2), calls=%async_computation.1 | async-start | bytes 4194304 | tf_op jit(solution)/shard_map/all_to_all | solution.py:73
  76.4 25.9 %collective-permute-start.3 = (bf16[128,32,128]{2,1,0:T(8,128)(2,1)}, bf16[128,32,128]{2,1,0:T(8,128)(2,1)S(1)}, u32[]{:S(2)}, u32[]{:S(2)}) collective-permute-start(bf16[128,32,128]{2,1,0:T(8,128)(2,1)} %all-to-all-done), channel_id=1, source_target_pairs={{0,1},{1,0},{2,3},{3,2},{4,5},{5,4},{6,7},{7,6},{8,9},{9,8},{10,11... | collective-permute-start | bytes 3145736 | tf_op jit(solution)/shard_map/ppermute | solution.py:17
  78.3 48.7 %collective-permute-start.4 = (bf16[128,32,128]{2,1,0:T(8,128)(2,1)}, bf16[128,32,128]{2,1,0:T(8,128)(2,1)S(1)}, u32[]{:S(2)}, u32[]{:S(2)}) collective-permute-start(bf16[128,32,128]{2,1,0:T(8,128)(2,1)} %all-to-all-done), channel_id=1, source_target_pairs={{0,2},{1,3},{2,0},{3,1},{4,6},{5,7},{6,4},{7,5},{8,10},{9,11},{10,... | collective-permute-start | bytes 3145736 | tf_op jit(solution)/shard_map/ppermute | solution.py:17
  83.9 48.9 %collective-permute-start.5 = (bf16[128,32,128]{2,1,0:T(8,128)(2,1)}, bf16[128,32,128]{2,1,0:T(8,128)(2,1)S(1)}, u32[]{:S(2)}, u32[]{:S(2)}) collective-permute-start(bf16[128,32,128]{2,1,0:T(8,128)(2,1)} %all-to-all-done), channel_id=1, source_target_pairs={{0,3},{1,2},{2,1},{3,0},{4,7},{5,6},{6,5},{7,4},{8,11},{9,10},{10,... | collective-permute-start | bytes 3145736 | tf_op jit(solution)/shard_map/ppermute | solution.py:17
  86.2 71.7 %copy-start.17 = (f32[96]{0:T(128)}, f32[96]{0:T(128)S(1)}, u32[]{:S(2)}) copy-start(f32[96]{0:T(128)S(1)} %fusion.57) | copy-start | bytes 1156
  168.4 67.2 %all-to-all-start.2 = ((bf16[64,128,128]{2,0,1:T(8,128)(2,1)}), bf16[64,128,128]{2,0,1:T(8,128)(2,1)}, u32[]{:S(2)}, u32[]{:S(2)}) async-start(bf16[64,128,128]{2,0,1:T(8,128)(2,1)} %select_bitcast_fusion.1), calls=%async_computation.2 | async-start | bytes 4194304 | tf_op jit(solution)/shard_map/all_to_all | solution.py:61
  184.7 10.4 %collective-permute-start.6 = (bf16[256,64]{0,1:T(8,128)(2,1)S(1)}, bf16[256,64]{0,1:T(8,128)(2,1)S(1)}, u32[]{:S(2)}, u32[]{:S(2)}) collective-permute-start(bf16[256,64]{0,1:T(8,128)(2,1)S(1)} %copy-done.7), channel_id=1, source_target_pairs={{0,1},{1,0},{2,3},{3,2},{4,5},{5,4},{6,7},{7,6},{8,9},{9,8},{10,11... | collective-permute-start | bytes 98312 | tf_op jit(solution)/shard_map/ppermute | solution.py:17
  186.6 8.5 %collective-permute-start.7 = (bf16[256,64]{0,1:T(8,128)(2,1)S(1)}, bf16[256,64]{0,1:T(8,128)(2,1)S(1)}, u32[]{:S(2)}, u32[]{:S(2)}) collective-permute-start(bf16[256,64]{0,1:T(8,128)(2,1)S(1)} %copy-done.7), channel_id=1, source_target_pairs={{0,2},{1,3},{2,0},{3,1},{4,6},{5,7},{6,4},{7,5},{8,10},{9,11},{10,... | collective-permute-start | bytes 98312 | tf_op jit(solution)/shard_map/ppermute | solution.py:17
  189.9 6.3 %collective-permute-start.8 = (bf16[256,64]{0,1:T(8,128)(2,1)S(1)}, bf16[256,64]{0,1:T(8,128)(2,1)S(1)}, u32[]{:S(2)}, u32[]{:S(2)}) collective-permute-start(bf16[256,64]{0,1:T(8,128)(2,1)S(1)} %copy-done.7), channel_id=1, source_target_pairs={{0,3},{1,2},{2,1},{3,0},{4,7},{5,6},{6,5},{7,4},{8,11},{9,10},{10,... | collective-permute-start | bytes 98312 | tf_op jit(solution)/shard_map/ppermute | solution.py:17
  207.4 32.3 %copy-start.21 = (s32[128]{0:T(128)S(1)}, s32[128]{0:T(128)}, u32[]{:S(2)}) copy-start(s32[128]{0:T(128)} %param.20) | copy-start | bytes 1540
  248.1 47.7 %collective-permute-start.9 = (bf16[64,2048]{1,0:T(8,128)(2,1)}, bf16[64,2048]{1,0:T(8,128)(2,1)}, u32[]{:S(2)}, u32[]{:S(2)}) collective-permute-start(bf16[64,2048]{1,0:T(8,128)(2,1)} %bitcast.103), channel_id=1, source_target_pairs={{0,1},{1,0},{2,3},{3,2},{4,5},{5,4},{6,7},{7,6},{8,9},{9,8},{10,11... | collective-permute-start | bytes 786440 | tf_op jit(solution)/shard_map/ppermute | solution.py:17
  250.0 45.8 %collective-permute-start.10 = (bf16[64,2048]{1,0:T(8,128)(2,1)}, bf16[64,2048]{1,0:T(8,128)(2,1)}, u32[]{:S(2)}, u32[]{:S(2)}) collective-permute-start(bf16[64,2048]{1,0:T(8,128)(2,1)} %bitcast.103), channel_id=1, source_target_pairs={{0,2},{1,3},{2,0},{3,1},{4,6},{5,7},{6,4},{7,5},{8,10},{9,11},{10,... | collective-permute-start | bytes 786440 | tf_op jit(solution)/shard_map/ppermute | solution.py:17
  253.3 42.5 %collective-permute-start.11 = (bf16[64,2048]{1,0:T(8,128)(2,1)}, bf16[64,2048]{1,0:T(8,128)(2,1)}, u32[]{:S(2)}, u32[]{:S(2)}) collective-permute-start(bf16[64,2048]{1,0:T(8,128)(2,1)} %bitcast.103), channel_id=1, source_target_pairs={{0,3},{1,2},{2,1},{3,0},{4,7},{5,6},{6,5},{7,4},{8,11},{9,10},{10,... | collective-permute-start | bytes 786440 | tf_op jit(solution)/shard_map/ppermute | solution.py:17
  263.6 22.4 %all-to-all-start.3 = ((f32[128,1,192]{2,1,0:T(1,128)}), f32[128,1,192]{2,1,0:T(1,128)S(1)}, u32[]{:S(2)}, u32[]{:S(2)}) async-start(f32[128,1,192]{2,1,0:T(1,128)} %reshape.222), calls=%async_computation.3 | async-start | bytes 262144 | tf_op jit(solution)/shard_map/all_to_all | solution.py:27
  290.2 18.4 %all-to-all-start.4 = ((f32[128,1,192]{2,1,0:T(1,128)}), f32[128,1,192]{2,1,0:T(1,128)S(1)}, u32[]{:S(2)}, u32[]{:S(2)}) async-start(f32[128,1,192]{2,1,0:T(1,128)} %reshape.224), calls=%async_computation.4 | async-start | bytes 262144 | tf_op jit(solution)/shard_map/all_to_all | solution.py:30
  (17 other events, 64.2 us)

commit v6 on v3

--- a/solution.py
+++ b/solution.py
@@ -81,10 +81,11 @@
     has_hit = jnp.any(slot_hit, axis=0)
     out_parts = jnp.where(
         has_hit[None, :, None], jnp.take(backward, hit_tile, axis=1), 0.0
-    )
+    ).astype(jnp.bfloat16)
     in_parts = lax.all_to_all(out_parts, "dom", split_axis=1, concat_axis=1, tiled=True)
+    remote_sum = in_parts.astype(jnp.float32)
     grad_sum = own_sum + jnp.einsum(
-        "oqb,qr->orb", in_parts, recv_place, precision=lax.Precision.HIGHEST
+        "oqb,qr->orb", remote_sum, recv_place, precision=lax.Precision.HIGHEST
     )
     grad_hidden = grad_sum.reshape(feat_rows, node_rows).astype(jnp.bfloat16)
     norm_scale = 1.0 / math.sqrt(domains * node_rows)

time: 328 us -> 263 us (0.80)
  waiting for transfers between devices: 163 us -> 105 us
  starting transfers between devices: 79.9 us -> 74.7 us
    all_to_all x1, waiting for transfers between devices: 83.6 us -> 31.7 us  [per_device(): lax.all_to_all(out_parts, 'dom', split_axis=1, concat_axis=1, tiled=True)]
    all_to_all x1, starting transfers between devices: 17 us -> 9.68 us  [scatter_gather_sum(): gathered = lax.all_to_all(padded, axis, 0, 0, tiled=True)]
    ppermute x9, waiting for transfers between devices: 13.2 us -> 6.84 us  [group_stack(): received.append(lax.ppermute(values, axis, pairs))]
    select_n x1 -> x0, other arithmetic: 4.09 us -> none  [per_device(): jnp.where(has_hit[None, :, None], jnp.take(backward, hit_tile, axis=1), 0.0)]
    all_to_all x1, starting transfers between devices: 18.1 us -> 22.2 us  [per_device(): lax.all_to_all(outgoing, 'dom', split_axis=1, concat_axis=1, tiled=True)]
    convert_element_type x0 -> x1, other arithmetic: none -> 3.35 us  [per_device(): out_parts = jnp.where(has_hit[None, :, None], jnp.take(backward, hit_tile...]
    unnamed x37 -> x35, local copies, waits for them, and re-layouts: 7.18 us -> 7.21 us
  transfers between devices with their start and end apart: 13 -> 13, of which waited for: 7 -> 8; matrix products, arithmetic and copies ran while one was open for 7% -> 11% of each run, Pallas kernels for 0% -> 0%
where the time goes in v6:
time: 263 us; the launch traced here: 262 us
  waiting for transfers between devices  105 us (40%)
  starting transfers between devices  74.7 us (28%)
  local copies, waits for them, and re-layouts  31.4 us (12%)
  other arithmetic  27.2 us (10%)
  matrix products  21.8 us (8%)
    all_to_all x1, waiting for transfers between devices, per_device(): lax.all_to_all(outgoing, 'dom', split_axis=1, concat_axis=1, tiled=True)  50.7 us
    all_to_all x1, waiting for transfers between devices, per_device(): lax.all_to_all(out_parts, 'dom', split_axis=1, concat_axis=1, tiled=True)  31.7 us
    ppermute x9, starting transfers between devices, group_stack(): received.append(lax.ppermute(values, axis, pairs))  27.8 us
    all_to_all x1, starting transfers between devices, per_device(): lax.all_to_all(outgoing, 'dom', split_axis=1, concat_axis=1, tiled=True)  22.2 us
    all_to_all x1, waiting for transfers between devices, scatter_gather_sum(): gathered = lax.all_to_all(padded, axis, 0, 0, tiled=True)  10.4 us
    all_to_all x1, starting transfers between devices, scatter_gather_sum(): gathered = lax.all_to_all(padded, axis, 0, 0, tiled=True)  9.68 us
    all_to_all x1, starting transfers between devices, per_device(): lax.all_to_all(out_parts, 'dom', split_axis=1, concat_axis=1, tiled=True)  9.49 us
    unnamed x35, local copies, waits for them, and re-layouts  7.21 us
  transfers between devices with their start and end apart: 13, of which 8 were waited for; matrix products, arithmetic and copies ran while one was open for 11% of the time, Pallas kernels for 0%

profile of v6, /device:TPU:1, one launch (start us, length us, event | category | flops | bytes accessed | tf_op | source)
XLA Modules:
  0.0 261.6 jit_solution(1138124288521197742)
XLA Ops:
  0.6 5.5 %collective-permute-start.2 = (bf16[64,2048]{1,0:T(8,128)(2,1)}, bf16[64,2048]{1,0:T(8,128)(2,1)S(1)}, u32[]{:S(2)}, u32[]{:S(2)}) collective-permute-start(bf16[64,2048]{1,0:T(8,128)(2,1)} %param.11), channel_id=1, source_target_pairs={{0,3},{1,2},{2,1},{3,0},{4,7},{5,6},{6,5},{7,4},{8,11},{9,10},{10,... | collective-permute-start | bytes 786440 | tf_op jit(solution)/shard_map/ppermute | solution.py:17
  6.1 2.4 collective-permute-start.1
  19.6 2.8 %gather_fusion.5 = bf16[4,64,2048]{2,1,0:T(8,128)(2,1)} fusion(bf16[4,64,2048]{2,1,0:T(8,128)(2,1)} %pad_maximum_fusion.1, s32[1024]{0:T(1024)S(1)} %pad_clamp_fusion.5), kind=kCustom, calls=%fused_computation.clone | custom fusion | bytes 2097168 | tf_op jit(solution)/shard_map/jit(_take)/gather | solution.py:20
  27.4 3.2 %select_bitcast_fusion = bf16[64,128,128]{2,0,1:T(8,128)(2,1)} fusion(bf16[128,64,128]{2,1,0:T(8,128)(2,1)} %gather_fusion, pred[128]{0:T(512)(128)(4,1)S(1)} %get-tuple-element.25), kind=kLoop, calls=%fused_computation.18 | loop fusion | flops 1048576 | bytes 4194432 | tf_op jit(solution)/shard_map/jit(_take)/select_n | solution.py:48
  30.6 22.2 %all-to-all-start = ((bf16[64,128,128]{2,0,1:T(8,128)(2,1)}), bf16[64,128,128]{2,0,1:T(8,128)(2,1)}, u32[]{:S(2)}, u32[]{:S(2)}) async-start(bf16[64,128,128]{2,0,1:T(8,128)(2,1)} %select_bitcast_fusion), calls=%async_computation | async-start | bytes 4194304 | tf_op jit(solution)/shard_map/all_to_all | solution.py:49
  53.0 50.7 %all-to-all-done = bf16[64,128,128]{2,0,1:T(8,128)(2,1)} async-done(((bf16[64,128,128]{2,0,1:T(8,128)(2,1)}), bf16[64,128,128]{2,0,1:T(8,128)(2,1)}, u32[]{:S(2)}, u32[]{:S(2)}) %all-to-all-start) | async-done | bytes 2097184 | tf_op jit(solution)/shard_map/all_to_all | solution.py:49
  103.7 3.2 %pad_maximum_fusion = bf16[64,144,128]{2,0,1:T(8,128)(2,1)} fusion(bf16[64,128,128]{2,0,1:T(8,128)(2,1)} %all-to-all-done, bf16[64,16,128]{2,0,1:T(8,128)(2,1)S(1)} %bitcast.97), kind=kLoop, calls=%fused_computation.12 | loop fusion | flops 1179648 | bytes 4718592 | tf_op jit(solution)/shard_map/concatenate | solution.py:50
  106.9 3.6 %gather_fusion.1 = bf16[96,64,128]{2,1,0:T(8,128)(2,1)} fusion(bf16[64,144,128]{2,0,1:T(8,128)(2,1)} %pad_maximum_fusion, s32[1024]{0:T(1024)S(1)} %pad_clamp_fusion.3), kind=kCustom, calls=%fused_computation.3 | custom fusion | bytes 3146112 | tf_op jit(solution)/shard_map/jit(_take)/gather | solution.py:56
  110.5 3.6 %convolution_bitcast_fusion.1 = f32[64,96,128]{2,0,1:T(8,128)S(1)} fusion(bf16[96,128,128]{2,1,0:T(8,128)(2,1)S(1)} %copy-done, bf16[96,64,128]{2,1,0:T(8,128)(2,1)} %gather_fusion.1, pred[96]{0:T(512)(128)(4,1)S(1)} %compare_and_fusion.5), kind=kOutput, calls=%fused_computation.20 | convolution fusion | flops 202113024 | bytes 7864416 | tf_op jit(solution)/shard_map/otb,tab->ota/dot_general | solution.py:57
  114.2 3.3 %fusion.2 = f32[16,64,128]{2,0,1:T(8,128)S(1)} fusion(f32[64,96,128]{2,0,1:T(8,128)S(1)} %convolution_bitcast_fusion.1, f32[96]{0:T(128)S(1)} %fusion.58, s32[96]{0:T(128)S(1)} %copy-done.12), kind=kOutput, calls=%fused_computation.10 | convolution fusion | flops 150998016 | bytes 3670784 | tf_op jit(solution)/shard_map/ota,tr->ora/dot_general | solution.py:58
  120.8 4.1 %convolution_bitcast_fusion = f32[64,96,128]{2,0,1:T(8,128)} fusion(bf16[96,128,128]{2,1,0:T(8,128)(2,1)S(1)} %copy-done, bf16[96,64,128]{2,1,0:T(8,128)(2,1)} %gather_fusion.3, pred[96]{0:T(512)(128)(4,1)S(1)} %compare_and_fusion.3), kind=kOutput, calls=%fused_computation.19 | convolution fusion | flops 202113024 | bytes 7864416 | tf_op jit(solution)/shard_map/ota,tab->otb/dot_general | solution.py:67
  124.9 4.0 %gather_fusion.4 = bf16[128,64,128]{2,1,0:T(8,128)(2,1)} fusion(f32[64,96,128]{2,0,1:T(8,128)} %convolution_bitcast_fusion, s32[1024]{0:T(1024)S(1)} %pad_clamp_fusion), kind=kCustom, calls=%fused_computation.6 | custom fusion | bytes 4194816 | tf_op jit(solution)/shard_map/jit(_take)/gather | solution.py:83
  128.9 3.4 %fusion.4 = bf16[64,128,128]{2,0,1:T(8,128)(2,1)} fusion(bf16[128,64,128]{2,1,0:T(8,128)(2,1)} %gather_fusion.4, pred[128]{0:T(512)(128)(4,1)S(1)} %fusion.35, pred[128]{0:T(512)(128)(4,1)S(1)} %get-tuple-element.24), kind=kLoop, calls=%fused_computation.15 | loop fusion | flops 2097152 | bytes 4194560 | tf_op jit(solution)/shard_map/convert_element_type | solution.py:84
  132.3 9.5 %all-to-all-start.1 = ((bf16[64,128,128]{2,0,1:T(8,128)(2,1)}), bf16[64,128,128]{2,0,1:T(8,128)(2,1)}, u32[]{:S(2)}, u32[]{:S(2)}) async-start(bf16[64,128,128]{2,0,1:T(8,128)(2,1)} %fusion.4), calls=%async_computation.1 | async-start | bytes 4194304 | tf_op jit(solution)/shard_map/all_to_all | solution.py:85
  141.8 4.4 %collective-permute-start.5 = (bf16[256,64]{0,1:T(8,128)(2,1)S(1)}, bf16[256,64]{0,1:T(8,128)(2,1)S(1)}, u32[]{:S(2)}, u32[]{:S(2)}) collective-permute-start(bf16[256,64]{0,1:T(8,128)(2,1)S(1)} %copy-done.5), channel_id=1, source_target_pairs={{0,3},{1,2},{2,1},{3,0},{4,7},{5,6},{6,5},{7,4},{8,11},{9,10},{10,... | collective-permute-start | bytes 98312 | tf_op jit(solution)/shard_map/ppermute | solution.py:17
  155.1 5.9 %fusion = f32[16,64,128]{2,0,1:T(8,128)} fusion(f32[64,96,128]{2,0,1:T(8,128)} %convolution_bitcast_fusion, s32[96]{0:T(128)S(1)} %copy-done.10, f32[96]{0:T(128)S(1)} %fusion.58), kind=kOutput, calls=%fused_computation.8 | convolution fusion | flops 150998016 | bytes 3670784 | tf_op jit(solution)/shard_map/otb,tr->orb/dot_general | solution.py:74
  161.0 31.7 %all-to-all-done.1 = bf16[64,128,128]{2,0,1:T(8,128)(2,1)} async-done(((bf16[64,128,128]{2,0,1:T(8,128)(2,1)}), bf16[64,128,128]{2,0,1:T(8,128)(2,1)}, u32[]{:S(2)}, u32[]{:S(2)}) %all-to-all-start.1) | async-done | bytes 2097184 | tf_op jit(solution)/shard_map/all_to_all | solution.py:85
  192.7 3.0 %fusion.16 = bf16[16,64,128]{2,0,1:T(8,128)(2,1)S(1)} fusion(f32[16,64,128]{2,0,1:T(8,128)} %fusion, bf16[64,128,128]{2,0,1:T(8,128)(2,1)} %all-to-all-done.1, s32[128]{0:T(128)S(1)} %copy-done.11), kind=kOutput, calls=%fused_computation.28 | convolution fusion | flops 33818624 | bytes 2884096 | tf_op jit(solution)/shard_map/oqb,qr->orb/dot_general | solution.py:87
  196.5 4.4 %collective-permute-start.8 = (bf16[64,2048]{1,0:T(8,128)(2,1)}, bf16[64,2048]{1,0:T(8,128)(2,1)}, u32[]{:S(2)}, u32[]{:S(2)}) collective-permute-start(bf16[64,2048]{1,0:T(8,128)(2,1)} %bitcast.92), channel_id=1, source_target_pairs={{0,3},{1,2},{2,1},{3,0},{4,7},{5,6},{6,5},{7,4},{8,11},{9,10},{10,... | collective-permute-start | bytes 786440 | tf_op jit(solution)/shard_map/ppermute | solution.py:17
  211.8 9.7 %all-to-all-start.2 = ((f32[128,1,192]{2,1,0:T(1,128)}), f32[128,1,192]{2,1,0:T(1,128)S(1)}, u32[]{:S(2)}, u32[]{:S(2)}) async-start(f32[128,1,192]{2,1,0:T(1,128)} %reshape.197), calls=%async_computation.2 | async-start | bytes 262144 | tf_op jit(solution)/shard_map/all_to_all | solution.py:27
  223.8 10.4 %all-to-all-done.2 = f32[128,1,192]{2,1,0:T(1,128)S(1)} async-done(((f32[128,1,192]{2,1,0:T(1,128)}), f32[128,1,192]{2,1,0:T(1,128)S(1)}, u32[]{:S(2)}, u32[]{:S(2)}) %all-to-all-start.2) | async-done | bytes 98336 | tf_op jit(solution)/shard_map/all_to_all | solution.py:27
  238.5 5.6 %all-to-all-start.3 = ((f32[128,1,192]{2,1,0:T(1,128)}), f32[128,1,192]{2,1,0:T(1,128)S(1)}, u32[]{:S(2)}, u32[]{:S(2)}) async-start(f32[128,1,192]{2,1,0:T(1,128)} %reshape.199), calls=%async_computation.3 | async-start | bytes 262144 | tf_op jit(solution)/shard_map/all_to_all | solution.py:30
  246.4 2.8 %gather_fusion.6 = bf16[4,64,2048]{2,1,0:T(8,128)(2,1)} fusion(bf16[4,64,2048]{2,1,0:T(8,128)(2,1)} %pad_maximum_fusion.2, s32[1024]{0:T(1024)S(1)} %pad_clamp_fusion.5), kind=kCustom, calls=%fused_computation.1.clone | custom fusion | bytes 2097168 | tf_op jit(solution)/shard_map/jit(_take)/gather | solution.py:20
  251.8 5.1 %all-to-all-done.3 = f32[128,1,192]{2,1,0:T(1,128)S(1)} async-done(((f32[128,1,192]{2,1,0:T(1,128)}), f32[128,1,192]{2,1,0:T(1,128)S(1)}, u32[]{:S(2)}, u32[]{:S(2)}) %all-to-all-start.3) | async-done | bytes 98336 | tf_op jit(solution)/shard_map/all_to_all | solution.py:30
  (100 shorter events, 55.4 us)
Async XLA Ops:
  0.6 109.9 %copy-start = (bf16[96,128,128]{2,1,0:T(8,128)(2,1)S(1)}, bf16[96,128,128]{2,1,0:T(8,128)(2,1)}, u32[]{:S(2)}) copy-start(bf16[96,128,128]{2,1,0:T(8,128)(2,1)} %param.14) | copy-start | bytes 9437188
  0.6 12.8 %collective-permute-start.2 = (bf16[64,2048]{1,0:T(8,128)(2,1)}, bf16[64,2048]{1,0:T(8,128)(2,1)S(1)}, u32[]{:S(2)}, u32[]{:S(2)}) collective-permute-start(bf16[64,2048]{1,0:T(8,128)(2,1)} %param.11), channel_id=1, source_target_pairs={{0,3},{1,2},{2,1},{3,0},{4,7},{5,6},{6,5},{7,4},{8,11},{9,10},{10,... | collective-permute-start | bytes 786440 | tf_op jit(solution)/shard_map/ppermute | solution.py:17
  6.1 9.0 %collective-permute-start.1 = (bf16[64,2048]{1,0:T(8,128)(2,1)}, bf16[64,2048]{1,0:T(8,128)(2,1)}, u32[]{:S(2)}, u32[]{:S(2)}) collective-permute-start(bf16[64,2048]{1,0:T(8,128)(2,1)} %param.11), channel_id=1, source_target_pairs={{0,2},{1,3},{2,0},{3,1},{4,6},{5,7},{6,4},{7,5},{8,10},{9,11},{10,... | collective-permute-start | bytes 786440 | tf_op jit(solution)/shard_map/ppermute | solution.py:17
  8.6 8.8 %collective-permute-start = (bf16[64,2048]{1,0:T(8,128)(2,1)}, bf16[64,2048]{1,0:T(8,128)(2,1)}, u32[]{:S(2)}, u32[]{:S(2)}) collective-permute-start(bf16[64,2048]{1,0:T(8,128)(2,1)} %param.11), channel_id=1, source_target_pairs={{0,1},{1,0},{2,3},{3,2},{4,5},{5,4},{6,7},{7,6},{8,9},{9,8},{10,11... | collective-permute-start | bytes 786440 | tf_op jit(solution)/shard_map/ppermute | solution.py:17
  19.6 5.3 %copy-start.5 = (bf16[256,64]{0,1:T(8,128)(2,1)S(1)}, bf16[256,64]{0,1:T(8,128)(2,1)}, u32[]{:S(2)}) copy-start(bf16[256,64]{0,1:T(8,128)(2,1)} %param.12) | copy-start | bytes 98308
  30.6 22.2 %copy-start.13 = (bf16[64]{0:T(256)(128)(2,1)S(1)}, bf16[64]{0:T(256)(128)(2,1)}, u32[]{:S(2)}) copy-start(bf16[64]{0:T(256)(128)(2,1)} %param.13) | copy-start | bytes 388
  30.6 22.2 %copy-start.10 = (s32[96]{0:T(128)S(1)}, s32[96]{0:T(128)}, u32[]{:S(2)}) copy-start(s32[96]{0:T(128)} %param.16) | copy-start | bytes 1156
  30.6 22.2 %copy-start.12 = (s32[96]{0:T(128)S(1)}, s32[96]{0:T(128)}, u32[]{:S(2)}) copy-start(s32[96]{0:T(128)} %param.15) | copy-start | bytes 1156
  30.6 73.1 %all-to-all-start = ((bf16[64,128,128]{2,0,1:T(8,128)(2,1)}), bf16[64,128,128]{2,0,1:T(8,128)(2,1)}, u32[]{:S(2)}, u32[]{:S(2)}) async-start(bf16[64,128,128]{2,0,1:T(8,128)(2,1)} %select_bitcast_fusion), calls=%async_computation | async-start | bytes 4194304 | tf_op jit(solution)/shard_map/all_to_all | solution.py:49
  132.3 60.4 %all-to-all-start.1 = ((bf16[64,128,128]{2,0,1:T(8,128)(2,1)}), bf16[64,128,128]{2,0,1:T(8,128)(2,1)}, u32[]{:S(2)}, u32[]{:S(2)}) async-start(bf16[64,128,128]{2,0,1:T(8,128)(2,1)} %fusion.4), calls=%async_computation.1 | async-start | bytes 4194304 | tf_op jit(solution)/shard_map/all_to_all | solution.py:85
  141.8 9.0 %collective-permute-start.5 = (bf16[256,64]{0,1:T(8,128)(2,1)S(1)}, bf16[256,64]{0,1:T(8,128)(2,1)S(1)}, u32[]{:S(2)}, u32[]{:S(2)}) collective-permute-start(bf16[256,64]{0,1:T(8,128)(2,1)S(1)} %copy-done.5), channel_id=1, source_target_pairs={{0,3},{1,2},{2,1},{3,0},{4,7},{5,6},{6,5},{7,4},{8,11},{9,10},{10,... | collective-permute-start | bytes 98312 | tf_op jit(solution)/shard_map/ppermute | solution.py:17
  146.2 6.6 %collective-permute-start.4 = (bf16[256,64]{0,1:T(8,128)(2,1)S(1)}, bf16[256,64]{0,1:T(8,128)(2,1)S(1)}, u32[]{:S(2)}, u32[]{:S(2)}) collective-permute-start(bf16[256,64]{0,1:T(8,128)(2,1)S(1)} %copy-done.5), channel_id=1, source_target_pairs={{0,2},{1,3},{2,0},{3,1},{4,6},{5,7},{6,4},{7,5},{8,10},{9,11},{10,... | collective-permute-start | bytes 98312 | tf_op jit(solution)/shard_map/ppermute | solution.py:17
  148.6 5.1 %collective-permute-start.3 = (bf16[256,64]{0,1:T(8,128)(2,1)S(1)}, bf16[256,64]{0,1:T(8,128)(2,1)S(1)}, u32[]{:S(2)}, u32[]{:S(2)}) collective-permute-start(bf16[256,64]{0,1:T(8,128)(2,1)S(1)} %copy-done.5), channel_id=1, source_target_pairs={{0,1},{1,0},{2,3},{3,2},{4,5},{5,4},{6,7},{7,6},{8,9},{9,8},{10,11... | collective-permute-start | bytes 98312 | tf_op jit(solution)/shard_map/ppermute | solution.py:17
  154.2 38.4 %copy-start.11 = (s32[128]{0:T(128)S(1)}, s32[128]{0:T(128)}, u32[]{:S(2)}) copy-start(s32[128]{0:T(128)} %param.18) | copy-start | bytes 1540
  192.7 12.8 %copy-start.2 = (bf16[4,64,2048]{2,1,0:T(8,128)(2,1)S(1)}, bf16[4,64,2048]{2,1,0:T(8,128)(2,1)}, u32[]{:S(2)}) copy-start(bf16[4,64,2048]{2,1,0:T(8,128)(2,1)} %copy-done.1) | copy-start | bytes 3145732
  196.5 47.6 %collective-permute-start.8 = (bf16[64,2048]{1,0:T(8,128)(2,1)}, bf16[64,2048]{1,0:T(8,128)(2,1)}, u32[]{:S(2)}, u32[]{:S(2)}) collective-permute-start(bf16[64,2048]{1,0:T(8,128)(2,1)} %bitcast.92), channel_id=1, source_target_pairs={{0,3},{1,2},{2,1},{3,0},{4,7},{5,6},{6,5},{7,4},{8,11},{9,10},{10,... | collective-permute-start | bytes 786440 | tf_op jit(solution)/shard_map/ppermute | solution.py:17
  200.9 43.2 %collective-permute-start.7 = (bf16[64,2048]{1,0:T(8,128)(2,1)}, bf16[64,2048]{1,0:T(8,128)(2,1)}, u32[]{:S(2)}, u32[]{:S(2)}) collective-permute-start(bf16[64,2048]{1,0:T(8,128)(2,1)} %bitcast.92), channel_id=1, source_target_pairs={{0,2},{1,3},{2,0},{3,1},{4,6},{5,7},{6,4},{7,5},{8,10},{9,11},{10,... | collective-permute-start | bytes 786440 | tf_op jit(solution)/shard_map/ppermute | solution.py:17
  203.3 40.8 %collective-permute-start.6 = (bf16[64,2048]{1,0:T(8,128)(2,1)}, bf16[64,2048]{1,0:T(8,128)(2,1)}, u32[]{:S(2)}, u32[]{:S(2)}) collective-permute-start(bf16[64,2048]{1,0:T(8,128)(2,1)} %bitcast.92), channel_id=1, source_target_pairs={{0,1},{1,0},{2,3},{3,2},{4,5},{5,4},{6,7},{7,6},{8,9},{9,8},{10,11... | collective-permute-start | bytes 786440 | tf_op jit(solution)/shard_map/ppermute | solution.py:17
  211.8 22.4 %all-to-all-start.2 = ((f32[128,1,192]{2,1,0:T(1,128)}), f32[128,1,192]{2,1,0:T(1,128)S(1)}, u32[]{:S(2)}, u32[]{:S(2)}) async-start(f32[128,1,192]{2,1,0:T(1,128)} %reshape.197), calls=%async_computation.2 | async-start | bytes 262144 | tf_op jit(solution)/shard_map/all_to_all | solution.py:27
  238.5 18.4 %all-to-all-start.3 = ((f32[128,1,192]{2,1,0:T(1,128)}), f32[128,1,192]{2,1,0:T(1,128)S(1)}, u32[]{:S(2)}, u32[]{:S(2)}) async-start(f32[128,1,192]{2,1,0:T(1,128)} %reshape.199), calls=%async_computation.3 | async-start | bytes 262144 | tf_op jit(solution)/shard_map/all_to_all | solution.py:30
  246.4 4.2 %copy-start.6 = (bf16[256,64]{0,1:T(8,128)(2,1)S(1)}, bf16[256,64]{0,1:T(8,128)(2,1)}, u32[]{:S(2)}) copy-start(bf16[256,64]{0,1:T(8,128)(2,1)} %get-tuple-element.20) | copy-start | bytes 98308
  246.4 4.3 %copy-start.7 = (bf16[256,64]{0,1:T(8,128)(2,1)S(1)}, bf16[256,64]{0,1:T(8,128)(2,1)}, u32[]{:S(2)}) copy-start(bf16[256,64]{0,1:T(8,128)(2,1)} %get-tuple-element.21) | copy-start | bytes 98308
  246.4 4.3 %copy-start.8 = (bf16[256,64]{0,1:T(8,128)(2,1)S(1)}, bf16[256,64]{0,1:T(8,128)(2,1)}, u32[]{:S(2)}) copy-start(bf16[256,64]{0,1:T(8,128)(2,1)} %get-tuple-element.22) | copy-start | bytes 98308
  246.4 4.3 %copy-start.9 = (bf16[256,64]{0,1:T(8,128)(2,1)S(1)}, bf16[256,64]{0,1:T(8,128)(2,1)}, u32[]{:S(2)}) copy-start(bf16[256,64]{0,1:T(8,128)(2,1)} %get-tuple-element.23) | copy-start | bytes 98308
  (3 other events, 5.0 us)

commit v7 on v6

--- a/solution.py
+++ b/solution.py
@@ -17,7 +17,15 @@
         received.append(lax.ppermute(values, axis, pairs))
     stacked = jnp.stack(received)
     mine = (lax.axis_index(axis) // stride) % count
-    return jnp.take(stacked, mine ^ jnp.arange(count), axis=0)
+    return jnp.take(stacked, mine ^ jnp.arange(count), axis=0, mode="clip")
+
+
+def exchange_order(values, axis, size, count, dim=0):
+    received = [values]
+    for offset in range(1, count):
+        pairs = [(i, i ^ offset) for i in range(size)]
+        received.append(lax.ppermute(values, axis, pairs))
+    return jnp.concatenate(received, axis=dim)
 
 
 def scatter_gather_sum(values, axis, size):
@@ -40,20 +48,36 @@
     blocks = node_rows // tile_size
     domains = lax.axis_size("dom")
     parts = lax.axis_size("feat")
-    whole = group_stack(node_feats, "feat", parts, 1, parts).reshape(parts * feat_rows, node_rows)
+    live_tiles = jnp.arange(tile_slots) < tile_count[0]
+    slot_hit = jnp.logical_and(
+        tile_col[:, None] == blocks + jnp.arange(domains)[None, :], live_tiles[:, None]
+    )
+    hit_tile = jnp.sum(jnp.where(slot_hit, jnp.arange(tile_slots)[:, None], 0), axis=0)
+    has_hit = jnp.any(slot_hit, axis=0)
+    slot_rows = jnp.sum(jnp.where(slot_hit, tile_row[:, None], 0), axis=0)
+    peer_tiles = jnp.where(
+        has_hit[:, None, None],
+        jnp.take(adj_tiles, hit_tile, axis=0, mode="clip"),
+        jnp.zeros((), adj_tiles.dtype),
+    )
+    order = lax.axis_index("feat") ^ jnp.arange(parts)
+    whole = exchange_order(node_feats, "feat", parts, parts)
+    in_rows = weight.shape[0] // parts
+    weight_ordered = jnp.take(
+        weight.reshape(parts, in_rows, weight.shape[1]), order, axis=0, mode="clip"
+    ).reshape(weight.shape)
     hidden = lax.dot_general(
-        weight, whole, (((0,), (0,)), ((), ())), preferred_element_type=jnp.float32
+        weight_ordered, whole, (((0,), (0,)), ((), ())), preferred_element_type=jnp.float32
     ).astype(jnp.bfloat16)
     hid_blocks = hidden.reshape(feat_rows, blocks, tile_size)
-    outgoing = jnp.take(hid_blocks, send_block, axis=1)
+    outgoing = jnp.take(hid_blocks, send_block, axis=1, mode="clip")
     incoming = lax.all_to_all(outgoing, "dom", split_axis=1, concat_axis=1, tiled=True)
     sources = jnp.concatenate([hid_blocks, incoming], axis=1)
-    live_tiles = jnp.arange(tile_slots) < tile_count[0]
     live_float = live_tiles.astype(jnp.float32)
     row_place = (tile_row[:, None] == jnp.arange(blocks)[None, :]).astype(jnp.float32) * live_float[
         :, None
     ]
-    picked = jnp.take(sources, tile_col, axis=1)
+    picked = jnp.take(sources, tile_col, axis=1, mode="clip")
     products = jnp.einsum("otb,tab->ota", picked, adj_tiles, preferred_element_type=jnp.float32)
     summed = jnp.einsum(
         "ota,tr->ora", products, row_place, precision=lax.Precision.HIGHEST
@@ -63,7 +87,7 @@
     grad_pre = pullback(cotangent.astype(jnp.float32))[0]
     grad_low = grad_pre.astype(jnp.bfloat16)
     grad_blocks = grad_low.reshape(feat_rows, blocks, tile_size)
-    rows_picked = jnp.take(grad_blocks, tile_row, axis=1)
+    rows_picked = jnp.take(grad_blocks, tile_row, axis=1, mode="clip")
     backward = jnp.einsum(
         "ota,tab->otb", rows_picked, adj_tiles, preferred_element_type=jnp.float32
     )
@@ -74,13 +98,9 @@
     own_sum = jnp.einsum(
         "otb,tr->orb", backward, src_place, precision=lax.Precision.HIGHEST
     )
-    slot_hit = jnp.logical_and(
-        tile_col[:, None] == blocks + jnp.arange(domains)[None, :], live_tiles[:, None]
-    )
-    hit_tile = jnp.sum(jnp.where(slot_hit, jnp.arange(tile_slots)[:, None], 0), axis=0)
-    has_hit = jnp.any(slot_hit, axis=0)
-    out_parts = jnp.where(
-        has_hit[None, :, None], jnp.take(backward, hit_tile, axis=1), 0.0
+    out_rows = jnp.take(grad_blocks, slot_rows, axis=1, mode="clip")
+    out_parts = jnp.einsum(
+        "oqa,qab->oqb", out_rows, peer_tiles, preferred_element_type=jnp.float32
     ).astype(jnp.bfloat16)
     in_parts = lax.all_to_all(out_parts, "dom", split_axis=1, concat_axis=1, tiled=True)
     remote_sum = in_parts.astype(jnp.float32)
@@ -92,13 +112,16 @@
     weight_part = lax.dot_general(
         whole, grad_hidden, (((1,), (1,)), ((), ())), preferred_element_type=jnp.float32
     )
+    weight_part = jnp.take(
+        weight_part.reshape(parts, in_rows, feat_rows), order, axis=0, mode="clip"
+    ).reshape(weight_part.shape)
     bias_part = jnp.sum(grad_pre, axis=1)
     packed = jnp.concatenate([weight_part, bias_part[None, :]], axis=0)
     packed = scatter_gather_sum(packed, "dom", domains)
     grad_weight = packed[:-1] * norm_scale
     grad_bias = packed[-1] * norm_scale
-    full_weight = jnp.concatenate(list(group_stack(weight, "feat", parts, 1, parts)), axis=1)
-    all_grad = group_stack(grad_hidden, "feat", parts, 1, parts).reshape(parts * feat_rows, node_rows)
+    full_weight = exchange_order(weight, "feat", parts, parts, dim=1)
+    all_grad = exchange_order(grad_hidden, "feat", parts, parts)
     my_rows = lax.dynamic_slice_in_dim(
         full_weight, lax.axis_index("feat") * feat_rows, feat_rows, 0
     )

time: 263 us -> 252 us (0.958)
  other arithmetic: 27.2 us -> 11.3 us
  matrix products: 21.8 us -> 27.9 us
  waiting for transfers between devices: 105 us -> 101 us
  starting transfers between devices: 74.7 us -> 78.2 us
    all_to_all x1, waiting for transfers between devices: 31.7 us -> 42.5 us  [per_device(): lax.all_to_all(out_parts, 'dom', split_axis=1, concat_axis=1, tiled=True)]
    all_to_all x1, waiting for transfers between devices: 10.4 us -> 2.36 us  [scatter_gather_sum(): gathered = lax.all_to_all(padded, axis, 0, 0, tiled=True)]
    select_n x10 -> x0, other arithmetic: 7.39 us -> none  [the longest x2 3.85 us: per_device(): outgoing = jnp.take(hid_blocks, send_block, axis=1)]
    dot_general x1 -> x2, matrix products: 0.3 us -> 6.98 us  [the longest x1 5.44 us: per_device(): jnp.einsum('oqa,qab->oqb', out_rows, peer_tiles, preferred_element_type=j...]
    all_to_all x1, starting transfers between devices: 5.55 us -> 12.2 us  [scatter_gather_sum(): total = lax.all_to_all(spread, axis, 0, 0, tiled=True)]
    all_to_all x1, waiting for transfers between devices: 5.14 us -> 0.01 us  [scatter_gather_sum(): total = lax.all_to_all(spread, axis, 0, 0, tiled=True)]
    another operation x3 -> x0, other arithmetic: 4.53 us -> none  [group_stack(): stacked = jnp.stack(received)]
    all_to_all x1, starting transfers between devices: 22.2 us -> 18.1 us  [per_device(): lax.all_to_all(outgoing, 'dom', split_axis=1, concat_axis=1, tiled=True)]
  transfers between devices with their start and end apart: 13 -> 13, of which waited for: 8 -> 6; matrix products, arithmetic and copies ran while one was open for 11% -> 10% of each run, Pallas kernels for 0% -> 0%
where the time goes in v7:
time: 252 us; the launch traced here: 250 us
  waiting for transfers between devices  101 us (40%)
  starting transfers between devices  78.2 us (31%)
  local copies, waits for them, and re-layouts  30.7 us (12%)
  matrix products  27.9 us (11%)
  other arithmetic  11.3 us (4%)
    all_to_all x1, waiting for transfers between devices, per_device(): lax.all_to_all(outgoing, 'dom', split_axis=1, concat_axis=1, tiled=True)  46.9 us
    all_to_all x1, waiting for transfers between devices, per_device(): lax.all_to_all(out_parts, 'dom', split_axis=1, concat_axis=1, tiled=True)  42.5 us
    ppermute x9, starting transfers between devices, exchange_order(): received.append(lax.ppermute(values, axis, pairs))  29.7 us
    all_to_all x1, starting transfers between devices, per_device(): lax.all_to_all(outgoing, 'dom', split_axis=1, concat_axis=1, tiled=True)  18.1 us
    all_to_all x1, starting transfers between devices, scatter_gather_sum(): total = lax.all_to_all(spread, axis, 0, 0, tiled=True)  12.2 us
    unnamed x24, local copies, waits for them, and re-layouts  11.1 us
    all_to_all x1, starting transfers between devices, per_device(): lax.all_to_all(out_parts, 'dom', split_axis=1, concat_axis=1, tiled=True)  9.31 us
    ppermute x9, waiting for transfers between devices, exchange_order(): received.append(lax.ppermute(values, axis, pairs))  8.85 us
  transfers between devices with their start and end apart: 13, of which 6 were waited for; matrix products, arithmetic and copies ran while one was open for 10% of the time, Pallas kernels for 0%

profile of v7, /device:TPU:1, one launch (start us, length us, event | category | flops | bytes accessed | tf_op | source)
XLA Modules:
  0.0 250.3 jit_solution(9386839918898697969)
XLA Ops:
  0.6 4.2 %collective-permute-start = (bf16[64,2048]{1,0:T(8,128)(2,1)}, bf16[64,2048]{1,0:T(8,128)(2,1)}, u32[]{:S(2)}, u32[]{:S(2)}) collective-permute-start(bf16[64,2048]{1,0:T(8,128)(2,1)} %param.9), channel_id=1, source_target_pairs={{0,1},{1,0},{2,3},{3,2},{4,5},{5,4},{6,7},{7,6},{8,9},{9,8},{10,11... | collective-permute-start | bytes 786440 | tf_op jit(solution)/shard_map/ppermute | solution.py:27
  4.9 4.4 %collective-permute-start.1 = (bf16[64,2048]{1,0:T(8,128)(2,1)}, bf16[64,2048]{1,0:T(8,128)(2,1)}, u32[]{:S(2)}, u32[]{:S(2)}) collective-permute-start(bf16[64,2048]{1,0:T(8,128)(2,1)} %param.9), channel_id=1, source_target_pairs={{0,2},{1,3},{2,0},{3,1},{4,6},{5,7},{6,4},{7,5},{8,10},{9,11},{10,... | collective-permute-start | bytes 786440 | tf_op jit(solution)/shard_map/ppermute | solution.py:27
  19.6 5.6 %collective-permute-done.2 = bf16[64,2048]{1,0:T(8,128)(2,1)S(1)} collective-permute-done((bf16[64,2048]{1,0:T(8,128)(2,1)}, bf16[64,2048]{1,0:T(8,128)(2,1)S(1)}, u32[]{:S(2)}, u32[]{:S(2)}) %collective-permute-start.2) | collective-permute-done | bytes 262176 | tf_op jit(solution)/shard_map/ppermute | solution.py:27
  29.7 18.1 %all-to-all-start = ((bf16[64,128,128]{2,0,1:T(8,128)(2,1)}), bf16[64,128,128]{2,0,1:T(8,128)(2,1)}, u32[]{:S(2)}, u32[]{:S(2)}) async-start(bf16[64,128,128]{2,0,1:T(8,128)(2,1)} %bitcast.79), calls=%async_computation | async-start | bytes 4194304 | tf_op jit(solution)/shard_map/all_to_all | solution.py:74
  48.7 3.0 %gather_fusion.4 = bf16[128,128,128]{2,1,0:T(8,128)(2,1)} fusion(bf16[96,128,128]{2,1,0:T(8,128)(2,1)S(1)} %copy-done, s32[1024]{0:T(1024)S(1)} %get-tuple-element.21), kind=kCustom, calls=%fused_computation.4 | custom fusion | bytes 8389120 | tf_op jit(solution)/shard_map/jit(_take)/gather | solution.py:60
  51.8 46.9 %all-to-all-done = bf16[64,128,128]{2,0,1:T(8,128)(2,1)} async-done(((bf16[64,128,128]{2,0,1:T(8,128)(2,1)}), bf16[64,128,128]{2,0,1:T(8,128)(2,1)}, u32[]{:S(2)}, u32[]{:S(2)}) %all-to-all-start) | async-done | bytes 2097184 | tf_op jit(solution)/shard_map/all_to_all | solution.py:74
  98.8 3.2 %pad_maximum_fusion = bf16[64,144,128]{2,0,1:T(8,128)(2,1)} fusion(bf16[64,128,128]{2,0,1:T(8,128)(2,1)} %all-to-all-done, bf16[64,16,128]{2,0,1:T(8,128)(2,1)S(1)} %bitcast.78), kind=kLoop, calls=%fused_computation.14 | loop fusion | flops 1179648 | bytes 4718592 | tf_op jit(solution)/shard_map/concatenate | solution.py:75
  102.0 3.6 %gather_fusion.2 = bf16[96,64,128]{2,1,0:T(8,128)(2,1)} fusion(bf16[64,144,128]{2,0,1:T(8,128)(2,1)} %pad_maximum_fusion, s32[1024]{0:T(1024)S(1)} %pad_clamp_fusion.3), kind=kCustom, calls=%fused_computation.2 | custom fusion | bytes 3146112 | tf_op jit(solution)/shard_map/jit(_take)/gather | solution.py:80
  105.6 3.7 %convolution_bitcast_fusion.1 = f32[64,96,128]{2,0,1:T(8,128)S(1)} fusion(bf16[96,128,128]{2,1,0:T(8,128)(2,1)S(1)} %copy-done, bf16[96,64,128]{2,1,0:T(8,128)(2,1)} %gather_fusion.2), kind=kOutput, calls=%fused_computation.23 | convolution fusion | flops 201326592 | bytes 7864320 | tf_op jit(solution)/shard_map/otb,tab->ota/dot_general | solution.py:81
  109.2 3.3 %fusion.5 = f32[16,64,128]{2,0,1:T(8,128)S(1)} fusion(f32[64,96,128]{2,0,1:T(8,128)S(1)} %convolution_bitcast_fusion.1, f32[96]{0:T(128)S(1)} %fusion.64, s32[96]{0:T(128)S(1)} %copy-done.4), kind=kOutput, calls=%fused_computation.12 | convolution fusion | flops 150998016 | bytes 3670784 | tf_op jit(solution)/shard_map/ota,tr->ora/dot_general | solution.py:82
  116.1 5.4 %convert_bitcast_fusion = bf16[64,128,128]{2,0,1:T(8,128)(2,1)} fusion(bf16[128,128,128]{2,1,0:T(8,128)(2,1)} %gather_fusion.4, pred[128]{0:T(512)(128)(4,1)S(1)} %fusion.44, bf16[128,64,128]{2,1,0:T(8,128)(2,1)} %gather_fusion.5), kind=kOutput, calls=%fused_computation.20 | convolution fusion | flops 271581184 | bytes 8388736 | tf_op jit(solution)/shard_map/oqa,qab->oqb/dot_general | solution.py:102
  121.6 9.3 %all-to-all-start.1 = ((bf16[64,128,128]{2,0,1:T(8,128)(2,1)}), bf16[64,128,128]{2,0,1:T(8,128)(2,1)}, u32[]{:S(2)}, u32[]{:S(2)}) async-start(bf16[64,128,128]{2,0,1:T(8,128)(2,1)} %convert_bitcast_fusion), calls=%async_computation.1 | async-start | bytes 4194304 | tf_op jit(solution)/shard_map/all_to_all | solution.py:105
  132.9 2.4 convolution_bitcast_fusion
  135.2 4.1 %fusion.3 = f32[16,64,128]{2,0,1:T(8,128)} fusion(f32[64,96,128]{2,0,1:T(8,128)S(1)} %convolution_bitcast_fusion, s32[96]{0:T(128)S(1)} %copy-done.3, f32[96]{0:T(128)S(1)} %fusion.64), kind=kOutput, calls=%fused_computation.10 | convolution fusion | flops 150998016 | bytes 3670784 | tf_op jit(solution)/shard_map/otb,tr->orb/dot_general | solution.py:98
  139.3 42.5 %all-to-all-done.1 = bf16[64,128,128]{2,0,1:T(8,128)(2,1)} async-done(((bf16[64,128,128]{2,0,1:T(8,128)(2,1)}), bf16[64,128,128]{2,0,1:T(8,128)(2,1)}, u32[]{:S(2)}, u32[]{:S(2)}) %all-to-all-start.1) | async-done | bytes 2097184 | tf_op jit(solution)/shard_map/all_to_all | solution.py:105
  181.8 2.9 %fusion.20 = bf16[16,64,128]{2,0,1:T(8,128)(2,1)S(1)} fusion(f32[16,64,128]{2,0,1:T(8,128)} %fusion.3, bf16[64,128,128]{2,0,1:T(8,128)(2,1)} %all-to-all-done.1, s32[128]{0:T(128)S(1)} %copy-done.5), kind=kOutput, calls=%fused_computation.27 | convolution fusion | flops 33818624 | bytes 2884096 | tf_op jit(solution)/shard_map/oqb,qr->orb/dot_general | solution.py:107
  185.6 2.3 fusion.67
  193.6 8.8 %all-to-all-start.2 = ((f32[128,1,192]{2,1,0:T(1,128)}), f32[128,1,192]{2,1,0:T(1,128)S(1)}, u32[]{:S(2)}, u32[]{:S(2)}) async-start(f32[128,1,192]{2,1,0:T(1,128)} %reshape.138), calls=%async_computation.2 | async-start | bytes 262144 | tf_op jit(solution)/shard_map/all_to_all | solution.py:35
  205.1 3.3 %collective-permute-start.7 = (bf16[64,2048]{1,0:T(8,128)(2,1)}, bf16[64,2048]{1,0:T(8,128)(2,1)}, u32[]{:S(2)}, u32[]{:S(2)}) collective-permute-start(bf16[64,2048]{1,0:T(8,128)(2,1)} %bitcast.73), channel_id=1, source_target_pairs={{0,2},{1,3},{2,0},{3,1},{4,6},{5,7},{6,4},{7,5},{8,10},{9,11},{10,... | collective-permute-start | bytes 786440 | tf_op jit(solution)/shard_map/ppermute | solution.py:27
  208.4 4.4 %collective-permute-start.8 = (bf16[64,2048]{1,0:T(8,128)(2,1)}, bf16[64,2048]{1,0:T(8,128)(2,1)}, u32[]{:S(2)}, u32[]{:S(2)}) collective-permute-start(bf16[64,2048]{1,0:T(8,128)(2,1)} %bitcast.73), channel_id=1, source_target_pairs={{0,3},{1,2},{2,1},{3,0},{4,7},{5,6},{6,5},{7,4},{8,11},{9,10},{10,... | collective-permute-start | bytes 786440 | tf_op jit(solution)/shard_map/ppermute | solution.py:27
  212.8 2.4 all-to-all-done.2
  219.4 12.2 %all-to-all-start.3 = ((f32[128,1,192]{2,1,0:T(1,128)}), f32[128,1,192]{2,1,0:T(1,128)S(1)}, u32[]{:S(2)}, u32[]{:S(2)}) async-start(f32[128,1,192]{2,1,0:T(1,128)} %reshape.140), calls=%async_computation.3 | async-start | bytes 262144 | tf_op jit(solution)/shard_map/all_to_all | solution.py:38
  233.6 3.3 %collective-permute-start.4 = (bf16[256,64]{0,1:T(8,128)(2,1)}, bf16[256,64]{0,1:T(8,128)(2,1)S(1)}, u32[]{:S(2)}, u32[]{:S(2)}) collective-permute-start(bf16[256,64]{0,1:T(8,128)(2,1)} %param.10), channel_id=1, source_target_pairs={{0,2},{1,3},{2,0},{3,1},{4,6},{5,7},{6,4},{7,5},{8,10},{9,11},{10,... | collective-permute-start | bytes 98312 | tf_op jit(solution)/shard_map/ppermute | solution.py:27
  236.9 4.4 %collective-permute-start.5 = (bf16[256,64]{0,1:T(8,128)(2,1)}, bf16[256,64]{0,1:T(8,128)(2,1)S(1)}, u32[]{:S(2)}, u32[]{:S(2)}) collective-permute-start(bf16[256,64]{0,1:T(8,128)(2,1)} %param.10), channel_id=1, source_target_pairs={{0,3},{1,2},{2,1},{3,0},{4,7},{5,6},{6,5},{7,4},{8,11},{9,10},{10,... | collective-permute-start | bytes 98312 | tf_op jit(solution)/shard_map/ppermute | solution.py:27
  (69 shorter events, 44.9 us)
Async XLA Ops:
  0.6 48.1 %copy-start = (bf16[96,128,128]{2,1,0:T(8,128)(2,1)S(1)}, bf16[96,128,128]{2,1,0:T(8,128)(2,1)}, u32[]{:S(2)}) copy-start(bf16[96,128,128]{2,1,0:T(8,128)(2,1)} %param.12) | copy-start | bytes 9437188
  0.6 14.3 %collective-permute-start = (bf16[64,2048]{1,0:T(8,128)(2,1)}, bf16[64,2048]{1,0:T(8,128)(2,1)}, u32[]{:S(2)}, u32[]{:S(2)}) collective-permute-start(bf16[64,2048]{1,0:T(8,128)(2,1)} %param.9), channel_id=1, source_target_pairs={{0,1},{1,0},{2,3},{3,2},{4,5},{5,4},{6,7},{7,6},{8,9},{9,8},{10,11... | collective-permute-start | bytes 786440 | tf_op jit(solution)/shard_map/ppermute | solution.py:27
  4.9 13.1 %collective-permute-start.1 = (bf16[64,2048]{1,0:T(8,128)(2,1)}, bf16[64,2048]{1,0:T(8,128)(2,1)}, u32[]{:S(2)}, u32[]{:S(2)}) collective-permute-start(bf16[64,2048]{1,0:T(8,128)(2,1)} %param.9), channel_id=1, source_target_pairs={{0,2},{1,3},{2,0},{3,1},{4,6},{5,7},{6,4},{7,5},{8,10},{9,11},{10,... | collective-permute-start | bytes 786440 | tf_op jit(solution)/shard_map/ppermute | solution.py:27
  9.2 16.0 %collective-permute-start.2 = (bf16[64,2048]{1,0:T(8,128)(2,1)}, bf16[64,2048]{1,0:T(8,128)(2,1)S(1)}, u32[]{:S(2)}, u32[]{:S(2)}) collective-permute-start(bf16[64,2048]{1,0:T(8,128)(2,1)} %param.9), channel_id=1, source_target_pairs={{0,3},{1,2},{2,1},{3,0},{4,7},{5,6},{6,5},{7,4},{8,11},{9,10},{10,... | collective-permute-start | bytes 786440 | tf_op jit(solution)/shard_map/ppermute | solution.py:27
  29.7 18.8 %copy-start.6 = (bf16[64]{0:T(256)(128)(2,1)S(1)}, bf16[64]{0:T(256)(128)(2,1)}, u32[]{:S(2)}) copy-start(bf16[64]{0:T(256)(128)(2,1)} %param.11) | copy-start | bytes 388
  29.7 18.8 %copy-start.3 = (s32[96]{0:T(128)S(1)}, s32[96]{0:T(128)}, u32[]{:S(2)}) copy-start(s32[96]{0:T(128)} %param.14) | copy-start | bytes 1156
  29.7 18.8 %copy-start.4 = (s32[96]{0:T(128)S(1)}, s32[96]{0:T(128)}, u32[]{:S(2)}) copy-start(s32[96]{0:T(128)} %param.13) | copy-start | bytes 1156
  29.7 69.1 %all-to-all-start = ((bf16[64,128,128]{2,0,1:T(8,128)(2,1)}), bf16[64,128,128]{2,0,1:T(8,128)(2,1)}, u32[]{:S(2)}, u32[]{:S(2)}) async-start(bf16[64,128,128]{2,0,1:T(8,128)(2,1)} %bitcast.79), calls=%async_computation | async-start | bytes 4194304 | tf_op jit(solution)/shard_map/all_to_all | solution.py:74
  109.2 3.3 %copy-start.2 = (bf16[64,2048]{1,0:T(8,128)(2,1)S(1)}, bf16[64,2048]{1,0:T(8,128)(2,1)}, u32[]{:S(2)}) copy-start(bf16[64,2048]{1,0:T(8,128)(2,1)} %param.17) | copy-start | bytes 786436
  121.6 60.2 %all-to-all-start.1 = ((bf16[64,128,128]{2,0,1:T(8,128)(2,1)}), bf16[64,128,128]{2,0,1:T(8,128)(2,1)}, u32[]{:S(2)}, u32[]{:S(2)}) async-start(bf16[64,128,128]{2,0,1:T(8,128)(2,1)} %convert_bitcast_fusion), calls=%async_computation.1 | async-start | bytes 4194304 | tf_op jit(solution)/shard_map/all_to_all | solution.py:105
  135.2 46.6 %copy-start.5 = (s32[128]{0:T(128)S(1)}, s32[128]{0:T(128)}, u32[]{:S(2)}) copy-start(s32[128]{0:T(128)} %param.16) | copy-start | bytes 1540
  193.6 21.6 %all-to-all-start.2 = ((f32[128,1,192]{2,1,0:T(1,128)}), f32[128,1,192]{2,1,0:T(1,128)S(1)}, u32[]{:S(2)}, u32[]{:S(2)}) async-start(f32[128,1,192]{2,1,0:T(1,128)} %reshape.138), calls=%async_computation.2 | async-start | bytes 262144 | tf_op jit(solution)/shard_map/all_to_all | solution.py:35
  203.2 40.1 %collective-permute-start.6 = (bf16[64,2048]{1,0:T(8,128)(2,1)}, bf16[64,2048]{1,0:T(8,128)(2,1)}, u32[]{:S(2)}, u32[]{:S(2)}) collective-permute-start(bf16[64,2048]{1,0:T(8,128)(2,1)} %bitcast.73), channel_id=1, source_target_pairs={{0,1},{1,0},{2,3},{3,2},{4,5},{5,4},{6,7},{7,6},{8,9},{9,8},{10,11... | collective-permute-start | bytes 786440 | tf_op jit(solution)/shard_map/ppermute | solution.py:27
  205.1 38.1 %collective-permute-start.7 = (bf16[64,2048]{1,0:T(8,128)(2,1)}, bf16[64,2048]{1,0:T(8,128)(2,1)}, u32[]{:S(2)}, u32[]{:S(2)}) collective-permute-start(bf16[64,2048]{1,0:T(8,128)(2,1)} %bitcast.73), channel_id=1, source_target_pairs={{0,2},{1,3},{2,0},{3,1},{4,6},{5,7},{6,4},{7,5},{8,10},{9,11},{10,... | collective-permute-start | bytes 786440 | tf_op jit(solution)/shard_map/ppermute | solution.py:27
  208.4 34.9 %collective-permute-start.8 = (bf16[64,2048]{1,0:T(8,128)(2,1)}, bf16[64,2048]{1,0:T(8,128)(2,1)}, u32[]{:S(2)}, u32[]{:S(2)}) collective-permute-start(bf16[64,2048]{1,0:T(8,128)(2,1)} %bitcast.73), channel_id=1, source_target_pairs={{0,3},{1,2},{2,1},{3,0},{4,7},{5,6},{6,5},{7,4},{8,11},{9,10},{10,... | collective-permute-start | bytes 786440 | tf_op jit(solution)/shard_map/ppermute | solution.py:27
  215.2 0.7 copy-start.1
  219.4 26.2 %all-to-all-start.3 = ((f32[128,1,192]{2,1,0:T(1,128)}), f32[128,1,192]{2,1,0:T(1,128)S(1)}, u32[]{:S(2)}, u32[]{:S(2)}) async-start(f32[128,1,192]{2,1,0:T(1,128)} %reshape.140), calls=%async_computation.3 | async-start | bytes 262144 | tf_op jit(solution)/shard_map/all_to_all | solution.py:38
  231.7 5.2 %collective-permute-start.3 = (bf16[256,64]{0,1:T(8,128)(2,1)}, bf16[256,64]{0,1:T(8,128)(2,1)S(1)}, u32[]{:S(2)}, u32[]{:S(2)}) collective-permute-start(bf16[256,64]{0,1:T(8,128)(2,1)} %param.10), channel_id=1, source_target_pairs={{0,1},{1,0},{2,3},{3,2},{4,5},{5,4},{6,7},{7,6},{8,9},{9,8},{10,11... | collective-permute-start | bytes 98312 | tf_op jit(solution)/shard_map/ppermute | solution.py:27
  233.6 7.7 %collective-permute-start.4 = (bf16[256,64]{0,1:T(8,128)(2,1)}, bf16[256,64]{0,1:T(8,128)(2,1)S(1)}, u32[]{:S(2)}, u32[]{:S(2)}) collective-permute-start(bf16[256,64]{0,1:T(8,128)(2,1)} %param.10), channel_id=1, source_target_pairs={{0,2},{1,3},{2,0},{3,1},{4,6},{5,7},{6,4},{7,5},{8,10},{9,11},{10,... | collective-permute-start | bytes 98312 | tf_op jit(solution)/shard_map/ppermute | solution.py:27
  236.9 6.4 %collective-permute-start.5 = (bf16[256,64]{0,1:T(8,128)(2,1)}, bf16[256,64]{0,1:T(8,128)(2,1)S(1)}, u32[]{:S(2)}, u32[]{:S(2)}) collective-permute-start(bf16[256,64]{0,1:T(8,128)(2,1)} %param.10), channel_id=1, source_target_pairs={{0,3},{1,2},{2,1},{3,0},{4,7},{5,6},{6,5},{7,4},{8,11},{9,10},{10,... | collective-permute-start | bytes 98312 | tf_op jit(solution)/shard_map/ppermute | solution.py:27

commit v8 on v7

--- a/solution.py
+++ b/solution.py
@@ -25,7 +25,7 @@
     for offset in range(1, count):
         pairs = [(i, i ^ offset) for i in range(size)]
         received.append(lax.ppermute(values, axis, pairs))
-    return jnp.concatenate(received, axis=dim)
+    return received
 
 
 def scatter_gather_sum(values, axis, size):
@@ -61,27 +61,37 @@
         jnp.zeros((), adj_tiles.dtype),
     )
     order = lax.axis_index("feat") ^ jnp.arange(parts)
-    whole = exchange_order(node_feats, "feat", parts, parts)
+    pieces = exchange_order(node_feats, "feat", parts, parts)
     in_rows = weight.shape[0] // parts
     weight_ordered = jnp.take(
         weight.reshape(parts, in_rows, weight.shape[1]), order, axis=0, mode="clip"
-    ).reshape(weight.shape)
-    hidden = lax.dot_general(
-        weight_ordered, whole, (((0,), (0,)), ((), ())), preferred_element_type=jnp.float32
+    )
+    hidden = sum(
+        lax.dot_general(
+            weight_ordered[s], piece, (((0,), (0,)), ((), ())), preferred_element_type=jnp.float32
+        )
+        for s, piece in enumerate(pieces)
     ).astype(jnp.bfloat16)
     hid_blocks = hidden.reshape(feat_rows, blocks, tile_size)
     outgoing = jnp.take(hid_blocks, send_block, axis=1, mode="clip")
     incoming = lax.all_to_all(outgoing, "dom", split_axis=1, concat_axis=1, tiled=True)
-    sources = jnp.concatenate([hid_blocks, incoming], axis=1)
     live_float = live_tiles.astype(jnp.float32)
-    row_place = (tile_row[:, None] == jnp.arange(blocks)[None, :]).astype(jnp.float32) * live_float[
+    local_ok = jnp.logical_and(live_tiles, tile_col < blocks).astype(jnp.float32)
+    row_place = (tile_row[:, None] == jnp.arange(blocks)[None, :]).astype(jnp.float32) * local_ok[
         :, None
     ]
-    picked = jnp.take(sources, tile_col, axis=1, mode="clip")
+    picked = jnp.take(hid_blocks, jnp.minimum(tile_col, blocks - 1), axis=1, mode="clip")
     products = jnp.einsum("otb,tab->ota", picked, adj_tiles, preferred_element_type=jnp.float32)
-    summed = jnp.einsum(
-        "ota,tr->ora", products, row_place, precision=lax.Precision.HIGHEST
-    ).reshape(feat_rows, node_rows)
+    summed_local = jnp.einsum("ota,tr->ora", products, row_place, precision=lax.Precision.HIGHEST)
+    summed_local, incoming = lax.optimization_barrier((summed_local, incoming))
+    far_place = (slot_rows[:, None] == jnp.arange(blocks)[None, :]).astype(jnp.float32) * has_hit[
+        :, None
+    ].astype(jnp.float32)
+    far_products = jnp.einsum(
+        "oqb,qab->oqa", incoming, peer_tiles, preferred_element_type=jnp.float32
+    )
+    summed_far = jnp.einsum("oqa,qr->ora", far_products, far_place, precision=lax.Precision.HIGHEST)
+    summed = (summed_local + summed_far).reshape(feat_rows, node_rows)
     preact = summed + bias_vec.astype(jnp.float32)[:, None]
     activated, pullback = jax.vjp(smooth_gate, preact)
     grad_pre = pullback(cotangent.astype(jnp.float32))[0]
@@ -109,19 +119,24 @@
     )
     grad_hidden = grad_sum.reshape(feat_rows, node_rows).astype(jnp.bfloat16)
     norm_scale = 1.0 / math.sqrt(domains * node_rows)
-    weight_part = lax.dot_general(
-        whole, grad_hidden, (((1,), (1,)), ((), ())), preferred_element_type=jnp.float32
+    weight_part = jnp.stack(
+        [
+            lax.dot_general(
+                piece, grad_hidden, (((1,), (1,)), ((), ())), preferred_element_type=jnp.float32
+            )
+            for piece in pieces
+        ]
     )
-    weight_part = jnp.take(
-        weight_part.reshape(parts, in_rows, feat_rows), order, axis=0, mode="clip"
-    ).reshape(weight_part.shape)
+    weight_part = jnp.take(weight_part, order, axis=0, mode="clip").reshape(
+        parts * in_rows, feat_rows
+    )
     bias_part = jnp.sum(grad_pre, axis=1)
     packed = jnp.concatenate([weight_part, bias_part[None, :]], axis=0)
     packed = scatter_gather_sum(packed, "dom", domains)
     grad_weight = packed[:-1] * norm_scale
     grad_bias = packed[-1] * norm_scale
-    full_weight = exchange_order(weight, "feat", parts, parts, dim=1)
-    all_grad = exchange_order(grad_hidden, "feat", parts, parts)
+    full_weight = jnp.concatenate(exchange_order(weight, "feat", parts, parts), axis=1)
+    all_grad = jnp.concatenate(exchange_order(grad_hidden, "feat", parts, parts), axis=0)
     my_rows = lax.dynamic_slice_in_dim(
         full_weight, lax.axis_index("feat") * feat_rows, feat_rows, 0
     )

time: 252 us -> 251 us (level)
  waiting for transfers between devices: 101 us -> 86 us
  matrix products: 27.9 us -> 41.8 us
  starting transfers between devices: 78.2 us -> 84.1 us
  local copies, waits for them, and re-layouts: 30.7 us -> 26.5 us
    dot_general x2 -> x10, matrix products: 3.88 us -> 16.8 us  [the longest x1 5.87 us: per_device(): jnp.einsum('oqb,qab->oqa', incoming, peer_tiles, preferred_element_type=j...]
    all_to_all x1, waiting for transfers between devices: 46.9 us -> 36.9 us  [per_device(): lax.all_to_all(outgoing, 'dom', split_axis=1, concat_axis=1, tiled=True)]
    all_to_all x1, starting transfers between devices: 18.1 us -> 24 us  [per_device(): lax.all_to_all(outgoing, 'dom', split_axis=1, concat_axis=1, tiled=True)]
    unnamed x24 -> x30, local copies, waits for them, and re-layouts: 11.1 us -> 7.05 us
    ppermute x9, waiting for transfers between devices: 8.85 us -> 4.98 us  [exchange_order(): received.append(lax.ppermute(values, axis, pairs))]
    concatenate x1 -> x0, other arithmetic: 3.21 us -> none  [per_device(): sources = jnp.concatenate([hid_blocks, incoming], axis=1)]
    gather x2 -> x3, local copies, waits for them, and re-layouts: 5.06 us -> 4.2 us  [the longest x2 2.2 us: per_device(): jnp.take(weight_part, order, axis=0, mode='clip')]
  transfers between devices with their start and end apart: 13 -> 13, of which waited for: 6 -> 5; matrix products, arithmetic and copies ran while one was open for 10% -> 14% of each run, Pallas kernels for 0% -> 0%
where the time goes in v8:
time: 251 us; the launch traced here: 249 us
  waiting for transfers between devices  86 us (34%)
  starting transfers between devices  84.1 us (34%)
  matrix products  41.8 us (17%)
  local copies, waits for them, and re-layouts  26.5 us (11%)
  other arithmetic  9.11 us (4%)
    all_to_all x1, waiting for transfers between devices, per_device(): lax.all_to_all(out_parts, 'dom', split_axis=1, concat_axis=1, tiled=True)  41.8 us
    all_to_all x1, waiting for transfers between devices, per_device(): lax.all_to_all(outgoing, 'dom', split_axis=1, concat_axis=1, tiled=True)  36.9 us
    ppermute x9, starting transfers between devices, exchange_order(): received.append(lax.ppermute(values, axis, pairs))  29.7 us
    all_to_all x1, starting transfers between devices, per_device(): lax.all_to_all(outgoing, 'dom', split_axis=1, concat_axis=1, tiled=True)  24 us
    all_to_all x1, starting transfers between devices, scatter_gather_sum(): total = lax.all_to_all(spread, axis, 0, 0, tiled=True)  12.2 us
    all_to_all x1, starting transfers between devices, per_device(): lax.all_to_all(out_parts, 'dom', split_axis=1, concat_axis=1, tiled=True)  9.3 us
    all_to_all x1, starting transfers between devices, scatter_gather_sum(): gathered = lax.all_to_all(padded, axis, 0, 0, tiled=True)  8.85 us
    unnamed x30, local copies, waits for them, and re-layouts  7.05 us
  transfers between devices with their start and end apart: 13, of which 5 were waited for; matrix products, arithmetic and copies ran while one was open for 14% of the time, Pallas kernels for 0%

profile of v8, /device:TPU:1, one launch (start us, length us, event | category | flops | bytes accessed | tf_op | source)
XLA Modules:
  0.0 249.2 jit_solution(11438060486219671618)
XLA Ops:
  0.6 4.2 %collective-permute-start = (bf16[64,2048]{1,0:T(8,128)(2,1)}, bf16[64,2048]{1,0:T(8,128)(2,1)}, u32[]{:S(2)}, u32[]{:S(2)}) collective-permute-start(bf16[64,2048]{1,0:T(8,128)(2,1)} %param.9), channel_id=1, source_target_pairs={{0,1},{1,0},{2,3},{3,2},{4,5},{5,4},{6,7},{7,6},{8,9},{9,8},{10,11... | collective-permute-start | bytes 786440 | tf_op jit(solution)/shard_map/ppermute | solution.py:27
  4.9 3.7 %collective-permute-start.2 = (bf16[64,2048]{1,0:T(8,128)(2,1)}, bf16[64,2048]{1,0:T(8,128)(2,1)S(1)}, u32[]{:S(2)}, u32[]{:S(2)}) collective-permute-start(bf16[64,2048]{1,0:T(8,128)(2,1)} %param.9), channel_id=1, source_target_pairs={{0,3},{1,2},{2,1},{3,0},{4,7},{5,6},{6,5},{7,4},{8,11},{9,10},{10,... | collective-permute-start | bytes 786440 | tf_op jit(solution)/shard_map/ppermute | solution.py:27
  8.6 2.6 %collective-permute-start.1 = (bf16[64,2048]{1,0:T(8,128)(2,1)}, bf16[64,2048]{1,0:T(8,128)(2,1)}, u32[]{:S(2)}, u32[]{:S(2)}) collective-permute-start(bf16[64,2048]{1,0:T(8,128)(2,1)} %param.9), channel_id=1, source_target_pairs={{0,2},{1,3},{2,0},{3,1},{4,6},{5,7},{6,4},{7,5},{8,10},{9,11},{10,... | collective-permute-start | bytes 786440 | tf_op jit(solution)/shard_map/ppermute | solution.py:27
  21.1 24.0 %all-to-all-start = ((bf16[64,128,128]{2,0,1:T(8,128)(2,1)}), bf16[64,128,128]{2,0,1:T(8,128)(2,1)}, u32[]{:S(2)}, u32[]{:S(2)}) async-start(bf16[64,128,128]{2,0,1:T(8,128)(2,1)} %bitcast.130), calls=%async_computation | async-start | bytes 4194304 | tf_op jit(solution)/shard_map/all_to_all | solution.py:77
  46.1 3.0 %gather_fusion.3 = bf16[128,128,128]{2,1,0:T(8,128)(2,1)} fusion(bf16[96,128,128]{2,1,0:T(8,128)(2,1)S(1)} %copy-done, s32[1024]{0:T(1024)S(1)} %pad_clamp_fusion.2), kind=kCustom, calls=%fused_computation.3 | custom fusion | bytes 8389120 | tf_op jit(solution)/shard_map/jit(_take)/gather | solution.py:60
  51.2 3.6 %convolution_bitcast_fusion.2 = f32[64,96,128]{2,0,1:T(8,128)S(1)} fusion(bf16[96,128,128]{2,1,0:T(8,128)(2,1)S(1)} %copy-done, bf16[96,64,128]{2,1,0:T(8,128)(2,1)} %gather_fusion.1), kind=kOutput, calls=%fused_computation.26 | convolution fusion | flops 201326592 | bytes 7864320 | tf_op jit(solution)/shard_map/otb,tab->ota/dot_general | solution.py:84
  54.8 4.1 %fusion.25 = f32[64,16,128]{2,1,0:T(8,128)} fusion(f32[64,96,128]{2,0,1:T(8,128)S(1)} %convolution_bitcast_fusion.2, f32[96]{0:T(128)S(1)} %get-tuple-element.25, s32[96]{0:T(128)S(1)} %copy-done.8), kind=kOutput, calls=%fused_computation.32 | convolution fusion | flops 150998016 | bytes 3670784 | tf_op jit(solution)/shard_map/ota,tr->ora/dot_general | solution.py:85
  59.0 36.9 %all-to-all-done = bf16[64,128,128]{2,0,1:T(8,128)(2,1)} async-done(((bf16[64,128,128]{2,0,1:T(8,128)(2,1)}), bf16[64,128,128]{2,0,1:T(8,128)(2,1)}, u32[]{:S(2)}, u32[]{:S(2)}) %all-to-all-start) | async-done | bytes 2097184 | tf_op jit(solution)/shard_map/all_to_all | solution.py:77
  95.9 5.9 %convolution_bitcast_fusion = f32[64,128,128]{2,0,1:T(8,128)S(1)} fusion(bf16[64,128,128]{2,0,1:T(8,128)(2,1)} %all-to-all-done, bf16[128,128,128]{2,1,0:T(8,128)(2,1)} %gather_fusion.3, pred[128]{0:T(512)(128)(4,1)S(1)} %fusion.52), kind=kOutput, calls=%fused_computation.19 | convolution fusion | flops 270532608 | bytes 10485888 | tf_op jit(solution)/shard_map/oqb,qab->oqa/dot_general | solution.py:90
  101.8 4.4 %fusion.22 = f32[64,16,128]{2,1,0:T(8,128)S(1)} fusion(f32[64,16,128]{2,1,0:T(8,128)S(1)} %copy-done.1, f32[64,128,128]{2,0,1:T(8,128)S(1)} %convolution_bitcast_fusion, f32[128]{0:T(128)S(1)} %convert_element_type.60, s32[128]{0:T(128)S(1)} %get-tuple-element.20), kind=kOutput, calls=%fused_computation.31 | convolution fusion | flops 201461760 | bytes 5243904 | tf_op jit(solution)/shard_map/oqa,qr->ora/dot_general | solution.py:93
  110.0 5.4 %convert_bitcast_fusion = bf16[64,128,128]{2,0,1:T(8,128)(2,1)} fusion(bf16[128,64,128]{2,1,0:T(8,128)(2,1)} %gather_fusion.5, bf16[128,128,128]{2,1,0:T(8,128)(2,1)} %gather_fusion.3, pred[128]{0:T(512)(128)(4,1)S(1)} %fusion.52), kind=kOutput, calls=%fused_computation.24 | convolution fusion | flops 271581184 | bytes 8388736 | tf_op jit(solution)/shard_map/oqa,qab->oqb/dot_general | solution.py:112
  115.4 9.3 %all-to-all-start.1 = ((bf16[64,128,128]{2,0,1:T(8,128)(2,1)}), bf16[64,128,128]{2,0,1:T(8,128)(2,1)}, u32[]{:S(2)}, u32[]{:S(2)}) async-start(bf16[64,128,128]{2,0,1:T(8,128)(2,1)} %convert_bitcast_fusion), calls=%async_computation.1 | async-start | bytes 4194304 | tf_op jit(solution)/shard_map/all_to_all | solution.py:115
  127.4 2.4 convolution_bitcast_fusion.1
  129.8 4.1 %fusion.2 = f32[16,64,128]{2,0,1:T(8,128)} fusion(f32[64,96,128]{2,0,1:T(8,128)S(1)} %convolution_bitcast_fusion.1, f32[96]{0:T(128)S(1)} %fusion.81, s32[96]{0:T(128)S(1)} %copy-done.7), kind=kOutput, calls=%fused_computation.10 | convolution fusion | flops 150998016 | bytes 3670784 | tf_op jit(solution)/shard_map/otb,tr->orb/dot_general | solution.py:108
  133.9 41.8 %all-to-all-done.1 = bf16[64,128,128]{2,0,1:T(8,128)(2,1)} async-done(((bf16[64,128,128]{2,0,1:T(8,128)(2,1)}), bf16[64,128,128]{2,0,1:T(8,128)(2,1)}, u32[]{:S(2)}, u32[]{:S(2)}) %all-to-all-start.1) | async-done | bytes 2097184 | tf_op jit(solution)/shard_map/all_to_all | solution.py:115
  175.6 3.0 %fusion.28 = bf16[16,64,128]{2,0,1:T(8,128)(2,1)S(1)} fusion(f32[16,64,128]{2,0,1:T(8,128)} %fusion.2, bf16[64,128,128]{2,0,1:T(8,128)(2,1)} %all-to-all-done.1, s32[128]{0:T(128)S(1)} %copy-done.9), kind=kOutput, calls=%fused_computation.33 | convolution fusion | flops 33818624 | bytes 2884096 | tf_op jit(solution)/shard_map/oqb,qr->orb/dot_general | solution.py:117
  191.2 8.9 %all-to-all-start.2 = ((f32[128,1,192]{2,1,0:T(1,128)}), f32[128,1,192]{2,1,0:T(1,128)S(1)}, u32[]{:S(2)}, u32[]{:S(2)}) async-start(f32[128,1,192]{2,1,0:T(1,128)} %reshape.136), calls=%async_computation.2 | async-start | bytes 262144 | tf_op jit(solution)/shard_map/all_to_all | solution.py:35
  202.7 4.9 %collective-permute-start.7 = (bf16[64,2048]{1,0:T(8,128)(2,1)}, bf16[64,2048]{1,0:T(8,128)(2,1)}, u32[]{:S(2)}, u32[]{:S(2)}) collective-permute-start(bf16[64,2048]{1,0:T(8,128)(2,1)} %bitcast.119), channel_id=1, source_target_pairs={{0,2},{1,3},{2,0},{3,1},{4,6},{5,7},{6,4},{7,5},{8,10},{9,11},{10,... | collective-permute-start | bytes 786440 | tf_op jit(solution)/shard_map/ppermute | solution.py:27
  207.6 2.8 %collective-permute-start.8 = (bf16[64,2048]{1,0:T(8,128)(2,1)}, bf16[64,2048]{1,0:T(8,128)(2,1)}, u32[]{:S(2)}, u32[]{:S(2)}) collective-permute-start(bf16[64,2048]{1,0:T(8,128)(2,1)} %bitcast.119), channel_id=1, source_target_pairs={{0,3},{1,2},{2,1},{3,0},{4,7},{5,6},{6,5},{7,4},{8,11},{9,10},{10,... | collective-permute-start | bytes 786440 | tf_op jit(solution)/shard_map/ppermute | solution.py:27
  210.4 2.4 all-to-all-done.2
  217.0 12.2 %all-to-all-start.3 = ((f32[128,1,192]{2,1,0:T(1,128)}), f32[128,1,192]{2,1,0:T(1,128)S(1)}, u32[]{:S(2)}, u32[]{:S(2)}) async-start(f32[128,1,192]{2,1,0:T(1,128)} %reshape.138), calls=%async_computation.3 | async-start | bytes 262144 | tf_op jit(solution)/shard_map/all_to_all | solution.py:38
  231.2 4.9 %collective-permute-start.4 = (bf16[256,64]{0,1:T(8,128)(2,1)}, bf16[256,64]{0,1:T(8,128)(2,1)S(1)}, u32[]{:S(2)}, u32[]{:S(2)}) collective-permute-start(bf16[256,64]{0,1:T(8,128)(2,1)} %param.10), channel_id=1, source_target_pairs={{0,2},{1,3},{2,0},{3,1},{4,6},{5,7},{6,4},{7,5},{8,10},{9,11},{10,... | collective-permute-start | bytes 98312 | tf_op jit(solution)/shard_map/ppermute | solution.py:27
  236.1 2.8 %collective-permute-start.5 = (bf16[256,64]{0,1:T(8,128)(2,1)}, bf16[256,64]{0,1:T(8,128)(2,1)S(1)}, u32[]{:S(2)}, u32[]{:S(2)}) collective-permute-start(bf16[256,64]{0,1:T(8,128)(2,1)} %param.10), channel_id=1, source_target_pairs={{0,3},{1,2},{2,1},{3,0},{4,7},{5,6},{6,5},{7,4},{8,11},{9,10},{10,... | collective-permute-start | bytes 98312 | tf_op jit(solution)/shard_map/ppermute | solution.py:27
  238.9 3.3 %collective-permute-done.5 = bf16[256,64]{0,1:T(8,128)(2,1)S(1)} collective-permute-done((bf16[256,64]{0,1:T(8,128)(2,1)}, bf16[256,64]{0,1:T(8,128)(2,1)S(1)}, u32[]{:S(2)}, u32[]{:S(2)}) %collective-permute-start.5) | collective-permute-done | bytes 32800 | tf_op jit(solution)/shard_map/ppermute | solution.py:27
  (89 shorter events, 47.0 us)
Async XLA Ops:
  0.6 45.5 %copy-start = (bf16[96,128,128]{2,1,0:T(8,128)(2,1)S(1)}, bf16[96,128,128]{2,1,0:T(8,128)(2,1)}, u32[]{:S(2)}) copy-start(bf16[96,128,128]{2,1,0:T(8,128)(2,1)} %param.12) | copy-start | bytes 9437188
  0.6 14.1 %collective-permute-start = (bf16[64,2048]{1,0:T(8,128)(2,1)}, bf16[64,2048]{1,0:T(8,128)(2,1)}, u32[]{:S(2)}, u32[]{:S(2)}) collective-permute-start(bf16[64,2048]{1,0:T(8,128)(2,1)} %param.9), channel_id=1, source_target_pairs={{0,1},{1,0},{2,3},{3,2},{4,5},{5,4},{6,7},{7,6},{8,9},{9,8},{10,11... | collective-permute-start | bytes 786440 | tf_op jit(solution)/shard_map/ppermute | solution.py:27
  4.9 9.6 %collective-permute-start.2 = (bf16[64,2048]{1,0:T(8,128)(2,1)}, bf16[64,2048]{1,0:T(8,128)(2,1)S(1)}, u32[]{:S(2)}, u32[]{:S(2)}) collective-permute-start(bf16[64,2048]{1,0:T(8,128)(2,1)} %param.9), channel_id=1, source_target_pairs={{0,3},{1,2},{2,1},{3,0},{4,7},{5,6},{6,5},{7,4},{8,11},{9,10},{10,... | collective-permute-start | bytes 786440 | tf_op jit(solution)/shard_map/ppermute | solution.py:27
  8.6 9.0 %collective-permute-start.1 = (bf16[64,2048]{1,0:T(8,128)(2,1)}, bf16[64,2048]{1,0:T(8,128)(2,1)}, u32[]{:S(2)}, u32[]{:S(2)}) collective-permute-start(bf16[64,2048]{1,0:T(8,128)(2,1)} %param.9), channel_id=1, source_target_pairs={{0,2},{1,3},{2,0},{3,1},{4,6},{5,7},{6,4},{7,5},{8,10},{9,11},{10,... | collective-permute-start | bytes 786440 | tf_op jit(solution)/shard_map/ppermute | solution.py:27
  14.5 3.1 %copy-start.3 = (bf16[64,2048]{1,0:T(8,128)(2,1)}, bf16[64,2048]{1,0:T(8,128)(2,1)S(1)}, u32[]{:S(2)}) copy-start(bf16[64,2048]{1,0:T(8,128)(2,1)S(1)} %collective-permute-done.2) | copy-start | bytes 786436
  21.1 24.7 %copy-start.7 = (s32[96]{0:T(128)S(1)}, s32[96]{0:T(128)}, u32[]{:S(2)}) copy-start(s32[96]{0:T(128)} %param.14) | copy-start | bytes 1156
  21.1 24.9 %copy-start.10 = (bf16[64]{0:T(256)(128)(2,1)S(1)}, bf16[64]{0:T(256)(128)(2,1)}, u32[]{:S(2)}) copy-start(bf16[64]{0:T(256)(128)(2,1)} %param.11) | copy-start | bytes 388
  21.1 24.9 %copy-start.8 = (s32[96]{0:T(128)S(1)}, s32[96]{0:T(128)}, u32[]{:S(2)}) copy-start(s32[96]{0:T(128)} %param.13) | copy-start | bytes 1156
  21.1 74.8 %all-to-all-start = ((bf16[64,128,128]{2,0,1:T(8,128)(2,1)}), bf16[64,128,128]{2,0,1:T(8,128)(2,1)}, u32[]{:S(2)}, u32[]{:S(2)}) async-start(bf16[64,128,128]{2,0,1:T(8,128)(2,1)} %bitcast.130), calls=%async_computation | async-start | bytes 4194304 | tf_op jit(solution)/shard_map/all_to_all | solution.py:77
  95.9 5.9 %copy-start.1 = (f32[64,16,128]{2,1,0:T(8,128)S(1)}, f32[64,16,128]{2,1,0:T(8,128)}, u32[]{:S(2)}) copy-start(f32[64,16,128]{2,1,0:T(8,128)} %fusion.25) | copy-start | bytes 1572868
  101.8 4.4 %copy-start.6 = (bf16[64,2048]{1,0:T(8,128)(2,1)S(1)}, bf16[64,2048]{1,0:T(8,128)(2,1)}, u32[]{:S(2)}) copy-start(bf16[64,2048]{1,0:T(8,128)(2,1)} %param.17) | copy-start | bytes 786436
  115.4 60.2 %all-to-all-start.1 = ((bf16[64,128,128]{2,0,1:T(8,128)(2,1)}), bf16[64,128,128]{2,0,1:T(8,128)(2,1)}, u32[]{:S(2)}, u32[]{:S(2)}) async-start(bf16[64,128,128]{2,0,1:T(8,128)(2,1)} %convert_bitcast_fusion), calls=%async_computation.1 | async-start | bytes 4194304 | tf_op jit(solution)/shard_map/all_to_all | solution.py:115
  129.8 45.9 %copy-start.9 = (s32[128]{0:T(128)S(1)}, s32[128]{0:T(128)}, u32[]{:S(2)}) copy-start(s32[128]{0:T(128)} %param.16) | copy-start | bytes 1540
  175.6 3.0 %copy-start.2 = (bf16[64,2048]{1,0:T(8,128)(2,1)S(1)}, bf16[64,2048]{1,0:T(8,128)(2,1)}, u32[]{:S(2)}) copy-start(bf16[64,2048]{1,0:T(8,128)(2,1)} %param.9) | copy-start | bytes 786436
  175.6 3.2 %copy-start.4 = (bf16[64,2048]{1,0:T(8,128)(2,1)S(1)}, bf16[64,2048]{1,0:T(8,128)(2,1)}, u32[]{:S(2)}) copy-start(bf16[64,2048]{1,0:T(8,128)(2,1)} %copy-done.3) | copy-start | bytes 786436
  191.2 21.6 %all-to-all-start.2 = ((f32[128,1,192]{2,1,0:T(1,128)}), f32[128,1,192]{2,1,0:T(1,128)S(1)}, u32[]{:S(2)}, u32[]{:S(2)}) async-start(f32[128,1,192]{2,1,0:T(1,128)} %reshape.136), calls=%async_computation.2 | async-start | bytes 262144 | tf_op jit(solution)/shard_map/all_to_all | solution.py:35
  200.8 41.4 %collective-permute-start.6 = (bf16[64,2048]{1,0:T(8,128)(2,1)}, bf16[64,2048]{1,0:T(8,128)(2,1)}, u32[]{:S(2)}, u32[]{:S(2)}) collective-permute-start(bf16[64,2048]{1,0:T(8,128)(2,1)} %bitcast.119), channel_id=1, source_target_pairs={{0,1},{1,0},{2,3},{3,2},{4,5},{5,4},{6,7},{7,6},{8,9},{9,8},{10,11... | collective-permute-start | bytes 786440 | tf_op jit(solution)/shard_map/ppermute | solution.py:27
  202.7 39.5 %collective-permute-start.7 = (bf16[64,2048]{1,0:T(8,128)(2,1)}, bf16[64,2048]{1,0:T(8,128)(2,1)}, u32[]{:S(2)}, u32[]{:S(2)}) collective-permute-start(bf16[64,2048]{1,0:T(8,128)(2,1)} %bitcast.119), channel_id=1, source_target_pairs={{0,2},{1,3},{2,0},{3,1},{4,6},{5,7},{6,4},{7,5},{8,10},{9,11},{10,... | collective-permute-start | bytes 786440 | tf_op jit(solution)/shard_map/ppermute | solution.py:27
  207.6 34.6 %collective-permute-start.8 = (bf16[64,2048]{1,0:T(8,128)(2,1)}, bf16[64,2048]{1,0:T(8,128)(2,1)}, u32[]{:S(2)}, u32[]{:S(2)}) collective-permute-start(bf16[64,2048]{1,0:T(8,128)(2,1)} %bitcast.119), channel_id=1, source_target_pairs={{0,3},{1,2},{2,1},{3,0},{4,7},{5,6},{6,5},{7,4},{8,11},{9,10},{10,... | collective-permute-start | bytes 786440 | tf_op jit(solution)/shard_map/ppermute | solution.py:27
  212.8 0.7 copy-start.5
  217.0 27.5 %all-to-all-start.3 = ((f32[128,1,192]{2,1,0:T(1,128)}), f32[128,1,192]{2,1,0:T(1,128)S(1)}, u32[]{:S(2)}, u32[]{:S(2)}) async-start(f32[128,1,192]{2,1,0:T(1,128)} %reshape.138), calls=%async_computation.3 | async-start | bytes 262144 | tf_op jit(solution)/shard_map/all_to_all | solution.py:38
  229.3 6.8 %collective-permute-start.3 = (bf16[256,64]{0,1:T(8,128)(2,1)}, bf16[256,64]{0,1:T(8,128)(2,1)S(1)}, u32[]{:S(2)}, u32[]{:S(2)}) collective-permute-start(bf16[256,64]{0,1:T(8,128)(2,1)} %param.10), channel_id=1, source_target_pairs={{0,1},{1,0},{2,3},{3,2},{4,5},{5,4},{6,7},{7,6},{8,9},{9,8},{10,11... | collective-permute-start | bytes 98312 | tf_op jit(solution)/shard_map/ppermute | solution.py:27
  231.2 7.7 %collective-permute-start.4 = (bf16[256,64]{0,1:T(8,128)(2,1)}, bf16[256,64]{0,1:T(8,128)(2,1)S(1)}, u32[]{:S(2)}, u32[]{:S(2)}) collective-permute-start(bf16[256,64]{0,1:T(8,128)(2,1)} %param.10), channel_id=1, source_target_pairs={{0,2},{1,3},{2,0},{3,1},{4,6},{5,7},{6,4},{7,5},{8,10},{9,11},{10,... | collective-permute-start | bytes 98312 | tf_op jit(solution)/shard_map/ppermute | solution.py:27
  236.1 6.1 %collective-permute-start.5 = (bf16[256,64]{0,1:T(8,128)(2,1)}, bf16[256,64]{0,1:T(8,128)(2,1)S(1)}, u32[]{:S(2)}, u32[]{:S(2)}) collective-permute-start(bf16[256,64]{0,1:T(8,128)(2,1)} %param.10), channel_id=1, source_target_pairs={{0,3},{1,2},{2,1},{3,0},{4,7},{5,6},{6,5},{7,4},{8,11},{9,10},{10,... | collective-permute-start | bytes 98312 | tf_op jit(solution)/shard_map/ppermute | solution.py:27

commit v9 on v8

--- a/solution.py
+++ b/solution.py
@@ -30,13 +30,12 @@
 
 def scatter_gather_sum(values, axis, size):
     rows, cols = values.shape
-    chunk = -(-rows // size)
-    padded = jnp.pad(values, ((0, chunk * size - rows), (0, 0))).reshape(size, chunk, cols)
-    gathered = lax.all_to_all(padded, axis, 0, 0, tiled=True)
+    chunk = rows // size
+    gathered = lax.all_to_all(values.reshape(size, chunk, cols), axis, 0, 0, tiled=True)
     reduced = jnp.sum(gathered, axis=0)
     spread = jnp.broadcast_to(reduced[None], (size, chunk, cols))
     total = lax.all_to_all(spread, axis, 0, 0, tiled=True)
-    return total.reshape(size * chunk, cols)[:rows]
+    return total.reshape(rows, cols)
 
 
 def per_device(
@@ -62,6 +61,8 @@
     )
     order = lax.axis_index("feat") ^ jnp.arange(parts)
     pieces = exchange_order(node_feats, "feat", parts, parts)
+    full_weight = jnp.concatenate(exchange_order(weight, "feat", parts, parts), axis=1)
+    pieces, full_weight = lax.optimization_barrier((pieces, full_weight))
     in_rows = weight.shape[0] // parts
     weight_ordered = jnp.take(
         weight.reshape(parts, in_rows, weight.shape[1]), order, axis=0, mode="clip"
@@ -119,23 +120,27 @@
     )
     grad_hidden = grad_sum.reshape(feat_rows, node_rows).astype(jnp.bfloat16)
     norm_scale = 1.0 / math.sqrt(domains * node_rows)
-    weight_part = jnp.stack(
+    weight_part = jnp.concatenate(
         [
             lax.dot_general(
-                piece, grad_hidden, (((1,), (1,)), ((), ())), preferred_element_type=jnp.float32
+                grad_hidden, piece, (((1,), (1,)), ((), ())), preferred_element_type=jnp.float32
             )
             for piece in pieces
-        ]
-    )
-    weight_part = jnp.take(weight_part, order, axis=0, mode="clip").reshape(
-        parts * in_rows, feat_rows
+        ],
+        axis=1,
     )
     bias_part = jnp.sum(grad_pre, axis=1)
-    packed = jnp.concatenate([weight_part, bias_part[None, :]], axis=0)
+    lanes = 128
+    weight_rows = weight_part.size // lanes
+    pack_rows = -(-(weight_rows + 1) // domains) * domains
+    packed = jnp.zeros((pack_rows, lanes), jnp.float32)
+    packed = packed.at[:weight_rows].set(weight_part.reshape(weight_rows, lanes))
+    packed = packed.at[weight_rows, : bias_part.shape[0]].set(bias_part)
     packed = scatter_gather_sum(packed, "dom", domains)
-    grad_weight = packed[:-1] * norm_scale
-    grad_bias = packed[-1] * norm_scale
-    full_weight = jnp.concatenate(exchange_order(weight, "feat", parts, parts), axis=1)
+    summed_weight = packed[:weight_rows].reshape(feat_rows, parts, in_rows)
+    summed_weight = jnp.take(summed_weight, order, axis=1, mode="clip").reshape(feat_rows, parts * in_rows)
+    grad_weight = summed_weight.T * norm_scale
+    grad_bias = packed[weight_rows, : bias_part.shape[0]] * norm_scale
     all_grad = jnp.concatenate(exchange_order(grad_hidden, "feat", parts, parts), axis=0)
     my_rows = lax.dynamic_slice_in_dim(
         full_weight, lax.axis_index("feat") * feat_rows, feat_rows, 0

time: 251 us -> 242 us (0.964)
  waiting for transfers between devices: 86 us -> 94.5 us
  local copies, waits for them, and re-layouts: 26.5 us -> 18.3 us
  other arithmetic: 9.11 us -> 4.74 us
  starting transfers between devices: 84.1 us -> 80.6 us
    all_to_all x1, waiting for transfers between devices: 0.01 us -> 10.4 us  [scatter_gather_sum(): total = lax.all_to_all(spread, axis, 0, 0, tiled=True)]
    unnamed x30 -> x28, local copies, waits for them, and re-layouts: 7.05 us -> 2.35 us
    all_to_all x1, starting transfers between devices: 24 us -> 20 us  [per_device(): lax.all_to_all(outgoing, 'dom', split_axis=1, concat_axis=1, tiled=True)]
    reshape x3 -> x2, local copies, waits for them, and re-layouts: 3.24 us -> 0.15 us  [per_device(): summed_weight = packed[:weight_rows].reshape(feat_rows, parts, in_rows)]
    all_to_all x2 -> x0, other arithmetic: 2.82 us -> none  [the longest x1 1.87 us: scatter_gather_sum(): gathered = lax.all_to_all(padded, axis, 0, 0, tiled=True)]
    ppermute x9, waiting for transfers between devices: 4.98 us -> 2.46 us  [exchange_order(): received.append(lax.ppermute(values, axis, pairs))]
  transfers between devices with their start and end apart: 13 -> 13, of which waited for: 5 -> 5; matrix products, arithmetic and copies ran while one was open for 14% -> 12% of each run, Pallas kernels for 0% -> 0%
where the time goes in v9:
time: 242 us; the launch traced here: 241 us
  waiting for transfers between devices  94.5 us (39%)
  starting transfers between devices  80.6 us (33%)
  matrix products  41 us (17%)
  local copies, waits for them, and re-layouts  18.3 us (8%)
  other arithmetic  4.74 us (2%)
    all_to_all x1, waiting for transfers between devices, per_device(): lax.all_to_all(out_parts, 'dom', split_axis=1, concat_axis=1, tiled=True)  42.5 us
    all_to_all x1, waiting for transfers between devices, per_device(): lax.all_to_all(outgoing, 'dom', split_axis=1, concat_axis=1, tiled=True)  36.9 us
    ppermute x9, starting transfers between devices, exchange_order(): received.append(lax.ppermute(values, axis, pairs))  30.3 us
    all_to_all x1, starting transfers between devices, per_device(): lax.all_to_all(outgoing, 'dom', split_axis=1, concat_axis=1, tiled=True)  20 us
    all_to_all x1, starting transfers between devices, scatter_gather_sum(): total = lax.all_to_all(spread, axis, 0, 0, tiled=True)  12.2 us
    all_to_all x1, waiting for transfers between devices, scatter_gather_sum(): total = lax.all_to_all(spread, axis, 0, 0, tiled=True)  10.4 us
    all_to_all x1, starting transfers between devices, per_device(): lax.all_to_all(out_parts, 'dom', split_axis=1, concat_axis=1, tiled=True)  9.31 us
    all_to_all x1, starting transfers between devices, scatter_gather_sum(): lax.all_to_all(values.reshape(size, chunk, cols), axis, 0, 0, tiled=True)  8.84 us
  transfers between devices with their start and end apart: 13, of which 5 were waited for; matrix products, arithmetic and copies ran while one was open for 12% of the time, Pallas kernels for 0%

profile of v9, /device:TPU:1, one launch (start us, length us, event | category | flops | bytes accessed | tf_op | source)
XLA Modules:
  0.0 241.1 jit_solution(17916616393791884257)
XLA Ops:
  0.6 4.2 %collective-permute-start = (bf16[64,2048]{1,0:T(8,128)(2,1)}, bf16[64,2048]{1,0:T(8,128)(2,1)S(1)}, u32[]{:S(2)}, u32[]{:S(2)}) collective-permute-start(bf16[64,2048]{1,0:T(8,128)(2,1)} %param.13), channel_id=1, source_target_pairs={{0,1},{1,0},{2,3},{3,2},{4,5},{5,4},{6,7},{7,6},{8,9},{9,8},{10,11... | collective-permute-start | bytes 786440 | tf_op jit(solution)/shard_map/ppermute | solution.py:27
  4.9 4.4 %collective-permute-start.1 = (bf16[64,2048]{1,0:T(8,128)(2,1)}, bf16[64,2048]{1,0:T(8,128)(2,1)}, u32[]{:S(2)}, u32[]{:S(2)}) collective-permute-start(bf16[64,2048]{1,0:T(8,128)(2,1)} %param.13), channel_id=1, source_target_pairs={{0,2},{1,3},{2,0},{3,1},{4,6},{5,7},{6,4},{7,5},{8,10},{9,11},{10,... | collective-permute-start | bytes 786440 | tf_op jit(solution)/shard_map/ppermute | solution.py:27
  13.3 5.6 %collective-permute-start.4 = (bf16[256,64]{0,1:T(8,128)(2,1)}, bf16[256,64]{0,1:T(8,128)(2,1)}, u32[]{:S(2)}, u32[]{:S(2)}) collective-permute-start(bf16[256,64]{0,1:T(8,128)(2,1)} %param.14), channel_id=1, source_target_pairs={{0,2},{1,3},{2,0},{3,1},{4,6},{5,7},{6,4},{7,5},{8,10},{9,11},{10,... | collective-permute-start | bytes 98312 | tf_op jit(solution)/shard_map/ppermute | solution.py:27
  18.9 2.5 %collective-permute-start.5 = (bf16[256,64]{0,1:T(8,128)(2,1)}, bf16[256,64]{0,1:T(8,128)(2,1)}, u32[]{:S(2)}, u32[]{:S(2)}) collective-permute-start(bf16[256,64]{0,1:T(8,128)(2,1)} %param.14), channel_id=1, source_target_pairs={{0,3},{1,2},{2,1},{3,0},{4,7},{5,6},{6,5},{7,4},{8,11},{9,10},{10,... | collective-permute-start | bytes 98312 | tf_op jit(solution)/shard_map/ppermute | solution.py:27
  23.6 2.4 %collective-permute-done.5 = bf16[256,64]{0,1:T(8,128)(2,1)} collective-permute-done((bf16[256,64]{0,1:T(8,128)(2,1)}, bf16[256,64]{0,1:T(8,128)(2,1)}, u32[]{:S(2)}, u32[]{:S(2)}) %collective-permute-start.5) | collective-permute-done | bytes 32800 | tf_op jit(solution)/shard_map/ppermute | solution.py:27
  32.8 20.0 %all-to-all-start = ((bf16[64,128,128]{2,0,1:T(8,128)(2,1)}), bf16[64,128,128]{2,0,1:T(8,128)(2,1)}, u32[]{:S(2)}, u32[]{:S(2)}) async-start(bf16[64,128,128]{2,0,1:T(8,128)(2,1)} %bitcast.117), calls=%async_computation | async-start | bytes 4194304 | tf_op jit(solution)/shard_map/all_to_all | solution.py:78
  53.8 3.0 %gather_fusion.3 = bf16[128,128,128]{2,1,0:T(8,128)(2,1)} fusion(bf16[96,128,128]{2,1,0:T(8,128)(2,1)S(1)} %copy-done, s32[1024]{0:T(1024)S(1)} %pad_clamp_fusion.2), kind=kCustom, calls=%fused_computation.3 | custom fusion | bytes 8389120 | tf_op jit(solution)/shard_map/jit(_take)/gather | solution.py:59
  58.8 3.6 %convolution_bitcast_fusion.2 = f32[64,96,128]{2,0,1:T(8,128)S(1)} fusion(bf16[96,128,128]{2,1,0:T(8,128)(2,1)S(1)} %copy-done, bf16[96,64,128]{2,1,0:T(8,128)(2,1)} %gather_fusion.1), kind=kOutput, calls=%fused_computation.26 | convolution fusion | flops 201326592 | bytes 7864320 | tf_op jit(solution)/shard_map/otb,tab->ota/dot_general | solution.py:85
  62.5 4.1 %fusion.26 = f32[64,16,128]{2,1,0:T(8,128)} fusion(f32[64,96,128]{2,0,1:T(8,128)S(1)} %convolution_bitcast_fusion.2, f32[96]{0:T(128)S(1)} %get-tuple-element.47, s32[96]{0:T(128)S(1)} %copy-done.10), kind=kOutput, calls=%fused_computation.32 | convolution fusion | flops 150998016 | bytes 3670784 | tf_op jit(solution)/shard_map/ota,tr->ora/dot_general | solution.py:86
  66.6 36.9 %all-to-all-done = bf16[64,128,128]{2,0,1:T(8,128)(2,1)} async-done(((bf16[64,128,128]{2,0,1:T(8,128)(2,1)}), bf16[64,128,128]{2,0,1:T(8,128)(2,1)}, u32[]{:S(2)}, u32[]{:S(2)}) %all-to-all-start) | async-done | bytes 2097184 | tf_op jit(solution)/shard_map/all_to_all | solution.py:78
  103.5 5.9 %convolution_bitcast_fusion = f32[64,128,128]{2,0,1:T(8,128)S(1)} fusion(bf16[64,128,128]{2,0,1:T(8,128)(2,1)} %all-to-all-done, bf16[128,128,128]{2,1,0:T(8,128)(2,1)} %gather_fusion.3, pred[128]{0:T(512)(128)(4,1)S(1)} %fusion.50), kind=kOutput, calls=%fused_computation.19 | convolution fusion | flops 270532608 | bytes 10485888 | tf_op jit(solution)/shard_map/oqb,qab->oqa/dot_general | solution.py:91
  109.4 4.4 %fusion.23 = f32[64,16,128]{2,1,0:T(8,128)S(1)} fusion(f32[64,16,128]{2,1,0:T(8,128)S(1)} %copy-done.1, f32[64,128,128]{2,0,1:T(8,128)S(1)} %convolution_bitcast_fusion, f32[128]{0:T(128)S(1)} %convert_element_type.58, s32[128]{0:T(128)S(1)} %get-tuple-element.42), kind=kOutput, calls=%fused_computation.31 | convolution fusion | flops 201461760 | bytes 5243904 | tf_op jit(solution)/shard_map/oqa,qr->ora/dot_general | solution.py:94
  117.6 5.5 %convert_bitcast_fusion = bf16[64,128,128]{2,0,1:T(8,128)(2,1)} fusion(bf16[128,64,128]{2,1,0:T(8,128)(2,1)} %gather_fusion.5, bf16[128,128,128]{2,1,0:T(8,128)(2,1)} %gather_fusion.3, pred[128]{0:T(512)(128)(4,1)S(1)} %fusion.50), kind=kOutput, calls=%fused_computation.24 | convolution fusion | flops 271581184 | bytes 8388736 | tf_op jit(solution)/shard_map/oqa,qab->oqb/dot_general | solution.py:113
  123.1 9.3 %all-to-all-start.1 = ((bf16[64,128,128]{2,0,1:T(8,128)(2,1)}), bf16[64,128,128]{2,0,1:T(8,128)(2,1)}, u32[]{:S(2)}, u32[]{:S(2)}) async-start(bf16[64,128,128]{2,0,1:T(8,128)(2,1)} %convert_bitcast_fusion), calls=%async_computation.1 | async-start | bytes 4194304 | tf_op jit(solution)/shard_map/all_to_all | solution.py:116
  134.4 2.4 convolution_bitcast_fusion.1
  136.8 4.1 %fusion.2 = f32[16,64,128]{2,0,1:T(8,128)} fusion(f32[64,96,128]{2,0,1:T(8,128)S(1)} %convolution_bitcast_fusion.1, f32[96]{0:T(128)S(1)} %fusion.80, s32[96]{0:T(128)S(1)} %copy-done.9), kind=kOutput, calls=%fused_computation.10 | convolution fusion | flops 150998016 | bytes 3670784 | tf_op jit(solution)/shard_map/otb,tr->orb/dot_general | solution.py:109
  140.9 42.5 %all-to-all-done.1 = bf16[64,128,128]{2,0,1:T(8,128)(2,1)} async-done(((bf16[64,128,128]{2,0,1:T(8,128)(2,1)}), bf16[64,128,128]{2,0,1:T(8,128)(2,1)}, u32[]{:S(2)}, u32[]{:S(2)}) %all-to-all-start.1) | async-done | bytes 2097184 | tf_op jit(solution)/shard_map/all_to_all | solution.py:116
  183.3 3.0 %fusion.29 = bf16[16,64,128]{2,0,1:T(8,128)(2,1)S(1)} fusion(f32[16,64,128]{2,0,1:T(8,128)} %fusion.2, bf16[64,128,128]{2,0,1:T(8,128)(2,1)} %all-to-all-done.1, s32[128]{0:T(128)S(1)} %copy-done.11), kind=kOutput, calls=%fused_computation.33 | convolution fusion | flops 33818624 | bytes 2884096 | tf_op jit(solution)/shard_map/oqb,qr->orb/dot_general | solution.py:118
  191.6 8.8 %all-to-all-start.2 = ((f32[128,2,128]{2,1,0:T(2,128)}), f32[128,2,128]{2,1,0:T(2,128)S(1)}, u32[]{:S(2)}, u32[]{:S(2)}) async-start(f32[128,2,128]{2,1,0:T(2,128)} %bitcast.119), calls=%async_computation.2 | async-start | bytes 262144 | tf_op jit(solution)/shard_map/all_to_all | solution.py:34
  203.1 3.9 %collective-permute-start.7 = (bf16[64,2048]{1,0:T(8,128)(2,1)}, bf16[64,2048]{1,0:T(8,128)(2,1)}, u32[]{:S(2)}, u32[]{:S(2)}) collective-permute-start(bf16[64,2048]{1,0:T(8,128)(2,1)} %bitcast.106), channel_id=1, source_target_pairs={{0,2},{1,3},{2,0},{3,1},{4,6},{5,7},{6,4},{7,5},{8,10},{9,11},{10,... | collective-permute-start | bytes 786440 | tf_op jit(solution)/shard_map/ppermute | solution.py:27
  207.0 3.8 %collective-permute-start.8 = (bf16[64,2048]{1,0:T(8,128)(2,1)}, bf16[64,2048]{1,0:T(8,128)(2,1)}, u32[]{:S(2)}, u32[]{:S(2)}) collective-permute-start(bf16[64,2048]{1,0:T(8,128)(2,1)} %bitcast.106), channel_id=1, source_target_pairs={{0,3},{1,2},{2,1},{3,0},{4,7},{5,6},{6,5},{7,4},{8,11},{9,10},{10,... | collective-permute-start | bytes 786440 | tf_op jit(solution)/shard_map/ppermute | solution.py:27
  210.8 2.4 all-to-all-done.2
  214.0 12.2 %all-to-all-start.3 = ((f32[128,2,128]{2,1,0:T(2,128)}), f32[128,2,128]{2,1,0:T(2,128)S(1)}, u32[]{:S(2)}, u32[]{:S(2)}) async-start(f32[128,2,128]{2,1,0:T(2,128)} %broadcast_in_dim.87), calls=%async_computation.3 | async-start | bytes 262144 | tf_op jit(solution)/shard_map/all_to_all | solution.py:37
  228.6 10.4 %all-to-all-done.3 = f32[128,2,128]{2,1,0:T(2,128)S(1)} async-done(((f32[128,2,128]{2,1,0:T(2,128)}), f32[128,2,128]{2,1,0:T(2,128)S(1)}, u32[]{:S(2)}, u32[]{:S(2)}) %all-to-all-start.3) | async-done | bytes 131104 | tf_op jit(solution)/shard_map/all_to_all | solution.py:37
  (86 shorter events, 34.1 us)
Async XLA Ops:
  0.6 53.1 %copy-start = (bf16[96,128,128]{2,1,0:T(8,128)(2,1)S(1)}, bf16[96,128,128]{2,1,0:T(8,128)(2,1)}, u32[]{:S(2)}) copy-start(bf16[96,128,128]{2,1,0:T(8,128)(2,1)} %param.16) | copy-start | bytes 9437188
  0.6 26.8 %collective-permute-start = (bf16[64,2048]{1,0:T(8,128)(2,1)}, bf16[64,2048]{1,0:T(8,128)(2,1)S(1)}, u32[]{:S(2)}, u32[]{:S(2)}) collective-permute-start(bf16[64,2048]{1,0:T(8,128)(2,1)} %param.13), channel_id=1, source_target_pairs={{0,1},{1,0},{2,3},{3,2},{4,5},{5,4},{6,7},{7,6},{8,9},{9,8},{10,11... | collective-permute-start | bytes 786440 | tf_op jit(solution)/shard_map/ppermute | solution.py:27
  4.9 22.6 %collective-permute-start.1 = (bf16[64,2048]{1,0:T(8,128)(2,1)}, bf16[64,2048]{1,0:T(8,128)(2,1)}, u32[]{:S(2)}, u32[]{:S(2)}) collective-permute-start(bf16[64,2048]{1,0:T(8,128)(2,1)} %param.13), channel_id=1, source_target_pairs={{0,2},{1,3},{2,0},{3,1},{4,6},{5,7},{6,4},{7,5},{8,10},{9,11},{10,... | collective-permute-start | bytes 786440 | tf_op jit(solution)/shard_map/ppermute | solution.py:27
  9.2 18.2 %collective-permute-start.2 = (bf16[64,2048]{1,0:T(8,128)(2,1)}, bf16[64,2048]{1,0:T(8,128)(2,1)}, u32[]{:S(2)}, u32[]{:S(2)}) collective-permute-start(bf16[64,2048]{1,0:T(8,128)(2,1)} %param.13), channel_id=1, source_target_pairs={{0,3},{1,2},{2,1},{3,0},{4,7},{5,6},{6,5},{7,4},{8,11},{9,10},{10,... | collective-permute-start | bytes 786440 | tf_op jit(solution)/shard_map/ppermute | solution.py:27
  11.2 7.7 %collective-permute-start.3 = (bf16[256,64]{0,1:T(8,128)(2,1)}, bf16[256,64]{0,1:T(8,128)(2,1)S(1)}, u32[]{:S(2)}, u32[]{:S(2)}) collective-permute-start(bf16[256,64]{0,1:T(8,128)(2,1)} %param.14), channel_id=1, source_target_pairs={{0,1},{1,0},{2,3},{3,2},{4,5},{5,4},{6,7},{7,6},{8,9},{9,8},{10,11... | collective-permute-start | bytes 98312 | tf_op jit(solution)/shard_map/ppermute | solution.py:27
  13.3 10.3 %collective-permute-start.4 = (bf16[256,64]{0,1:T(8,128)(2,1)}, bf16[256,64]{0,1:T(8,128)(2,1)}, u32[]{:S(2)}, u32[]{:S(2)}) collective-permute-start(bf16[256,64]{0,1:T(8,128)(2,1)} %param.14), channel_id=1, source_target_pairs={{0,2},{1,3},{2,0},{3,1},{4,6},{5,7},{6,4},{7,5},{8,10},{9,11},{10,... | collective-permute-start | bytes 98312 | tf_op jit(solution)/shard_map/ppermute | solution.py:27
  18.9 4.1 %copy-start.8 = (bf16[256,64]{0,1:T(8,128)(2,1)}, bf16[256,64]{0,1:T(8,128)(2,1)S(1)}, u32[]{:S(2)}) copy-start(bf16[256,64]{0,1:T(8,128)(2,1)S(1)} %collective-permute-done.3) | copy-start | bytes 98308
  18.9 7.1 %collective-permute-start.5 = (bf16[256,64]{0,1:T(8,128)(2,1)}, bf16[256,64]{0,1:T(8,128)(2,1)}, u32[]{:S(2)}, u32[]{:S(2)}) collective-permute-start(bf16[256,64]{0,1:T(8,128)(2,1)} %param.14), channel_id=1, source_target_pairs={{0,3},{1,2},{2,1},{3,0},{4,7},{5,6},{6,5},{7,4},{8,11},{9,10},{10,... | collective-permute-start | bytes 98312 | tf_op jit(solution)/shard_map/ppermute | solution.py:27
  23.5 6.7 %copy-start.4 = (bf16[64,2048]{1,0:T(8,128)(2,1)S(1)}, bf16[64,2048]{1,0:T(8,128)(2,1)}, u32[]{:S(2)}) copy-start(bf16[64,2048]{1,0:T(8,128)(2,1)} %param.13) | copy-start | bytes 786436
  32.8 20.7 %copy-start.9 = (s32[96]{0:T(128)S(1)}, s32[96]{0:T(128)}, u32[]{:S(2)}) copy-start(s32[96]{0:T(128)} %param.18) | copy-start | bytes 1156
  32.8 20.8 %copy-start.12 = (bf16[64]{0:T(256)(128)(2,1)S(1)}, bf16[64]{0:T(256)(128)(2,1)}, u32[]{:S(2)}) copy-start(bf16[64]{0:T(256)(128)(2,1)} %param.15) | copy-start | bytes 388
  32.8 20.8 %copy-start.10 = (s32[96]{0:T(128)S(1)}, s32[96]{0:T(128)}, u32[]{:S(2)}) copy-start(s32[96]{0:T(128)} %param.17) | copy-start | bytes 1156
  32.8 70.8 %all-to-all-start = ((bf16[64,128,128]{2,0,1:T(8,128)(2,1)}), bf16[64,128,128]{2,0,1:T(8,128)(2,1)}, u32[]{:S(2)}, u32[]{:S(2)}) async-start(bf16[64,128,128]{2,0,1:T(8,128)(2,1)} %bitcast.117), calls=%async_computation | async-start | bytes 4194304 | tf_op jit(solution)/shard_map/all_to_all | solution.py:78
  103.5 5.9 %copy-start.1 = (f32[64,16,128]{2,1,0:T(8,128)S(1)}, f32[64,16,128]{2,1,0:T(8,128)}, u32[]{:S(2)}) copy-start(f32[64,16,128]{2,1,0:T(8,128)} %fusion.26) | copy-start | bytes 1572868
  109.4 4.4 %copy-start.7 = (bf16[64,2048]{1,0:T(8,128)(2,1)S(1)}, bf16[64,2048]{1,0:T(8,128)(2,1)}, u32[]{:S(2)}) copy-start(bf16[64,2048]{1,0:T(8,128)(2,1)} %param.21) | copy-start | bytes 786436
  123.1 60.2 %all-to-all-start.1 = ((bf16[64,128,128]{2,0,1:T(8,128)(2,1)}), bf16[64,128,128]{2,0,1:T(8,128)(2,1)}, u32[]{:S(2)}, u32[]{:S(2)}) async-start(bf16[64,128,128]{2,0,1:T(8,128)(2,1)} %convert_bitcast_fusion), calls=%async_computation.1 | async-start | bytes 4194304 | tf_op jit(solution)/shard_map/all_to_all | solution.py:116
  136.7 46.6 %copy-start.11 = (s32[128]{0:T(128)S(1)}, s32[128]{0:T(128)}, u32[]{:S(2)}) copy-start(s32[128]{0:T(128)} %param.20) | copy-start | bytes 1540
  183.3 5.3 %copy-start.3 = (bf16[64,2048]{1,0:T(8,128)(2,1)S(1)}, bf16[64,2048]{1,0:T(8,128)(2,1)}, u32[]{:S(2)}) copy-start(bf16[64,2048]{1,0:T(8,128)(2,1)} %copy-done.2) | copy-start | bytes 786436
  183.3 5.6 %copy-start.5 = (bf16[64,2048]{1,0:T(8,128)(2,1)S(1)}, bf16[64,2048]{1,0:T(8,128)(2,1)}, u32[]{:S(2)}) copy-start(bf16[64,2048]{1,0:T(8,128)(2,1)} %param.13) | copy-start | bytes 786436
  191.6 21.6 %all-to-all-start.2 = ((f32[128,2,128]{2,1,0:T(2,128)}), f32[128,2,128]{2,1,0:T(2,128)S(1)}, u32[]{:S(2)}, u32[]{:S(2)}) async-start(f32[128,2,128]{2,1,0:T(2,128)} %bitcast.119), calls=%async_computation.2 | async-start | bytes 262144 | tf_op jit(solution)/shard_map/all_to_all | solution.py:34
  201.2 25.0 %collective-permute-start.6 = (bf16[64,2048]{1,0:T(8,128)(2,1)}, bf16[64,2048]{1,0:T(8,128)(2,1)}, u32[]{:S(2)}, u32[]{:S(2)}) collective-permute-start(bf16[64,2048]{1,0:T(8,128)(2,1)} %bitcast.106), channel_id=1, source_target_pairs={{0,1},{1,0},{2,3},{3,2},{4,5},{5,4},{6,7},{7,6},{8,9},{9,8},{10,11... | collective-permute-start | bytes 786440 | tf_op jit(solution)/shard_map/ppermute | solution.py:27
  203.1 23.1 %collective-permute-start.7 = (bf16[64,2048]{1,0:T(8,128)(2,1)}, bf16[64,2048]{1,0:T(8,128)(2,1)}, u32[]{:S(2)}, u32[]{:S(2)}) collective-permute-start(bf16[64,2048]{1,0:T(8,128)(2,1)} %bitcast.106), channel_id=1, source_target_pairs={{0,2},{1,3},{2,0},{3,1},{4,6},{5,7},{6,4},{7,5},{8,10},{9,11},{10,... | collective-permute-start | bytes 786440 | tf_op jit(solution)/shard_map/ppermute | solution.py:27
  207.0 19.3 %collective-permute-start.8 = (bf16[64,2048]{1,0:T(8,128)(2,1)}, bf16[64,2048]{1,0:T(8,128)(2,1)}, u32[]{:S(2)}, u32[]{:S(2)}) collective-permute-start(bf16[64,2048]{1,0:T(8,128)(2,1)} %bitcast.106), channel_id=1, source_target_pairs={{0,3},{1,2},{2,1},{3,0},{4,7},{5,6},{6,5},{7,4},{8,11},{9,10},{10,... | collective-permute-start | bytes 786440 | tf_op jit(solution)/shard_map/ppermute | solution.py:27
  214.0 24.9 %all-to-all-start.3 = ((f32[128,2,128]{2,1,0:T(2,128)}), f32[128,2,128]{2,1,0:T(2,128)S(1)}, u32[]{:S(2)}, u32[]{:S(2)}) async-start(f32[128,2,128]{2,1,0:T(2,128)} %broadcast_in_dim.87), calls=%async_computation.3 | async-start | bytes 262144 | tf_op jit(solution)/shard_map/all_to_all | solution.py:37
  (2 other events, 3.4 us)

commit v10 on v9

--- a/solution.py
+++ b/solution.py
@@ -61,8 +61,6 @@
     )
     order = lax.axis_index("feat") ^ jnp.arange(parts)
     pieces = exchange_order(node_feats, "feat", parts, parts)
-    full_weight = jnp.concatenate(exchange_order(weight, "feat", parts, parts), axis=1)
-    pieces, full_weight = lax.optimization_barrier((pieces, full_weight))
     in_rows = weight.shape[0] // parts
     weight_ordered = jnp.take(
         weight.reshape(parts, in_rows, weight.shape[1]), order, axis=0, mode="clip"
@@ -114,6 +112,9 @@
         "oqa,qab->oqb", out_rows, peer_tiles, preferred_element_type=jnp.float32
     ).astype(jnp.bfloat16)
     in_parts = lax.all_to_all(out_parts, "dom", split_axis=1, concat_axis=1, tiled=True)
+    late_weight, out_parts = lax.optimization_barrier((weight, out_parts))
+    full_weight = jnp.concatenate(exchange_order(late_weight, "feat", parts, parts), axis=1)
+    full_weight, in_parts = lax.optimization_barrier((full_weight, in_parts))
     remote_sum = in_parts.astype(jnp.float32)
     grad_sum = own_sum + jnp.einsum(
         "oqb,qr->orb", remote_sum, recv_place, precision=lax.Precision.HIGHEST

time: 242 us -> 237 us (0.979)
  waiting for transfers between devices: 94.5 us -> 83 us
  starting transfers between devices: 80.6 us -> 84.2 us
  matrix products: 41 us -> 43.7 us
    all_to_all x1, waiting for transfers between devices: 42.5 us -> 31.6 us  [per_device(): lax.all_to_all(out_parts, 'dom', split_axis=1, concat_axis=1, tiled=True)]
    all_to_all x1, starting transfers between devices: 20 us -> 24 us  [per_device(): lax.all_to_all(outgoing, 'dom', split_axis=1, concat_axis=1, tiled=True)]
  transfers between devices with their start and end apart: 13 -> 13, of which waited for: 5 -> 5; matrix products, arithmetic and copies ran while one was open for 12% -> 13% of each run, Pallas kernels for 0% -> 0%
where the time goes in v10:
time: 237 us; the launch traced here: 235 us
  starting transfers between devices  84.2 us (36%)
  waiting for transfers between devices  83 us (35%)
  matrix products  43.7 us (18%)
  local copies, waits for them, and re-layouts  18.3 us (8%)
  other arithmetic  4.44 us (2%)
    all_to_all x1, waiting for transfers between devices, per_device(): lax.all_to_all(outgoing, 'dom', split_axis=1, concat_axis=1, tiled=True)  36.9 us
    all_to_all x1, waiting for transfers between devices, per_device(): lax.all_to_all(out_parts, 'dom', split_axis=1, concat_axis=1, tiled=True)  31.6 us
    ppermute x9, starting transfers between devices, exchange_order(): received.append(lax.ppermute(values, axis, pairs))  29.7 us
    all_to_all x1, starting transfers between devices, per_device(): lax.all_to_all(outgoing, 'dom', split_axis=1, concat_axis=1, tiled=True)  24 us
    all_to_all x1, starting transfers between devices, scatter_gather_sum(): total = lax.all_to_all(spread, axis, 0, 0, tiled=True)  12.2 us
    all_to_all x1, waiting for transfers between devices, scatter_gather_sum(): total = lax.all_to_all(spread, axis, 0, 0, tiled=True)  10.4 us
    all_to_all x1, starting transfers between devices, per_device(): lax.all_to_all(out_parts, 'dom', split_axis=1, concat_axis=1, tiled=True)  9.44 us
    all_to_all x1, starting transfers between devices, scatter_gather_sum(): lax.all_to_all(values.reshape(size, chunk, cols), axis, 0, 0, tiled=True)  8.84 us
  transfers between devices with their start and end apart: 13, of which 5 were waited for; matrix products, arithmetic and copies ran while one was open for 13% of the time, Pallas kernels for 0%

profile of v10, /device:TPU:1, one launch (start us, length us, event | category | flops | bytes accessed | tf_op | source)
XLA Modules:
  0.0 235.4 jit_solution(1055373123991370795)
XLA Ops:
  0.6 4.2 %collective-permute-start = (bf16[64,2048]{1,0:T(8,128)(2,1)}, bf16[64,2048]{1,0:T(8,128)(2,1)}, u32[]{:S(2)}, u32[]{:S(2)}) collective-permute-start(bf16[64,2048]{1,0:T(8,128)(2,1)} %param.13), channel_id=1, source_target_pairs={{0,1},{1,0},{2,3},{3,2},{4,5},{5,4},{6,7},{7,6},{8,9},{9,8},{10,11... | collective-permute-start | bytes 786440 | tf_op jit(solution)/shard_map/ppermute | solution.py:27
  4.9 3.7 %collective-permute-start.2 = (bf16[64,2048]{1,0:T(8,128)(2,1)}, bf16[64,2048]{1,0:T(8,128)(2,1)S(1)}, u32[]{:S(2)}, u32[]{:S(2)}) collective-permute-start(bf16[64,2048]{1,0:T(8,128)(2,1)} %param.13), channel_id=1, source_target_pairs={{0,3},{1,2},{2,1},{3,0},{4,7},{5,6},{6,5},{7,4},{8,11},{9,10},{10,... | collective-permute-start | bytes 786440 | tf_op jit(solution)/shard_map/ppermute | solution.py:27
  8.6 2.6 %collective-permute-start.1 = (bf16[64,2048]{1,0:T(8,128)(2,1)}, bf16[64,2048]{1,0:T(8,128)(2,1)}, u32[]{:S(2)}, u32[]{:S(2)}) collective-permute-start(bf16[64,2048]{1,0:T(8,128)(2,1)} %param.13), channel_id=1, source_target_pairs={{0,2},{1,3},{2,0},{3,1},{4,6},{5,7},{6,4},{7,5},{8,10},{9,11},{10,... | collective-permute-start | bytes 786440 | tf_op jit(solution)/shard_map/ppermute | solution.py:27
  21.1 24.0 %all-to-all-start = ((bf16[64,128,128]{2,0,1:T(8,128)(2,1)}), bf16[64,128,128]{2,0,1:T(8,128)(2,1)}, u32[]{:S(2)}, u32[]{:S(2)}) async-start(bf16[64,128,128]{2,0,1:T(8,128)(2,1)} %bitcast.117), calls=%async_computation | async-start | bytes 4194304 | tf_op jit(solution)/shard_map/all_to_all | solution.py:76
  46.1 3.1 %gather_fusion.3 = bf16[128,128,128]{2,1,0:T(8,128)(2,1)} fusion(bf16[96,128,128]{2,1,0:T(8,128)(2,1)S(1)} %copy-done, s32[1024]{0:T(1024)S(1)} %pad_clamp_fusion.2), kind=kCustom, calls=%fused_computation.3 | custom fusion | bytes 8389120 | tf_op jit(solution)/shard_map/jit(_take)/gather | solution.py:59
  51.2 3.6 %convolution_bitcast_fusion.2 = f32[64,96,128]{2,0,1:T(8,128)S(1)} fusion(bf16[96,128,128]{2,1,0:T(8,128)(2,1)S(1)} %copy-done, bf16[96,64,128]{2,1,0:T(8,128)(2,1)} %gather_fusion.1), kind=kOutput, calls=%fused_computation.26 | convolution fusion | flops 201326592 | bytes 7864320 | tf_op jit(solution)/shard_map/otb,tab->ota/dot_general | solution.py:83
  54.9 4.1 %fusion.25 = f32[64,16,128]{2,1,0:T(8,128)} fusion(f32[64,96,128]{2,0,1:T(8,128)S(1)} %convolution_bitcast_fusion.2, f32[96]{0:T(128)S(1)} %get-tuple-element.43, s32[96]{0:T(128)S(1)} %copy-done.7), kind=kOutput, calls=%fused_computation.32 | convolution fusion | flops 150998016 | bytes 3670784 | tf_op jit(solution)/shard_map/ota,tr->ora/dot_general | solution.py:84
  59.0 36.9 %all-to-all-done = bf16[64,128,128]{2,0,1:T(8,128)(2,1)} async-done(((bf16[64,128,128]{2,0,1:T(8,128)(2,1)}), bf16[64,128,128]{2,0,1:T(8,128)(2,1)}, u32[]{:S(2)}, u32[]{:S(2)}) %all-to-all-start) | async-done | bytes 2097184 | tf_op jit(solution)/shard_map/all_to_all | solution.py:76
  95.9 5.9 %convolution_bitcast_fusion = f32[64,128,128]{2,0,1:T(8,128)S(1)} fusion(bf16[64,128,128]{2,0,1:T(8,128)(2,1)} %all-to-all-done, bf16[128,128,128]{2,1,0:T(8,128)(2,1)} %gather_fusion.3, pred[128]{0:T(512)(128)(4,1)S(1)} %fusion.49), kind=kOutput, calls=%fused_computation.19 | convolution fusion | flops 270532608 | bytes 10485888 | tf_op jit(solution)/shard_map/oqb,qab->oqa/dot_general | solution.py:89
  101.8 4.4 %fusion.22 = f32[64,16,128]{2,1,0:T(8,128)S(1)} fusion(f32[64,16,128]{2,1,0:T(8,128)S(1)} %copy-done.1, f32[64,128,128]{2,0,1:T(8,128)S(1)} %convolution_bitcast_fusion, f32[128]{0:T(128)S(1)} %convert_element_type.58, s32[128]{0:T(128)S(1)} %get-tuple-element.38), kind=kOutput, calls=%fused_computation.31 | convolution fusion | flops 201461760 | bytes 5243904 | tf_op jit(solution)/shard_map/oqa,qr->ora/dot_general | solution.py:92
  110.0 5.5 %convert_bitcast_fusion = bf16[64,128,128]{2,0,1:T(8,128)(2,1)} fusion(bf16[128,64,128]{2,1,0:T(8,128)(2,1)} %gather_fusion.4, bf16[128,128,128]{2,1,0:T(8,128)(2,1)} %gather_fusion.3, pred[128]{0:T(512)(128)(4,1)S(1)} %fusion.49), kind=kOutput, calls=%fused_computation.24 | convolution fusion | flops 271581184 | bytes 8388736 | tf_op jit(solution)/shard_map/oqa,qab->oqb/dot_general | solution.py:111
  115.5 9.4 %all-to-all-start.1 = ((bf16[64,128,128]{2,0,1:T(8,128)(2,1)}), bf16[64,128,128]{2,0,1:T(8,128)(2,1)}, u32[]{:S(2)}, u32[]{:S(2)}) async-start(bf16[64,128,128]{2,0,1:T(8,128)(2,1)} %convert_bitcast_fusion), calls=%async_computation.1 | async-start | bytes 4194304 | tf_op jit(solution)/shard_map/all_to_all | solution.py:114
  127.4 4.9 %collective-permute-start.4 = (bf16[256,64]{0,1:T(8,128)(2,1)S(1)}, bf16[256,64]{0,1:T(8,128)(2,1)S(1)}, u32[]{:S(2)}, u32[]{:S(2)}) collective-permute-start(bf16[256,64]{0,1:T(8,128)(2,1)S(1)} %copy-done.5), channel_id=1, source_target_pairs={{0,2},{1,3},{2,0},{3,1},{4,6},{5,7},{6,4},{7,5},{8,10},{9,11},{10,... | collective-permute-start | bytes 98312 | tf_op jit(solution)/shard_map/ppermute | solution.py:27
  132.3 2.8 %collective-permute-start.5 = (bf16[256,64]{0,1:T(8,128)(2,1)S(1)}, bf16[256,64]{0,1:T(8,128)(2,1)S(1)}, u32[]{:S(2)}, u32[]{:S(2)}) collective-permute-start(bf16[256,64]{0,1:T(8,128)(2,1)S(1)} %copy-done.5), channel_id=1, source_target_pairs={{0,3},{1,2},{2,1},{3,0},{4,7},{5,6},{6,5},{7,4},{8,11},{9,10},{10,... | collective-permute-start | bytes 98312 | tf_op jit(solution)/shard_map/ppermute | solution.py:27
  137.0 2.4 %convolution_bitcast_fusion.1 = f32[64,96,128]{2,0,1:T(8,128)S(1)} fusion(bf16[96,128,128]{2,1,0:T(8,128)(2,1)S(1)} %copy-done, bf16[96,64,128]{2,1,0:T(8,128)(2,1)} %gather_fusion.5), kind=kOutput, calls=%fused_computation.25 | convolution fusion | flops 201326592 | bytes 7864320 | tf_op jit(solution)/shard_map/ota,tab->otb/dot_general | solution.py:100
  139.4 4.1 %fusion.2 = f32[16,64,128]{2,0,1:T(8,128)} fusion(f32[64,96,128]{2,0,1:T(8,128)S(1)} %convolution_bitcast_fusion.1, f32[96]{0:T(128)S(1)} %copy-done.9, s32[96]{0:T(128)S(1)} %copy-done.6), kind=kOutput, calls=%fused_computation.10 | convolution fusion | flops 150998016 | bytes 3670784 | tf_op jit(solution)/shard_map/otb,tr->orb/dot_general | solution.py:107
  144.2 31.6 %all-to-all-done.1 = bf16[64,128,128]{2,0,1:T(8,128)(2,1)} async-done(((bf16[64,128,128]{2,0,1:T(8,128)(2,1)}), bf16[64,128,128]{2,0,1:T(8,128)(2,1)}, u32[]{:S(2)}, u32[]{:S(2)}) %all-to-all-start.1) | async-done | bytes 2097184 | tf_op jit(solution)/shard_map/all_to_all | solution.py:114
  175.8 2.9 %fusion.28 = bf16[16,64,128]{2,0,1:T(8,128)(2,1)S(1)} fusion(f32[16,64,128]{2,0,1:T(8,128)} %fusion.2, bf16[64,128,128]{2,0,1:T(8,128)(2,1)} %all-to-all-done.1, s32[128]{0:T(128)S(1)} %copy-done.8), kind=kOutput, calls=%fused_computation.33 | convolution fusion | flops 33818624 | bytes 2884096 | tf_op jit(solution)/shard_map/oqb,qr->orb/dot_general | solution.py:119
  185.9 8.8 %all-to-all-start.2 = ((f32[128,2,128]{2,1,0:T(2,128)}), f32[128,2,128]{2,1,0:T(2,128)S(1)}, u32[]{:S(2)}, u32[]{:S(2)}) async-start(f32[128,2,128]{2,1,0:T(2,128)} %bitcast.119), calls=%async_computation.2 | async-start | bytes 262144 | tf_op jit(solution)/shard_map/all_to_all | solution.py:34
  197.4 4.9 %collective-permute-start.7 = (bf16[64,2048]{1,0:T(8,128)(2,1)}, bf16[64,2048]{1,0:T(8,128)(2,1)}, u32[]{:S(2)}, u32[]{:S(2)}) collective-permute-start(bf16[64,2048]{1,0:T(8,128)(2,1)} %bitcast.106), channel_id=1, source_target_pairs={{0,2},{1,3},{2,0},{3,1},{4,6},{5,7},{6,4},{7,5},{8,10},{9,11},{10,... | collective-permute-start | bytes 786440 | tf_op jit(solution)/shard_map/ppermute | solution.py:27
  202.3 2.8 %collective-permute-start.8 = (bf16[64,2048]{1,0:T(8,128)(2,1)}, bf16[64,2048]{1,0:T(8,128)(2,1)}, u32[]{:S(2)}, u32[]{:S(2)}) collective-permute-start(bf16[64,2048]{1,0:T(8,128)(2,1)} %bitcast.106), channel_id=1, source_target_pairs={{0,3},{1,2},{2,1},{3,0},{4,7},{5,6},{6,5},{7,4},{8,11},{9,10},{10,... | collective-permute-start | bytes 786440 | tf_op jit(solution)/shard_map/ppermute | solution.py:27
  205.1 2.4 %all-to-all-done.2 = f32[128,2,128]{2,1,0:T(2,128)S(1)} async-done(((f32[128,2,128]{2,1,0:T(2,128)}), f32[128,2,128]{2,1,0:T(2,128)S(1)}, u32[]{:S(2)}, u32[]{:S(2)}) %all-to-all-start.2) | async-done | bytes 131104 | tf_op jit(solution)/shard_map/all_to_all | solution.py:34
  208.3 12.2 %all-to-all-start.3 = ((f32[128,2,128]{2,1,0:T(2,128)}), f32[128,2,128]{2,1,0:T(2,128)S(1)}, u32[]{:S(2)}, u32[]{:S(2)}) async-start(f32[128,2,128]{2,1,0:T(2,128)} %broadcast_in_dim.87), calls=%async_computation.3 | async-start | bytes 262144 | tf_op jit(solution)/shard_map/all_to_all | solution.py:37
  222.8 10.4 %all-to-all-done.3 = f32[128,2,128]{2,1,0:T(2,128)S(1)} async-done(((f32[128,2,128]{2,1,0:T(2,128)}), f32[128,2,128]{2,1,0:T(2,128)S(1)}, u32[]{:S(2)}, u32[]{:S(2)}) %all-to-all-start.3) | async-done | bytes 131104 | tf_op jit(solution)/shard_map/all_to_all | solution.py:37
  (82 shorter events, 36.0 us)
Async XLA Ops:
  0.6 45.5 %copy-start = (bf16[96,128,128]{2,1,0:T(8,128)(2,1)S(1)}, bf16[96,128,128]{2,1,0:T(8,128)(2,1)}, u32[]{:S(2)}) copy-start(bf16[96,128,128]{2,1,0:T(8,128)(2,1)} %param.16) | copy-start | bytes 9437188
  0.6 14.1 %collective-permute-start = (bf16[64,2048]{1,0:T(8,128)(2,1)}, bf16[64,2048]{1,0:T(8,128)(2,1)}, u32[]{:S(2)}, u32[]{:S(2)}) collective-permute-start(bf16[64,2048]{1,0:T(8,128)(2,1)} %param.13), channel_id=1, source_target_pairs={{0,1},{1,0},{2,3},{3,2},{4,5},{5,4},{6,7},{7,6},{8,9},{9,8},{10,11... | collective-permute-start | bytes 786440 | tf_op jit(solution)/shard_map/ppermute | solution.py:27
  4.9 9.6 %collective-permute-start.2 = (bf16[64,2048]{1,0:T(8,128)(2,1)}, bf16[64,2048]{1,0:T(8,128)(2,1)S(1)}, u32[]{:S(2)}, u32[]{:S(2)}) collective-permute-start(bf16[64,2048]{1,0:T(8,128)(2,1)} %param.13), channel_id=1, source_target_pairs={{0,3},{1,2},{2,1},{3,0},{4,7},{5,6},{6,5},{7,4},{8,11},{9,10},{10,... | collective-permute-start | bytes 786440 | tf_op jit(solution)/shard_map/ppermute | solution.py:27
  8.6 9.0 %collective-permute-start.1 = (bf16[64,2048]{1,0:T(8,128)(2,1)}, bf16[64,2048]{1,0:T(8,128)(2,1)}, u32[]{:S(2)}, u32[]{:S(2)}) collective-permute-start(bf16[64,2048]{1,0:T(8,128)(2,1)} %param.13), channel_id=1, source_target_pairs={{0,2},{1,3},{2,0},{3,1},{4,6},{5,7},{6,4},{7,5},{8,10},{9,11},{10,... | collective-permute-start | bytes 786440 | tf_op jit(solution)/shard_map/ppermute | solution.py:27
  14.5 3.1 %copy-start.2 = (bf16[64,2048]{1,0:T(8,128)(2,1)}, bf16[64,2048]{1,0:T(8,128)(2,1)S(1)}, u32[]{:S(2)}) copy-start(bf16[64,2048]{1,0:T(8,128)(2,1)S(1)} %collective-permute-done.2) | copy-start | bytes 786436
  21.1 24.7 %copy-start.6 = (s32[96]{0:T(128)S(1)}, s32[96]{0:T(128)}, u32[]{:S(2)}) copy-start(s32[96]{0:T(128)} %param.18) | copy-start | bytes 1156
  21.1 24.9 %copy-start.10 = (bf16[64]{0:T(256)(128)(2,1)S(1)}, bf16[64]{0:T(256)(128)(2,1)}, u32[]{:S(2)}) copy-start(bf16[64]{0:T(256)(128)(2,1)} %param.15) | copy-start | bytes 388
  21.1 24.9 %copy-start.7 = (s32[96]{0:T(128)S(1)}, s32[96]{0:T(128)}, u32[]{:S(2)}) copy-start(s32[96]{0:T(128)} %param.17) | copy-start | bytes 1156
  21.1 74.8 %all-to-all-start = ((bf16[64,128,128]{2,0,1:T(8,128)(2,1)}), bf16[64,128,128]{2,0,1:T(8,128)(2,1)}, u32[]{:S(2)}, u32[]{:S(2)}) async-start(bf16[64,128,128]{2,0,1:T(8,128)(2,1)} %bitcast.117), calls=%async_computation | async-start | bytes 4194304 | tf_op jit(solution)/shard_map/all_to_all | solution.py:76
  95.9 5.9 %copy-start.1 = (f32[64,16,128]{2,1,0:T(8,128)S(1)}, f32[64,16,128]{2,1,0:T(8,128)}, u32[]{:S(2)}) copy-start(f32[64,16,128]{2,1,0:T(8,128)} %fusion.25) | copy-start | bytes 1572868
  101.8 4.4 %copy-start.4 = (bf16[64,2048]{1,0:T(8,128)(2,1)S(1)}, bf16[64,2048]{1,0:T(8,128)(2,1)}, u32[]{:S(2)}) copy-start(bf16[64,2048]{1,0:T(8,128)(2,1)} %param.21) | copy-start | bytes 786436
  115.5 10.0 %copy-start.5 = (bf16[256,64]{0,1:T(8,128)(2,1)S(1)}, bf16[256,64]{0,1:T(8,128)(2,1)}, u32[]{:S(2)}) copy-start(bf16[256,64]{0,1:T(8,128)(2,1)} %param.14) | copy-start | bytes 98308
  115.5 60.4 %all-to-all-start.1 = ((bf16[64,128,128]{2,0,1:T(8,128)(2,1)}), bf16[64,128,128]{2,0,1:T(8,128)(2,1)}, u32[]{:S(2)}, u32[]{:S(2)}) async-start(bf16[64,128,128]{2,0,1:T(8,128)(2,1)} %convert_bitcast_fusion), calls=%async_computation.1 | async-start | bytes 4194304 | tf_op jit(solution)/shard_map/all_to_all | solution.py:114
  125.4 18.1 %collective-permute-start.3 = (bf16[256,64]{0,1:T(8,128)(2,1)S(1)}, bf16[256,64]{0,1:T(8,128)(2,1)S(1)}, u32[]{:S(2)}, u32[]{:S(2)}) collective-permute-start(bf16[256,64]{0,1:T(8,128)(2,1)S(1)} %copy-done.5), channel_id=1, source_target_pairs={{0,1},{1,0},{2,3},{3,2},{4,5},{5,4},{6,7},{7,6},{8,9},{9,8},{10,11... | collective-permute-start | bytes 98312 | tf_op jit(solution)/shard_map/ppermute | solution.py:27
  127.4 16.1 %collective-permute-start.4 = (bf16[256,64]{0,1:T(8,128)(2,1)S(1)}, bf16[256,64]{0,1:T(8,128)(2,1)S(1)}, u32[]{:S(2)}, u32[]{:S(2)}) collective-permute-start(bf16[256,64]{0,1:T(8,128)(2,1)S(1)} %copy-done.5), channel_id=1, source_target_pairs={{0,2},{1,3},{2,0},{3,1},{4,6},{5,7},{6,4},{7,5},{8,10},{9,11},{10,... | collective-permute-start | bytes 98312 | tf_op jit(solution)/shard_map/ppermute | solution.py:27
  132.3 11.2 %collective-permute-start.5 = (bf16[256,64]{0,1:T(8,128)(2,1)S(1)}, bf16[256,64]{0,1:T(8,128)(2,1)S(1)}, u32[]{:S(2)}, u32[]{:S(2)}) collective-permute-start(bf16[256,64]{0,1:T(8,128)(2,1)S(1)} %copy-done.5), channel_id=1, source_target_pairs={{0,3},{1,2},{2,1},{3,0},{4,7},{5,6},{6,5},{7,4},{8,11},{9,10},{10,... | collective-permute-start | bytes 98312 | tf_op jit(solution)/shard_map/ppermute | solution.py:27
  137.0 2.4 %copy-start.9 = (f32[96]{0:T(128)S(1)}, f32[96]{0:T(128)}, u32[]{:S(2)}) copy-start(f32[96]{0:T(128)} %fusion.78) | copy-start | bytes 1156
  139.4 36.4 %copy-start.8 = (s32[128]{0:T(128)S(1)}, s32[128]{0:T(128)}, u32[]{:S(2)}) copy-start(s32[128]{0:T(128)} %param.20) | copy-start | bytes 1540
  185.2 0.7 copy-start.3
  185.9 21.6 %all-to-all-start.2 = ((f32[128,2,128]{2,1,0:T(2,128)}), f32[128,2,128]{2,1,0:T(2,128)S(1)}, u32[]{:S(2)}, u32[]{:S(2)}) async-start(f32[128,2,128]{2,1,0:T(2,128)} %bitcast.119), calls=%async_computation.2 | async-start | bytes 262144 | tf_op jit(solution)/shard_map/all_to_all | solution.py:34
  195.5 25.0 %collective-permute-start.6 = (bf16[64,2048]{1,0:T(8,128)(2,1)}, bf16[64,2048]{1,0:T(8,128)(2,1)S(1)}, u32[]{:S(2)}, u32[]{:S(2)}) collective-permute-start(bf16[64,2048]{1,0:T(8,128)(2,1)} %bitcast.106), channel_id=1, source_target_pairs={{0,1},{1,0},{2,3},{3,2},{4,5},{5,4},{6,7},{7,6},{8,9},{9,8},{10,11... | collective-permute-start | bytes 786440 | tf_op jit(solution)/shard_map/ppermute | solution.py:27
  197.4 23.1 %collective-permute-start.7 = (bf16[64,2048]{1,0:T(8,128)(2,1)}, bf16[64,2048]{1,0:T(8,128)(2,1)}, u32[]{:S(2)}, u32[]{:S(2)}) collective-permute-start(bf16[64,2048]{1,0:T(8,128)(2,1)} %bitcast.106), channel_id=1, source_target_pairs={{0,2},{1,3},{2,0},{3,1},{4,6},{5,7},{6,4},{7,5},{8,10},{9,11},{10,... | collective-permute-start | bytes 786440 | tf_op jit(solution)/shard_map/ppermute | solution.py:27
  202.3 18.2 %collective-permute-start.8 = (bf16[64,2048]{1,0:T(8,128)(2,1)}, bf16[64,2048]{1,0:T(8,128)(2,1)}, u32[]{:S(2)}, u32[]{:S(2)}) collective-permute-start(bf16[64,2048]{1,0:T(8,128)(2,1)} %bitcast.106), channel_id=1, source_target_pairs={{0,3},{1,2},{2,1},{3,0},{4,7},{5,6},{6,5},{7,4},{8,11},{9,10},{10,... | collective-permute-start | bytes 786440 | tf_op jit(solution)/shard_map/ppermute | solution.py:27
  208.3 24.9 %all-to-all-start.3 = ((f32[128,2,128]{2,1,0:T(2,128)}), f32[128,2,128]{2,1,0:T(2,128)S(1)}, u32[]{:S(2)}, u32[]{:S(2)}) async-start(f32[128,2,128]{2,1,0:T(2,128)} %broadcast_in_dim.87), calls=%async_computation.3 | async-start | bytes 262144 | tf_op jit(solution)/shard_map/all_to_all | solution.py:37

commit v11 on v10

--- a/solution.py
+++ b/solution.py
@@ -28,14 +28,15 @@
     return received
 
 
-def scatter_gather_sum(values, axis, size):
+def scatter_gather_sum(values, axis, size, rider):
     rows, cols = values.shape
     chunk = rows // size
     gathered = lax.all_to_all(values.reshape(size, chunk, cols), axis, 0, 0, tiled=True)
     reduced = jnp.sum(gathered, axis=0)
+    reduced, rider = lax.optimization_barrier((reduced, rider))
     spread = jnp.broadcast_to(reduced[None], (size, chunk, cols))
     total = lax.all_to_all(spread, axis, 0, 0, tiled=True)
-    return total.reshape(rows, cols)
+    return total.reshape(rows, cols), rider
 
 
 def per_device(
@@ -82,7 +83,8 @@
     picked = jnp.take(hid_blocks, jnp.minimum(tile_col, blocks - 1), axis=1, mode="clip")
     products = jnp.einsum("otb,tab->ota", picked, adj_tiles, preferred_element_type=jnp.float32)
     summed_local = jnp.einsum("ota,tr->ora", products, row_place, precision=lax.Precision.HIGHEST)
-    summed_local, incoming = lax.optimization_barrier((summed_local, incoming))
+    whole = jnp.concatenate(pieces, axis=0)
+    summed_local, whole, incoming = lax.optimization_barrier((summed_local, whole, incoming))
     far_place = (slot_rows[:, None] == jnp.arange(blocks)[None, :]).astype(jnp.float32) * has_hit[
         :, None
     ].astype(jnp.float32)
@@ -121,14 +123,8 @@
     )
     grad_hidden = grad_sum.reshape(feat_rows, node_rows).astype(jnp.bfloat16)
     norm_scale = 1.0 / math.sqrt(domains * node_rows)
-    weight_part = jnp.concatenate(
-        [
-            lax.dot_general(
-                grad_hidden, piece, (((1,), (1,)), ((), ())), preferred_element_type=jnp.float32
-            )
-            for piece in pieces
-        ],
-        axis=1,
+    weight_part = lax.dot_general(
+        grad_hidden, whole, (((1,), (1,)), ((), ())), preferred_element_type=jnp.float32
     )
     bias_part = jnp.sum(grad_pre, axis=1)
     lanes = 128
@@ -137,12 +133,12 @@
     packed = jnp.zeros((pack_rows, lanes), jnp.float32)
     packed = packed.at[:weight_rows].set(weight_part.reshape(weight_rows, lanes))
     packed = packed.at[weight_rows, : bias_part.shape[0]].set(bias_part)
-    packed = scatter_gather_sum(packed, "dom", domains)
+    packed, late_grad = scatter_gather_sum(packed, "dom", domains, grad_hidden)
     summed_weight = packed[:weight_rows].reshape(feat_rows, parts, in_rows)
     summed_weight = jnp.take(summed_weight, order, axis=1, mode="clip").reshape(feat_rows, parts * in_rows)
     grad_weight = summed_weight.T * norm_scale
     grad_bias = packed[weight_rows, : bias_part.shape[0]] * norm_scale
-    all_grad = jnp.concatenate(exchange_order(grad_hidden, "feat", parts, parts), axis=0)
+    all_grad = jnp.concatenate(exchange_order(late_grad, "feat", parts, parts), axis=0)
     my_rows = lax.dynamic_slice_in_dim(
         full_weight, lax.axis_index("feat") * feat_rows, feat_rows, 0
     )

time: 237 us -> 235 us (level)
  waiting for transfers between devices: 83 us -> 91.9 us
  starting transfers between devices: 84.2 us -> 77.6 us
  matrix products: 43.7 us -> 38.1 us
  other arithmetic: 4.44 us -> 6.82 us
    all_to_all x1, waiting for transfers between devices: 2.37 us -> 12 us  [scatter_gather_sum(): lax.all_to_all(values.reshape(size, chunk, cols), axis, 0, 0, tiled=True)]
    ppermute x9, waiting for transfers between devices: 1.69 us -> 9.22 us  [exchange_order(): received.append(lax.ppermute(values, axis, pairs))]
    all_to_all x1, waiting for transfers between devices: 10.4 us -> 3.23 us  [scatter_gather_sum(): total = lax.all_to_all(spread, axis, 0, 0, tiled=True)]
    all_to_all x1, starting transfers between devices: 12.2 us -> 5.56 us  [scatter_gather_sum(): total = lax.all_to_all(spread, axis, 0, 0, tiled=True)]
    dot_general x4 -> x1, matrix products: 4.68 us -> 0.44 us  [per_device(): lax.dot_general(grad_hidden, whole, (((1,), (1,)), ((), ())), preferred_e...]
  transfers between devices with their start and end apart: 13 -> 13, of which waited for: 5 -> 7; matrix products, arithmetic and copies ran while one was open for 13% -> 13% of each run, Pallas kernels for 0% -> 0%
where the time goes in v11:
time: 235 us; the launch traced here: 234 us
  waiting for transfers between devices  91.9 us (39%)
  starting transfers between devices  77.6 us (33%)
  matrix products  38.1 us (16%)
  local copies, waits for them, and re-layouts  18.3 us (8%)
  other arithmetic  6.82 us (3%)
    all_to_all x1, waiting for transfers between devices, per_device(): lax.all_to_all(outgoing, 'dom', split_axis=1, concat_axis=1, tiled=True)  35.9 us
    all_to_all x1, waiting for transfers between devices, per_device(): lax.all_to_all(out_parts, 'dom', split_axis=1, concat_axis=1, tiled=True)  31.6 us
    ppermute x9, starting transfers between devices, exchange_order(): received.append(lax.ppermute(values, axis, pairs))  29.7 us
    all_to_all x1, starting transfers between devices, per_device(): lax.all_to_all(outgoing, 'dom', split_axis=1, concat_axis=1, tiled=True)  24 us
    all_to_all x1, waiting for transfers between devices, scatter_gather_sum(): lax.all_to_all(values.reshape(size, chunk, cols), axis, 0, 0, tiled=True)  12 us
    all_to_all x1, starting transfers between devices, per_device(): lax.all_to_all(out_parts, 'dom', split_axis=1, concat_axis=1, tiled=True)  9.44 us
    ppermute x9, waiting for transfers between devices, exchange_order(): received.append(lax.ppermute(values, axis, pairs))  9.22 us
    all_to_all x1, starting transfers between devices, scatter_gather_sum(): lax.all_to_all(values.reshape(size, chunk, cols), axis, 0, 0, tiled=True)  8.85 us
  transfers between devices with their start and end apart: 13, of which 7 were waited for; matrix products, arithmetic and copies ran while one was open for 13% of the time, Pallas kernels for 0%

profile of v11, /device:TPU:1, one launch (start us, length us, event | category | flops | bytes accessed | tf_op | source)
XLA Modules:
  0.0 234.5 jit_solution(12804099327952471786)
XLA Ops:
  0.6 4.2 %collective-permute-start = (bf16[64,2048]{1,0:T(8,128)(2,1)}, bf16[64,2048]{1,0:T(8,128)(2,1)}, u32[]{:S(2)}, u32[]{:S(2)}) collective-permute-start(bf16[64,2048]{1,0:T(8,128)(2,1)} %param.13), channel_id=1, source_target_pairs={{0,1},{1,0},{2,3},{3,2},{4,5},{5,4},{6,7},{7,6},{8,9},{9,8},{10,11... | collective-permute-start | bytes 786440 | tf_op jit(solution)/shard_map/ppermute | solution.py:27
  4.9 3.7 %collective-permute-start.2 = (bf16[64,2048]{1,0:T(8,128)(2,1)}, bf16[64,2048]{1,0:T(8,128)(2,1)S(1)}, u32[]{:S(2)}, u32[]{:S(2)}) collective-permute-start(bf16[64,2048]{1,0:T(8,128)(2,1)} %param.13), channel_id=1, source_target_pairs={{0,3},{1,2},{2,1},{3,0},{4,7},{5,6},{6,5},{7,4},{8,11},{9,10},{10,... | collective-permute-start | bytes 786440 | tf_op jit(solution)/shard_map/ppermute | solution.py:27
  8.6 2.6 %collective-permute-start.1 = (bf16[64,2048]{1,0:T(8,128)(2,1)}, bf16[64,2048]{1,0:T(8,128)(2,1)}, u32[]{:S(2)}, u32[]{:S(2)}) collective-permute-start(bf16[64,2048]{1,0:T(8,128)(2,1)} %param.13), channel_id=1, source_target_pairs={{0,2},{1,3},{2,0},{3,1},{4,6},{5,7},{6,4},{7,5},{8,10},{9,11},{10,... | collective-permute-start | bytes 786440 | tf_op jit(solution)/shard_map/ppermute | solution.py:27
  21.1 24.0 %all-to-all-start = ((bf16[64,128,128]{2,0,1:T(8,128)(2,1)}), bf16[64,128,128]{2,0,1:T(8,128)(2,1)}, u32[]{:S(2)}, u32[]{:S(2)}) async-start(bf16[64,128,128]{2,0,1:T(8,128)(2,1)} %bitcast.105), calls=%async_computation | async-start | bytes 4194304 | tf_op jit(solution)/shard_map/all_to_all | solution.py:77
  46.1 3.0 %gather_fusion.3 = bf16[128,128,128]{2,1,0:T(8,128)(2,1)} fusion(bf16[96,128,128]{2,1,0:T(8,128)(2,1)S(1)} %copy-done, s32[1024]{0:T(1024)S(1)} %pad_clamp_fusion.2), kind=kCustom, calls=%fused_computation.3 | custom fusion | bytes 8389120 | tf_op jit(solution)/shard_map/jit(_take)/gather | solution.py:60
  51.2 2.4 %pad_maximum_fusion = bf16[256,2048]{1,0:T(8,128)(2,1)} fusion(bf16[64,2048]{1,0:T(8,128)(2,1)} %copy-done.4, bf16[64,2048]{1,0:T(8,128)(2,1)} %collective-permute-done.1, bf16[64,2048]{1,0:T(8,128)(2,1)} %collective-permute-done, bf16[64,2048]{1,0:T(8,128)(2,1)} %param.13), kind=kLoop, calls=%fused_computation.34 | loop fusion | flops 4194304 | bytes 2097152 | tf_op jit(solution)/shard_map/concatenate | solution.py:86
  55.9 4.2 %fusion.22 = f32[64,16,128]{2,1,0:T(8,128)} fusion(f32[64,96,128]{2,0,1:T(8,128)S(1)} %convolution_bitcast_fusion.2, f32[96]{0:T(128)S(1)} %and_convert_fusion, s32[96]{0:T(128)S(1)} %copy-done.8), kind=kOutput, calls=%fused_computation.31 | convolution fusion | flops 150998016 | bytes 3670784 | tf_op jit(solution)/shard_map/ota,tr->ora/dot_general | solution.py:85
  60.0 35.9 %all-to-all-done = bf16[64,128,128]{2,0,1:T(8,128)(2,1)} async-done(((bf16[64,128,128]{2,0,1:T(8,128)(2,1)}), bf16[64,128,128]{2,0,1:T(8,128)(2,1)}, u32[]{:S(2)}, u32[]{:S(2)}) %all-to-all-start) | async-done | bytes 2097184 | tf_op jit(solution)/shard_map/all_to_all | solution.py:77
  95.9 5.8 %convolution_bitcast_fusion = f32[64,128,128]{2,0,1:T(8,128)S(1)} fusion(bf16[64,128,128]{2,0,1:T(8,128)(2,1)} %all-to-all-done, bf16[128,128,128]{2,1,0:T(8,128)(2,1)} %gather_fusion.3, pred[128]{0:T(512)(128)(4,1)S(1)} %fusion.46), kind=kOutput, calls=%fused_computation.19 | convolution fusion | flops 270532608 | bytes 10485888 | tf_op jit(solution)/shard_map/oqb,qab->oqa/dot_general | solution.py:91
  101.7 4.4 %fusion.16 = f32[64,16,128]{2,1,0:T(8,128)S(1)} fusion(f32[64,128,128]{2,0,1:T(8,128)S(1)} %convolution_bitcast_fusion, f32[128]{0:T(128)S(1)} %convert_element_type.58, s32[128]{0:T(128)S(1)} %get-tuple-element.44), kind=kOutput, calls=%fused_computation.29 | convolution fusion | flops 201330688 | bytes 4719616 | tf_op jit(solution)/shard_map/oqa,qr->ora/dot_general | solution.py:94
  110.0 5.5 %convert_bitcast_fusion = bf16[64,128,128]{2,0,1:T(8,128)(2,1)} fusion(bf16[128,64,128]{2,1,0:T(8,128)(2,1)} %gather_fusion.4, bf16[128,128,128]{2,1,0:T(8,128)(2,1)} %gather_fusion.3, pred[128]{0:T(512)(128)(4,1)S(1)} %fusion.46), kind=kOutput, calls=%fused_computation.24 | convolution fusion | flops 271581184 | bytes 8388736 | tf_op jit(solution)/shard_map/oqa,qab->oqb/dot_general | solution.py:113
  115.5 9.4 %all-to-all-start.1 = ((bf16[64,128,128]{2,0,1:T(8,128)(2,1)}), bf16[64,128,128]{2,0,1:T(8,128)(2,1)}, u32[]{:S(2)}, u32[]{:S(2)}) async-start(bf16[64,128,128]{2,0,1:T(8,128)(2,1)} %convert_bitcast_fusion), calls=%async_computation.1 | async-start | bytes 4194304 | tf_op jit(solution)/shard_map/all_to_all | solution.py:116
  127.4 4.9 %collective-permute-start.4 = (bf16[256,64]{0,1:T(8,128)(2,1)S(1)}, bf16[256,64]{0,1:T(8,128)(2,1)S(1)}, u32[]{:S(2)}, u32[]{:S(2)}) collective-permute-start(bf16[256,64]{0,1:T(8,128)(2,1)S(1)} %copy-done.7), channel_id=1, source_target_pairs={{0,2},{1,3},{2,0},{3,1},{4,6},{5,7},{6,4},{7,5},{8,10},{9,11},{10,... | collective-permute-start | bytes 98312 | tf_op jit(solution)/shard_map/ppermute | solution.py:27
  132.3 2.8 %collective-permute-start.5 = (bf16[256,64]{0,1:T(8,128)(2,1)S(1)}, bf16[256,64]{0,1:T(8,128)(2,1)S(1)}, u32[]{:S(2)}, u32[]{:S(2)}) collective-permute-start(bf16[256,64]{0,1:T(8,128)(2,1)S(1)} %copy-done.7), channel_id=1, source_target_pairs={{0,3},{1,2},{2,1},{3,0},{4,7},{5,6},{6,5},{7,4},{8,11},{9,10},{10,... | collective-permute-start | bytes 98312 | tf_op jit(solution)/shard_map/ppermute | solution.py:27
  139.4 4.1 %fusion.2 = f32[16,64,128]{2,0,1:T(8,128)} fusion(f32[64,96,128]{2,0,1:T(8,128)S(1)} %convolution_bitcast_fusion.1, f32[96]{0:T(128)S(1)} %copy-done.11, s32[96]{0:T(128)S(1)} %copy-done.9), kind=kOutput, calls=%fused_computation.10 | convolution fusion | flops 150998016 | bytes 3670784 | tf_op jit(solution)/shard_map/otb,tr->orb/dot_general | solution.py:109
  144.2 31.6 %all-to-all-done.1 = bf16[64,128,128]{2,0,1:T(8,128)(2,1)} async-done(((bf16[64,128,128]{2,0,1:T(8,128)(2,1)}), bf16[64,128,128]{2,0,1:T(8,128)(2,1)}, u32[]{:S(2)}, u32[]{:S(2)}) %all-to-all-start.1) | async-done | bytes 2097184 | tf_op jit(solution)/shard_map/all_to_all | solution.py:116
  175.8 3.0 %fusion.25 = bf16[16,64,128]{2,0,1:T(8,128)(2,1)S(1)} fusion(f32[16,64,128]{2,0,1:T(8,128)} %fusion.2, bf16[64,128,128]{2,0,1:T(8,128)(2,1)} %all-to-all-done.1, s32[128]{0:T(128)S(1)} %copy-done.10), kind=kOutput, calls=%fused_computation.32 | convolution fusion | flops 33818624 | bytes 2884096 | tf_op jit(solution)/shard_map/oqb,qr->orb/dot_general | solution.py:121
  181.6 8.8 %all-to-all-start.2 = ((f32[128,2,128]{2,1,0:T(2,128)}), f32[128,2,128]{2,1,0:T(2,128)S(1)}, u32[]{:S(2)}, u32[]{:S(2)}) async-start(f32[128,2,128]{2,1,0:T(2,128)} %bitcast.109), calls=%async_computation.2 | async-start | bytes 262144 | tf_op jit(solution)/shard_map/all_to_all | solution.py:34
  191.3 12.0 %all-to-all-done.2 = f32[128,2,128]{2,1,0:T(2,128)S(1)} async-done(((f32[128,2,128]{2,1,0:T(2,128)}), f32[128,2,128]{2,1,0:T(2,128)S(1)}, u32[]{:S(2)}, u32[]{:S(2)}) %all-to-all-start.2) | async-done | bytes 131104 | tf_op jit(solution)/shard_map/all_to_all | solution.py:34
  204.1 5.6 %all-to-all-start.3 = ((f32[128,2,128]{2,1,0:T(2,128)}), f32[128,2,128]{2,1,0:T(2,128)S(1)}, u32[]{:S(2)}, u32[]{:S(2)}) async-start(f32[128,2,128]{2,1,0:T(2,128)} %broadcast_in_dim.87), calls=%async_computation.3 | async-start | bytes 262144 | tf_op jit(solution)/shard_map/all_to_all | solution.py:38
  211.6 4.9 %collective-permute-start.7 = (bf16[64,2048]{1,0:T(8,128)(2,1)}, bf16[64,2048]{1,0:T(8,128)(2,1)}, u32[]{:S(2)}, u32[]{:S(2)}) collective-permute-start(bf16[64,2048]{1,0:T(8,128)(2,1)} %bitcast.112), channel_id=1, source_target_pairs={{0,2},{1,3},{2,0},{3,1},{4,6},{5,7},{6,4},{7,5},{8,10},{9,11},{10,... | collective-permute-start | bytes 786440 | tf_op jit(solution)/shard_map/ppermute | solution.py:27
  216.5 2.8 %collective-permute-start.8 = (bf16[64,2048]{1,0:T(8,128)(2,1)}, bf16[64,2048]{1,0:T(8,128)(2,1)}, u32[]{:S(2)}, u32[]{:S(2)}) collective-permute-start(bf16[64,2048]{1,0:T(8,128)(2,1)} %bitcast.113), channel_id=1, source_target_pairs={{0,3},{1,2},{2,1},{3,0},{4,7},{5,6},{6,5},{7,4},{8,11},{9,10},{10,... | collective-permute-start | bytes 786440 | tf_op jit(solution)/shard_map/ppermute | solution.py:27
  219.2 3.2 %all-to-all-done.3 = f32[128,2,128]{2,1,0:T(2,128)S(1)} async-done(((f32[128,2,128]{2,1,0:T(2,128)}), f32[128,2,128]{2,1,0:T(2,128)S(1)}, u32[]{:S(2)}, u32[]{:S(2)}) %all-to-all-start.3) | async-done | bytes 131104 | tf_op jit(solution)/shard_map/all_to_all | solution.py:38
  225.8 6.3 %collective-permute-done.8 = bf16[64,2048]{1,0:T(8,128)(2,1)} collective-permute-done((bf16[64,2048]{1,0:T(8,128)(2,1)}, bf16[64,2048]{1,0:T(8,128)(2,1)}, u32[]{:S(2)}, u32[]{:S(2)}) %collective-permute-start.8) | collective-permute-done | bytes 262176 | tf_op jit(solution)/shard_map/ppermute | solution.py:27
  (85 shorter events, 37.7 us)
Async XLA Ops:
  0.6 45.5 %copy-start = (bf16[96,128,128]{2,1,0:T(8,128)(2,1)S(1)}, bf16[96,128,128]{2,1,0:T(8,128)(2,1)}, u32[]{:S(2)}) copy-start(bf16[96,128,128]{2,1,0:T(8,128)(2,1)} %param.16) | copy-start | bytes 9437188
  0.6 14.1 %collective-permute-start = (bf16[64,2048]{1,0:T(8,128)(2,1)}, bf16[64,2048]{1,0:T(8,128)(2,1)}, u32[]{:S(2)}, u32[]{:S(2)}) collective-permute-start(bf16[64,2048]{1,0:T(8,128)(2,1)} %param.13), channel_id=1, source_target_pairs={{0,1},{1,0},{2,3},{3,2},{4,5},{5,4},{6,7},{7,6},{8,9},{9,8},{10,11... | collective-permute-start | bytes 786440 | tf_op jit(solution)/shard_map/ppermute | solution.py:27
  4.9 9.6 %collective-permute-start.2 = (bf16[64,2048]{1,0:T(8,128)(2,1)}, bf16[64,2048]{1,0:T(8,128)(2,1)S(1)}, u32[]{:S(2)}, u32[]{:S(2)}) collective-permute-start(bf16[64,2048]{1,0:T(8,128)(2,1)} %param.13), channel_id=1, source_target_pairs={{0,3},{1,2},{2,1},{3,0},{4,7},{5,6},{6,5},{7,4},{8,11},{9,10},{10,... | collective-permute-start | bytes 786440 | tf_op jit(solution)/shard_map/ppermute | solution.py:27
  8.6 9.0 %collective-permute-start.1 = (bf16[64,2048]{1,0:T(8,128)(2,1)}, bf16[64,2048]{1,0:T(8,128)(2,1)}, u32[]{:S(2)}, u32[]{:S(2)}) collective-permute-start(bf16[64,2048]{1,0:T(8,128)(2,1)} %param.13), channel_id=1, source_target_pairs={{0,2},{1,3},{2,0},{3,1},{4,6},{5,7},{6,4},{7,5},{8,10},{9,11},{10,... | collective-permute-start | bytes 786440 | tf_op jit(solution)/shard_map/ppermute | solution.py:27
  14.5 3.1 %copy-start.4 = (bf16[64,2048]{1,0:T(8,128)(2,1)}, bf16[64,2048]{1,0:T(8,128)(2,1)S(1)}, u32[]{:S(2)}) copy-start(bf16[64,2048]{1,0:T(8,128)(2,1)S(1)} %collective-permute-done.2) | copy-start | bytes 786436
  21.1 24.7 %copy-start.9 = (s32[96]{0:T(128)S(1)}, s32[96]{0:T(128)}, u32[]{:S(2)}) copy-start(s32[96]{0:T(128)} %param.18) | copy-start | bytes 1156
  21.1 24.9 %copy-start.12 = (bf16[64]{0:T(256)(128)(2,1)S(1)}, bf16[64]{0:T(256)(128)(2,1)}, u32[]{:S(2)}) copy-start(bf16[64]{0:T(256)(128)(2,1)} %param.15) | copy-start | bytes 388
  21.1 24.9 %copy-start.8 = (s32[96]{0:T(128)S(1)}, s32[96]{0:T(128)}, u32[]{:S(2)}) copy-start(s32[96]{0:T(128)} %param.17) | copy-start | bytes 1156
  21.1 74.8 %all-to-all-start = ((bf16[64,128,128]{2,0,1:T(8,128)(2,1)}), bf16[64,128,128]{2,0,1:T(8,128)(2,1)}, u32[]{:S(2)}, u32[]{:S(2)}) async-start(bf16[64,128,128]{2,0,1:T(8,128)(2,1)} %bitcast.105), calls=%async_computation | async-start | bytes 4194304 | tf_op jit(solution)/shard_map/all_to_all | solution.py:77
  51.2 2.4 %copy-start.1 = (bf16[96,64,128]{2,1,0:T(8,128)(2,1)S(1)}, bf16[96,64,128]{2,1,0:T(8,128)(2,1)}, u32[]{:S(2)}) copy-start(bf16[96,64,128]{2,1,0:T(8,128)(2,1)} %gather_fusion.1) | copy-start | bytes 4718596
  101.7 4.4 %copy-start.3 = (f32[64,16,128]{2,1,0:T(8,128)S(1)}, f32[64,16,128]{2,1,0:T(8,128)}, u32[]{:S(2)}) copy-start(f32[64,16,128]{2,1,0:T(8,128)} %fusion.22) | copy-start | bytes 1572868
  101.7 4.4 %copy-start.6 = (bf16[64,2048]{1,0:T(8,128)(2,1)S(1)}, bf16[64,2048]{1,0:T(8,128)(2,1)}, u32[]{:S(2)}) copy-start(bf16[64,2048]{1,0:T(8,128)(2,1)} %param.21) | copy-start | bytes 786436
  115.5 10.0 %copy-start.7 = (bf16[256,64]{0,1:T(8,128)(2,1)S(1)}, bf16[256,64]{0,1:T(8,128)(2,1)}, u32[]{:S(2)}) copy-start(bf16[256,64]{0,1:T(8,128)(2,1)} %param.14) | copy-start | bytes 98308
  115.5 60.4 %all-to-all-start.1 = ((bf16[64,128,128]{2,0,1:T(8,128)(2,1)}), bf16[64,128,128]{2,0,1:T(8,128)(2,1)}, u32[]{:S(2)}, u32[]{:S(2)}) async-start(bf16[64,128,128]{2,0,1:T(8,128)(2,1)} %convert_bitcast_fusion), calls=%async_computation.1 | async-start | bytes 4194304 | tf_op jit(solution)/shard_map/all_to_all | solution.py:116
  125.4 18.1 %collective-permute-start.3 = (bf16[256,64]{0,1:T(8,128)(2,1)S(1)}, bf16[256,64]{0,1:T(8,128)(2,1)S(1)}, u32[]{:S(2)}, u32[]{:S(2)}) collective-permute-start(bf16[256,64]{0,1:T(8,128)(2,1)S(1)} %copy-done.7), channel_id=1, source_target_pairs={{0,1},{1,0},{2,3},{3,2},{4,5},{5,4},{6,7},{7,6},{8,9},{9,8},{10,11... | collective-permute-start | bytes 98312 | tf_op jit(solution)/shard_map/ppermute | solution.py:27
  127.4 16.1 %collective-permute-start.4 = (bf16[256,64]{0,1:T(8,128)(2,1)S(1)}, bf16[256,64]{0,1:T(8,128)(2,1)S(1)}, u32[]{:S(2)}, u32[]{:S(2)}) collective-permute-start(bf16[256,64]{0,1:T(8,128)(2,1)S(1)} %copy-done.7), channel_id=1, source_target_pairs={{0,2},{1,3},{2,0},{3,1},{4,6},{5,7},{6,4},{7,5},{8,10},{9,11},{10,... | collective-permute-start | bytes 98312 | tf_op jit(solution)/shard_map/ppermute | solution.py:27
  132.3 11.2 %collective-permute-start.5 = (bf16[256,64]{0,1:T(8,128)(2,1)S(1)}, bf16[256,64]{0,1:T(8,128)(2,1)S(1)}, u32[]{:S(2)}, u32[]{:S(2)}) collective-permute-start(bf16[256,64]{0,1:T(8,128)(2,1)S(1)} %copy-done.7), channel_id=1, source_target_pairs={{0,3},{1,2},{2,1},{3,0},{4,7},{5,6},{6,5},{7,4},{8,11},{9,10},{10,... | collective-permute-start | bytes 98312 | tf_op jit(solution)/shard_map/ppermute | solution.py:27
  139.4 36.5 %copy-start.10 = (s32[128]{0:T(128)S(1)}, s32[128]{0:T(128)}, u32[]{:S(2)}) copy-start(s32[128]{0:T(128)} %param.20) | copy-start | bytes 1540
  175.8 3.0 %copy-start.2 = (bf16[256,2048]{1,0:T(8,128)(2,1)S(1)}, bf16[256,2048]{1,0:T(8,128)(2,1)}, u32[]{:S(2)}) copy-start(bf16[256,2048]{1,0:T(8,128)(2,1)} %pad_maximum_fusion) | copy-start | bytes 3145732
  181.6 21.6 %all-to-all-start.2 = ((f32[128,2,128]{2,1,0:T(2,128)}), f32[128,2,128]{2,1,0:T(2,128)S(1)}, u32[]{:S(2)}, u32[]{:S(2)}) async-start(f32[128,2,128]{2,1,0:T(2,128)} %bitcast.109), calls=%async_computation.2 | async-start | bytes 262144 | tf_op jit(solution)/shard_map/all_to_all | solution.py:34
  204.1 18.4 %all-to-all-start.3 = ((f32[128,2,128]{2,1,0:T(2,128)}), f32[128,2,128]{2,1,0:T(2,128)S(1)}, u32[]{:S(2)}, u32[]{:S(2)}) async-start(f32[128,2,128]{2,1,0:T(2,128)} %broadcast_in_dim.87), calls=%async_computation.3 | async-start | bytes 262144 | tf_op jit(solution)/shard_map/all_to_all | solution.py:38
  209.6 15.0 %collective-permute-start.6 = (bf16[64,2048]{1,0:T(8,128)(2,1)}, bf16[64,2048]{1,0:T(8,128)(2,1)}, u32[]{:S(2)}, u32[]{:S(2)}) collective-permute-start(bf16[64,2048]{1,0:T(8,128)(2,1)} %bitcast.111), channel_id=1, source_target_pairs={{0,1},{1,0},{2,3},{3,2},{4,5},{5,4},{6,7},{7,6},{8,9},{9,8},{10,11... | collective-permute-start | bytes 786440 | tf_op jit(solution)/shard_map/ppermute | solution.py:27
  211.6 14.3 %collective-permute-start.7 = (bf16[64,2048]{1,0:T(8,128)(2,1)}, bf16[64,2048]{1,0:T(8,128)(2,1)}, u32[]{:S(2)}, u32[]{:S(2)}) collective-permute-start(bf16[64,2048]{1,0:T(8,128)(2,1)} %bitcast.112), channel_id=1, source_target_pairs={{0,2},{1,3},{2,0},{3,1},{4,6},{5,7},{6,4},{7,5},{8,10},{9,11},{10,... | collective-permute-start | bytes 786440 | tf_op jit(solution)/shard_map/ppermute | solution.py:27
  216.5 15.7 %collective-permute-start.8 = (bf16[64,2048]{1,0:T(8,128)(2,1)}, bf16[64,2048]{1,0:T(8,128)(2,1)}, u32[]{:S(2)}, u32[]{:S(2)}) collective-permute-start(bf16[64,2048]{1,0:T(8,128)(2,1)} %bitcast.113), channel_id=1, source_target_pairs={{0,3},{1,2},{2,1},{3,0},{4,7},{5,6},{6,5},{7,4},{8,11},{9,10},{10,... | collective-permute-start | bytes 786440 | tf_op jit(solution)/shard_map/ppermute | solution.py:27
  (2 other events, 3.0 us)

commit v12 on v11

--- a/solution.py
+++ b/solution.py
@@ -117,9 +117,8 @@
     late_weight, out_parts = lax.optimization_barrier((weight, out_parts))
     full_weight = jnp.concatenate(exchange_order(late_weight, "feat", parts, parts), axis=1)
     full_weight, in_parts = lax.optimization_barrier((full_weight, in_parts))
-    remote_sum = in_parts.astype(jnp.float32)
     grad_sum = own_sum + jnp.einsum(
-        "oqb,qr->orb", remote_sum, recv_place, precision=lax.Precision.HIGHEST
+        "oqb,qr->orb", in_parts, recv_place.astype(jnp.bfloat16), preferred_element_type=jnp.float32
     )
     grad_hidden = grad_sum.reshape(feat_rows, node_rows).astype(jnp.bfloat16)
     norm_scale = 1.0 / math.sqrt(domains * node_rows)
@@ -138,7 +137,12 @@
     summed_weight = jnp.take(summed_weight, order, axis=1, mode="clip").reshape(feat_rows, parts * in_rows)
     grad_weight = summed_weight.T * norm_scale
     grad_bias = packed[weight_rows, : bias_part.shape[0]] * norm_scale
-    all_grad = jnp.concatenate(exchange_order(late_grad, "feat", parts, parts), axis=0)
+    grad_pieces = [grad_hidden]
+    for offset in range(1, parts):
+        source = grad_hidden if offset in (1, parts - 1) else late_grad
+        pairs = [(i, i ^ offset) for i in range(parts)]
+        grad_pieces.append(lax.ppermute(source, "feat", pairs))
+    all_grad = jnp.concatenate(grad_pieces, axis=0)
     my_rows = lax.dynamic_slice_in_dim(
         full_weight, lax.axis_index("feat") * feat_rows, feat_rows, 0
     )

time: 235 us -> 231 us (0.983); the launches traced: 234 us -> 228 us
  waiting for transfers between devices: 91.9 us -> 86.1 us
    ppermute x9 -> x6, starting transfers between devices: 29.7 us -> 20.1 us  [exchange_order(): received.append(lax.ppermute(values, axis, pairs))]
    ppermute x0 -> x3, starting transfers between devices: none -> 8.98 us  [per_device(): grad_pieces.append(lax.ppermute(source, 'feat', pairs))]
    ppermute x9 -> x6, waiting for transfers between devices: 9.22 us -> 1.68 us  [exchange_order(): received.append(lax.ppermute(values, axis, pairs))]
  transfers between devices with their start and end apart: 13 -> 13, of which waited for: 7 -> 6; matrix products, arithmetic and copies ran while one was open for 13% -> 14% of each run, Pallas kernels for 0% -> 0%
where the time goes in v12:
time: 231 us; the launch traced here: 228 us
  waiting for transfers between devices  86.1 us (37%)
  starting transfers between devices  77 us (33%)
  matrix products  38.1 us (16%)
  local copies, waits for them, and re-layouts  18.3 us (8%)
  other arithmetic  6.82 us (3%)
    all_to_all x1, waiting for transfers between devices, per_device(): lax.all_to_all(outgoing, 'dom', split_axis=1, concat_axis=1, tiled=True)  35.9 us
    all_to_all x1, waiting for transfers between devices, per_device(): lax.all_to_all(out_parts, 'dom', split_axis=1, concat_axis=1, tiled=True)  31.6 us
    all_to_all x1, starting transfers between devices, per_device(): lax.all_to_all(outgoing, 'dom', split_axis=1, concat_axis=1, tiled=True)  24 us
    ppermute x6, starting transfers between devices, exchange_order(): received.append(lax.ppermute(values, axis, pairs))  20.1 us
    all_to_all x1, waiting for transfers between devices, scatter_gather_sum(): lax.all_to_all(values.reshape(size, chunk, cols), axis, 0, 0, tiled=True)  12 us
    all_to_all x1, starting transfers between devices, per_device(): lax.all_to_all(out_parts, 'dom', split_axis=1, concat_axis=1, tiled=True)  9.44 us
    ppermute x3, starting transfers between devices, per_device(): grad_pieces.append(lax.ppermute(source, 'feat', pairs))  8.98 us
    all_to_all x1, starting transfers between devices, scatter_gather_sum(): lax.all_to_all(values.reshape(size, chunk, cols), axis, 0, 0, tiled=True)  8.84 us
  transfers between devices with their start and end apart: 13, of which 6 were waited for; matrix products, arithmetic and copies ran while one was open for 14% of the time, Pallas kernels for 0%

profile of v12, /device:TPU:1, one launch (start us, length us, event | category | flops | bytes accessed | tf_op | source)
XLA Modules:
  0.0 228.0 jit_solution(2282564103791909630)
XLA Ops:
  0.6 4.2 %collective-permute-start = (bf16[64,2048]{1,0:T(8,128)(2,1)}, bf16[64,2048]{1,0:T(8,128)(2,1)}, u32[]{:S(2)}, u32[]{:S(2)}) collective-permute-start(bf16[64,2048]{1,0:T(8,128)(2,1)} %param.13), channel_id=1, source_target_pairs={{0,1},{1,0},{2,3},{3,2},{4,5},{5,4},{6,7},{7,6},{8,9},{9,8},{10,11... | collective-permute-start | bytes 786440 | tf_op jit(solution)/shard_map/ppermute | solution.py:27
  4.9 3.7 %collective-permute-start.2 = (bf16[64,2048]{1,0:T(8,128)(2,1)}, bf16[64,2048]{1,0:T(8,128)(2,1)S(1)}, u32[]{:S(2)}, u32[]{:S(2)}) collective-permute-start(bf16[64,2048]{1,0:T(8,128)(2,1)} %param.13), channel_id=1, source_target_pairs={{0,3},{1,2},{2,1},{3,0},{4,7},{5,6},{6,5},{7,4},{8,11},{9,10},{10,... | collective-permute-start | bytes 786440 | tf_op jit(solution)/shard_map/ppermute | solution.py:27
  8.6 2.6 %collective-permute-start.1 = (bf16[64,2048]{1,0:T(8,128)(2,1)}, bf16[64,2048]{1,0:T(8,128)(2,1)}, u32[]{:S(2)}, u32[]{:S(2)}) collective-permute-start(bf16[64,2048]{1,0:T(8,128)(2,1)} %param.13), channel_id=1, source_target_pairs={{0,2},{1,3},{2,0},{3,1},{4,6},{5,7},{6,4},{7,5},{8,10},{9,11},{10,... | collective-permute-start | bytes 786440 | tf_op jit(solution)/shard_map/ppermute | solution.py:27
  21.1 24.0 %all-to-all-start = ((bf16[64,128,128]{2,0,1:T(8,128)(2,1)}), bf16[64,128,128]{2,0,1:T(8,128)(2,1)}, u32[]{:S(2)}, u32[]{:S(2)}) async-start(bf16[64,128,128]{2,0,1:T(8,128)(2,1)} %bitcast.105), calls=%async_computation | async-start | bytes 4194304 | tf_op jit(solution)/shard_map/all_to_all | solution.py:77
  46.1 3.0 %gather_fusion.3 = bf16[128,128,128]{2,1,0:T(8,128)(2,1)} fusion(bf16[96,128,128]{2,1,0:T(8,128)(2,1)S(1)} %copy-done, s32[1024]{0:T(1024)S(1)} %pad_clamp_fusion.2), kind=kCustom, calls=%fused_computation.3 | custom fusion | bytes 8389120 | tf_op jit(solution)/shard_map/jit(_take)/gather | solution.py:60
  51.2 2.4 %pad_maximum_fusion = bf16[256,2048]{1,0:T(8,128)(2,1)} fusion(bf16[64,2048]{1,0:T(8,128)(2,1)} %copy-done.4, bf16[64,2048]{1,0:T(8,128)(2,1)} %collective-permute-done.1, bf16[64,2048]{1,0:T(8,128)(2,1)} %collective-permute-done, bf16[64,2048]{1,0:T(8,128)(2,1)} %param.13), kind=kLoop, calls=%fused_computation.34 | loop fusion | flops 4194304 | bytes 2097152 | tf_op jit(solution)/shard_map/concatenate | solution.py:86
  55.9 4.2 %fusion.22 = f32[64,16,128]{2,1,0:T(8,128)} fusion(f32[64,96,128]{2,0,1:T(8,128)S(1)} %convolution_bitcast_fusion.2, f32[96]{0:T(128)S(1)} %and_convert_fusion, s32[96]{0:T(128)S(1)} %copy-done.8), kind=kOutput, calls=%fused_computation.31 | convolution fusion | flops 150998016 | bytes 3670784 | tf_op jit(solution)/shard_map/ota,tr->ora/dot_general | solution.py:85
  60.0 35.9 %all-to-all-done = bf16[64,128,128]{2,0,1:T(8,128)(2,1)} async-done(((bf16[64,128,128]{2,0,1:T(8,128)(2,1)}), bf16[64,128,128]{2,0,1:T(8,128)(2,1)}, u32[]{:S(2)}, u32[]{:S(2)}) %all-to-all-start) | async-done | bytes 2097184 | tf_op jit(solution)/shard_map/all_to_all | solution.py:77
  95.9 5.8 %convolution_bitcast_fusion = f32[64,128,128]{2,0,1:T(8,128)S(1)} fusion(bf16[64,128,128]{2,0,1:T(8,128)(2,1)} %all-to-all-done, bf16[128,128,128]{2,1,0:T(8,128)(2,1)} %gather_fusion.3, pred[128]{0:T(512)(128)(4,1)S(1)} %fusion.46), kind=kOutput, calls=%fused_computation.19 | convolution fusion | flops 270532608 | bytes 10485888 | tf_op jit(solution)/shard_map/oqb,qab->oqa/dot_general | solution.py:91
  101.7 4.4 %fusion.16 = f32[64,16,128]{2,1,0:T(8,128)S(1)} fusion(f32[64,128,128]{2,0,1:T(8,128)S(1)} %convolution_bitcast_fusion, f32[128]{0:T(128)S(1)} %convert_element_type.62, s32[128]{0:T(128)S(1)} %get-tuple-element.44), kind=kOutput, calls=%fused_computation.29 | convolution fusion | flops 201330688 | bytes 4719616 | tf_op jit(solution)/shard_map/oqa,qr->ora/dot_general | solution.py:94
  110.0 5.5 %convert_bitcast_fusion = bf16[64,128,128]{2,0,1:T(8,128)(2,1)} fusion(bf16[128,64,128]{2,1,0:T(8,128)(2,1)} %gather_fusion.4, bf16[128,128,128]{2,1,0:T(8,128)(2,1)} %gather_fusion.3, pred[128]{0:T(512)(128)(4,1)S(1)} %fusion.46), kind=kOutput, calls=%fused_computation.24 | convolution fusion | flops 271581184 | bytes 8388736 | tf_op jit(solution)/shard_map/oqa,qab->oqb/dot_general | solution.py:113
  115.5 9.4 %all-to-all-start.1 = ((bf16[64,128,128]{2,0,1:T(8,128)(2,1)}), bf16[64,128,128]{2,0,1:T(8,128)(2,1)}, u32[]{:S(2)}, u32[]{:S(2)}) async-start(bf16[64,128,128]{2,0,1:T(8,128)(2,1)} %convert_bitcast_fusion), calls=%async_computation.1 | async-start | bytes 4194304 | tf_op jit(solution)/shard_map/all_to_all | solution.py:116
  127.4 4.9 %collective-permute-start.4 = (bf16[256,64]{0,1:T(8,128)(2,1)S(1)}, bf16[256,64]{0,1:T(8,128)(2,1)S(1)}, u32[]{:S(2)}, u32[]{:S(2)}) collective-permute-start(bf16[256,64]{0,1:T(8,128)(2,1)S(1)} %copy-done.7), channel_id=1, source_target_pairs={{0,2},{1,3},{2,0},{3,1},{4,6},{5,7},{6,4},{7,5},{8,10},{9,11},{10,... | collective-permute-start | bytes 98312 | tf_op jit(solution)/shard_map/ppermute | solution.py:27
  132.3 2.8 %collective-permute-start.5 = (bf16[256,64]{0,1:T(8,128)(2,1)S(1)}, bf16[256,64]{0,1:T(8,128)(2,1)S(1)}, u32[]{:S(2)}, u32[]{:S(2)}) collective-permute-start(bf16[256,64]{0,1:T(8,128)(2,1)S(1)} %copy-done.7), channel_id=1, source_target_pairs={{0,3},{1,2},{2,1},{3,0},{4,7},{5,6},{6,5},{7,4},{8,11},{9,10},{10,... | collective-permute-start | bytes 98312 | tf_op jit(solution)/shard_map/ppermute | solution.py:27
  137.0 2.4 %convolution_bitcast_fusion.1 = f32[64,96,128]{2,0,1:T(8,128)S(1)} fusion(bf16[96,128,128]{2,1,0:T(8,128)(2,1)S(1)} %copy-done, bf16[96,64,128]{2,1,0:T(8,128)(2,1)} %gather_fusion.5), kind=kOutput, calls=%fused_computation.25 | convolution fusion | flops 201326592 | bytes 7864320 | tf_op jit(solution)/shard_map/ota,tab->otb/dot_general | solution.py:102
  139.4 4.1 %fusion.2 = f32[16,64,128]{2,0,1:T(8,128)} fusion(f32[64,96,128]{2,0,1:T(8,128)S(1)} %convolution_bitcast_fusion.1, f32[96]{0:T(128)S(1)} %copy-done.11, s32[96]{0:T(128)S(1)} %copy-done.9), kind=kOutput, calls=%fused_computation.10 | convolution fusion | flops 150998016 | bytes 3670784 | tf_op jit(solution)/shard_map/otb,tr->orb/dot_general | solution.py:109
  144.2 31.6 %all-to-all-done.1 = bf16[64,128,128]{2,0,1:T(8,128)(2,1)} async-done(((bf16[64,128,128]{2,0,1:T(8,128)(2,1)}), bf16[64,128,128]{2,0,1:T(8,128)(2,1)}, u32[]{:S(2)}, u32[]{:S(2)}) %all-to-all-start.1) | async-done | bytes 2097184 | tf_op jit(solution)/shard_map/all_to_all | solution.py:116
  175.8 3.0 %fusion.25 = bf16[16,64,128]{2,0,1:T(8,128)(2,1)S(1)} fusion(f32[16,64,128]{2,0,1:T(8,128)} %fusion.2, bf16[64,128,128]{2,0,1:T(8,128)(2,1)} %all-to-all-done.1, s32[128]{0:T(128)S(1)} %copy-done.10), kind=kOutput, calls=%fused_computation.32 | convolution fusion | flops 33822720 | bytes 2884096 | tf_op jit(solution)/shard_map/oqb,qr->orb/dot_general | solution.py:120
  181.6 8.8 %all-to-all-start.2 = ((f32[128,2,128]{2,1,0:T(2,128)}), f32[128,2,128]{2,1,0:T(2,128)S(1)}, u32[]{:S(2)}, u32[]{:S(2)}) async-start(f32[128,2,128]{2,1,0:T(2,128)} %bitcast.109), calls=%async_computation.2 | async-start | bytes 262144 | tf_op jit(solution)/shard_map/all_to_all | solution.py:34
  191.2 12.0 %all-to-all-done.2 = f32[128,2,128]{2,1,0:T(2,128)S(1)} async-done(((f32[128,2,128]{2,1,0:T(2,128)}), f32[128,2,128]{2,1,0:T(2,128)S(1)}, u32[]{:S(2)}, u32[]{:S(2)}) %all-to-all-start.2) | async-done | bytes 131104 | tf_op jit(solution)/shard_map/all_to_all | solution.py:34
  204.1 5.6 %all-to-all-start.3 = ((f32[128,2,128]{2,1,0:T(2,128)}), f32[128,2,128]{2,1,0:T(2,128)S(1)}, u32[]{:S(2)}, u32[]{:S(2)}) async-start(f32[128,2,128]{2,1,0:T(2,128)} %broadcast_in_dim.87), calls=%async_computation.3 | async-start | bytes 262144 | tf_op jit(solution)/shard_map/all_to_all | solution.py:38
  211.6 3.7 %collective-permute-start.8 = (bf16[64,2048]{1,0:T(8,128)(2,1)}, bf16[64,2048]{1,0:T(8,128)(2,1)}, u32[]{:S(2)}, u32[]{:S(2)}) collective-permute-start(bf16[64,2048]{1,0:T(8,128)(2,1)} %bitcast.112), channel_id=1, source_target_pairs={{0,3},{1,2},{2,1},{3,0},{4,7},{5,6},{6,5},{7,4},{8,11},{9,10},{10,... | collective-permute-start | bytes 786440 | tf_op jit(solution)/shard_map/ppermute | solution.py:144
  215.3 3.3 %collective-permute-start.7 = (bf16[64,2048]{1,0:T(8,128)(2,1)}, bf16[64,2048]{1,0:T(8,128)(2,1)}, u32[]{:S(2)}, u32[]{:S(2)}) collective-permute-start(bf16[64,2048]{1,0:T(8,128)(2,1)} %bitcast.113), channel_id=1, source_target_pairs={{0,2},{1,3},{2,0},{3,1},{4,6},{5,7},{6,4},{7,5},{8,10},{9,11},{10,... | collective-permute-start | bytes 786440 | tf_op jit(solution)/shard_map/ppermute | solution.py:144
  218.6 3.8 %all-to-all-done.3 = f32[128,2,128]{2,1,0:T(2,128)S(1)} async-done(((f32[128,2,128]{2,1,0:T(2,128)}), f32[128,2,128]{2,1,0:T(2,128)S(1)}, u32[]{:S(2)}, u32[]{:S(2)}) %all-to-all-start.3) | async-done | bytes 131104 | tf_op jit(solution)/shard_map/all_to_all | solution.py:38
  (85 shorter events, 35.1 us)
Async XLA Ops:
  0.6 45.5 %copy-start = (bf16[96,128,128]{2,1,0:T(8,128)(2,1)S(1)}, bf16[96,128,128]{2,1,0:T(8,128)(2,1)}, u32[]{:S(2)}) copy-start(bf16[96,128,128]{2,1,0:T(8,128)(2,1)} %param.16) | copy-start | bytes 9437188
  0.6 14.1 %collective-permute-start = (bf16[64,2048]{1,0:T(8,128)(2,1)}, bf16[64,2048]{1,0:T(8,128)(2,1)}, u32[]{:S(2)}, u32[]{:S(2)}) collective-permute-start(bf16[64,2048]{1,0:T(8,128)(2,1)} %param.13), channel_id=1, source_target_pairs={{0,1},{1,0},{2,3},{3,2},{4,5},{5,4},{6,7},{7,6},{8,9},{9,8},{10,11... | collective-permute-start | bytes 786440 | tf_op jit(solution)/shard_map/ppermute | solution.py:27
  4.9 9.6 %collective-permute-start.2 = (bf16[64,2048]{1,0:T(8,128)(2,1)}, bf16[64,2048]{1,0:T(8,128)(2,1)S(1)}, u32[]{:S(2)}, u32[]{:S(2)}) collective-permute-start(bf16[64,2048]{1,0:T(8,128)(2,1)} %param.13), channel_id=1, source_target_pairs={{0,3},{1,2},{2,1},{3,0},{4,7},{5,6},{6,5},{7,4},{8,11},{9,10},{10,... | collective-permute-start | bytes 786440 | tf_op jit(solution)/shard_map/ppermute | solution.py:27
  8.6 9.0 %collective-permute-start.1 = (bf16[64,2048]{1,0:T(8,128)(2,1)}, bf16[64,2048]{1,0:T(8,128)(2,1)}, u32[]{:S(2)}, u32[]{:S(2)}) collective-permute-start(bf16[64,2048]{1,0:T(8,128)(2,1)} %param.13), channel_id=1, source_target_pairs={{0,2},{1,3},{2,0},{3,1},{4,6},{5,7},{6,4},{7,5},{8,10},{9,11},{10,... | collective-permute-start | bytes 786440 | tf_op jit(solution)/shard_map/ppermute | solution.py:27
  14.5 3.1 %copy-start.4 = (bf16[64,2048]{1,0:T(8,128)(2,1)}, bf16[64,2048]{1,0:T(8,128)(2,1)S(1)}, u32[]{:S(2)}) copy-start(bf16[64,2048]{1,0:T(8,128)(2,1)S(1)} %collective-permute-done.2) | copy-start | bytes 786436
  21.1 24.7 %copy-start.9 = (s32[96]{0:T(128)S(1)}, s32[96]{0:T(128)}, u32[]{:S(2)}) copy-start(s32[96]{0:T(128)} %param.18) | copy-start | bytes 1156
  21.1 24.9 %copy-start.12 = (bf16[64]{0:T(256)(128)(2,1)S(1)}, bf16[64]{0:T(256)(128)(2,1)}, u32[]{:S(2)}) copy-start(bf16[64]{0:T(256)(128)(2,1)} %param.15) | copy-start | bytes 388
  21.1 24.9 %copy-start.8 = (s32[96]{0:T(128)S(1)}, s32[96]{0:T(128)}, u32[]{:S(2)}) copy-start(s32[96]{0:T(128)} %param.17) | copy-start | bytes 1156
  21.1 74.8 %all-to-all-start = ((bf16[64,128,128]{2,0,1:T(8,128)(2,1)}), bf16[64,128,128]{2,0,1:T(8,128)(2,1)}, u32[]{:S(2)}, u32[]{:S(2)}) async-start(bf16[64,128,128]{2,0,1:T(8,128)(2,1)} %bitcast.105), calls=%async_computation | async-start | bytes 4194304 | tf_op jit(solution)/shard_map/all_to_all | solution.py:77
  51.2 2.4 %copy-start.1 = (bf16[96,64,128]{2,1,0:T(8,128)(2,1)S(1)}, bf16[96,64,128]{2,1,0:T(8,128)(2,1)}, u32[]{:S(2)}) copy-start(bf16[96,64,128]{2,1,0:T(8,128)(2,1)} %gather_fusion.1) | copy-start | bytes 4718596
  101.7 4.4 %copy-start.3 = (f32[64,16,128]{2,1,0:T(8,128)S(1)}, f32[64,16,128]{2,1,0:T(8,128)}, u32[]{:S(2)}) copy-start(f32[64,16,128]{2,1,0:T(8,128)} %fusion.22) | copy-start | bytes 1572868
  101.7 4.4 %copy-start.6 = (bf16[64,2048]{1,0:T(8,128)(2,1)S(1)}, bf16[64,2048]{1,0:T(8,128)(2,1)}, u32[]{:S(2)}) copy-start(bf16[64,2048]{1,0:T(8,128)(2,1)} %param.21) | copy-start | bytes 786436
  115.5 10.0 %copy-start.7 = (bf16[256,64]{0,1:T(8,128)(2,1)S(1)}, bf16[256,64]{0,1:T(8,128)(2,1)}, u32[]{:S(2)}) copy-start(bf16[256,64]{0,1:T(8,128)(2,1)} %param.14) | copy-start | bytes 98308
  115.5 60.4 %all-to-all-start.1 = ((bf16[64,128,128]{2,0,1:T(8,128)(2,1)}), bf16[64,128,128]{2,0,1:T(8,128)(2,1)}, u32[]{:S(2)}, u32[]{:S(2)}) async-start(bf16[64,128,128]{2,0,1:T(8,128)(2,1)} %convert_bitcast_fusion), calls=%async_computation.1 | async-start | bytes 4194304 | tf_op jit(solution)/shard_map/all_to_all | solution.py:116
  125.4 18.1 %collective-permute-start.3 = (bf16[256,64]{0,1:T(8,128)(2,1)S(1)}, bf16[256,64]{0,1:T(8,128)(2,1)S(1)}, u32[]{:S(2)}, u32[]{:S(2)}) collective-permute-start(bf16[256,64]{0,1:T(8,128)(2,1)S(1)} %copy-done.7), channel_id=1, source_target_pairs={{0,1},{1,0},{2,3},{3,2},{4,5},{5,4},{6,7},{7,6},{8,9},{9,8},{10,11... | collective-permute-start | bytes 98312 | tf_op jit(solution)/shard_map/ppermute | solution.py:27
  127.4 16.1 %collective-permute-start.4 = (bf16[256,64]{0,1:T(8,128)(2,1)S(1)}, bf16[256,64]{0,1:T(8,128)(2,1)S(1)}, u32[]{:S(2)}, u32[]{:S(2)}) collective-permute-start(bf16[256,64]{0,1:T(8,128)(2,1)S(1)} %copy-done.7), channel_id=1, source_target_pairs={{0,2},{1,3},{2,0},{3,1},{4,6},{5,7},{6,4},{7,5},{8,10},{9,11},{10,... | collective-permute-start | bytes 98312 | tf_op jit(solution)/shard_map/ppermute | solution.py:27
  132.3 11.2 %collective-permute-start.5 = (bf16[256,64]{0,1:T(8,128)(2,1)S(1)}, bf16[256,64]{0,1:T(8,128)(2,1)S(1)}, u32[]{:S(2)}, u32[]{:S(2)}) collective-permute-start(bf16[256,64]{0,1:T(8,128)(2,1)S(1)} %copy-done.7), channel_id=1, source_target_pairs={{0,3},{1,2},{2,1},{3,0},{4,7},{5,6},{6,5},{7,4},{8,11},{9,10},{10,... | collective-permute-start | bytes 98312 | tf_op jit(solution)/shard_map/ppermute | solution.py:27
  139.4 36.5 %copy-start.10 = (s32[128]{0:T(128)S(1)}, s32[128]{0:T(128)}, u32[]{:S(2)}) copy-start(s32[128]{0:T(128)} %param.20) | copy-start | bytes 1540
  175.8 3.0 %copy-start.2 = (bf16[256,2048]{1,0:T(8,128)(2,1)S(1)}, bf16[256,2048]{1,0:T(8,128)(2,1)}, u32[]{:S(2)}) copy-start(bf16[256,2048]{1,0:T(8,128)(2,1)} %pad_maximum_fusion) | copy-start | bytes 3145732
  181.6 21.6 %all-to-all-start.2 = ((f32[128,2,128]{2,1,0:T(2,128)}), f32[128,2,128]{2,1,0:T(2,128)S(1)}, u32[]{:S(2)}, u32[]{:S(2)}) async-start(f32[128,2,128]{2,1,0:T(2,128)} %bitcast.109), calls=%async_computation.2 | async-start | bytes 262144 | tf_op jit(solution)/shard_map/all_to_all | solution.py:34
  204.1 18.4 %all-to-all-start.3 = ((f32[128,2,128]{2,1,0:T(2,128)}), f32[128,2,128]{2,1,0:T(2,128)S(1)}, u32[]{:S(2)}, u32[]{:S(2)}) async-start(f32[128,2,128]{2,1,0:T(2,128)} %broadcast_in_dim.87), calls=%async_computation.3 | async-start | bytes 262144 | tf_op jit(solution)/shard_map/all_to_all | solution.py:38
  209.6 15.0 %collective-permute-start.6 = (bf16[64,2048]{1,0:T(8,128)(2,1)}, bf16[64,2048]{1,0:T(8,128)(2,1)}, u32[]{:S(2)}, u32[]{:S(2)}) collective-permute-start(bf16[64,2048]{1,0:T(8,128)(2,1)} %bitcast.111), channel_id=1, source_target_pairs={{0,1},{1,0},{2,3},{3,2},{4,5},{5,4},{6,7},{7,6},{8,9},{9,8},{10,11... | collective-permute-start | bytes 786440 | tf_op jit(solution)/shard_map/ppermute | solution.py:144
  211.6 14.1 %collective-permute-start.8 = (bf16[64,2048]{1,0:T(8,128)(2,1)}, bf16[64,2048]{1,0:T(8,128)(2,1)}, u32[]{:S(2)}, u32[]{:S(2)}) collective-permute-start(bf16[64,2048]{1,0:T(8,128)(2,1)} %bitcast.112), channel_id=1, source_target_pairs={{0,3},{1,2},{2,1},{3,0},{4,7},{5,6},{6,5},{7,4},{8,11},{9,10},{10,... | collective-permute-start | bytes 786440 | tf_op jit(solution)/shard_map/ppermute | solution.py:144
  215.3 10.4 %collective-permute-start.7 = (bf16[64,2048]{1,0:T(8,128)(2,1)}, bf16[64,2048]{1,0:T(8,128)(2,1)}, u32[]{:S(2)}, u32[]{:S(2)}) collective-permute-start(bf16[64,2048]{1,0:T(8,128)(2,1)} %bitcast.113), channel_id=1, source_target_pairs={{0,2},{1,3},{2,0},{3,1},{4,6},{5,7},{6,4},{7,5},{8,10},{9,11},{10,... | collective-permute-start | bytes 786440 | tf_op jit(solution)/shard_map/ppermute | solution.py:144
  (2 other events, 3.0 us)

commit v13 on v12

--- a/solution.py
+++ b/solution.py
@@ -91,7 +91,15 @@
     far_products = jnp.einsum(
         "oqb,qab->oqa", incoming, peer_tiles, preferred_element_type=jnp.float32
     )
-    summed_far = jnp.einsum("oqa,qr->ora", far_products, far_place, precision=lax.Precision.HIGHEST)
+    far_hi = far_products.astype(jnp.bfloat16)
+    far_rest = far_products - far_hi.astype(jnp.float32)
+    far_mid = far_rest.astype(jnp.bfloat16)
+    far_lo = (far_rest - far_mid.astype(jnp.float32)).astype(jnp.bfloat16)
+    far_place_low = far_place.astype(jnp.bfloat16)
+    summed_far = sum(
+        jnp.einsum("oqa,qr->ora", part, far_place_low, preferred_element_type=jnp.float32)
+        for part in (far_hi, far_mid, far_lo)
+    )
     summed = (summed_local + summed_far).reshape(feat_rows, node_rows)
     preact = summed + bias_vec.astype(jnp.float32)[:, None]
     activated, pullback = jax.vjp(smooth_gate, preact)

time: 231 us -> 231 us (level)
  no operation moved by 1% of the time
where the time goes in v13:
time: 231 us; the launch traced here: 228 us
  waiting for transfers between devices  86.1 us (37%)
  starting transfers between devices  77.2 us (33%)
  matrix products  37.5 us (16%)
  local copies, waits for them, and re-layouts  18.6 us (8%)
  other arithmetic  6.6 us (3%)
    all_to_all x1, waiting for transfers between devices, per_device(): lax.all_to_all(outgoing, 'dom', split_axis=1, concat_axis=1, tiled=True)  35.9 us
    all_to_all x1, waiting for transfers between devices, per_device(): lax.all_to_all(out_parts, 'dom', split_axis=1, concat_axis=1, tiled=True)  31.7 us
    all_to_all x1, starting transfers between devices, per_device(): lax.all_to_all(outgoing, 'dom', split_axis=1, concat_axis=1, tiled=True)  24 us
    ppermute x6, starting transfers between devices, exchange_order(): received.append(lax.ppermute(values, axis, pairs))  20.1 us
    all_to_all x1, waiting for transfers between devices, scatter_gather_sum(): lax.all_to_all(values.reshape(size, chunk, cols), axis, 0, 0, tiled=True)  12 us
    all_to_all x1, starting transfers between devices, per_device(): lax.all_to_all(out_parts, 'dom', split_axis=1, concat_axis=1, tiled=True)  9.44 us
    ppermute x3, starting transfers between devices, per_device(): grad_pieces.append(lax.ppermute(source, 'feat', pairs))  8.98 us
    all_to_all x1, starting transfers between devices, scatter_gather_sum(): lax.all_to_all(values.reshape(size, chunk, cols), axis, 0, 0, tiled=True)  8.85 us
  transfers between devices with their start and end apart: 13, of which 6 were waited for; matrix products, arithmetic and copies ran while one was open for 14% of the time, Pallas kernels for 0%

profile of v13, /device:TPU:1, one launch (start us, length us, event | category | flops | bytes accessed | tf_op | source)
XLA Modules:
  0.0 227.6 jit_solution(8515774345415321378)
XLA Ops:
  0.6 4.2 %collective-permute-start = (bf16[64,2048]{1,0:T(8,128)(2,1)}, bf16[64,2048]{1,0:T(8,128)(2,1)}, u32[]{:S(2)}, u32[]{:S(2)}) collective-permute-start(bf16[64,2048]{1,0:T(8,128)(2,1)} %param.13), channel_id=1, source_target_pairs={{0,1},{1,0},{2,3},{3,2},{4,5},{5,4},{6,7},{7,6},{8,9},{9,8},{10,11... | collective-permute-start | bytes 786440 | tf_op jit(solution)/shard_map/ppermute | solution.py:27
  4.9 3.7 %collective-permute-start.2 = (bf16[64,2048]{1,0:T(8,128)(2,1)}, bf16[64,2048]{1,0:T(8,128)(2,1)S(1)}, u32[]{:S(2)}, u32[]{:S(2)}) collective-permute-start(bf16[64,2048]{1,0:T(8,128)(2,1)} %param.13), channel_id=1, source_target_pairs={{0,3},{1,2},{2,1},{3,0},{4,7},{5,6},{6,5},{7,4},{8,11},{9,10},{10,... | collective-permute-start | bytes 786440 | tf_op jit(solution)/shard_map/ppermute | solution.py:27
  8.6 2.6 %collective-permute-start.1 = (bf16[64,2048]{1,0:T(8,128)(2,1)}, bf16[64,2048]{1,0:T(8,128)(2,1)}, u32[]{:S(2)}, u32[]{:S(2)}) collective-permute-start(bf16[64,2048]{1,0:T(8,128)(2,1)} %param.13), channel_id=1, source_target_pairs={{0,2},{1,3},{2,0},{3,1},{4,6},{5,7},{6,4},{7,5},{8,10},{9,11},{10,... | collective-permute-start | bytes 786440 | tf_op jit(solution)/shard_map/ppermute | solution.py:27
  21.1 24.0 %all-to-all-start = ((bf16[64,128,128]{2,0,1:T(8,128)(2,1)}), bf16[64,128,128]{2,0,1:T(8,128)(2,1)}, u32[]{:S(2)}, u32[]{:S(2)}) async-start(bf16[64,128,128]{2,0,1:T(8,128)(2,1)} %bitcast.119), calls=%async_computation | async-start | bytes 4194304 | tf_op jit(solution)/shard_map/all_to_all | solution.py:77
  46.1 3.0 %gather_fusion.3 = bf16[128,128,128]{2,1,0:T(8,128)(2,1)} fusion(bf16[96,128,128]{2,1,0:T(8,128)(2,1)S(1)} %copy-done, s32[1024]{0:T(1024)S(1)} %pad_clamp_fusion.2), kind=kCustom, calls=%fused_computation.3 | custom fusion | bytes 8389120 | tf_op jit(solution)/shard_map/jit(_take)/gather | solution.py:60
  51.2 2.4 %pad_maximum_fusion = bf16[256,2048]{1,0:T(8,128)(2,1)} fusion(bf16[64,2048]{1,0:T(8,128)(2,1)} %copy-done.4, bf16[64,2048]{1,0:T(8,128)(2,1)} %collective-permute-done.1, bf16[64,2048]{1,0:T(8,128)(2,1)} %collective-permute-done, bf16[64,2048]{1,0:T(8,128)(2,1)} %param.13), kind=kLoop, calls=%fused_computation.44 | loop fusion | flops 4194304 | bytes 2097152 | tf_op jit(solution)/shard_map/concatenate | solution.py:86
  55.9 4.1 %fusion.34 = f32[64,16,128]{2,1,0:T(8,128)} fusion(f32[64,96,128]{2,0,1:T(8,128)S(1)} %convolution_bitcast_fusion.1, f32[96]{0:T(128)S(1)} %and_convert_fusion, s32[96]{0:T(128)S(1)} %copy-done.8), kind=kOutput, calls=%fused_computation.41 | convolution fusion | flops 150998016 | bytes 3670784 | tf_op jit(solution)/shard_map/ota,tr->ora/dot_general | solution.py:85
  60.0 35.9 %all-to-all-done = bf16[64,128,128]{2,0,1:T(8,128)(2,1)} async-done(((bf16[64,128,128]{2,0,1:T(8,128)(2,1)}), bf16[64,128,128]{2,0,1:T(8,128)(2,1)}, u32[]{:S(2)}, u32[]{:S(2)}) %all-to-all-start) | async-done | bytes 2097184 | tf_op jit(solution)/shard_map/all_to_all | solution.py:77
  95.9 5.8 %subtract_convert_fusion = (bf16[64,128,128]{2,0,1:T(8,128)(2,1)S(1)}, bf16[64,128,128]{2,0,1:T(8,128)(2,1)S(1)}, bf16[128,128,64]{1,2,0:T(8,128)(2,1)S(1)}) fusion(bf16[64,128,128]{2,0,1:T(8,128)(2,1)} %all-to-all-done, bf16[128,128,128]{2,1,0:T(8,128)(2,1)} %gather_fusion.3, pred[128]{0:T(512)(128)(4,1)S(1)} %fusion.58), kind=kOutput, calls=%fused_computation.9 | convolution fusion | flops 278921216 | bytes 12583040 | tf_op jit(solution)/shard_map/oqb,qab->oqa/dot_general | solution.py:91
  107.0 2.4 %gather_fusion.4 = bf16[128,64,128]{2,1,0:T(8,128)(2,1)} fusion(bf16[64,16,128]{2,0,1:T(8,128)(2,1)S(1)} %copy_bitcast_fusion.1, s32[1024]{0:T(1024)S(1)} %pad_clamp_fusion.1), kind=kCustom, calls=%fused_computation.4 | custom fusion | bytes 4194816 | tf_op jit(solution)/shard_map/jit(_take)/gather | solution.py:120
  109.3 5.5 %convert_bitcast_fusion = bf16[64,128,128]{2,0,1:T(8,128)(2,1)} fusion(bf16[128,64,128]{2,1,0:T(8,128)(2,1)} %gather_fusion.4, bf16[128,128,128]{2,1,0:T(8,128)(2,1)} %gather_fusion.3, pred[128]{0:T(512)(128)(4,1)S(1)} %fusion.58), kind=kOutput, calls=%fused_computation.31 | convolution fusion | flops 271581184 | bytes 8388736 | tf_op jit(solution)/shard_map/oqa,qab->oqb/dot_general | solution.py:121
  114.8 9.4 %all-to-all-start.1 = ((bf16[64,128,128]{2,0,1:T(8,128)(2,1)}), bf16[64,128,128]{2,0,1:T(8,128)(2,1)}, u32[]{:S(2)}, u32[]{:S(2)}) async-start(bf16[64,128,128]{2,0,1:T(8,128)(2,1)} %convert_bitcast_fusion), calls=%async_computation.1 | async-start | bytes 4194304 | tf_op jit(solution)/shard_map/all_to_all | solution.py:124
  126.7 4.9 %collective-permute-start.4 = (bf16[256,64]{0,1:T(8,128)(2,1)S(1)}, bf16[256,64]{0,1:T(8,128)(2,1)S(1)}, u32[]{:S(2)}, u32[]{:S(2)}) collective-permute-start(bf16[256,64]{0,1:T(8,128)(2,1)S(1)} %copy-done.7), channel_id=1, source_target_pairs={{0,2},{1,3},{2,0},{3,1},{4,6},{5,7},{6,4},{7,5},{8,10},{9,11},{10,... | collective-permute-start | bytes 98312 | tf_op jit(solution)/shard_map/ppermute | solution.py:27
  131.6 2.8 %collective-permute-start.5 = (bf16[256,64]{0,1:T(8,128)(2,1)S(1)}, bf16[256,64]{0,1:T(8,128)(2,1)S(1)}, u32[]{:S(2)}, u32[]{:S(2)}) collective-permute-start(bf16[256,64]{0,1:T(8,128)(2,1)S(1)} %copy-done.7), channel_id=1, source_target_pairs={{0,3},{1,2},{2,1},{3,0},{4,7},{5,6},{6,5},{7,4},{8,11},{9,10},{10,... | collective-permute-start | bytes 98312 | tf_op jit(solution)/shard_map/ppermute | solution.py:27
  136.4 2.4 %convolution_bitcast_fusion = f32[64,96,128]{2,0,1:T(8,128)S(1)} fusion(bf16[96,128,128]{2,1,0:T(8,128)(2,1)S(1)} %copy-done, bf16[96,64,128]{2,1,0:T(8,128)(2,1)} %gather_fusion.5), kind=kOutput, calls=%fused_computation.32 | convolution fusion | flops 201326592 | bytes 7864320 | tf_op jit(solution)/shard_map/ota,tab->otb/dot_general | solution.py:110
  138.8 4.1 %fusion = f32[16,64,128]{2,0,1:T(8,128)} fusion(f32[64,96,128]{2,0,1:T(8,128)S(1)} %convolution_bitcast_fusion, f32[96]{0:T(128)S(1)} %copy-done.11, s32[96]{0:T(128)S(1)} %copy-done.9), kind=kOutput, calls=%fused_computation.11 | convolution fusion | flops 150998016 | bytes 3670784 | tf_op jit(solution)/shard_map/otb,tr->orb/dot_general | solution.py:117
  143.5 31.7 %all-to-all-done.1 = bf16[64,128,128]{2,0,1:T(8,128)(2,1)} async-done(((bf16[64,128,128]{2,0,1:T(8,128)(2,1)}), bf16[64,128,128]{2,0,1:T(8,128)(2,1)}, u32[]{:S(2)}, u32[]{:S(2)}) %all-to-all-start.1) | async-done | bytes 2097184 | tf_op jit(solution)/shard_map/all_to_all | solution.py:124
  175.2 3.0 %fusion.37 = bf16[16,64,128]{2,0,1:T(8,128)(2,1)S(1)} fusion(f32[16,64,128]{2,0,1:T(8,128)} %fusion, bf16[64,128,128]{2,0,1:T(8,128)(2,1)} %all-to-all-done.1, s32[128]{0:T(128)S(1)} %copy-done.10), kind=kOutput, calls=%fused_computation.42 | convolution fusion | flops 33822720 | bytes 2884096 | tf_op jit(solution)/shard_map/oqb,qr->orb/dot_general | solution.py:128
  181.0 8.8 %all-to-all-start.2 = ((f32[128,2,128]{2,1,0:T(2,128)}), f32[128,2,128]{2,1,0:T(2,128)S(1)}, u32[]{:S(2)}, u32[]{:S(2)}) async-start(f32[128,2,128]{2,1,0:T(2,128)} %bitcast.124), calls=%async_computation.2 | async-start | bytes 262144 | tf_op jit(solution)/shard_map/all_to_all | solution.py:34
  190.6 12.0 %all-to-all-done.2 = f32[128,2,128]{2,1,0:T(2,128)S(1)} async-done(((f32[128,2,128]{2,1,0:T(2,128)}), f32[128,2,128]{2,1,0:T(2,128)S(1)}, u32[]{:S(2)}, u32[]{:S(2)}) %all-to-all-start.2) | async-done | bytes 131104 | tf_op jit(solution)/shard_map/all_to_all | solution.py:34
  203.4 5.8 %all-to-all-start.3 = ((f32[128,2,128]{2,1,0:T(2,128)}), f32[128,2,128]{2,1,0:T(2,128)S(1)}, u32[]{:S(2)}, u32[]{:S(2)}) async-start(f32[128,2,128]{2,1,0:T(2,128)} %broadcast_in_dim.87), calls=%async_computation.3 | async-start | bytes 262144 | tf_op jit(solution)/shard_map/all_to_all | solution.py:38
  211.2 3.7 %collective-permute-start.8 = (bf16[64,2048]{1,0:T(8,128)(2,1)}, bf16[64,2048]{1,0:T(8,128)(2,1)}, u32[]{:S(2)}, u32[]{:S(2)}) collective-permute-start(bf16[64,2048]{1,0:T(8,128)(2,1)} %bitcast.127), channel_id=1, source_target_pairs={{0,3},{1,2},{2,1},{3,0},{4,7},{5,6},{6,5},{7,4},{8,11},{9,10},{10,... | collective-permute-start | bytes 786440 | tf_op jit(solution)/shard_map/ppermute | solution.py:152
  214.9 3.3 %collective-permute-start.7 = (bf16[64,2048]{1,0:T(8,128)(2,1)}, bf16[64,2048]{1,0:T(8,128)(2,1)}, u32[]{:S(2)}, u32[]{:S(2)}) collective-permute-start(bf16[64,2048]{1,0:T(8,128)(2,1)} %bitcast.128), channel_id=1, source_target_pairs={{0,2},{1,3},{2,0},{3,1},{4,6},{5,7},{6,4},{7,5},{8,10},{9,11},{10,... | collective-permute-start | bytes 786440 | tf_op jit(solution)/shard_map/ppermute | solution.py:152
  218.3 3.8 %all-to-all-done.3 = f32[128,2,128]{2,1,0:T(2,128)S(1)} async-done(((f32[128,2,128]{2,1,0:T(2,128)}), f32[128,2,128]{2,1,0:T(2,128)S(1)}, u32[]{:S(2)}, u32[]{:S(2)}) %all-to-all-start.3) | async-done | bytes 131104 | tf_op jit(solution)/shard_map/all_to_all | solution.py:38
  (87 shorter events, 36.4 us)
Async XLA Ops:
  0.6 45.5 %copy-start = (bf16[96,128,128]{2,1,0:T(8,128)(2,1)S(1)}, bf16[96,128,128]{2,1,0:T(8,128)(2,1)}, u32[]{:S(2)}) copy-start(bf16[96,128,128]{2,1,0:T(8,128)(2,1)} %param.16) | copy-start | bytes 9437188
  0.6 14.1 %collective-permute-start = (bf16[64,2048]{1,0:T(8,128)(2,1)}, bf16[64,2048]{1,0:T(8,128)(2,1)}, u32[]{:S(2)}, u32[]{:S(2)}) collective-permute-start(bf16[64,2048]{1,0:T(8,128)(2,1)} %param.13), channel_id=1, source_target_pairs={{0,1},{1,0},{2,3},{3,2},{4,5},{5,4},{6,7},{7,6},{8,9},{9,8},{10,11... | collective-permute-start | bytes 786440 | tf_op jit(solution)/shard_map/ppermute | solution.py:27
  4.9 9.6 %collective-permute-start.2 = (bf16[64,2048]{1,0:T(8,128)(2,1)}, bf16[64,2048]{1,0:T(8,128)(2,1)S(1)}, u32[]{:S(2)}, u32[]{:S(2)}) collective-permute-start(bf16[64,2048]{1,0:T(8,128)(2,1)} %param.13), channel_id=1, source_target_pairs={{0,3},{1,2},{2,1},{3,0},{4,7},{5,6},{6,5},{7,4},{8,11},{9,10},{10,... | collective-permute-start | bytes 786440 | tf_op jit(solution)/shard_map/ppermute | solution.py:27
  8.6 9.0 %collective-permute-start.1 = (bf16[64,2048]{1,0:T(8,128)(2,1)}, bf16[64,2048]{1,0:T(8,128)(2,1)}, u32[]{:S(2)}, u32[]{:S(2)}) collective-permute-start(bf16[64,2048]{1,0:T(8,128)(2,1)} %param.13), channel_id=1, source_target_pairs={{0,2},{1,3},{2,0},{3,1},{4,6},{5,7},{6,4},{7,5},{8,10},{9,11},{10,... | collective-permute-start | bytes 786440 | tf_op jit(solution)/shard_map/ppermute | solution.py:27
  14.5 3.1 %copy-start.4 = (bf16[64,2048]{1,0:T(8,128)(2,1)}, bf16[64,2048]{1,0:T(8,128)(2,1)S(1)}, u32[]{:S(2)}) copy-start(bf16[64,2048]{1,0:T(8,128)(2,1)S(1)} %collective-permute-done.2) | copy-start | bytes 786436
  21.1 24.7 %copy-start.9 = (s32[96]{0:T(128)S(1)}, s32[96]{0:T(128)}, u32[]{:S(2)}) copy-start(s32[96]{0:T(128)} %param.18) | copy-start | bytes 1156
  21.1 24.9 %copy-start.12 = (bf16[64]{0:T(256)(128)(2,1)S(1)}, bf16[64]{0:T(256)(128)(2,1)}, u32[]{:S(2)}) copy-start(bf16[64]{0:T(256)(128)(2,1)} %param.15) | copy-start | bytes 388
  21.1 24.9 %copy-start.8 = (s32[96]{0:T(128)S(1)}, s32[96]{0:T(128)}, u32[]{:S(2)}) copy-start(s32[96]{0:T(128)} %param.17) | copy-start | bytes 1156
  21.1 74.8 %all-to-all-start = ((bf16[64,128,128]{2,0,1:T(8,128)(2,1)}), bf16[64,128,128]{2,0,1:T(8,128)(2,1)}, u32[]{:S(2)}, u32[]{:S(2)}) async-start(bf16[64,128,128]{2,0,1:T(8,128)(2,1)} %bitcast.119), calls=%async_computation | async-start | bytes 4194304 | tf_op jit(solution)/shard_map/all_to_all | solution.py:77
  51.2 2.4 %copy-start.1 = (bf16[96,64,128]{2,1,0:T(8,128)(2,1)S(1)}, bf16[96,64,128]{2,1,0:T(8,128)(2,1)}, u32[]{:S(2)}) copy-start(bf16[96,64,128]{2,1,0:T(8,128)(2,1)} %gather_fusion.1) | copy-start | bytes 4718596
  104.2 1.3 copy-start.6
  114.8 10.0 %copy-start.7 = (bf16[256,64]{0,1:T(8,128)(2,1)S(1)}, bf16[256,64]{0,1:T(8,128)(2,1)}, u32[]{:S(2)}) copy-start(bf16[256,64]{0,1:T(8,128)(2,1)} %param.14) | copy-start | bytes 98308
  114.8 60.4 %all-to-all-start.1 = ((bf16[64,128,128]{2,0,1:T(8,128)(2,1)}), bf16[64,128,128]{2,0,1:T(8,128)(2,1)}, u32[]{:S(2)}, u32[]{:S(2)}) async-start(bf16[64,128,128]{2,0,1:T(8,128)(2,1)} %convert_bitcast_fusion), calls=%async_computation.1 | async-start | bytes 4194304 | tf_op jit(solution)/shard_map/all_to_all | solution.py:124
  124.8 18.0 %collective-permute-start.3 = (bf16[256,64]{0,1:T(8,128)(2,1)S(1)}, bf16[256,64]{0,1:T(8,128)(2,1)S(1)}, u32[]{:S(2)}, u32[]{:S(2)}) collective-permute-start(bf16[256,64]{0,1:T(8,128)(2,1)S(1)} %copy-done.7), channel_id=1, source_target_pairs={{0,1},{1,0},{2,3},{3,2},{4,5},{5,4},{6,7},{7,6},{8,9},{9,8},{10,11... | collective-permute-start | bytes 98312 | tf_op jit(solution)/shard_map/ppermute | solution.py:27
  126.7 16.1 %collective-permute-start.4 = (bf16[256,64]{0,1:T(8,128)(2,1)S(1)}, bf16[256,64]{0,1:T(8,128)(2,1)S(1)}, u32[]{:S(2)}, u32[]{:S(2)}) collective-permute-start(bf16[256,64]{0,1:T(8,128)(2,1)S(1)} %copy-done.7), channel_id=1, source_target_pairs={{0,2},{1,3},{2,0},{3,1},{4,6},{5,7},{6,4},{7,5},{8,10},{9,11},{10,... | collective-permute-start | bytes 98312 | tf_op jit(solution)/shard_map/ppermute | solution.py:27
  131.6 11.2 %collective-permute-start.5 = (bf16[256,64]{0,1:T(8,128)(2,1)S(1)}, bf16[256,64]{0,1:T(8,128)(2,1)S(1)}, u32[]{:S(2)}, u32[]{:S(2)}) collective-permute-start(bf16[256,64]{0,1:T(8,128)(2,1)S(1)} %copy-done.7), channel_id=1, source_target_pairs={{0,3},{1,2},{2,1},{3,0},{4,7},{5,6},{6,5},{7,4},{8,11},{9,10},{10,... | collective-permute-start | bytes 98312 | tf_op jit(solution)/shard_map/ppermute | solution.py:27
  136.4 2.4 %copy-start.11 = (f32[96]{0:T(128)S(1)}, f32[96]{0:T(128)}, u32[]{:S(2)}) copy-start(f32[96]{0:T(128)} %fusion.97) | copy-start | bytes 1156
  138.7 36.5 %copy-start.10 = (s32[128]{0:T(128)S(1)}, s32[128]{0:T(128)}, u32[]{:S(2)}) copy-start(s32[128]{0:T(128)} %param.20) | copy-start | bytes 1540
  175.2 3.0 %copy-start.2 = (bf16[256,2048]{1,0:T(8,128)(2,1)S(1)}, bf16[256,2048]{1,0:T(8,128)(2,1)}, u32[]{:S(2)}) copy-start(bf16[256,2048]{1,0:T(8,128)(2,1)} %pad_maximum_fusion) | copy-start | bytes 3145732
  181.0 21.6 %all-to-all-start.2 = ((f32[128,2,128]{2,1,0:T(2,128)}), f32[128,2,128]{2,1,0:T(2,128)S(1)}, u32[]{:S(2)}, u32[]{:S(2)}) async-start(f32[128,2,128]{2,1,0:T(2,128)} %bitcast.124), calls=%async_computation.2 | async-start | bytes 262144 | tf_op jit(solution)/shard_map/all_to_all | solution.py:34
  203.4 18.7 %all-to-all-start.3 = ((f32[128,2,128]{2,1,0:T(2,128)}), f32[128,2,128]{2,1,0:T(2,128)S(1)}, u32[]{:S(2)}, u32[]{:S(2)}) async-start(f32[128,2,128]{2,1,0:T(2,128)} %broadcast_in_dim.87), calls=%async_computation.3 | async-start | bytes 262144 | tf_op jit(solution)/shard_map/all_to_all | solution.py:38
  209.3 15.0 %collective-permute-start.6 = (bf16[64,2048]{1,0:T(8,128)(2,1)}, bf16[64,2048]{1,0:T(8,128)(2,1)}, u32[]{:S(2)}, u32[]{:S(2)}) collective-permute-start(bf16[64,2048]{1,0:T(8,128)(2,1)} %bitcast.126), channel_id=1, source_target_pairs={{0,1},{1,0},{2,3},{3,2},{4,5},{5,4},{6,7},{7,6},{8,9},{9,8},{10,11... | collective-permute-start | bytes 786440 | tf_op jit(solution)/shard_map/ppermute | solution.py:152
  211.2 14.1 %collective-permute-start.8 = (bf16[64,2048]{1,0:T(8,128)(2,1)}, bf16[64,2048]{1,0:T(8,128)(2,1)}, u32[]{:S(2)}, u32[]{:S(2)}) collective-permute-start(bf16[64,2048]{1,0:T(8,128)(2,1)} %bitcast.127), channel_id=1, source_target_pairs={{0,3},{1,2},{2,1},{3,0},{4,7},{5,6},{6,5},{7,4},{8,11},{9,10},{10,... | collective-permute-start | bytes 786440 | tf_op jit(solution)/shard_map/ppermute | solution.py:152
  214.9 10.4 %collective-permute-start.7 = (bf16[64,2048]{1,0:T(8,128)(2,1)}, bf16[64,2048]{1,0:T(8,128)(2,1)}, u32[]{:S(2)}, u32[]{:S(2)}) collective-permute-start(bf16[64,2048]{1,0:T(8,128)(2,1)} %bitcast.128), channel_id=1, source_target_pairs={{0,2},{1,3},{2,0},{3,1},{4,6},{5,7},{6,4},{7,5},{8,10},{9,11},{10,... | collective-permute-start | bytes 786440 | tf_op jit(solution)/shard_map/ppermute | solution.py:152
  (2 other events, 1.9 us)

commit v14 on v12

--- a/solution.py
+++ b/solution.py
@@ -39,6 +39,16 @@
     return total.reshape(rows, cols), rider
 
 
+def neighbour_order(values, axis, count):
+    if count != 4:
+        return exchange_order(values, axis, count, count)
+    pairs = lambda offset: [(i, i ^ offset) for i in range(count)]
+    first = lax.ppermute(values, axis, pairs(1))
+    third = lax.ppermute(values, axis, pairs(3))
+    second = lax.ppermute(first, axis, pairs(3))
+    return [values, first, second, third]
+
+
 def per_device(
     node_feats, weight, bias_vec, adj_tiles, tile_row, tile_col, tile_count, send_block, cotangent
 ):
@@ -61,7 +71,7 @@
         jnp.zeros((), adj_tiles.dtype),
     )
     order = lax.axis_index("feat") ^ jnp.arange(parts)
-    pieces = exchange_order(node_feats, "feat", parts, parts)
+    pieces = neighbour_order(node_feats, "feat", parts)
     in_rows = weight.shape[0] // parts
     weight_ordered = jnp.take(
         weight.reshape(parts, in_rows, weight.shape[1]), order, axis=0, mode="clip"

time: 231 us -> 231 us (level)
  waiting for transfers between devices: 86.1 us -> 90.7 us
  starting transfers between devices: 77 us -> 74 us
    ppermute x0 -> x3, starting transfers between devices: none -> 11.5 us  [the longest x1 4.22 us: neighbour_order(): first = lax.ppermute(values, axis, pairs(1))]
    ppermute x6 -> x3, starting transfers between devices: 20.1 us -> 9.58 us  [exchange_order(): received.append(lax.ppermute(values, axis, pairs))]
    ppermute x0 -> x3, waiting for transfers between devices: none -> 4.55 us  [the longest x1 4.55 us: neighbour_order(): second = lax.ppermute(first, axis, pairs(3))]
    all_to_all x1, starting transfers between devices: 24 us -> 20.1 us  [per_device(): lax.all_to_all(outgoing, 'dom', split_axis=1, concat_axis=1, tiled=True)]
where the time goes in v14:
time: 231 us; the launch traced here: 229 us
  waiting for transfers between devices  90.7 us (39%)
  starting transfers between devices  74 us (32%)
  matrix products  37.2 us (16%)
  local copies, waits for them, and re-layouts  18.7 us (8%)
  other arithmetic  6.82 us (3%)
    all_to_all x1, waiting for transfers between devices, per_device(): lax.all_to_all(outgoing, 'dom', split_axis=1, concat_axis=1, tiled=True)  35.9 us
    all_to_all x1, waiting for transfers between devices, per_device(): lax.all_to_all(out_parts, 'dom', split_axis=1, concat_axis=1, tiled=True)  31.7 us
    all_to_all x1, starting transfers between devices, per_device(): lax.all_to_all(outgoing, 'dom', split_axis=1, concat_axis=1, tiled=True)  20.1 us
    all_to_all x1, waiting for transfers between devices, scatter_gather_sum(): lax.all_to_all(values.reshape(size, chunk, cols), axis, 0, 0, tiled=True)  12 us
    ppermute x3, starting transfers between devices, exchange_order(): received.append(lax.ppermute(values, axis, pairs))  9.58 us
    all_to_all x1, starting transfers between devices, per_device(): lax.all_to_all(out_parts, 'dom', split_axis=1, concat_axis=1, tiled=True)  9.44 us
    ppermute x3, starting transfers between devices, per_device(): grad_pieces.append(lax.ppermute(source, 'feat', pairs))  8.98 us
    all_to_all x1, starting transfers between devices, scatter_gather_sum(): lax.all_to_all(values.reshape(size, chunk, cols), axis, 0, 0, tiled=True)  8.85 us
  transfers between devices with their start and end apart: 13, of which 6 were waited for; matrix products, arithmetic and copies ran while one was open for 14% of the time, Pallas kernels for 0%

profile of v14, /device:TPU:1, one launch (start us, length us, event | category | flops | bytes accessed | tf_op | source)
XLA Modules:
  0.0 229.2 jit_solution(9045415145215383179)
XLA Ops:
  0.6 4.2 %collective-permute-start = (bf16[64,2048]{1,0:T(8,128)(2,1)}, bf16[64,2048]{1,0:T(8,128)(2,1)}, u32[]{:S(2)}, u32[]{:S(2)}) collective-permute-start(bf16[64,2048]{1,0:T(8,128)(2,1)} %param.13), channel_id=1, source_target_pairs={{0,1},{1,0},{2,3},{3,2},{4,5},{5,4},{6,7},{7,6},{8,9},{9,8},{10,11... | collective-permute-start | bytes 786440 | tf_op jit(solution)/shard_map/ppermute | solution.py:46
  4.9 3.7 %collective-permute-start.2 = (bf16[64,2048]{1,0:T(8,128)(2,1)}, bf16[64,2048]{1,0:T(8,128)(2,1)S(1)}, u32[]{:S(2)}, u32[]{:S(2)}) collective-permute-start(bf16[64,2048]{1,0:T(8,128)(2,1)} %param.13), channel_id=1, source_target_pairs={{0,3},{1,2},{2,1},{3,0},{4,7},{5,6},{6,5},{7,4},{8,11},{9,10},{10,... | collective-permute-start | bytes 786440 | tf_op jit(solution)/shard_map/ppermute | solution.py:47
  12.0 3.5 %collective-permute-start.1 = (bf16[64,2048]{1,0:T(8,128)(2,1)}, bf16[64,2048]{1,0:T(8,128)(2,1)S(1)}, u32[]{:S(2)}, u32[]{:S(2)}) collective-permute-start(bf16[64,2048]{1,0:T(8,128)(2,1)} %collective-permute-done), channel_id=1, source_target_pairs={{0,3},{1,2},{2,1},{3,0},{4,7},{5,6},{6,5},{7,4},{8,11},{9,10},{10,... | collective-permute-start | bytes 786440 | tf_op jit(solution)/shard_map/ppermute | solution.py:48
  17.0 4.5 %collective-permute-done.1 = bf16[64,2048]{1,0:T(8,128)(2,1)S(1)} collective-permute-done((bf16[64,2048]{1,0:T(8,128)(2,1)}, bf16[64,2048]{1,0:T(8,128)(2,1)S(1)}, u32[]{:S(2)}, u32[]{:S(2)}) %collective-permute-start.1) | collective-permute-done | bytes 262176 | tf_op jit(solution)/shard_map/ppermute | solution.py:48
  24.4 20.1 %all-to-all-start = ((bf16[64,128,128]{2,0,1:T(8,128)(2,1)}), bf16[64,128,128]{2,0,1:T(8,128)(2,1)}, u32[]{:S(2)}, u32[]{:S(2)}) async-start(bf16[64,128,128]{2,0,1:T(8,128)(2,1)} %bitcast.105), calls=%async_computation | async-start | bytes 4194304 | tf_op jit(solution)/shard_map/all_to_all | solution.py:87
  45.5 3.0 %gather_fusion.3 = bf16[128,128,128]{2,1,0:T(8,128)(2,1)} fusion(bf16[96,128,128]{2,1,0:T(8,128)(2,1)S(1)} %copy-done, s32[1024]{0:T(1024)S(1)} %pad_clamp_fusion.2), kind=kCustom, calls=%fused_computation.3 | custom fusion | bytes 8389120 | tf_op jit(solution)/shard_map/jit(_take)/gather | solution.py:70
  55.3 4.1 %fusion.22 = f32[64,16,128]{2,1,0:T(8,128)} fusion(f32[64,96,128]{2,0,1:T(8,128)S(1)} %convolution_bitcast_fusion.2, f32[96]{0:T(128)S(1)} %and_convert_fusion, s32[96]{0:T(128)S(1)} %copy-done.9), kind=kOutput, calls=%fused_computation.31 | convolution fusion | flops 150998016 | bytes 3670784 | tf_op jit(solution)/shard_map/ota,tr->ora/dot_general | solution.py:95
  59.4 35.9 %all-to-all-done = bf16[64,128,128]{2,0,1:T(8,128)(2,1)} async-done(((bf16[64,128,128]{2,0,1:T(8,128)(2,1)}), bf16[64,128,128]{2,0,1:T(8,128)(2,1)}, u32[]{:S(2)}, u32[]{:S(2)}) %all-to-all-start) | async-done | bytes 2097184 | tf_op jit(solution)/shard_map/all_to_all | solution.py:87
  95.3 5.8 %convolution_bitcast_fusion = f32[64,128,128]{2,0,1:T(8,128)S(1)} fusion(bf16[64,128,128]{2,0,1:T(8,128)(2,1)} %all-to-all-done, bf16[128,128,128]{2,1,0:T(8,128)(2,1)} %gather_fusion.3, pred[128]{0:T(512)(128)(4,1)S(1)} %fusion.46), kind=kOutput, calls=%fused_computation.19 | convolution fusion | flops 270532608 | bytes 10485888 | tf_op jit(solution)/shard_map/oqb,qab->oqa/dot_general | solution.py:101
  101.2 4.4 %fusion.16 = f32[64,16,128]{2,1,0:T(8,128)S(1)} fusion(f32[64,128,128]{2,0,1:T(8,128)S(1)} %convolution_bitcast_fusion, f32[128]{0:T(128)S(1)} %convert_element_type.62, s32[128]{0:T(128)S(1)} %get-tuple-element.44), kind=kOutput, calls=%fused_computation.29 | convolution fusion | flops 201330688 | bytes 4719616 | tf_op jit(solution)/shard_map/oqa,qr->ora/dot_general | solution.py:104
  109.4 5.5 %convert_bitcast_fusion = bf16[64,128,128]{2,0,1:T(8,128)(2,1)} fusion(bf16[128,64,128]{2,1,0:T(8,128)(2,1)} %gather_fusion.4, bf16[128,128,128]{2,1,0:T(8,128)(2,1)} %gather_fusion.3, pred[128]{0:T(512)(128)(4,1)S(1)} %fusion.46), kind=kOutput, calls=%fused_computation.24 | convolution fusion | flops 271581184 | bytes 8388736 | tf_op jit(solution)/shard_map/oqa,qab->oqb/dot_general | solution.py:123
  114.9 9.4 %all-to-all-start.1 = ((bf16[64,128,128]{2,0,1:T(8,128)(2,1)}), bf16[64,128,128]{2,0,1:T(8,128)(2,1)}, u32[]{:S(2)}, u32[]{:S(2)}) async-start(bf16[64,128,128]{2,0,1:T(8,128)(2,1)} %convert_bitcast_fusion), calls=%async_computation.1 | async-start | bytes 4194304 | tf_op jit(solution)/shard_map/all_to_all | solution.py:126
  126.8 4.7 %collective-permute-start.4 = (bf16[256,64]{0,1:T(8,128)(2,1)S(1)}, bf16[256,64]{0,1:T(8,128)(2,1)S(1)}, u32[]{:S(2)}, u32[]{:S(2)}) collective-permute-start(bf16[256,64]{0,1:T(8,128)(2,1)S(1)} %copy-done.8), channel_id=1, source_target_pairs={{0,2},{1,3},{2,0},{3,1},{4,6},{5,7},{6,4},{7,5},{8,10},{9,11},{10,... | collective-permute-start | bytes 98312 | tf_op jit(solution)/shard_map/ppermute | solution.py:27
  131.5 2.9 %collective-permute-start.5 = (bf16[256,64]{0,1:T(8,128)(2,1)S(1)}, bf16[256,64]{0,1:T(8,128)(2,1)S(1)}, u32[]{:S(2)}, u32[]{:S(2)}) collective-permute-start(bf16[256,64]{0,1:T(8,128)(2,1)S(1)} %copy-done.8), channel_id=1, source_target_pairs={{0,3},{1,2},{2,1},{3,0},{4,7},{5,6},{6,5},{7,4},{8,11},{9,10},{10,... | collective-permute-start | bytes 98312 | tf_op jit(solution)/shard_map/ppermute | solution.py:27
  138.8 4.1 %fusion.2 = f32[16,64,128]{2,0,1:T(8,128)} fusion(f32[64,96,128]{2,0,1:T(8,128)S(1)} %convolution_bitcast_fusion.1, f32[96]{0:T(128)S(1)} %copy-done.12, s32[96]{0:T(128)S(1)} %copy-done.10), kind=kOutput, calls=%fused_computation.10 | convolution fusion | flops 150998016 | bytes 3670784 | tf_op jit(solution)/shard_map/otb,tr->orb/dot_general | solution.py:119
  143.6 31.7 %all-to-all-done.1 = bf16[64,128,128]{2,0,1:T(8,128)(2,1)} async-done(((bf16[64,128,128]{2,0,1:T(8,128)(2,1)}), bf16[64,128,128]{2,0,1:T(8,128)(2,1)}, u32[]{:S(2)}, u32[]{:S(2)}) %all-to-all-start.1) | async-done | bytes 2097184 | tf_op jit(solution)/shard_map/all_to_all | solution.py:126
  175.3 3.0 %fusion.25 = bf16[16,64,128]{2,0,1:T(8,128)(2,1)S(1)} fusion(f32[16,64,128]{2,0,1:T(8,128)} %fusion.2, bf16[64,128,128]{2,0,1:T(8,128)(2,1)} %all-to-all-done.1, s32[128]{0:T(128)S(1)} %copy-done.11), kind=kOutput, calls=%fused_computation.32 | convolution fusion | flops 33822720 | bytes 2884096 | tf_op jit(solution)/shard_map/oqb,qr->orb/dot_general | solution.py:130
  181.1 8.8 %all-to-all-start.2 = ((f32[128,2,128]{2,1,0:T(2,128)}), f32[128,2,128]{2,1,0:T(2,128)S(1)}, u32[]{:S(2)}, u32[]{:S(2)}) async-start(f32[128,2,128]{2,1,0:T(2,128)} %bitcast.109), calls=%async_computation.2 | async-start | bytes 262144 | tf_op jit(solution)/shard_map/all_to_all | solution.py:34
  190.7 12.0 %all-to-all-done.2 = f32[128,2,128]{2,1,0:T(2,128)S(1)} async-done(((f32[128,2,128]{2,1,0:T(2,128)}), f32[128,2,128]{2,1,0:T(2,128)S(1)}, u32[]{:S(2)}, u32[]{:S(2)}) %all-to-all-start.2) | async-done | bytes 131104 | tf_op jit(solution)/shard_map/all_to_all | solution.py:34
  203.5 5.6 %all-to-all-start.3 = ((f32[128,2,128]{2,1,0:T(2,128)}), f32[128,2,128]{2,1,0:T(2,128)S(1)}, u32[]{:S(2)}, u32[]{:S(2)}) async-start(f32[128,2,128]{2,1,0:T(2,128)} %broadcast_in_dim.87), calls=%async_computation.3 | async-start | bytes 262144 | tf_op jit(solution)/shard_map/all_to_all | solution.py:38
  211.0 3.5 %collective-permute-start.8 = (bf16[64,2048]{1,0:T(8,128)(2,1)}, bf16[64,2048]{1,0:T(8,128)(2,1)}, u32[]{:S(2)}, u32[]{:S(2)}) collective-permute-start(bf16[64,2048]{1,0:T(8,128)(2,1)} %bitcast.112), channel_id=1, source_target_pairs={{0,3},{1,2},{2,1},{3,0},{4,7},{5,6},{6,5},{7,4},{8,11},{9,10},{10,... | collective-permute-start | bytes 786440 | tf_op jit(solution)/shard_map/ppermute | solution.py:154
  214.6 3.5 %collective-permute-start.7 = (bf16[64,2048]{1,0:T(8,128)(2,1)}, bf16[64,2048]{1,0:T(8,128)(2,1)}, u32[]{:S(2)}, u32[]{:S(2)}) collective-permute-start(bf16[64,2048]{1,0:T(8,128)(2,1)} %bitcast.113), channel_id=1, source_target_pairs={{0,2},{1,3},{2,0},{3,1},{4,6},{5,7},{6,4},{7,5},{8,10},{9,11},{10,... | collective-permute-start | bytes 786440 | tf_op jit(solution)/shard_map/ppermute | solution.py:154
  218.1 3.8 %all-to-all-done.3 = f32[128,2,128]{2,1,0:T(2,128)S(1)} async-done(((f32[128,2,128]{2,1,0:T(2,128)}), f32[128,2,128]{2,1,0:T(2,128)S(1)}, u32[]{:S(2)}, u32[]{:S(2)}) %all-to-all-start.3) | async-done | bytes 131104 | tf_op jit(solution)/shard_map/all_to_all | solution.py:38
  224.0 2.8 %collective-permute-done.8 = bf16[64,2048]{1,0:T(8,128)(2,1)} collective-permute-done((bf16[64,2048]{1,0:T(8,128)(2,1)}, bf16[64,2048]{1,0:T(8,128)(2,1)}, u32[]{:S(2)}, u32[]{:S(2)}) %collective-permute-start.8) | collective-permute-done | bytes 262176 | tf_op jit(solution)/shard_map/ppermute | solution.py:154
  (87 shorter events, 36.6 us)
Async XLA Ops:
  0.6 44.9 %copy-start = (bf16[96,128,128]{2,1,0:T(8,128)(2,1)S(1)}, bf16[96,128,128]{2,1,0:T(8,128)(2,1)}, u32[]{:S(2)}) copy-start(bf16[96,128,128]{2,1,0:T(8,128)(2,1)} %param.16) | copy-start | bytes 9437188
  0.6 11.3 %collective-permute-start = (bf16[64,2048]{1,0:T(8,128)(2,1)}, bf16[64,2048]{1,0:T(8,128)(2,1)}, u32[]{:S(2)}, u32[]{:S(2)}) collective-permute-start(bf16[64,2048]{1,0:T(8,128)(2,1)} %param.13), channel_id=1, source_target_pairs={{0,1},{1,0},{2,3},{3,2},{4,5},{5,4},{6,7},{7,6},{8,9},{9,8},{10,11... | collective-permute-start | bytes 786440 | tf_op jit(solution)/shard_map/ppermute | solution.py:46
  4.9 10.6 %collective-permute-start.2 = (bf16[64,2048]{1,0:T(8,128)(2,1)}, bf16[64,2048]{1,0:T(8,128)(2,1)S(1)}, u32[]{:S(2)}, u32[]{:S(2)}) collective-permute-start(bf16[64,2048]{1,0:T(8,128)(2,1)} %param.13), channel_id=1, source_target_pairs={{0,3},{1,2},{2,1},{3,0},{4,7},{5,6},{6,5},{7,4},{8,11},{9,10},{10,... | collective-permute-start | bytes 786440 | tf_op jit(solution)/shard_map/ppermute | solution.py:47
  12.0 9.6 %collective-permute-start.1 = (bf16[64,2048]{1,0:T(8,128)(2,1)}, bf16[64,2048]{1,0:T(8,128)(2,1)S(1)}, u32[]{:S(2)}, u32[]{:S(2)}) collective-permute-start(bf16[64,2048]{1,0:T(8,128)(2,1)} %collective-permute-done), channel_id=1, source_target_pairs={{0,3},{1,2},{2,1},{3,0},{4,7},{5,6},{6,5},{7,4},{8,11},{9,10},{10,... | collective-permute-start | bytes 786440 | tf_op jit(solution)/shard_map/ppermute | solution.py:48
  15.5 6.0 %copy-start.4 = (bf16[64,2048]{1,0:T(8,128)(2,1)}, bf16[64,2048]{1,0:T(8,128)(2,1)S(1)}, u32[]{:S(2)}) copy-start(bf16[64,2048]{1,0:T(8,128)(2,1)S(1)} %collective-permute-done.2) | copy-start | bytes 786436
  24.4 20.8 %copy-start.10 = (s32[96]{0:T(128)S(1)}, s32[96]{0:T(128)}, u32[]{:S(2)}) copy-start(s32[96]{0:T(128)} %param.18) | copy-start | bytes 1156
  24.4 21.0 %copy-start.13 = (bf16[64]{0:T(256)(128)(2,1)S(1)}, bf16[64]{0:T(256)(128)(2,1)}, u32[]{:S(2)}) copy-start(bf16[64]{0:T(256)(128)(2,1)} %param.15) | copy-start | bytes 388
  24.4 21.0 %copy-start.9 = (s32[96]{0:T(128)S(1)}, s32[96]{0:T(128)}, u32[]{:S(2)}) copy-start(s32[96]{0:T(128)} %param.17) | copy-start | bytes 1156
  24.4 70.9 %all-to-all-start = ((bf16[64,128,128]{2,0,1:T(8,128)(2,1)}), bf16[64,128,128]{2,0,1:T(8,128)(2,1)}, u32[]{:S(2)}, u32[]{:S(2)}) async-start(bf16[64,128,128]{2,0,1:T(8,128)(2,1)} %bitcast.105), calls=%async_computation | async-start | bytes 4194304 | tf_op jit(solution)/shard_map/all_to_all | solution.py:87
  50.6 2.4 %copy-start.1 = (bf16[96,64,128]{2,1,0:T(8,128)(2,1)S(1)}, bf16[96,64,128]{2,1,0:T(8,128)(2,1)}, u32[]{:S(2)}) copy-start(bf16[96,64,128]{2,1,0:T(8,128)(2,1)} %gather_fusion.1) | copy-start | bytes 4718596
  101.1 4.4 %copy-start.3 = (f32[64,16,128]{2,1,0:T(8,128)S(1)}, f32[64,16,128]{2,1,0:T(8,128)}, u32[]{:S(2)}) copy-start(f32[64,16,128]{2,1,0:T(8,128)} %fusion.22) | copy-start | bytes 1572868
  101.1 4.4 %copy-start.7 = (bf16[64,2048]{1,0:T(8,128)(2,1)S(1)}, bf16[64,2048]{1,0:T(8,128)(2,1)}, u32[]{:S(2)}) copy-start(bf16[64,2048]{1,0:T(8,128)(2,1)} %param.21) | copy-start | bytes 786436
  114.9 10.0 %copy-start.8 = (bf16[256,64]{0,1:T(8,128)(2,1)S(1)}, bf16[256,64]{0,1:T(8,128)(2,1)}, u32[]{:S(2)}) copy-start(bf16[256,64]{0,1:T(8,128)(2,1)} %param.14) | copy-start | bytes 98308
  114.9 60.4 %all-to-all-start.1 = ((bf16[64,128,128]{2,0,1:T(8,128)(2,1)}), bf16[64,128,128]{2,0,1:T(8,128)(2,1)}, u32[]{:S(2)}, u32[]{:S(2)}) async-start(bf16[64,128,128]{2,0,1:T(8,128)(2,1)} %convert_bitcast_fusion), calls=%async_computation.1 | async-start | bytes 4194304 | tf_op jit(solution)/shard_map/all_to_all | solution.py:126
  124.9 18.1 %collective-permute-start.3 = (bf16[256,64]{0,1:T(8,128)(2,1)S(1)}, bf16[256,64]{0,1:T(8,128)(2,1)S(1)}, u32[]{:S(2)}, u32[]{:S(2)}) collective-permute-start(bf16[256,64]{0,1:T(8,128)(2,1)S(1)} %copy-done.8), channel_id=1, source_target_pairs={{0,1},{1,0},{2,3},{3,2},{4,5},{5,4},{6,7},{7,6},{8,9},{9,8},{10,11... | collective-permute-start | bytes 98312 | tf_op jit(solution)/shard_map/ppermute | solution.py:27
  126.8 16.1 %collective-permute-start.4 = (bf16[256,64]{0,1:T(8,128)(2,1)S(1)}, bf16[256,64]{0,1:T(8,128)(2,1)S(1)}, u32[]{:S(2)}, u32[]{:S(2)}) collective-permute-start(bf16[256,64]{0,1:T(8,128)(2,1)S(1)} %copy-done.8), channel_id=1, source_target_pairs={{0,2},{1,3},{2,0},{3,1},{4,6},{5,7},{6,4},{7,5},{8,10},{9,11},{10,... | collective-permute-start | bytes 98312 | tf_op jit(solution)/shard_map/ppermute | solution.py:27
  131.5 11.4 %collective-permute-start.5 = (bf16[256,64]{0,1:T(8,128)(2,1)S(1)}, bf16[256,64]{0,1:T(8,128)(2,1)S(1)}, u32[]{:S(2)}, u32[]{:S(2)}) collective-permute-start(bf16[256,64]{0,1:T(8,128)(2,1)S(1)} %copy-done.8), channel_id=1, source_target_pairs={{0,3},{1,2},{2,1},{3,0},{4,7},{5,6},{6,5},{7,4},{8,11},{9,10},{10,... | collective-permute-start | bytes 98312 | tf_op jit(solution)/shard_map/ppermute | solution.py:27
  138.8 36.5 %copy-start.11 = (s32[128]{0:T(128)S(1)}, s32[128]{0:T(128)}, u32[]{:S(2)}) copy-start(s32[128]{0:T(128)} %param.20) | copy-start | bytes 1540
  175.3 3.0 %copy-start.2 = (bf16[256,2048]{1,0:T(8,128)(2,1)S(1)}, bf16[256,2048]{1,0:T(8,128)(2,1)}, u32[]{:S(2)}) copy-start(bf16[256,2048]{1,0:T(8,128)(2,1)} %pad_maximum_fusion) | copy-start | bytes 3145732
  181.1 21.6 %all-to-all-start.2 = ((f32[128,2,128]{2,1,0:T(2,128)}), f32[128,2,128]{2,1,0:T(2,128)S(1)}, u32[]{:S(2)}, u32[]{:S(2)}) async-start(f32[128,2,128]{2,1,0:T(2,128)} %bitcast.109), calls=%async_computation.2 | async-start | bytes 262144 | tf_op jit(solution)/shard_map/all_to_all | solution.py:34
  203.5 18.4 %all-to-all-start.3 = ((f32[128,2,128]{2,1,0:T(2,128)}), f32[128,2,128]{2,1,0:T(2,128)S(1)}, u32[]{:S(2)}, u32[]{:S(2)}) async-start(f32[128,2,128]{2,1,0:T(2,128)} %broadcast_in_dim.87), calls=%async_computation.3 | async-start | bytes 262144 | tf_op jit(solution)/shard_map/all_to_all | solution.py:38
  209.1 15.0 %collective-permute-start.6 = (bf16[64,2048]{1,0:T(8,128)(2,1)}, bf16[64,2048]{1,0:T(8,128)(2,1)}, u32[]{:S(2)}, u32[]{:S(2)}) collective-permute-start(bf16[64,2048]{1,0:T(8,128)(2,1)} %bitcast.111), channel_id=1, source_target_pairs={{0,1},{1,0},{2,3},{3,2},{4,5},{5,4},{6,7},{7,6},{8,9},{9,8},{10,11... | collective-permute-start | bytes 786440 | tf_op jit(solution)/shard_map/ppermute | solution.py:154
  211.0 15.8 %collective-permute-start.8 = (bf16[64,2048]{1,0:T(8,128)(2,1)}, bf16[64,2048]{1,0:T(8,128)(2,1)}, u32[]{:S(2)}, u32[]{:S(2)}) collective-permute-start(bf16[64,2048]{1,0:T(8,128)(2,1)} %bitcast.112), channel_id=1, source_target_pairs={{0,3},{1,2},{2,1},{3,0},{4,7},{5,6},{6,5},{7,4},{8,11},{9,10},{10,... | collective-permute-start | bytes 786440 | tf_op jit(solution)/shard_map/ppermute | solution.py:154
  214.6 12.3 %collective-permute-start.7 = (bf16[64,2048]{1,0:T(8,128)(2,1)}, bf16[64,2048]{1,0:T(8,128)(2,1)}, u32[]{:S(2)}, u32[]{:S(2)}) collective-permute-start(bf16[64,2048]{1,0:T(8,128)(2,1)} %bitcast.113), channel_id=1, source_target_pairs={{0,2},{1,3},{2,0},{3,1},{4,6},{5,7},{6,4},{7,5},{8,10},{9,11},{10,... | collective-permute-start | bytes 786440 | tf_op jit(solution)/shard_map/ppermute | solution.py:154
  (3 other events, 3.7 us)

commit v15 on v12

--- a/solution.py
+++ b/solution.py
@@ -91,7 +91,7 @@
     far_products = jnp.einsum(
         "oqb,qab->oqa", incoming, peer_tiles, preferred_element_type=jnp.float32
     )
-    summed_far = jnp.einsum("oqa,qr->ora", far_products, far_place, precision=lax.Precision.HIGHEST)
+    summed_far = jnp.einsum("oqa,qr->ora", far_products, far_place, precision=lax.Precision.HIGH)
     summed = (summed_local + summed_far).reshape(feat_rows, node_rows)
     preact = summed + bias_vec.astype(jnp.float32)[:, None]
     activated, pullback = jax.vjp(smooth_gate, preact)

time: 231 us -> 230 us (level)
  no operation moved by 1% of the time
where the time goes in v15:
time: 230 us; the launch traced here: 227 us
  waiting for transfers between devices  86.1 us (37%)
  starting transfers between devices  77 us (33%)
  matrix products  37.3 us (16%)
  local copies, waits for them, and re-layouts  18.3 us (8%)
  other arithmetic  6.6 us (3%)
    all_to_all x1, waiting for transfers between devices, per_device(): lax.all_to_all(outgoing, 'dom', split_axis=1, concat_axis=1, tiled=True)  35.9 us
    all_to_all x1, waiting for transfers between devices, per_device(): lax.all_to_all(out_parts, 'dom', split_axis=1, concat_axis=1, tiled=True)  31.6 us
    all_to_all x1, starting transfers between devices, per_device(): lax.all_to_all(outgoing, 'dom', split_axis=1, concat_axis=1, tiled=True)  24 us
    ppermute x6, starting transfers between devices, exchange_order(): received.append(lax.ppermute(values, axis, pairs))  20.1 us
    all_to_all x1, waiting for transfers between devices, scatter_gather_sum(): lax.all_to_all(values.reshape(size, chunk, cols), axis, 0, 0, tiled=True)  12 us
    all_to_all x1, starting transfers between devices, per_device(): lax.all_to_all(out_parts, 'dom', split_axis=1, concat_axis=1, tiled=True)  9.44 us
    ppermute x3, starting transfers between devices, per_device(): grad_pieces.append(lax.ppermute(source, 'feat', pairs))  8.98 us
    all_to_all x1, starting transfers between devices, scatter_gather_sum(): lax.all_to_all(values.reshape(size, chunk, cols), axis, 0, 0, tiled=True)  8.85 us
  transfers between devices with their start and end apart: 13, of which 6 were waited for; matrix products, arithmetic and copies ran while one was open for 14% of the time, Pallas kernels for 0%

profile of v15, /device:TPU:1, one launch (start us, length us, event | category | flops | bytes accessed | tf_op | source)
XLA Modules:
  0.0 226.9 jit_solution(926858819540599487)
XLA Ops:
  0.6 4.2 %collective-permute-start = (bf16[64,2048]{1,0:T(8,128)(2,1)}, bf16[64,2048]{1,0:T(8,128)(2,1)}, u32[]{:S(2)}, u32[]{:S(2)}) collective-permute-start(bf16[64,2048]{1,0:T(8,128)(2,1)} %param.13), channel_id=1, source_target_pairs={{0,1},{1,0},{2,3},{3,2},{4,5},{5,4},{6,7},{7,6},{8,9},{9,8},{10,11... | collective-permute-start | bytes 786440 | tf_op jit(solution)/shard_map/ppermute | solution.py:27
  4.9 3.7 %collective-permute-start.2 = (bf16[64,2048]{1,0:T(8,128)(2,1)}, bf16[64,2048]{1,0:T(8,128)(2,1)S(1)}, u32[]{:S(2)}, u32[]{:S(2)}) collective-permute-start(bf16[64,2048]{1,0:T(8,128)(2,1)} %param.13), channel_id=1, source_target_pairs={{0,3},{1,2},{2,1},{3,0},{4,7},{5,6},{6,5},{7,4},{8,11},{9,10},{10,... | collective-permute-start | bytes 786440 | tf_op jit(solution)/shard_map/ppermute | solution.py:27
  8.6 2.6 %collective-permute-start.1 = (bf16[64,2048]{1,0:T(8,128)(2,1)}, bf16[64,2048]{1,0:T(8,128)(2,1)}, u32[]{:S(2)}, u32[]{:S(2)}) collective-permute-start(bf16[64,2048]{1,0:T(8,128)(2,1)} %param.13), channel_id=1, source_target_pairs={{0,2},{1,3},{2,0},{3,1},{4,6},{5,7},{6,4},{7,5},{8,10},{9,11},{10,... | collective-permute-start | bytes 786440 | tf_op jit(solution)/shard_map/ppermute | solution.py:27
  21.1 24.0 %all-to-all-start = ((bf16[64,128,128]{2,0,1:T(8,128)(2,1)}), bf16[64,128,128]{2,0,1:T(8,128)(2,1)}, u32[]{:S(2)}, u32[]{:S(2)}) async-start(bf16[64,128,128]{2,0,1:T(8,128)(2,1)} %bitcast.105), calls=%async_computation | async-start | bytes 4194304 | tf_op jit(solution)/shard_map/all_to_all | solution.py:77
  46.1 3.0 %gather_fusion.3 = bf16[128,128,128]{2,1,0:T(8,128)(2,1)} fusion(bf16[96,128,128]{2,1,0:T(8,128)(2,1)S(1)} %copy-done, s32[1024]{0:T(1024)S(1)} %pad_clamp_fusion.2), kind=kCustom, calls=%fused_computation.3 | custom fusion | bytes 8389120 | tf_op jit(solution)/shard_map/jit(_take)/gather | solution.py:60
  51.2 2.4 %pad_maximum_fusion = bf16[256,2048]{1,0:T(8,128)(2,1)} fusion(bf16[64,2048]{1,0:T(8,128)(2,1)} %copy-done.4, bf16[64,2048]{1,0:T(8,128)(2,1)} %collective-permute-done.1, bf16[64,2048]{1,0:T(8,128)(2,1)} %collective-permute-done, bf16[64,2048]{1,0:T(8,128)(2,1)} %param.13), kind=kLoop, calls=%fused_computation.34 | loop fusion | flops 4194304 | bytes 2097152 | tf_op jit(solution)/shard_map/concatenate | solution.py:86
  55.9 4.2 %fusion.22 = f32[64,16,128]{2,1,0:T(8,128)} fusion(f32[64,96,128]{2,0,1:T(8,128)S(1)} %convolution_bitcast_fusion.2, f32[96]{0:T(128)S(1)} %and_convert_fusion, s32[96]{0:T(128)S(1)} %copy-done.8), kind=kOutput, calls=%fused_computation.31 | convolution fusion | flops 150998016 | bytes 3670784 | tf_op jit(solution)/shard_map/ota,tr->ora/dot_general | solution.py:85
  60.0 35.9 %all-to-all-done = bf16[64,128,128]{2,0,1:T(8,128)(2,1)} async-done(((bf16[64,128,128]{2,0,1:T(8,128)(2,1)}), bf16[64,128,128]{2,0,1:T(8,128)(2,1)}, u32[]{:S(2)}, u32[]{:S(2)}) %all-to-all-start) | async-done | bytes 2097184 | tf_op jit(solution)/shard_map/all_to_all | solution.py:77
  95.9 5.8 %convolution_bitcast_fusion = f32[64,128,128]{2,0,1:T(8,128)S(1)} fusion(bf16[64,128,128]{2,0,1:T(8,128)(2,1)} %all-to-all-done, bf16[128,128,128]{2,1,0:T(8,128)(2,1)} %gather_fusion.3, pred[128]{0:T(512)(128)(4,1)S(1)} %fusion.46), kind=kOutput, calls=%fused_computation.19 | convolution fusion | flops 270532608 | bytes 10485888 | tf_op jit(solution)/shard_map/oqb,qab->oqa/dot_general | solution.py:91
  101.7 3.3 %fusion.16 = f32[64,16,128]{2,1,0:T(8,128)S(1)} fusion(f32[64,128,128]{2,0,1:T(8,128)S(1)} %convolution_bitcast_fusion, f32[128]{0:T(128)S(1)} %convert_element_type.62, s32[128]{0:T(128)S(1)} %get-tuple-element.44), kind=kOutput, calls=%fused_computation.29 | convolution fusion | flops 100667392 | bytes 4719616 | tf_op jit(solution)/shard_map/oqa,qr->ora/dot_general | solution.py:94
  108.7 5.7 %convert_bitcast_fusion = bf16[64,128,128]{2,0,1:T(8,128)(2,1)} fusion(bf16[128,64,128]{2,1,0:T(8,128)(2,1)} %gather_fusion.4, bf16[128,128,128]{2,1,0:T(8,128)(2,1)} %gather_fusion.3, pred[128]{0:T(512)(128)(4,1)S(1)} %fusion.46), kind=kOutput, calls=%fused_computation.24 | convolution fusion | flops 271581184 | bytes 8388736 | tf_op jit(solution)/shard_map/oqa,qab->oqb/dot_general | solution.py:113
  114.4 9.4 %all-to-all-start.1 = ((bf16[64,128,128]{2,0,1:T(8,128)(2,1)}), bf16[64,128,128]{2,0,1:T(8,128)(2,1)}, u32[]{:S(2)}, u32[]{:S(2)}) async-start(bf16[64,128,128]{2,0,1:T(8,128)(2,1)} %convert_bitcast_fusion), calls=%async_computation.1 | async-start | bytes 4194304 | tf_op jit(solution)/shard_map/all_to_all | solution.py:116
  126.3 4.9 %collective-permute-start.4 = (bf16[256,64]{0,1:T(8,128)(2,1)S(1)}, bf16[256,64]{0,1:T(8,128)(2,1)S(1)}, u32[]{:S(2)}, u32[]{:S(2)}) collective-permute-start(bf16[256,64]{0,1:T(8,128)(2,1)S(1)} %copy-done.7), channel_id=1, source_target_pairs={{0,2},{1,3},{2,0},{3,1},{4,6},{5,7},{6,4},{7,5},{8,10},{9,11},{10,... | collective-permute-start | bytes 98312 | tf_op jit(solution)/shard_map/ppermute | solution.py:27
  131.2 2.8 %collective-permute-start.5 = (bf16[256,64]{0,1:T(8,128)(2,1)S(1)}, bf16[256,64]{0,1:T(8,128)(2,1)S(1)}, u32[]{:S(2)}, u32[]{:S(2)}) collective-permute-start(bf16[256,64]{0,1:T(8,128)(2,1)S(1)} %copy-done.7), channel_id=1, source_target_pairs={{0,3},{1,2},{2,1},{3,0},{4,7},{5,6},{6,5},{7,4},{8,11},{9,10},{10,... | collective-permute-start | bytes 98312 | tf_op jit(solution)/shard_map/ppermute | solution.py:27
  135.9 2.4 %convolution_bitcast_fusion.1 = f32[64,96,128]{2,0,1:T(8,128)S(1)} fusion(bf16[96,128,128]{2,1,0:T(8,128)(2,1)S(1)} %copy-done, bf16[96,64,128]{2,1,0:T(8,128)(2,1)} %gather_fusion.5), kind=kOutput, calls=%fused_computation.25 | convolution fusion | flops 201326592 | bytes 7864320 | tf_op jit(solution)/shard_map/ota,tab->otb/dot_general | solution.py:102
  138.3 4.1 %fusion.2 = f32[16,64,128]{2,0,1:T(8,128)} fusion(f32[64,96,128]{2,0,1:T(8,128)S(1)} %convolution_bitcast_fusion.1, f32[96]{0:T(128)S(1)} %copy-done.11, s32[96]{0:T(128)S(1)} %copy-done.9), kind=kOutput, calls=%fused_computation.10 | convolution fusion | flops 150998016 | bytes 3670784 | tf_op jit(solution)/shard_map/otb,tr->orb/dot_general | solution.py:109
  143.1 31.6 %all-to-all-done.1 = bf16[64,128,128]{2,0,1:T(8,128)(2,1)} async-done(((bf16[64,128,128]{2,0,1:T(8,128)(2,1)}), bf16[64,128,128]{2,0,1:T(8,128)(2,1)}, u32[]{:S(2)}, u32[]{:S(2)}) %all-to-all-start.1) | async-done | bytes 2097184 | tf_op jit(solution)/shard_map/all_to_all | solution.py:116
  174.8 3.0 %fusion.25 = bf16[16,64,128]{2,0,1:T(8,128)(2,1)S(1)} fusion(f32[16,64,128]{2,0,1:T(8,128)} %fusion.2, bf16[64,128,128]{2,0,1:T(8,128)(2,1)} %all-to-all-done.1, s32[128]{0:T(128)S(1)} %copy-done.10), kind=kOutput, calls=%fused_computation.32 | convolution fusion | flops 33822720 | bytes 2884096 | tf_op jit(solution)/shard_map/oqb,qr->orb/dot_general | solution.py:120
  180.6 8.8 %all-to-all-start.2 = ((f32[128,2,128]{2,1,0:T(2,128)}), f32[128,2,128]{2,1,0:T(2,128)S(1)}, u32[]{:S(2)}, u32[]{:S(2)}) async-start(f32[128,2,128]{2,1,0:T(2,128)} %bitcast.109), calls=%async_computation.2 | async-start | bytes 262144 | tf_op jit(solution)/shard_map/all_to_all | solution.py:34
  190.2 12.0 %all-to-all-done.2 = f32[128,2,128]{2,1,0:T(2,128)S(1)} async-done(((f32[128,2,128]{2,1,0:T(2,128)}), f32[128,2,128]{2,1,0:T(2,128)S(1)}, u32[]{:S(2)}, u32[]{:S(2)}) %all-to-all-start.2) | async-done | bytes 131104 | tf_op jit(solution)/shard_map/all_to_all | solution.py:34
  203.0 5.6 %all-to-all-start.3 = ((f32[128,2,128]{2,1,0:T(2,128)}), f32[128,2,128]{2,1,0:T(2,128)S(1)}, u32[]{:S(2)}, u32[]{:S(2)}) async-start(f32[128,2,128]{2,1,0:T(2,128)} %broadcast_in_dim.87), calls=%async_computation.3 | async-start | bytes 262144 | tf_op jit(solution)/shard_map/all_to_all | solution.py:38
  210.5 3.7 %collective-permute-start.8 = (bf16[64,2048]{1,0:T(8,128)(2,1)}, bf16[64,2048]{1,0:T(8,128)(2,1)}, u32[]{:S(2)}, u32[]{:S(2)}) collective-permute-start(bf16[64,2048]{1,0:T(8,128)(2,1)} %bitcast.112), channel_id=1, source_target_pairs={{0,3},{1,2},{2,1},{3,0},{4,7},{5,6},{6,5},{7,4},{8,11},{9,10},{10,... | collective-permute-start | bytes 786440 | tf_op jit(solution)/shard_map/ppermute | solution.py:144
  214.2 3.3 %collective-permute-start.7 = (bf16[64,2048]{1,0:T(8,128)(2,1)}, bf16[64,2048]{1,0:T(8,128)(2,1)}, u32[]{:S(2)}, u32[]{:S(2)}) collective-permute-start(bf16[64,2048]{1,0:T(8,128)(2,1)} %bitcast.113), channel_id=1, source_target_pairs={{0,2},{1,3},{2,0},{3,1},{4,6},{5,7},{6,4},{7,5},{8,10},{9,11},{10,... | collective-permute-start | bytes 786440 | tf_op jit(solution)/shard_map/ppermute | solution.py:144
  217.6 3.8 %all-to-all-done.3 = f32[128,2,128]{2,1,0:T(2,128)S(1)} async-done(((f32[128,2,128]{2,1,0:T(2,128)}), f32[128,2,128]{2,1,0:T(2,128)S(1)}, u32[]{:S(2)}, u32[]{:S(2)}) %all-to-all-start.3) | async-done | bytes 131104 | tf_op jit(solution)/shard_map/all_to_all | solution.py:38
  (85 shorter events, 34.9 us)
Async XLA Ops:
  0.6 45.5 %copy-start = (bf16[96,128,128]{2,1,0:T(8,128)(2,1)S(1)}, bf16[96,128,128]{2,1,0:T(8,128)(2,1)}, u32[]{:S(2)}) copy-start(bf16[96,128,128]{2,1,0:T(8,128)(2,1)} %param.16) | copy-start | bytes 9437188
  0.6 14.1 %collective-permute-start = (bf16[64,2048]{1,0:T(8,128)(2,1)}, bf16[64,2048]{1,0:T(8,128)(2,1)}, u32[]{:S(2)}, u32[]{:S(2)}) collective-permute-start(bf16[64,2048]{1,0:T(8,128)(2,1)} %param.13), channel_id=1, source_target_pairs={{0,1},{1,0},{2,3},{3,2},{4,5},{5,4},{6,7},{7,6},{8,9},{9,8},{10,11... | collective-permute-start | bytes 786440 | tf_op jit(solution)/shard_map/ppermute | solution.py:27
  4.9 9.6 %collective-permute-start.2 = (bf16[64,2048]{1,0:T(8,128)(2,1)}, bf16[64,2048]{1,0:T(8,128)(2,1)S(1)}, u32[]{:S(2)}, u32[]{:S(2)}) collective-permute-start(bf16[64,2048]{1,0:T(8,128)(2,1)} %param.13), channel_id=1, source_target_pairs={{0,3},{1,2},{2,1},{3,0},{4,7},{5,6},{6,5},{7,4},{8,11},{9,10},{10,... | collective-permute-start | bytes 786440 | tf_op jit(solution)/shard_map/ppermute | solution.py:27
  8.6 9.0 %collective-permute-start.1 = (bf16[64,2048]{1,0:T(8,128)(2,1)}, bf16[64,2048]{1,0:T(8,128)(2,1)}, u32[]{:S(2)}, u32[]{:S(2)}) collective-permute-start(bf16[64,2048]{1,0:T(8,128)(2,1)} %param.13), channel_id=1, source_target_pairs={{0,2},{1,3},{2,0},{3,1},{4,6},{5,7},{6,4},{7,5},{8,10},{9,11},{10,... | collective-permute-start | bytes 786440 | tf_op jit(solution)/shard_map/ppermute | solution.py:27
  14.5 3.1 %copy-start.4 = (bf16[64,2048]{1,0:T(8,128)(2,1)}, bf16[64,2048]{1,0:T(8,128)(2,1)S(1)}, u32[]{:S(2)}) copy-start(bf16[64,2048]{1,0:T(8,128)(2,1)S(1)} %collective-permute-done.2) | copy-start | bytes 786436
  21.1 24.7 %copy-start.9 = (s32[96]{0:T(128)S(1)}, s32[96]{0:T(128)}, u32[]{:S(2)}) copy-start(s32[96]{0:T(128)} %param.18) | copy-start | bytes 1156
  21.1 24.9 %copy-start.12 = (bf16[64]{0:T(256)(128)(2,1)S(1)}, bf16[64]{0:T(256)(128)(2,1)}, u32[]{:S(2)}) copy-start(bf16[64]{0:T(256)(128)(2,1)} %param.15) | copy-start | bytes 388
  21.1 24.9 %copy-start.8 = (s32[96]{0:T(128)S(1)}, s32[96]{0:T(128)}, u32[]{:S(2)}) copy-start(s32[96]{0:T(128)} %param.17) | copy-start | bytes 1156
  21.1 74.8 %all-to-all-start = ((bf16[64,128,128]{2,0,1:T(8,128)(2,1)}), bf16[64,128,128]{2,0,1:T(8,128)(2,1)}, u32[]{:S(2)}, u32[]{:S(2)}) async-start(bf16[64,128,128]{2,0,1:T(8,128)(2,1)} %bitcast.105), calls=%async_computation | async-start | bytes 4194304 | tf_op jit(solution)/shard_map/all_to_all | solution.py:77
  51.2 2.4 %copy-start.1 = (bf16[96,64,128]{2,1,0:T(8,128)(2,1)S(1)}, bf16[96,64,128]{2,1,0:T(8,128)(2,1)}, u32[]{:S(2)}) copy-start(bf16[96,64,128]{2,1,0:T(8,128)(2,1)} %gather_fusion.1) | copy-start | bytes 4718596
  101.7 3.3 %copy-start.3 = (f32[64,16,128]{2,1,0:T(8,128)S(1)}, f32[64,16,128]{2,1,0:T(8,128)}, u32[]{:S(2)}) copy-start(f32[64,16,128]{2,1,0:T(8,128)} %fusion.22) | copy-start | bytes 1572868
  101.7 3.4 %copy-start.6 = (bf16[64,2048]{1,0:T(8,128)(2,1)S(1)}, bf16[64,2048]{1,0:T(8,128)(2,1)}, u32[]{:S(2)}) copy-start(bf16[64,2048]{1,0:T(8,128)(2,1)} %param.21) | copy-start | bytes 786436
  114.4 10.0 %copy-start.7 = (bf16[256,64]{0,1:T(8,128)(2,1)S(1)}, bf16[256,64]{0,1:T(8,128)(2,1)}, u32[]{:S(2)}) copy-start(bf16[256,64]{0,1:T(8,128)(2,1)} %param.14) | copy-start | bytes 98308
  114.4 60.4 %all-to-all-start.1 = ((bf16[64,128,128]{2,0,1:T(8,128)(2,1)}), bf16[64,128,128]{2,0,1:T(8,128)(2,1)}, u32[]{:S(2)}, u32[]{:S(2)}) async-start(bf16[64,128,128]{2,0,1:T(8,128)(2,1)} %convert_bitcast_fusion), calls=%async_computation.1 | async-start | bytes 4194304 | tf_op jit(solution)/shard_map/all_to_all | solution.py:116
  124.4 18.1 %collective-permute-start.3 = (bf16[256,64]{0,1:T(8,128)(2,1)S(1)}, bf16[256,64]{0,1:T(8,128)(2,1)S(1)}, u32[]{:S(2)}, u32[]{:S(2)}) collective-permute-start(bf16[256,64]{0,1:T(8,128)(2,1)S(1)} %copy-done.7), channel_id=1, source_target_pairs={{0,1},{1,0},{2,3},{3,2},{4,5},{5,4},{6,7},{7,6},{8,9},{9,8},{10,11... | collective-permute-start | bytes 98312 | tf_op jit(solution)/shard_map/ppermute | solution.py:27
  126.3 16.1 %collective-permute-start.4 = (bf16[256,64]{0,1:T(8,128)(2,1)S(1)}, bf16[256,64]{0,1:T(8,128)(2,1)S(1)}, u32[]{:S(2)}, u32[]{:S(2)}) collective-permute-start(bf16[256,64]{0,1:T(8,128)(2,1)S(1)} %copy-done.7), channel_id=1, source_target_pairs={{0,2},{1,3},{2,0},{3,1},{4,6},{5,7},{6,4},{7,5},{8,10},{9,11},{10,... | collective-permute-start | bytes 98312 | tf_op jit(solution)/shard_map/ppermute | solution.py:27
  131.2 11.2 %collective-permute-start.5 = (bf16[256,64]{0,1:T(8,128)(2,1)S(1)}, bf16[256,64]{0,1:T(8,128)(2,1)S(1)}, u32[]{:S(2)}, u32[]{:S(2)}) collective-permute-start(bf16[256,64]{0,1:T(8,128)(2,1)S(1)} %copy-done.7), channel_id=1, source_target_pairs={{0,3},{1,2},{2,1},{3,0},{4,7},{5,6},{6,5},{7,4},{8,11},{9,10},{10,... | collective-permute-start | bytes 98312 | tf_op jit(solution)/shard_map/ppermute | solution.py:27
  138.3 36.5 %copy-start.10 = (s32[128]{0:T(128)S(1)}, s32[128]{0:T(128)}, u32[]{:S(2)}) copy-start(s32[128]{0:T(128)} %param.20) | copy-start | bytes 1540
  174.8 3.0 %copy-start.2 = (bf16[256,2048]{1,0:T(8,128)(2,1)S(1)}, bf16[256,2048]{1,0:T(8,128)(2,1)}, u32[]{:S(2)}) copy-start(bf16[256,2048]{1,0:T(8,128)(2,1)} %pad_maximum_fusion) | copy-start | bytes 3145732
  180.6 21.6 %all-to-all-start.2 = ((f32[128,2,128]{2,1,0:T(2,128)}), f32[128,2,128]{2,1,0:T(2,128)S(1)}, u32[]{:S(2)}, u32[]{:S(2)}) async-start(f32[128,2,128]{2,1,0:T(2,128)} %bitcast.109), calls=%async_computation.2 | async-start | bytes 262144 | tf_op jit(solution)/shard_map/all_to_all | solution.py:34
  203.0 18.4 %all-to-all-start.3 = ((f32[128,2,128]{2,1,0:T(2,128)}), f32[128,2,128]{2,1,0:T(2,128)S(1)}, u32[]{:S(2)}, u32[]{:S(2)}) async-start(f32[128,2,128]{2,1,0:T(2,128)} %broadcast_in_dim.87), calls=%async_computation.3 | async-start | bytes 262144 | tf_op jit(solution)/shard_map/all_to_all | solution.py:38
  208.6 15.0 %collective-permute-start.6 = (bf16[64,2048]{1,0:T(8,128)(2,1)}, bf16[64,2048]{1,0:T(8,128)(2,1)}, u32[]{:S(2)}, u32[]{:S(2)}) collective-permute-start(bf16[64,2048]{1,0:T(8,128)(2,1)} %bitcast.111), channel_id=1, source_target_pairs={{0,1},{1,0},{2,3},{3,2},{4,5},{5,4},{6,7},{7,6},{8,9},{9,8},{10,11... | collective-permute-start | bytes 786440 | tf_op jit(solution)/shard_map/ppermute | solution.py:144
  210.5 14.1 %collective-permute-start.8 = (bf16[64,2048]{1,0:T(8,128)(2,1)}, bf16[64,2048]{1,0:T(8,128)(2,1)}, u32[]{:S(2)}, u32[]{:S(2)}) collective-permute-start(bf16[64,2048]{1,0:T(8,128)(2,1)} %bitcast.112), channel_id=1, source_target_pairs={{0,3},{1,2},{2,1},{3,0},{4,7},{5,6},{6,5},{7,4},{8,11},{9,10},{10,... | collective-permute-start | bytes 786440 | tf_op jit(solution)/shard_map/ppermute | solution.py:144
  214.2 10.4 %collective-permute-start.7 = (bf16[64,2048]{1,0:T(8,128)(2,1)}, bf16[64,2048]{1,0:T(8,128)(2,1)}, u32[]{:S(2)}, u32[]{:S(2)}) collective-permute-start(bf16[64,2048]{1,0:T(8,128)(2,1)} %bitcast.113), channel_id=1, source_target_pairs={{0,2},{1,3},{2,0},{3,1},{4,6},{5,7},{6,4},{7,5},{8,10},{9,11},{10,... | collective-permute-start | bytes 786440 | tf_op jit(solution)/shard_map/ppermute | solution.py:144
  (2 other events, 3.0 us)

commit v16 on v15

--- a/solution.py
+++ b/solution.py
@@ -142,11 +142,13 @@
         source = grad_hidden if offset in (1, parts - 1) else late_grad
         pairs = [(i, i ^ offset) for i in range(parts)]
         grad_pieces.append(lax.ppermute(source, "feat", pairs))
-    all_grad = jnp.concatenate(grad_pieces, axis=0)
     my_rows = lax.dynamic_slice_in_dim(
         full_weight, lax.axis_index("feat") * feat_rows, feat_rows, 0
     )
-    grad_input = jnp.dot(my_rows, all_grad, preferred_element_type=jnp.float32).astype(jnp.bfloat16)
+    grad_input = sum(
+        jnp.dot(my_rows[:, s * feat_rows : (s + 1) * feat_rows], piece, preferred_element_type=jnp.float32)
+        for s, piece in enumerate(grad_pieces)
+    ).astype(jnp.bfloat16)
     return (activated.astype(jnp.bfloat16), grad_input, grad_weight, grad_bias)
 
 

time: 230 us -> 232 us (level)
  matrix products: 37.3 us -> 43.5 us
  waiting for transfers between devices: 86.1 us -> 83.1 us
    dot_general x1 -> x4, matrix products: 2.32 us -> 8.56 us  [per_device(): jnp.dot(my_rows[:, s * feat_rows:(s + 1) * feat_rows], piece, preferred_e...]
    all_to_all x1, waiting for transfers between devices: 12 us -> 8.96 us  [scatter_gather_sum(): lax.all_to_all(values.reshape(size, chunk, cols), axis, 0, 0, tiled=True)]
  transfers between devices with their start and end apart: 13 -> 13, of which waited for: 6 -> 5; matrix products, arithmetic and copies ran while one was open for 14% -> 17% of each run, Pallas kernels for 0% -> 0%
where the time goes in v16:
time: 232 us; the launch traced here: 231 us
  waiting for transfers between devices  83.1 us (36%)
  starting transfers between devices  77.6 us (33%)
  matrix products  43.5 us (19%)
  local copies, waits for them, and re-layouts  18.3 us (8%)
  other arithmetic  6.6 us (3%)
    all_to_all x1, waiting for transfers between devices, per_device(): lax.all_to_all(outgoing, 'dom', split_axis=1, concat_axis=1, tiled=True)  35.9 us
    all_to_all x1, waiting for transfers between devices, per_device(): lax.all_to_all(out_parts, 'dom', split_axis=1, concat_axis=1, tiled=True)  31.6 us
    all_to_all x1, starting transfers between devices, per_device(): lax.all_to_all(outgoing, 'dom', split_axis=1, concat_axis=1, tiled=True)  24 us
    ppermute x6, starting transfers between devices, exchange_order(): received.append(lax.ppermute(values, axis, pairs))  20.1 us
    all_to_all x1, starting transfers between devices, per_device(): lax.all_to_all(out_parts, 'dom', split_axis=1, concat_axis=1, tiled=True)  9.44 us
    all_to_all x1, starting transfers between devices, scatter_gather_sum(): lax.all_to_all(values.reshape(size, chunk, cols), axis, 0, 0, tiled=True)  9.13 us
    ppermute x3, starting transfers between devices, per_device(): grad_pieces.append(lax.ppermute(source, 'feat', pairs))  9.07 us
    all_to_all x1, waiting for transfers between devices, scatter_gather_sum(): lax.all_to_all(values.reshape(size, chunk, cols), axis, 0, 0, tiled=True)  8.96 us
  transfers between devices with their start and end apart: 13, of which 5 were waited for; matrix products, arithmetic and copies ran while one was open for 17% of the time, Pallas kernels for 0%

profile of v16, /device:TPU:1, one launch (start us, length us, event | category | flops | bytes accessed | tf_op | source)
XLA Modules:
  0.0 230.9 jit_solution(16130369889930164600)
XLA Ops:
  0.6 4.2 %collective-permute-start = (bf16[64,2048]{1,0:T(8,128)(2,1)}, bf16[64,2048]{1,0:T(8,128)(2,1)}, u32[]{:S(2)}, u32[]{:S(2)}) collective-permute-start(bf16[64,2048]{1,0:T(8,128)(2,1)} %param.13), channel_id=1, source_target_pairs={{0,1},{1,0},{2,3},{3,2},{4,5},{5,4},{6,7},{7,6},{8,9},{9,8},{10,11... | collective-permute-start | bytes 786440 | tf_op jit(solution)/shard_map/ppermute | solution.py:27
  4.9 3.7 %collective-permute-start.2 = (bf16[64,2048]{1,0:T(8,128)(2,1)}, bf16[64,2048]{1,0:T(8,128)(2,1)S(1)}, u32[]{:S(2)}, u32[]{:S(2)}) collective-permute-start(bf16[64,2048]{1,0:T(8,128)(2,1)} %param.13), channel_id=1, source_target_pairs={{0,3},{1,2},{2,1},{3,0},{4,7},{5,6},{6,5},{7,4},{8,11},{9,10},{10,... | collective-permute-start | bytes 786440 | tf_op jit(solution)/shard_map/ppermute | solution.py:27
  8.6 2.6 %collective-permute-start.1 = (bf16[64,2048]{1,0:T(8,128)(2,1)}, bf16[64,2048]{1,0:T(8,128)(2,1)}, u32[]{:S(2)}, u32[]{:S(2)}) collective-permute-start(bf16[64,2048]{1,0:T(8,128)(2,1)} %param.13), channel_id=1, source_target_pairs={{0,2},{1,3},{2,0},{3,1},{4,6},{5,7},{6,4},{7,5},{8,10},{9,11},{10,... | collective-permute-start | bytes 786440 | tf_op jit(solution)/shard_map/ppermute | solution.py:27
  21.1 24.0 %all-to-all-start = ((bf16[64,128,128]{2,0,1:T(8,128)(2,1)}), bf16[64,128,128]{2,0,1:T(8,128)(2,1)}, u32[]{:S(2)}, u32[]{:S(2)}) async-start(bf16[64,128,128]{2,0,1:T(8,128)(2,1)} %bitcast.109), calls=%async_computation | async-start | bytes 4194304 | tf_op jit(solution)/shard_map/all_to_all | solution.py:77
  46.1 3.0 %gather_fusion.3 = bf16[128,128,128]{2,1,0:T(8,128)(2,1)} fusion(bf16[96,128,128]{2,1,0:T(8,128)(2,1)S(1)} %copy-done, s32[1024]{0:T(1024)S(1)} %pad_clamp_fusion.2), kind=kCustom, calls=%fused_computation.3 | custom fusion | bytes 8389120 | tf_op jit(solution)/shard_map/jit(_take)/gather | solution.py:60
  51.2 2.4 %pad_maximum_fusion = bf16[256,2048]{1,0:T(8,128)(2,1)} fusion(bf16[64,2048]{1,0:T(8,128)(2,1)} %copy-done.4, bf16[64,2048]{1,0:T(8,128)(2,1)} %collective-permute-done.1, bf16[64,2048]{1,0:T(8,128)(2,1)} %collective-permute-done, bf16[64,2048]{1,0:T(8,128)(2,1)} %param.13), kind=kLoop, calls=%fused_computation.37 | loop fusion | flops 4194304 | bytes 2097152 | tf_op jit(solution)/shard_map/concatenate | solution.py:86
  55.9 4.2 %fusion.24 = f32[64,16,128]{2,1,0:T(8,128)} fusion(f32[64,96,128]{2,0,1:T(8,128)S(1)} %convolution_bitcast_fusion.2, f32[96]{0:T(128)S(1)} %and_convert_fusion, s32[96]{0:T(128)S(1)} %copy-done.8), kind=kOutput, calls=%fused_computation.34 | convolution fusion | flops 150998016 | bytes 3670784 | tf_op jit(solution)/shard_map/ota,tr->ora/dot_general | solution.py:85
  60.0 35.9 %all-to-all-done = bf16[64,128,128]{2,0,1:T(8,128)(2,1)} async-done(((bf16[64,128,128]{2,0,1:T(8,128)(2,1)}), bf16[64,128,128]{2,0,1:T(8,128)(2,1)}, u32[]{:S(2)}, u32[]{:S(2)}) %all-to-all-start) | async-done | bytes 2097184 | tf_op jit(solution)/shard_map/all_to_all | solution.py:77
  95.9 5.8 %convolution_bitcast_fusion = f32[64,128,128]{2,0,1:T(8,128)S(1)} fusion(bf16[64,128,128]{2,0,1:T(8,128)(2,1)} %all-to-all-done, bf16[128,128,128]{2,1,0:T(8,128)(2,1)} %gather_fusion.3, pred[128]{0:T(512)(128)(4,1)S(1)} %fusion.40), kind=kOutput, calls=%fused_computation.22 | convolution fusion | flops 270532608 | bytes 10485888 | tf_op jit(solution)/shard_map/oqb,qab->oqa/dot_general | solution.py:91
  101.7 3.3 %fusion.18 = f32[64,16,128]{2,1,0:T(8,128)S(1)} fusion(f32[64,128,128]{2,0,1:T(8,128)S(1)} %convolution_bitcast_fusion, f32[128]{0:T(128)S(1)} %convert_element_type.62, s32[128]{0:T(128)S(1)} %get-tuple-element.44), kind=kOutput, calls=%fused_computation.32 | convolution fusion | flops 100667392 | bytes 4719616 | tf_op jit(solution)/shard_map/oqa,qr->ora/dot_general | solution.py:94
  108.7 5.7 %convert_bitcast_fusion = bf16[64,128,128]{2,0,1:T(8,128)(2,1)} fusion(bf16[128,64,128]{2,1,0:T(8,128)(2,1)} %gather_fusion.4, bf16[128,128,128]{2,1,0:T(8,128)(2,1)} %gather_fusion.3, pred[128]{0:T(512)(128)(4,1)S(1)} %fusion.40), kind=kOutput, calls=%fused_computation.27 | convolution fusion | flops 271581184 | bytes 8388736 | tf_op jit(solution)/shard_map/oqa,qab->oqb/dot_general | solution.py:113
  114.4 9.4 %all-to-all-start.1 = ((bf16[64,128,128]{2,0,1:T(8,128)(2,1)}), bf16[64,128,128]{2,0,1:T(8,128)(2,1)}, u32[]{:S(2)}, u32[]{:S(2)}) async-start(bf16[64,128,128]{2,0,1:T(8,128)(2,1)} %convert_bitcast_fusion), calls=%async_computation.1 | async-start | bytes 4194304 | tf_op jit(solution)/shard_map/all_to_all | solution.py:116
  126.3 4.9 %collective-permute-start.4 = (bf16[256,64]{0,1:T(8,128)(2,1)S(1)}, bf16[256,64]{0,1:T(8,128)(2,1)S(1)}, u32[]{:S(2)}, u32[]{:S(2)}) collective-permute-start(bf16[256,64]{0,1:T(8,128)(2,1)S(1)} %copy-done.7), channel_id=1, source_target_pairs={{0,2},{1,3},{2,0},{3,1},{4,6},{5,7},{6,4},{7,5},{8,10},{9,11},{10,... | collective-permute-start | bytes 98312 | tf_op jit(solution)/shard_map/ppermute | solution.py:27
  131.2 2.8 %collective-permute-start.5 = (bf16[256,64]{0,1:T(8,128)(2,1)S(1)}, bf16[256,64]{0,1:T(8,128)(2,1)S(1)}, u32[]{:S(2)}, u32[]{:S(2)}) collective-permute-start(bf16[256,64]{0,1:T(8,128)(2,1)S(1)} %copy-done.7), channel_id=1, source_target_pairs={{0,3},{1,2},{2,1},{3,0},{4,7},{5,6},{6,5},{7,4},{8,11},{9,10},{10,... | collective-permute-start | bytes 98312 | tf_op jit(solution)/shard_map/ppermute | solution.py:27
  135.9 2.4 %convolution_bitcast_fusion.1 = f32[64,96,128]{2,0,1:T(8,128)S(1)} fusion(bf16[96,128,128]{2,1,0:T(8,128)(2,1)S(1)} %copy-done, bf16[96,64,128]{2,1,0:T(8,128)(2,1)} %gather_fusion.5), kind=kOutput, calls=%fused_computation.28 | convolution fusion | flops 201326592 | bytes 7864320 | tf_op jit(solution)/shard_map/ota,tab->otb/dot_general | solution.py:102
  138.3 4.1 %fusion.2 = f32[16,64,128]{2,0,1:T(8,128)} fusion(f32[64,96,128]{2,0,1:T(8,128)S(1)} %convolution_bitcast_fusion.1, f32[96]{0:T(128)S(1)} %copy-done.11, s32[96]{0:T(128)S(1)} %copy-done.9), kind=kOutput, calls=%fused_computation.10 | convolution fusion | flops 150998016 | bytes 3670784 | tf_op jit(solution)/shard_map/otb,tr->orb/dot_general | solution.py:109
  143.1 31.6 %all-to-all-done.1 = bf16[64,128,128]{2,0,1:T(8,128)(2,1)} async-done(((bf16[64,128,128]{2,0,1:T(8,128)(2,1)}), bf16[64,128,128]{2,0,1:T(8,128)(2,1)}, u32[]{:S(2)}, u32[]{:S(2)}) %all-to-all-start.1) | async-done | bytes 2097184 | tf_op jit(solution)/shard_map/all_to_all | solution.py:116
  174.8 3.0 %fusion.27 = bf16[16,64,128]{2,0,1:T(8,128)(2,1)S(1)} fusion(f32[16,64,128]{2,0,1:T(8,128)} %fusion.2, bf16[64,128,128]{2,0,1:T(8,128)(2,1)} %all-to-all-done.1, s32[128]{0:T(128)S(1)} %copy-done.10), kind=kOutput, calls=%fused_computation.35 | convolution fusion | flops 33822720 | bytes 2884096 | tf_op jit(solution)/shard_map/oqb,qr->orb/dot_general | solution.py:120
  178.6 3.7 %collective-permute-start.8 = (bf16[64,2048]{1,0:T(8,128)(2,1)}, bf16[64,2048]{1,0:T(8,128)(2,1)}, u32[]{:S(2)}, u32[]{:S(2)}) collective-permute-start(bf16[64,2048]{1,0:T(8,128)(2,1)} %bitcast.102), channel_id=1, source_target_pairs={{0,3},{1,2},{2,1},{3,0},{4,7},{5,6},{6,5},{7,4},{8,11},{9,10},{10,... | collective-permute-start | bytes 786440 | tf_op jit(solution)/shard_map/ppermute | solution.py:144
  185.1 9.1 %all-to-all-start.2 = ((f32[128,2,128]{2,1,0:T(2,128)}), f32[128,2,128]{2,1,0:T(2,128)S(1)}, u32[]{:S(2)}, u32[]{:S(2)}) async-start(f32[128,2,128]{2,1,0:T(2,128)} %bitcast.114), calls=%async_computation.2 | async-start | bytes 262144 | tf_op jit(solution)/shard_map/all_to_all | solution.py:34
  198.0 9.0 %all-to-all-done.2 = f32[128,2,128]{2,1,0:T(2,128)S(1)} async-done(((f32[128,2,128]{2,1,0:T(2,128)}), f32[128,2,128]{2,1,0:T(2,128)S(1)}, u32[]{:S(2)}, u32[]{:S(2)}) %all-to-all-start.2) | async-done | bytes 131104 | tf_op jit(solution)/shard_map/all_to_all | solution.py:34
  207.8 5.8 %all-to-all-start.3 = ((f32[128,2,128]{2,1,0:T(2,128)}), f32[128,2,128]{2,1,0:T(2,128)S(1)}, u32[]{:S(2)}, u32[]{:S(2)}) async-start(f32[128,2,128]{2,1,0:T(2,128)} %broadcast_in_dim.87), calls=%async_computation.3 | async-start | bytes 262144 | tf_op jit(solution)/shard_map/all_to_all | solution.py:38
  213.6 3.4 %collective-permute-start.7 = (bf16[64,2048]{1,0:T(8,128)(2,1)}, bf16[64,2048]{1,0:T(8,128)(2,1)}, u32[]{:S(2)}, u32[]{:S(2)}) collective-permute-start(bf16[64,2048]{1,0:T(8,128)(2,1)} %bitcast.102), channel_id=1, source_target_pairs={{0,2},{1,3},{2,0},{3,1},{4,6},{5,7},{6,4},{7,5},{8,10},{9,11},{10,... | collective-permute-start | bytes 786440 | tf_op jit(solution)/shard_map/ppermute | solution.py:144
  221.5 5.0 %all-to-all-done.3 = f32[128,2,128]{2,1,0:T(2,128)S(1)} async-done(((f32[128,2,128]{2,1,0:T(2,128)}), f32[128,2,128]{2,1,0:T(2,128)S(1)}, u32[]{:S(2)}, u32[]{:S(2)}) %all-to-all-start.3) | async-done | bytes 131104 | tf_op jit(solution)/shard_map/all_to_all | solution.py:38
  (88 shorter events, 40.1 us)
Async XLA Ops:
  0.6 45.5 %copy-start = (bf16[96,128,128]{2,1,0:T(8,128)(2,1)S(1)}, bf16[96,128,128]{2,1,0:T(8,128)(2,1)}, u32[]{:S(2)}) copy-start(bf16[96,128,128]{2,1,0:T(8,128)(2,1)} %param.16) | copy-start | bytes 9437188
  0.6 14.1 %collective-permute-start = (bf16[64,2048]{1,0:T(8,128)(2,1)}, bf16[64,2048]{1,0:T(8,128)(2,1)}, u32[]{:S(2)}, u32[]{:S(2)}) collective-permute-start(bf16[64,2048]{1,0:T(8,128)(2,1)} %param.13), channel_id=1, source_target_pairs={{0,1},{1,0},{2,3},{3,2},{4,5},{5,4},{6,7},{7,6},{8,9},{9,8},{10,11... | collective-permute-start | bytes 786440 | tf_op jit(solution)/shard_map/ppermute | solution.py:27
  4.9 9.6 %collective-permute-start.2 = (bf16[64,2048]{1,0:T(8,128)(2,1)}, bf16[64,2048]{1,0:T(8,128)(2,1)S(1)}, u32[]{:S(2)}, u32[]{:S(2)}) collective-permute-start(bf16[64,2048]{1,0:T(8,128)(2,1)} %param.13), channel_id=1, source_target_pairs={{0,3},{1,2},{2,1},{3,0},{4,7},{5,6},{6,5},{7,4},{8,11},{9,10},{10,... | collective-permute-start | bytes 786440 | tf_op jit(solution)/shard_map/ppermute | solution.py:27
  8.6 9.0 %collective-permute-start.1 = (bf16[64,2048]{1,0:T(8,128)(2,1)}, bf16[64,2048]{1,0:T(8,128)(2,1)}, u32[]{:S(2)}, u32[]{:S(2)}) collective-permute-start(bf16[64,2048]{1,0:T(8,128)(2,1)} %param.13), channel_id=1, source_target_pairs={{0,2},{1,3},{2,0},{3,1},{4,6},{5,7},{6,4},{7,5},{8,10},{9,11},{10,... | collective-permute-start | bytes 786440 | tf_op jit(solution)/shard_map/ppermute | solution.py:27
  14.5 3.1 %copy-start.4 = (bf16[64,2048]{1,0:T(8,128)(2,1)}, bf16[64,2048]{1,0:T(8,128)(2,1)S(1)}, u32[]{:S(2)}) copy-start(bf16[64,2048]{1,0:T(8,128)(2,1)S(1)} %collective-permute-done.2) | copy-start | bytes 786436
  21.1 24.7 %copy-start.9 = (s32[96]{0:T(128)S(1)}, s32[96]{0:T(128)}, u32[]{:S(2)}) copy-start(s32[96]{0:T(128)} %param.18) | copy-start | bytes 1156
  21.1 24.9 %copy-start.12 = (bf16[64]{0:T(256)(128)(2,1)S(1)}, bf16[64]{0:T(256)(128)(2,1)}, u32[]{:S(2)}) copy-start(bf16[64]{0:T(256)(128)(2,1)} %param.15) | copy-start | bytes 388
  21.1 24.9 %copy-start.8 = (s32[96]{0:T(128)S(1)}, s32[96]{0:T(128)}, u32[]{:S(2)}) copy-start(s32[96]{0:T(128)} %param.17) | copy-start | bytes 1156
  21.1 74.8 %all-to-all-start = ((bf16[64,128,128]{2,0,1:T(8,128)(2,1)}), bf16[64,128,128]{2,0,1:T(8,128)(2,1)}, u32[]{:S(2)}, u32[]{:S(2)}) async-start(bf16[64,128,128]{2,0,1:T(8,128)(2,1)} %bitcast.109), calls=%async_computation | async-start | bytes 4194304 | tf_op jit(solution)/shard_map/all_to_all | solution.py:77
  51.2 2.4 %copy-start.1 = (bf16[96,64,128]{2,1,0:T(8,128)(2,1)S(1)}, bf16[96,64,128]{2,1,0:T(8,128)(2,1)}, u32[]{:S(2)}) copy-start(bf16[96,64,128]{2,1,0:T(8,128)(2,1)} %gather_fusion.1) | copy-start | bytes 4718596
  101.7 3.3 %copy-start.3 = (f32[64,16,128]{2,1,0:T(8,128)S(1)}, f32[64,16,128]{2,1,0:T(8,128)}, u32[]{:S(2)}) copy-start(f32[64,16,128]{2,1,0:T(8,128)} %fusion.24) | copy-start | bytes 1572868
  101.7 3.4 %copy-start.6 = (bf16[64,2048]{1,0:T(8,128)(2,1)S(1)}, bf16[64,2048]{1,0:T(8,128)(2,1)}, u32[]{:S(2)}) copy-start(bf16[64,2048]{1,0:T(8,128)(2,1)} %param.21) | copy-start | bytes 786436
  114.4 10.0 %copy-start.7 = (bf16[256,64]{0,1:T(8,128)(2,1)S(1)}, bf16[256,64]{0,1:T(8,128)(2,1)}, u32[]{:S(2)}) copy-start(bf16[256,64]{0,1:T(8,128)(2,1)} %param.14) | copy-start | bytes 98308
  114.4 60.4 %all-to-all-start.1 = ((bf16[64,128,128]{2,0,1:T(8,128)(2,1)}), bf16[64,128,128]{2,0,1:T(8,128)(2,1)}, u32[]{:S(2)}, u32[]{:S(2)}) async-start(bf16[64,128,128]{2,0,1:T(8,128)(2,1)} %convert_bitcast_fusion), calls=%async_computation.1 | async-start | bytes 4194304 | tf_op jit(solution)/shard_map/all_to_all | solution.py:116
  124.4 18.1 %collective-permute-start.3 = (bf16[256,64]{0,1:T(8,128)(2,1)S(1)}, bf16[256,64]{0,1:T(8,128)(2,1)S(1)}, u32[]{:S(2)}, u32[]{:S(2)}) collective-permute-start(bf16[256,64]{0,1:T(8,128)(2,1)S(1)} %copy-done.7), channel_id=1, source_target_pairs={{0,1},{1,0},{2,3},{3,2},{4,5},{5,4},{6,7},{7,6},{8,9},{9,8},{10,11... | collective-permute-start | bytes 98312 | tf_op jit(solution)/shard_map/ppermute | solution.py:27
  126.3 16.1 %collective-permute-start.4 = (bf16[256,64]{0,1:T(8,128)(2,1)S(1)}, bf16[256,64]{0,1:T(8,128)(2,1)S(1)}, u32[]{:S(2)}, u32[]{:S(2)}) collective-permute-start(bf16[256,64]{0,1:T(8,128)(2,1)S(1)} %copy-done.7), channel_id=1, source_target_pairs={{0,2},{1,3},{2,0},{3,1},{4,6},{5,7},{6,4},{7,5},{8,10},{9,11},{10,... | collective-permute-start | bytes 98312 | tf_op jit(solution)/shard_map/ppermute | solution.py:27
  131.2 11.2 %collective-permute-start.5 = (bf16[256,64]{0,1:T(8,128)(2,1)S(1)}, bf16[256,64]{0,1:T(8,128)(2,1)S(1)}, u32[]{:S(2)}, u32[]{:S(2)}) collective-permute-start(bf16[256,64]{0,1:T(8,128)(2,1)S(1)} %copy-done.7), channel_id=1, source_target_pairs={{0,3},{1,2},{2,1},{3,0},{4,7},{5,6},{6,5},{7,4},{8,11},{9,10},{10,... | collective-permute-start | bytes 98312 | tf_op jit(solution)/shard_map/ppermute | solution.py:27
  138.3 36.5 %copy-start.10 = (s32[128]{0:T(128)S(1)}, s32[128]{0:T(128)}, u32[]{:S(2)}) copy-start(s32[128]{0:T(128)} %param.20) | copy-start | bytes 1540
  174.8 7.5 %copy-start.2 = (bf16[256,2048]{1,0:T(8,128)(2,1)S(1)}, bf16[256,2048]{1,0:T(8,128)(2,1)}, u32[]{:S(2)}) copy-start(bf16[256,2048]{1,0:T(8,128)(2,1)} %pad_maximum_fusion) | copy-start | bytes 3145732
  178.6 38.5 %collective-permute-start.8 = (bf16[64,2048]{1,0:T(8,128)(2,1)}, bf16[64,2048]{1,0:T(8,128)(2,1)}, u32[]{:S(2)}, u32[]{:S(2)}) collective-permute-start(bf16[64,2048]{1,0:T(8,128)(2,1)} %bitcast.102), channel_id=1, source_target_pairs={{0,3},{1,2},{2,1},{3,0},{4,7},{5,6},{6,5},{7,4},{8,11},{9,10},{10,... | collective-permute-start | bytes 786440 | tf_op jit(solution)/shard_map/ppermute | solution.py:144
  185.1 21.9 %all-to-all-start.2 = ((f32[128,2,128]{2,1,0:T(2,128)}), f32[128,2,128]{2,1,0:T(2,128)S(1)}, u32[]{:S(2)}, u32[]{:S(2)}) async-start(f32[128,2,128]{2,1,0:T(2,128)} %bitcast.114), calls=%async_computation.2 | async-start | bytes 262144 | tf_op jit(solution)/shard_map/all_to_all | solution.py:34
  194.2 25.0 %collective-permute-start.6 = (bf16[64,2048]{1,0:T(8,128)(2,1)}, bf16[64,2048]{1,0:T(8,128)(2,1)}, u32[]{:S(2)}, u32[]{:S(2)}) collective-permute-start(bf16[64,2048]{1,0:T(8,128)(2,1)} %bitcast.102), channel_id=1, source_target_pairs={{0,1},{1,0},{2,3},{3,2},{4,5},{5,4},{6,7},{7,6},{8,9},{9,8},{10,11... | collective-permute-start | bytes 786440 | tf_op jit(solution)/shard_map/ppermute | solution.py:144
  207.8 18.6 %all-to-all-start.3 = ((f32[128,2,128]{2,1,0:T(2,128)}), f32[128,2,128]{2,1,0:T(2,128)S(1)}, u32[]{:S(2)}, u32[]{:S(2)}) async-start(f32[128,2,128]{2,1,0:T(2,128)} %broadcast_in_dim.87), calls=%async_computation.3 | async-start | bytes 262144 | tf_op jit(solution)/shard_map/all_to_all | solution.py:38
  213.6 14.9 %collective-permute-start.7 = (bf16[64,2048]{1,0:T(8,128)(2,1)}, bf16[64,2048]{1,0:T(8,128)(2,1)}, u32[]{:S(2)}, u32[]{:S(2)}) collective-permute-start(bf16[64,2048]{1,0:T(8,128)(2,1)} %bitcast.102), channel_id=1, source_target_pairs={{0,2},{1,3},{2,0},{3,1},{4,6},{5,7},{6,4},{7,5},{8,10},{9,11},{10,... | collective-permute-start | bytes 786440 | tf_op jit(solution)/shard_map/ppermute | solution.py:144
  (2 other events, 3.0 us)
